TPU v7x, 128 devices: a whole 4x4x4 slice. The times are simulated.
128 devices in a mesh: pts: 8 (over y, core), cen: 16 (over x, z).
Axes of the slice: x: 4, y: 4, z: 4, core: 2. Of those that a mesh axis runs over, the one named last changes fastest.
Arguments:
- points: bfloat16 [16384, 768], P('pts', 'cen'), may hold values from -6 to 6
- centroids: bfloat16 [32768, 768], P('cen'), may hold values from -6 to 6
Outputs:
- new_centroids: float32 [32768, 768], P('cen', 'pts')
- masses: float32 [32768], P('cen')
All inputs are finite; a program needn't handle non-finite values.
Results may differ from a plain program's by a relative error of at most 0.00089.
Values may be sent and summed in bfloat16 or wider, within the bound.
No kernel may reach another device: no remote copies, remote signals or barrier semaphores. Data moves between devices by JAX's collectives and lax.ppermute only.
A program may use at most 128 MiB of HBM per device.

v0:
```python
import jax
import jax.numpy as jnp
from jax import lax
from jax.sharding import PartitionSpec as P

ITERS = 3


temper = 0.05


def unit_rows(values):
    wide = values.astype(jnp.float32)
    return (wide * lax.rsqrt(jnp.mean(wide * wide, axis=1, keepdims=True) + 1e-06)).astype(
        jnp.bfloat16
    )


def column_total(col_part):
    return lax.psum(col_part, "pts")


def row_total(row_part):
    return lax.psum(row_part, "cen")


def weighted_sum(weights, point_rows):
    return lax.dot_general(
        weights,
        point_rows.astype(jnp.float32),
        (((0,), (0,)), ((), ())),
        precision=lax.Precision.HIGHEST,
        preferred_element_type=jnp.float32,
    )


def local(points, centroids):
    gathered = lax.all_gather(points, "cen", axis=1, tiled=True)
    unit_points = unit_rows(gathered)
    unit_centroids = unit_rows(centroids)
    width = gathered.shape[1]
    local_pts = gathered.shape[0]
    local_cen = centroids.shape[0]
    balance = local_pts * lax.axis_size("pts") / (local_cen * lax.axis_size("cen"))
    row_scale = jnp.ones((local_pts,), jnp.float32)
    col_scale = jnp.ones((local_cen,), jnp.float32)
    scores = jnp.dot(unit_points, unit_centroids.T, preferred_element_type=jnp.float32)
    kernel = jnp.exp(scores / (width * temper))
    for sweep in range(ITERS):
        col_part = jnp.sum(kernel * row_scale[:, None], axis=0)
        col_scale = balance / column_total(col_part)
        row_part = jnp.sum(kernel * col_scale[None, :], axis=1)
        row_scale = 1.0 / row_total(row_part)
    weights = row_scale[:, None] * kernel * col_scale[None, :]
    partial_value = weighted_sum(weights, gathered)
    mass_part = jnp.sum(weights, axis=0) / balance
    moved = lax.psum_scatter(partial_value, "pts", scatter_dimension=1, tiled=True)
    squares = jnp.sum(moved * moved, axis=1)
    squares, masses = lax.psum((squares, mass_part), "pts")
    new_centroids = moved * lax.rsqrt(squares / width + 1e-06)[:, None]
    return (new_centroids, masses)


def solution(mesh):
    in_specs = (P("pts", "cen"), P("cen", None))
    out_specs = (P("cen", "pts"), P("cen"))
    return jax.shard_map(local, mesh=mesh, in_specs=in_specs, out_specs=out_specs, check_vma=False)
```

profile of v0, /device:TPU:0, one launch (start us, length us, event | category | flops | bytes accessed | tf_op | source)
XLA Modules:
  0.0 361.0 jit_solution(312511793301997710)
XLA Ops:
  7.2 0.0 all-gather.2.cloned.1.call-start
  7.2 0.7 all-gather.2.cloned.1.call-update
  7.9 0.0 reduce-scatter.2.cloned.1.call-start
  7.9 2.6 fusion.6
  10.5 50.1 %all-gather.2.cloned.1.call-done = bf16[2048,768]{0,1:T(8,128)(2,1)} async-done(((bf16[2048,48]{0,1:T(8,128)(2,1)}), bf16[2048,768]{0,1:T(8,128)(2,1)}) %all-gather.2.cloned.1.call-update) | async-done | bytes 3145744 | tf_op jit(solution)/shard_map/all_gather | solution.py:38
  60.6 2.6 fusion.4
  63.2 14.0 %fusion.12 = (f32[2048]{0:T(1024)S(1)}, f32[2048,2048]{1,0:T(8,128)}) fusion(bf16[2048,768]{1,0:T(8,128)(2,1)} %param.3, f32[2048]{0:T(1024)S(1)} %add_rsqrt_fusion.1, bf16[2048,768]{0,1:T(8,128)(2,1)} %all-gather.2.cloned.1.call-done, f32[2048]{0:T(1024)S(1)} %add_rsqrt_fusion.2), kind=kOutput, calls=%fused_computation.33 | convolution fusion | flops 6460274688 | bytes 23093248 | tf_op jit(solution)/shard_map/dot_general | solution.py:47
  77.2 14.2 %psum.56 = f32[2048]{0:T(1024)S(1)} all-reduce(f32[2048]{0:T(1024)S(1)} %get-tuple-element.4), channel_id=1, replica_groups=mesh['pts'=8,'cen'=16] {'pts'}, use_global_device_ids=true, to_apply=%region_3.0 | all-reduce | flops 2048 | bytes 16384 | tf_op jit(solution)/shard_map/psum | solution.py:20
  91.4 7.0 %multiply_reduce_fusion.4 = f32[2048]{0:T(1024)S(1)} fusion(f32[2048,2048]{1,0:T(8,128)} %get-tuple-element.5, f32[2048]{0:T(1024)S(1)} %broadcast_divide_fusion.2), kind=kLoop, calls=%fused_computation.5 | loop fusion | flops 8386560 | bytes 16793600 | tf_op jit(solution)/shard_map/reduce_sum | solution.py:52
  98.4 38.6 %psum.57 = f32[2048]{0:T(1024)S(1)} all-reduce(f32[2048]{0:T(1024)S(1)} %multiply_reduce_fusion.4), channel_id=1, replica_groups=mesh['pts'=8,'cen'=16] {'cen'}, use_global_device_ids=true, to_apply=%region_5.0 | all-reduce | flops 2048 | bytes 16384 | tf_op jit(solution)/shard_map/psum | solution.py:24
  137.1 6.9 %multiply_reduce_fusion.3 = f32[2048]{0:T(1024)S(1)} fusion(f32[2048,2048]{1,0:T(8,128)} %get-tuple-element.5, f32[2048]{0:T(1024)S(1)} %broadcast_divide_fusion.5), kind=kLoop, calls=%fused_computation.4 | loop fusion | flops 8386560 | bytes 16793600 | tf_op jit(solution)/shard_map/reduce_sum | solution.py:50
  144.0 12.7 %psum.58 = f32[2048]{0:T(1024)S(1)} all-reduce(f32[2048]{0:T(1024)S(1)} %multiply_reduce_fusion.3), channel_id=1, replica_groups=mesh['pts'=8,'cen'=16] {'pts'}, use_global_device_ids=true, to_apply=%region_7.0 | all-reduce | flops 2048 | bytes 16384 | tf_op jit(solution)/shard_map/psum | solution.py:20
  156.7 7.0 %multiply_reduce_fusion.2 = f32[2048]{0:T(1024)S(1)} fusion(f32[2048,2048]{1,0:T(8,128)} %get-tuple-element.5, f32[2048]{0:T(1024)S(1)} %broadcast_divide_fusion.1), kind=kLoop, calls=%fused_computation.3 | loop fusion | flops 8386560 | bytes 16793600 | tf_op jit(solution)/shard_map/reduce_sum | solution.py:52
  163.7 36.0 %psum.59 = f32[2048]{0:T(1024)S(1)} all-reduce(f32[2048]{0:T(1024)S(1)} %multiply_reduce_fusion.2), channel_id=1, replica_groups=mesh['pts'=8,'cen'=16] {'cen'}, use_global_device_ids=true, to_apply=%region_9.0 | all-reduce | flops 2048 | bytes 16384 | tf_op jit(solution)/shard_map/psum | solution.py:24
  199.7 0.0 copy-start
  199.7 7.1 %multiply_reduce_fusion.1 = f32[2048]{0:T(1024)S(1)} fusion(f32[2048,2048]{1,0:T(8,128)} %get-tuple-element.5, f32[2048]{0:T(1024)S(1)} %broadcast_divide_fusion.4), kind=kLoop, calls=%fused_computation.2 | loop fusion | flops 8386560 | bytes 16793600 | tf_op jit(solution)/shard_map/reduce_sum | solution.py:50
  206.8 12.8 %psum.60 = f32[2048]{0:T(1024)S(1)} all-reduce(f32[2048]{0:T(1024)S(1)} %multiply_reduce_fusion.1), channel_id=1, replica_groups=mesh['pts'=8,'cen'=16] {'pts'}, use_global_device_ids=true, to_apply=%region_11.0 | all-reduce | flops 2048 | bytes 16384 | tf_op jit(solution)/shard_map/psum | solution.py:20
  219.7 6.9 %multiply_reduce_fusion = f32[2048]{0:T(1024)S(1)} fusion(f32[2048,2048]{1,0:T(8,128)} %get-tuple-element.5, f32[2048]{0:T(1024)S(1)} %broadcast_divide_fusion), kind=kLoop, calls=%fused_computation.1 | loop fusion | flops 8386560 | bytes 16793600 | tf_op jit(solution)/shard_map/reduce_sum | solution.py:52
  226.6 38.0 %psum.61 = f32[2048]{0:T(1024)S(1)} all-reduce(f32[2048]{0:T(1024)S(1)} %multiply_reduce_fusion), channel_id=1, replica_groups=mesh['pts'=8,'cen'=16] {'cen'}, use_global_device_ids=true, to_apply=%region_13.0 | all-reduce | flops 2048 | bytes 16384 | tf_op jit(solution)/shard_map/psum | solution.py:24
  264.6 0.0 copy-done
  264.6 24.8 %fusion.1 = f32[2048,768]{0,1:T(8,128)} fusion(bf16[2048,768]{0,1:T(8,128)(2,1)S(1)} %copy-done, f32[2048,2048]{1,0:T(8,128)} %get-tuple-element.5, f32[2048]{0:T(1024)S(1)} %broadcast_divide_fusion.3, f32[2048]{0:T(1024)S(1)} %broadcast_divide_fusion), kind=kOutput, calls=%fused_computation.8 | convolution fusion | flops 38663094272 | bytes 26230784 | tf_op jit(solution)/shard_map/dot_general | solution.py:28
  289.4 0.0 reduce-scatter.2.cloned.1.call-update
  289.4 8.1 %fusion = f32[2048]{0:T(1024)S(1)} fusion(f32[2048,2048]{1,0:T(8,128)} %get-tuple-element.5, f32[2048]{0:T(1024)S(1)} %broadcast_divide_fusion.3, f32[2048]{0:T(1024)S(1)} %broadcast_divide_fusion), kind=kLoop, calls=%fused_computation.7 | loop fusion | flops 12580864 | bytes 16801792 | tf_op jit(solution)/shard_map/reduce_sum | solution.py:56
  297.5 27.9 %reduce-scatter.2.cloned.1.call-done = f32[2048,96]{0,1:T(8,128)} async-done(((f32[2048,768]{0,1:T(8,128)}), f32[2048,96]{0,1:T(8,128)}) %reduce-scatter.2.cloned.1.call-update) | async-done | bytes 786448 | tf_op jit(solution)/shard_map/reduce_scatter | solution.py:57
  325.4 1.2 multiply_reduce_fusion.5
  326.6 25.4 %all-reduce = (f32[2048]{0:T(1024)S(1)}, f32[2048]{0:T(1024)}) all-reduce(f32[2048]{0:T(1024)S(1)} %multiply_reduce_fusion.5, f32[2048]{0:T(1024)S(1)} %broadcast_multiply_fusion.1), channel_id=1, replica_groups=mesh['pts'=8,'cen'=16] {'pts'}, use_global_device_ids=true, to_apply=%region_16.0 | all-reduce | flops 4096 | bytes 32768 | tf_op jit(solution)/shard_map/psum | solution.py:59
  352.0 2.1 broadcast_multiply_fusion
  (10 shorter events, 0.1 us)
Async XLA Ops:
  7.2 53.4 %all-gather.2.cloned.1.call-start = ((), (), s32[]{:S(2)}) async-start(), calls=%async_computation.1 | async-start | bytes 3342336 | tf_op jit(solution)/shard_map/all_gather | solution.py:38
  7.9 317.5 %reduce-scatter.2.cloned.1.call-start = ((), (), s32[]{:S(2)}) async-start(), calls=%async_computation.2 | async-start | bytes 7077888 | tf_op jit(solution)/shard_map/reduce_scatter | solution.py:57
  199.7 64.9 %copy-start = (bf16[2048,768]{0,1:T(8,128)(2,1)S(1)}, bf16[2048,768]{0,1:T(8,128)(2,1)}, u32[]{:S(2)}) copy-start(bf16[2048,768]{0,1:T(8,128)(2,1)} %all-gather.2.cloned.1.call-done) | copy-start | bytes 9437188
Sparse Core Ops, SparseCore 0:
  10.2 50.3 all-gather.1
  289.5 35.8 reduce-scatter.1
where the time goes:
time: 362 us; the launch traced here: 361 us
  blocking collectives  178 us (49%)
  waiting for transfers between devices  78.7 us (22%)
  other arithmetic  51.5 us (14%)
  matrix products  38.8 us (11%)
  between operations  14.2 us (4%)
    psum x3, blocking collectives, row_total(): return lax.psum(row_part, 'cen')  113 us
    all_gather x1, waiting for transfers between devices, local(): gathered = lax.all_gather(points, 'cen', axis=1, tiled=True)  50.1 us
    psum x3, blocking collectives, column_total(): return lax.psum(col_part, 'pts')  39.7 us
    reduce_scatter x1, waiting for transfers between devices, local(): lax.psum_scatter(partial_value, 'pts', scatter_dimension=1, tiled=True)  27.9 us
    psum x1, blocking collectives, local(): squares, masses = lax.psum((squares, mass_part), 'pts')  25.4 us
    dot_general x1, matrix products, weighted_sum(): lax.dot_general(weights, point_rows.astype(jnp.float32), (((0,), (0,)), (...  24.8 us
    reduce_sum x3, other arithmetic, local(): row_part = jnp.sum(kernel * col_scale[None, :], axis=1)  20.9 us
    dot_general x1, matrix products, local(): jnp.dot(unit_points, unit_centroids.T, preferred_element_type=jnp.float32)  14 us
  transfers between devices with their start and end apart: 2, of which 2 were waited for; matrix products, arithmetic and copies ran while one was open for 3% of the time, Pallas kernels for 0%

commit v1 on v0

v1 whole, which is shorter than its diff:
```python
import jax
import jax.numpy as jnp
from jax import lax
from jax.sharding import Mesh
from jax.sharding import PartitionSpec as P

ITERS = 3


temper = 0.05

PTS_AXES = ("y", "c")
CEN_AXES = ("x", "z")


def unit_rows(values):
    wide = values.astype(jnp.float32)
    return (wide * lax.rsqrt(jnp.mean(wide * wide, axis=1, keepdims=True) + 1e-06)).astype(
        jnp.bfloat16
    )


def axis_sum(v, axis, n):
    if n == 1:
        return v
    got = [v] + [
        lax.ppermute(v, axis, [(i, (i + s) % n) for i in range(n)]) for s in range(1, n)
    ]
    if n == 2:
        return got[0] + got[1]
    if n == 4:
        return (got[0] + got[2]) + (got[1] + got[3])
    idx = lax.axis_index(axis)
    canon = jnp.stack(got)[(idx - jnp.arange(n)) % n]
    total = canon[0]
    for j in range(1, n):
        total = total + canon[j]
    return total


def multi_sum(v, axes):
    for axis, n in axes:
        v = axis_sum(v, axis, n)
    return v


def weighted_sum(weights, point_rows):
    return lax.dot_general(
        weights,
        point_rows.astype(jnp.float32),
        (((0,), (0,)), ((), ())),
        precision=lax.Precision.HIGHEST,
        preferred_element_type=jnp.float32,
    )


def make_local(sizes):
    pts_red = [("c", sizes["c"]), ("y", sizes["y"])]
    cen_red = [("z", sizes["z"]), ("x", sizes["x"])]

    def local(points, centroids):
        gathered = lax.all_gather(points, CEN_AXES, axis=1, tiled=True)
        unit_points = unit_rows(gathered)
        unit_centroids = unit_rows(centroids)
        width = gathered.shape[1]
        local_pts = gathered.shape[0]
        local_cen = centroids.shape[0]
        n_pts = sizes["y"] * sizes["c"]
        n_cen = sizes["x"] * sizes["z"]
        balance = local_pts * n_pts / (local_cen * n_cen)
        row_scale = jnp.ones((local_pts,), jnp.float32)
        col_scale = jnp.ones((local_cen,), jnp.float32)
        scores = jnp.dot(unit_points, unit_centroids.T, preferred_element_type=jnp.float32)
        kernel = jnp.exp(scores / (width * temper))
        for sweep in range(ITERS):
            col_part = jnp.sum(kernel * row_scale[:, None], axis=0)
            col_scale = balance / multi_sum(col_part, pts_red)
            row_part = jnp.sum(kernel * col_scale[None, :], axis=1)
            row_scale = 1.0 / multi_sum(row_part, cen_red)
        weights = row_scale[:, None] * kernel * col_scale[None, :]
        partial_value = weighted_sum(weights, gathered)
        mass_part = jnp.sum(weights, axis=0) / balance
        moved = lax.psum_scatter(partial_value, PTS_AXES, scatter_dimension=1, tiled=True)
        squares = jnp.sum(moved * moved, axis=1)
        both = multi_sum(jnp.stack([squares, mass_part]), pts_red)
        squares, masses = both[0], both[1]
        new_centroids = moved * lax.rsqrt(squares / width + 1e-06)[:, None]
        return (new_centroids, masses)

    return local


def solution(mesh):
    pts_n, cen_n = mesh.shape["pts"], mesh.shape["cen"]
    cores = 2 if pts_n % 2 == 0 else 1
    zs = 4 if cen_n % 4 == 0 else 1
    sizes = {"y": pts_n // cores, "c": cores, "x": cen_n // zs, "z": zs}
    mesh4 = Mesh(
        mesh.devices.reshape(sizes["y"], sizes["c"], sizes["x"], sizes["z"]),
        ("y", "c", "x", "z"),
    )
    in_specs = (P(PTS_AXES, CEN_AXES), P(CEN_AXES, None))
    out_specs = (P(CEN_AXES, PTS_AXES), P(CEN_AXES))
    return jax.shard_map(
        make_local(sizes), mesh=mesh4, in_specs=in_specs, out_specs=out_specs, check_vma=False
    )
```

time: 362 us -> 274 us (0.76)
  blocking collectives: 178 us -> 0 us
  waiting for transfers between devices: 78.7 us -> 131 us
  starting transfers between devices: 0.08 us -> 36.8 us
    psum x7 -> x0, blocking collectives: 178 us -> none  [the longest x3 113 us: row_total(): return lax.psum(row_part, 'cen')]
    ppermute x0 -> x34, waiting for transfers between devices: none -> 52.6 us  [axis_sum(): lax.ppermute(v, axis, [(i, (i + s) % n) for i in range(n)])]
    ppermute x0 -> x34, starting transfers between devices: none -> 36.7 us  [axis_sum(): lax.ppermute(v, axis, [(i, (i + s) % n) for i in range(n)])]
  transfers between devices with their start and end apart: 2 -> 36, of which waited for: 2 -> 26; matrix products, arithmetic and copies ran while one was open for 3% -> 4% of each run, Pallas kernels for 0% -> 0%
where the time goes in v1:
time: 274 us
  waiting for transfers between devices  131 us (48%)
  other arithmetic  52.3 us (19%)
  matrix products  39 us (14%)
  starting transfers between devices  36.8 us (13%)
  between operations  14.2 us (5%)
    ppermute x34, waiting for transfers between devices, axis_sum(): lax.ppermute(v, axis, [(i, (i + s) % n) for i in range(n)])  52.6 us
    all_gather x1, waiting for transfers between devices, local(): gathered = lax.all_gather(points, CEN_AXES, axis=1, tiled=True)  50.1 us
    ppermute x34, starting transfers between devices, axis_sum(): lax.ppermute(v, axis, [(i, (i + s) % n) for i in range(n)])  36.7 us
    reduce_scatter x1, waiting for transfers between devices, local(): lax.psum_scatter(partial_value, PTS_AXES, scatter_dimension=1, tiled=True)  27.9 us
    dot_general x1, matrix products, weighted_sum(): lax.dot_general(weights, point_rows.astype(jnp.float32), (((0,), (0,)), (...  24.8 us
    reduce_sum x3, other arithmetic, local(): row_part = jnp.sum(kernel * col_scale[None, :], axis=1)  21 us
    dot_general x1, matrix products, local(): jnp.dot(unit_points, unit_centroids.T, preferred_element_type=jnp.float32)  14.2 us
    reduce_sum x2, other arithmetic, local(): col_part = jnp.sum(kernel * row_scale[:, None], axis=0)  14 us
  transfers between devices with their start and end apart: 36, of which 26 were waited for; matrix products, arithmetic and copies ran while one was open for 4% of the time, Pallas kernels for 0%

profile of v1, /device:TPU:0, one launch (start us, length us, event | category | flops | bytes accessed | tf_op | source)
XLA Modules:
  0.0 273.6 jit_solution(4073084074301750110)
XLA Ops:
  7.9 2.6 fusion.6
  10.5 50.1 %all-gather.2.cloned.1.call-done = bf16[2048,768]{0,1:T(8,128)(2,1)} async-done(((bf16[2048,48]{0,1:T(8,128)(2,1)}), bf16[2048,768]{0,1:T(8,128)(2,1)}) %all-gather.2.cloned.1.call-update) | async-done | bytes 3145744 | tf_op jit(solution)/shard_map/all_gather | solution.py:62
  60.6 2.6 fusion.4
  63.2 14.2 %fusion.16 = (f32[2048]{0:T(1024)S(1)}, f32[2048,2048]{1,0:T(8,128)}) fusion(bf16[2048,768]{1,0:T(8,128)(2,1)} %param.3, f32[2048]{0:T(1024)S(1)} %add_rsqrt_fusion, bf16[2048,768]{0,1:T(8,128)(2,1)} %all-gather.2.cloned.1.call-done, f32[2048]{0:T(1024)S(1)} %add_rsqrt_fusion.1), kind=kOutput, calls=%fused_computation.42 | convolution fusion | flops 6460274688 | bytes 23093248 | tf_op jit(solution)/shard_map/dot_general | solution.py:73
  83.6 3.3 %collective-permute-done.1 = f32[2048]{0:T(1024)S(1)} collective-permute-done((f32[2048]{0:T(1024)S(1)}, f32[2048]{0:T(1024)S(1)}, u32[]{:S(2)}, u32[]{:S(2)}) %collective-permute-start.1) | collective-permute-done | bytes 8224 | tf_op jit(solution)/shard_map/ppermute | solution.py:27
  86.9 7.0 %multiply_reduce_fusion.4 = f32[2048]{0:T(1024)S(1)} fusion(f32[2048,2048]{1,0:T(8,128)} %get-tuple-element.5, f32[2048]{0:T(1024)S(1)} %add_divide_fusion.5), kind=kLoop, calls=%fused_computation.5 | loop fusion | flops 8386560 | bytes 16793600 | tf_op jit(solution)/shard_map/reduce_sum | solution.py:78
  94.5 2.7 %collective-permute-start.6 = (f32[2048]{0:T(1024)S(1)}, f32[2048]{0:T(1024)S(1)}, u32[]{:S(2)}, u32[]{:S(2)}) collective-permute-start(f32[2048]{0:T(1024)S(1)} %multiply_reduce_fusion.4), channel_id=1, source_target_pairs={{0,3},{1,0},{2,1},{3,2},{4,7},{5,4},{6,5},{7,6},{8,11},{9,8},{10,9... | collective-permute-start | bytes 24584 | tf_op jit(solution)/shard_map/ppermute | solution.py:27
  98.8 3.5 %collective-permute-done.4 = f32[2048]{0:T(1024)S(1)} collective-permute-done((f32[2048]{0:T(1024)S(1)}, f32[2048]{0:T(1024)S(1)}, u32[]{:S(2)}, u32[]{:S(2)}) %collective-permute-start.4) | collective-permute-done | bytes 8224 | tf_op jit(solution)/shard_map/ppermute | solution.py:27
  102.9 2.7 %collective-permute-start.9 = (f32[2048]{0:T(1024)S(1)}, f32[2048]{0:T(1024)S(1)}, u32[]{:S(2)}, u32[]{:S(2)}) collective-permute-start(f32[2048]{0:T(1024)S(1)} %add_add_fusion.3), channel_id=1, source_target_pairs={{0,12},{4,0},{8,4},{12,8},{1,13},{5,1},{9,5},{13,9},{2,14},{6,2},{... | collective-permute-start | bytes 24584 | tf_op jit(solution)/shard_map/ppermute | solution.py:27
  107.2 3.5 %collective-permute-done.7 = f32[2048]{0:T(1024)S(1)} collective-permute-done((f32[2048]{0:T(1024)S(1)}, f32[2048]{0:T(1024)S(1)}, u32[]{:S(2)}, u32[]{:S(2)}) %collective-permute-start.7) | collective-permute-done | bytes 8224 | tf_op jit(solution)/shard_map/ppermute | solution.py:27
  110.8 6.9 %multiply_reduce_fusion.3 = f32[2048]{0:T(1024)S(1)} fusion(f32[2048,2048]{1,0:T(8,128)} %get-tuple-element.5, f32[2048]{0:T(1024)S(1)} %add_divide_fusion.4), kind=kLoop, calls=%fused_computation.4 | loop fusion | flops 8386560 | bytes 16793600 | tf_op jit(solution)/shard_map/reduce_sum | solution.py:76
  119.4 3.0 %collective-permute-start.13 = (f32[2048]{0:T(1024)S(1)}, f32[2048]{0:T(1024)S(1)}, u32[]{:S(2)}, u32[]{:S(2)}) collective-permute-start(f32[2048]{0:T(1024)S(1)} %add.141), channel_id=1, source_target_pairs={{0,96},{32,0},{64,32},{96,64},{1,97},{33,1},{65,33},{97,65},{2,98}... | collective-permute-start | bytes 24584 | tf_op jit(solution)/shard_map/ppermute | solution.py:27
  124.0 3.5 %collective-permute-done.11 = f32[2048]{0:T(1024)S(1)} collective-permute-done((f32[2048]{0:T(1024)S(1)}, f32[2048]{0:T(1024)S(1)}, u32[]{:S(2)}, u32[]{:S(2)}) %collective-permute-start.11) | collective-permute-done | bytes 8224 | tf_op jit(solution)/shard_map/ppermute | solution.py:27
  127.6 7.0 %multiply_reduce_fusion.2 = f32[2048]{0:T(1024)S(1)} fusion(f32[2048,2048]{1,0:T(8,128)} %get-tuple-element.5, f32[2048]{0:T(1024)S(1)} %add_divide_fusion.3), kind=kLoop, calls=%fused_computation.3 | loop fusion | flops 8386560 | bytes 16793600 | tf_op jit(solution)/shard_map/reduce_sum | solution.py:78
  134.7 3.2 %collective-permute-start.16 = (f32[2048]{0:T(1024)S(1)}, f32[2048]{0:T(1024)S(1)}, u32[]{:S(2)}, u32[]{:S(2)}) collective-permute-start(f32[2048]{0:T(1024)S(1)} %multiply_reduce_fusion.2), channel_id=1, source_target_pairs={{0,3},{1,0},{2,1},{3,2},{4,7},{5,4},{6,5},{7,6},{8,11},{9,8},{10,9... | collective-permute-start | bytes 24584 | tf_op jit(solution)/shard_map/ppermute | solution.py:27
  139.5 3.5 %collective-permute-done.14 = f32[2048]{0:T(1024)S(1)} collective-permute-done((f32[2048]{0:T(1024)S(1)}, f32[2048]{0:T(1024)S(1)}, u32[]{:S(2)}, u32[]{:S(2)}) %collective-permute-start.14) | collective-permute-done | bytes 8224 | tf_op jit(solution)/shard_map/ppermute | solution.py:27
  143.1 3.2 %collective-permute-start.19 = (f32[2048]{0:T(1024)S(1)}, f32[2048]{0:T(1024)S(1)}, u32[]{:S(2)}, u32[]{:S(2)}) collective-permute-start(f32[2048]{0:T(1024)S(1)} %add_add_fusion.2), channel_id=1, source_target_pairs={{0,12},{4,0},{8,4},{12,8},{1,13},{5,1},{9,5},{13,9},{2,14},{6,2},{... | collective-permute-start | bytes 24584 | tf_op jit(solution)/shard_map/ppermute | solution.py:27
  147.9 3.5 %collective-permute-done.17 = f32[2048]{0:T(1024)S(1)} collective-permute-done((f32[2048]{0:T(1024)S(1)}, f32[2048]{0:T(1024)S(1)}, u32[]{:S(2)}, u32[]{:S(2)}) %collective-permute-start.17) | collective-permute-done | bytes 8224 | tf_op jit(solution)/shard_map/ppermute | solution.py:27
  151.5 7.1 %multiply_reduce_fusion.1 = f32[2048]{0:T(1024)S(1)} fusion(f32[2048,2048]{1,0:T(8,128)} %get-tuple-element.5, f32[2048]{0:T(1024)S(1)} %add_divide_fusion.2), kind=kLoop, calls=%fused_computation.2 | loop fusion | flops 8386560 | bytes 16793600 | tf_op jit(solution)/shard_map/reduce_sum | solution.py:76
  159.8 3.2 %collective-permute-start.23 = (f32[2048]{0:T(1024)S(1)}, f32[2048]{0:T(1024)S(1)}, u32[]{:S(2)}, u32[]{:S(2)}) collective-permute-start(f32[2048]{0:T(1024)S(1)} %add.151), channel_id=1, source_target_pairs={{0,96},{32,0},{64,32},{96,64},{1,97},{33,1},{65,33},{97,65},{2,98}... | collective-permute-start | bytes 24584 | tf_op jit(solution)/shard_map/ppermute | solution.py:27
  164.7 3.5 %collective-permute-done.21 = f32[2048]{0:T(1024)S(1)} collective-permute-done((f32[2048]{0:T(1024)S(1)}, f32[2048]{0:T(1024)S(1)}, u32[]{:S(2)}, u32[]{:S(2)}) %collective-permute-start.21) | collective-permute-done | bytes 8224 | tf_op jit(solution)/shard_map/ppermute | solution.py:27
  168.2 7.0 %multiply_reduce_fusion = f32[2048]{0:T(1024)S(1)} fusion(f32[2048,2048]{1,0:T(8,128)} %get-tuple-element.5, f32[2048]{0:T(1024)S(1)} %add_divide_fusion.1), kind=kLoop, calls=%fused_computation.1 | loop fusion | flops 8386560 | bytes 16793600 | tf_op jit(solution)/shard_map/reduce_sum | solution.py:78
  175.3 3.2 %collective-permute-start.26 = (f32[2048]{0:T(1024)S(1)}, f32[2048]{0:T(1024)S(1)}, u32[]{:S(2)}, u32[]{:S(2)}) collective-permute-start(f32[2048]{0:T(1024)S(1)} %multiply_reduce_fusion), channel_id=1, source_target_pairs={{0,3},{1,0},{2,1},{3,2},{4,7},{5,4},{6,5},{7,6},{8,11},{9,8},{10,9... | collective-permute-start | bytes 24584 | tf_op jit(solution)/shard_map/ppermute | solution.py:27
  180.1 3.5 %collective-permute-done.24 = f32[2048]{0:T(1024)S(1)} collective-permute-done((f32[2048]{0:T(1024)S(1)}, f32[2048]{0:T(1024)S(1)}, u32[]{:S(2)}, u32[]{:S(2)}) %collective-permute-start.24) | collective-permute-done | bytes 8224 | tf_op jit(solution)/shard_map/ppermute | solution.py:27
  183.7 3.2 %collective-permute-start.29 = (f32[2048]{0:T(1024)S(1)}, f32[2048]{0:T(1024)S(1)}, u32[]{:S(2)}, u32[]{:S(2)}) collective-permute-start(f32[2048]{0:T(1024)S(1)} %add_add_fusion.1), channel_id=1, source_target_pairs={{0,12},{4,0},{8,4},{12,8},{1,13},{5,1},{9,5},{13,9},{2,14},{6,2},{... | collective-permute-start | bytes 24584 | tf_op jit(solution)/shard_map/ppermute | solution.py:27
  188.5 3.5 %collective-permute-done.27 = f32[2048]{0:T(1024)S(1)} collective-permute-done((f32[2048]{0:T(1024)S(1)}, f32[2048]{0:T(1024)S(1)}, u32[]{:S(2)}, u32[]{:S(2)}) %collective-permute-start.27) | collective-permute-done | bytes 8224 | tf_op jit(solution)/shard_map/ppermute | solution.py:27
  192.1 24.8 %fusion.1 = f32[2048,768]{0,1:T(8,128)} fusion(bf16[2048,768]{0,1:T(8,128)(2,1)S(1)} %copy-done, f32[2048,2048]{1,0:T(8,128)} %get-tuple-element.5, f32[2048]{0:T(1024)S(1)} %add_divide_fusion, f32[2048]{0:T(1024)S(1)} %add_divide_fusion.1), kind=kOutput, calls=%fused_computation.8 | convolution fusion | flops 38663094272 | bytes 26230784 | tf_op jit(solution)/shard_map/dot_general | solution.py:48
  216.9 8.1 %fusion = f32[2048]{0:T(1024)S(1)} fusion(f32[2048,2048]{1,0:T(8,128)} %get-tuple-element.5, f32[2048]{0:T(1024)S(1)} %add_divide_fusion, f32[2048]{0:T(1024)S(1)} %add_divide_fusion.1), kind=kLoop, calls=%fused_computation.7 | loop fusion | flops 12580864 | bytes 16801792 | tf_op jit(solution)/shard_map/reduce_sum | solution.py:82
  225.1 27.9 %reduce-scatter.2.cloned.1.call-done = f32[2048,96]{0,1:T(8,128)} async-done(((f32[2048,768]{0,1:T(8,128)}), f32[2048,96]{0,1:T(8,128)}) %reduce-scatter.2.cloned.1.call-update) | async-done | bytes 786448 | tf_op jit(solution)/shard_map/reduce_scatter | solution.py:83
  255.7 3.1 %collective-permute-start.33 = (f32[2,2048]{1,0:T(2,128)S(1)}, f32[2,2048]{1,0:T(2,128)S(1)}, u32[]{:S(2)}, u32[]{:S(2)}) collective-permute-start(f32[2,2048]{1,0:T(2,128)S(1)} %fusion.14), channel_id=1, source_target_pairs={{0,96},{32,0},{64,32},{96,64},{1,97},{33,1},{65,33},{97,65},{2,98}... | collective-permute-start | bytes 49160 | tf_op jit(solution)/shard_map/ppermute | solution.py:27
  260.5 3.5 %collective-permute-done.31 = f32[2,2048]{1,0:T(2,128)S(1)} collective-permute-done((f32[2,2048]{1,0:T(2,128)S(1)}, f32[2,2048]{1,0:T(2,128)S(1)}, u32[]{:S(2)}, u32[]{:S(2)}) %collective-permute-start.31) | collective-permute-done | bytes 16416 | tf_op jit(solution)/shard_map/ppermute | solution.py:27
  264.7 2.1 broadcast_multiply_fusion
  (75 shorter events, 29.4 us)
Async XLA Ops:
  7.2 53.4 %all-gather.2.cloned.1.call-start = ((), (), s32[]{:S(2)}) async-start(), calls=%async_computation.1 | async-start | bytes 3342336 | tf_op jit(solution)/shard_map/all_gather | solution.py:62
  7.9 245.1 %reduce-scatter.2.cloned.1.call-start = ((), (), s32[]{:S(2)}) async-start(), calls=%async_computation.2 | async-start | bytes 7077888 | tf_op jit(solution)/shard_map/reduce_scatter | solution.py:83
  78.5 5.0 %collective-permute-start.2 = (f32[2048]{0:T(1024)S(1)}, f32[2048]{0:T(1024)S(1)}, u32[]{:S(2)}, u32[]{:S(2)}) collective-permute-start(f32[2048]{0:T(1024)S(1)} %add.131), channel_id=1, source_target_pairs={{0,32},{32,64},{64,96},{96,0},{1,33},{33,65},{65,97},{97,1},{2,34}... | collective-permute-start | bytes 24584 | tf_op jit(solution)/shard_map/ppermute | solution.py:27
  80.0 3.7 %collective-permute-start.3 = (f32[2048]{0:T(1024)S(1)}, f32[2048]{0:T(1024)S(1)}, u32[]{:S(2)}, u32[]{:S(2)}) collective-permute-start(f32[2048]{0:T(1024)S(1)} %add.131), channel_id=1, source_target_pairs={{0,96},{32,0},{64,32},{96,64},{1,97},{33,1},{65,33},{97,65},{2,98}... | collective-permute-start | bytes 24584 | tf_op jit(solution)/shard_map/ppermute | solution.py:27
  81.7 5.2 %collective-permute-start.1 = (f32[2048]{0:T(1024)S(1)}, f32[2048]{0:T(1024)S(1)}, u32[]{:S(2)}, u32[]{:S(2)}) collective-permute-start(f32[2048]{0:T(1024)S(1)} %add.131), channel_id=1, source_target_pairs={{0,64},{32,96},{64,0},{96,32},{1,65},{33,97},{65,1},{97,33},{2,66}... | collective-permute-start | bytes 24584 | tf_op jit(solution)/shard_map/ppermute | solution.py:27
  93.9 4.9 %collective-permute-start.5 = (f32[2048]{0:T(1024)S(1)}, f32[2048]{0:T(1024)S(1)}, u32[]{:S(2)}, u32[]{:S(2)}) collective-permute-start(f32[2048]{0:T(1024)S(1)} %multiply_reduce_fusion.4), channel_id=1, source_target_pairs={{0,1},{1,2},{2,3},{3,0},{4,5},{5,6},{6,7},{7,4},{8,9},{9,10},{10,1... | collective-permute-start | bytes 24584 | tf_op jit(solution)/shard_map/ppermute | solution.py:27
  94.5 4.4 %collective-permute-start.6 = (f32[2048]{0:T(1024)S(1)}, f32[2048]{0:T(1024)S(1)}, u32[]{:S(2)}, u32[]{:S(2)}) collective-permute-start(f32[2048]{0:T(1024)S(1)} %multiply_reduce_fusion.4), channel_id=1, source_target_pairs={{0,3},{1,0},{2,1},{3,2},{4,7},{5,4},{6,5},{7,6},{8,11},{9,8},{10,9... | collective-permute-start | bytes 24584 | tf_op jit(solution)/shard_map/ppermute | solution.py:27
  97.2 5.2 %collective-permute-start.4 = (f32[2048]{0:T(1024)S(1)}, f32[2048]{0:T(1024)S(1)}, u32[]{:S(2)}, u32[]{:S(2)}) collective-permute-start(f32[2048]{0:T(1024)S(1)} %multiply_reduce_fusion.4), channel_id=1, source_target_pairs={{0,2},{1,3},{2,0},{3,1},{4,6},{5,7},{6,4},{7,5},{8,10},{9,11},{10,... | collective-permute-start | bytes 24584 | tf_op jit(solution)/shard_map/ppermute | solution.py:27
  102.4 4.9 %collective-permute-start.8 = (f32[2048]{0:T(1024)S(1)}, f32[2048]{0:T(1024)S(1)}, u32[]{:S(2)}, u32[]{:S(2)}) collective-permute-start(f32[2048]{0:T(1024)S(1)} %add_add_fusion.3), channel_id=1, source_target_pairs={{0,4},{4,8},{8,12},{12,0},{1,5},{5,9},{9,13},{13,1},{2,6},{6,10},{... | collective-permute-start | bytes 24584 | tf_op jit(solution)/shard_map/ppermute | solution.py:27
  102.9 4.4 %collective-permute-start.9 = (f32[2048]{0:T(1024)S(1)}, f32[2048]{0:T(1024)S(1)}, u32[]{:S(2)}, u32[]{:S(2)}) collective-permute-start(f32[2048]{0:T(1024)S(1)} %add_add_fusion.3), channel_id=1, source_target_pairs={{0,12},{4,0},{8,4},{12,8},{1,13},{5,1},{9,5},{13,9},{2,14},{6,2},{... | collective-permute-start | bytes 24584 | tf_op jit(solution)/shard_map/ppermute | solution.py:27
  105.6 5.2 %collective-permute-start.7 = (f32[2048]{0:T(1024)S(1)}, f32[2048]{0:T(1024)S(1)}, u32[]{:S(2)}, u32[]{:S(2)}) collective-permute-start(f32[2048]{0:T(1024)S(1)} %add_add_fusion.3), channel_id=1, source_target_pairs={{0,8},{4,12},{8,0},{12,4},{1,9},{5,13},{9,1},{13,5},{2,10},{6,14},... | collective-permute-start | bytes 24584 | tf_op jit(solution)/shard_map/ppermute | solution.py:27
  119.2 4.9 %collective-permute-start.12 = (f32[2048]{0:T(1024)S(1)}, f32[2048]{0:T(1024)S(1)}, u32[]{:S(2)}, u32[]{:S(2)}) collective-permute-start(f32[2048]{0:T(1024)S(1)} %add.141), channel_id=1, source_target_pairs={{0,32},{32,64},{64,96},{96,0},{1,33},{33,65},{65,97},{97,1},{2,34}... | collective-permute-start | bytes 24584 | tf_op jit(solution)/shard_map/ppermute | solution.py:27
  119.4 4.6 %collective-permute-start.13 = (f32[2048]{0:T(1024)S(1)}, f32[2048]{0:T(1024)S(1)}, u32[]{:S(2)}, u32[]{:S(2)}) collective-permute-start(f32[2048]{0:T(1024)S(1)} %add.141), channel_id=1, source_target_pairs={{0,96},{32,0},{64,32},{96,64},{1,97},{33,1},{65,33},{97,65},{2,98}... | collective-permute-start | bytes 24584 | tf_op jit(solution)/shard_map/ppermute | solution.py:27
  122.4 5.2 %collective-permute-start.11 = (f32[2048]{0:T(1024)S(1)}, f32[2048]{0:T(1024)S(1)}, u32[]{:S(2)}, u32[]{:S(2)}) collective-permute-start(f32[2048]{0:T(1024)S(1)} %add.141), channel_id=1, source_target_pairs={{0,64},{32,96},{64,0},{96,32},{1,65},{33,97},{65,1},{97,33},{2,66}... | collective-permute-start | bytes 24584 | tf_op jit(solution)/shard_map/ppermute | solution.py:27
  134.6 4.9 %collective-permute-start.15 = (f32[2048]{0:T(1024)S(1)}, f32[2048]{0:T(1024)S(1)}, u32[]{:S(2)}, u32[]{:S(2)}) collective-permute-start(f32[2048]{0:T(1024)S(1)} %multiply_reduce_fusion.2), channel_id=1, source_target_pairs={{0,1},{1,2},{2,3},{3,0},{4,5},{5,6},{6,7},{7,4},{8,9},{9,10},{10,1... | collective-permute-start | bytes 24584 | tf_op jit(solution)/shard_map/ppermute | solution.py:27
  134.7 4.9 %collective-permute-start.16 = (f32[2048]{0:T(1024)S(1)}, f32[2048]{0:T(1024)S(1)}, u32[]{:S(2)}, u32[]{:S(2)}) collective-permute-start(f32[2048]{0:T(1024)S(1)} %multiply_reduce_fusion.2), channel_id=1, source_target_pairs={{0,3},{1,0},{2,1},{3,2},{4,7},{5,4},{6,5},{7,6},{8,11},{9,8},{10,9... | collective-permute-start | bytes 24584 | tf_op jit(solution)/shard_map/ppermute | solution.py:27
  137.9 5.2 %collective-permute-start.14 = (f32[2048]{0:T(1024)S(1)}, f32[2048]{0:T(1024)S(1)}, u32[]{:S(2)}, u32[]{:S(2)}) collective-permute-start(f32[2048]{0:T(1024)S(1)} %multiply_reduce_fusion.2), channel_id=1, source_target_pairs={{0,2},{1,3},{2,0},{3,1},{4,6},{5,7},{6,4},{7,5},{8,10},{9,11},{10,... | collective-permute-start | bytes 24584 | tf_op jit(solution)/shard_map/ppermute | solution.py:27
  143.0 4.9 %collective-permute-start.18 = (f32[2048]{0:T(1024)S(1)}, f32[2048]{0:T(1024)S(1)}, u32[]{:S(2)}, u32[]{:S(2)}) collective-permute-start(f32[2048]{0:T(1024)S(1)} %add_add_fusion.2), channel_id=1, source_target_pairs={{0,4},{4,8},{8,12},{12,0},{1,5},{5,9},{9,13},{13,1},{2,6},{6,10},{... | collective-permute-start | bytes 24584 | tf_op jit(solution)/shard_map/ppermute | solution.py:27
  143.1 4.9 %collective-permute-start.19 = (f32[2048]{0:T(1024)S(1)}, f32[2048]{0:T(1024)S(1)}, u32[]{:S(2)}, u32[]{:S(2)}) collective-permute-start(f32[2048]{0:T(1024)S(1)} %add_add_fusion.2), channel_id=1, source_target_pairs={{0,12},{4,0},{8,4},{12,8},{1,13},{5,1},{9,5},{13,9},{2,14},{6,2},{... | collective-permute-start | bytes 24584 | tf_op jit(solution)/shard_map/ppermute | solution.py:27
  146.3 5.2 %collective-permute-start.17 = (f32[2048]{0:T(1024)S(1)}, f32[2048]{0:T(1024)S(1)}, u32[]{:S(2)}, u32[]{:S(2)}) collective-permute-start(f32[2048]{0:T(1024)S(1)} %add_add_fusion.2), channel_id=1, source_target_pairs={{0,8},{4,12},{8,0},{12,4},{1,9},{5,13},{9,1},{13,5},{2,10},{6,14},... | collective-permute-start | bytes 24584 | tf_op jit(solution)/shard_map/ppermute | solution.py:27
  159.8 4.9 %collective-permute-start.22 = (f32[2048]{0:T(1024)S(1)}, f32[2048]{0:T(1024)S(1)}, u32[]{:S(2)}, u32[]{:S(2)}) collective-permute-start(f32[2048]{0:T(1024)S(1)} %add.151), channel_id=1, source_target_pairs={{0,32},{32,64},{64,96},{96,0},{1,33},{33,65},{65,97},{97,1},{2,34}... | collective-permute-start | bytes 24584 | tf_op jit(solution)/shard_map/ppermute | solution.py:27
  159.8 4.9 %collective-permute-start.23 = (f32[2048]{0:T(1024)S(1)}, f32[2048]{0:T(1024)S(1)}, u32[]{:S(2)}, u32[]{:S(2)}) collective-permute-start(f32[2048]{0:T(1024)S(1)} %add.151), channel_id=1, source_target_pairs={{0,96},{32,0},{64,32},{96,64},{1,97},{33,1},{65,33},{97,65},{2,98}... | collective-permute-start | bytes 24584 | tf_op jit(solution)/shard_map/ppermute | solution.py:27
  163.0 5.2 %collective-permute-start.21 = (f32[2048]{0:T(1024)S(1)}, f32[2048]{0:T(1024)S(1)}, u32[]{:S(2)}, u32[]{:S(2)}) collective-permute-start(f32[2048]{0:T(1024)S(1)} %add.151), channel_id=1, source_target_pairs={{0,64},{32,96},{64,0},{96,32},{1,65},{33,97},{65,1},{97,33},{2,66}... | collective-permute-start | bytes 24584 | tf_op jit(solution)/shard_map/ppermute | solution.py:27
  175.2 4.9 %collective-permute-start.25 = (f32[2048]{0:T(1024)S(1)}, f32[2048]{0:T(1024)S(1)}, u32[]{:S(2)}, u32[]{:S(2)}) collective-permute-start(f32[2048]{0:T(1024)S(1)} %multiply_reduce_fusion), channel_id=1, source_target_pairs={{0,1},{1,2},{2,3},{3,0},{4,5},{5,6},{6,7},{7,4},{8,9},{9,10},{10,1... | collective-permute-start | bytes 24584 | tf_op jit(solution)/shard_map/ppermute | solution.py:27
  175.3 4.9 %collective-permute-start.26 = (f32[2048]{0:T(1024)S(1)}, f32[2048]{0:T(1024)S(1)}, u32[]{:S(2)}, u32[]{:S(2)}) collective-permute-start(f32[2048]{0:T(1024)S(1)} %multiply_reduce_fusion), channel_id=1, source_target_pairs={{0,3},{1,0},{2,1},{3,2},{4,7},{5,4},{6,5},{7,6},{8,11},{9,8},{10,9... | collective-permute-start | bytes 24584 | tf_op jit(solution)/shard_map/ppermute | solution.py:27
  178.5 5.2 %collective-permute-start.24 = (f32[2048]{0:T(1024)S(1)}, f32[2048]{0:T(1024)S(1)}, u32[]{:S(2)}, u32[]{:S(2)}) collective-permute-start(f32[2048]{0:T(1024)S(1)} %multiply_reduce_fusion), channel_id=1, source_target_pairs={{0,2},{1,3},{2,0},{3,1},{4,6},{5,7},{6,4},{7,5},{8,10},{9,11},{10,... | collective-permute-start | bytes 24584 | tf_op jit(solution)/shard_map/ppermute | solution.py:27
  183.7 4.9 %collective-permute-start.28 = (f32[2048]{0:T(1024)S(1)}, f32[2048]{0:T(1024)S(1)}, u32[]{:S(2)}, u32[]{:S(2)}) collective-permute-start(f32[2048]{0:T(1024)S(1)} %add_add_fusion.1), channel_id=1, source_target_pairs={{0,4},{4,8},{8,12},{12,0},{1,5},{5,9},{9,13},{13,1},{2,6},{6,10},{... | collective-permute-start | bytes 24584 | tf_op jit(solution)/shard_map/ppermute | solution.py:27
  183.7 4.9 %collective-permute-start.29 = (f32[2048]{0:T(1024)S(1)}, f32[2048]{0:T(1024)S(1)}, u32[]{:S(2)}, u32[]{:S(2)}) collective-permute-start(f32[2048]{0:T(1024)S(1)} %add_add_fusion.1), channel_id=1, source_target_pairs={{0,12},{4,0},{8,4},{12,8},{1,13},{5,1},{9,5},{13,9},{2,14},{6,2},{... | collective-permute-start | bytes 24584 | tf_op jit(solution)/shard_map/ppermute | solution.py:27
  186.9 5.2 %collective-permute-start.27 = (f32[2048]{0:T(1024)S(1)}, f32[2048]{0:T(1024)S(1)}, u32[]{:S(2)}, u32[]{:S(2)}) collective-permute-start(f32[2048]{0:T(1024)S(1)} %add_add_fusion.1), channel_id=1, source_target_pairs={{0,8},{4,12},{8,0},{12,4},{1,9},{5,13},{9,1},{13,5},{2,10},{6,14},... | collective-permute-start | bytes 24584 | tf_op jit(solution)/shard_map/ppermute | solution.py:27
  255.5 5.0 %collective-permute-start.32 = (f32[2,2048]{1,0:T(2,128)S(1)}, f32[2,2048]{1,0:T(2,128)S(1)}, u32[]{:S(2)}, u32[]{:S(2)}) collective-permute-start(f32[2,2048]{1,0:T(2,128)S(1)} %fusion.14), channel_id=1, source_target_pairs={{0,32},{32,64},{64,96},{96,0},{1,33},{33,65},{65,97},{97,1},{2,34}... | collective-permute-start | bytes 49160 | tf_op jit(solution)/shard_map/ppermute | solution.py:27
  255.7 4.8 %collective-permute-start.33 = (f32[2,2048]{1,0:T(2,128)S(1)}, f32[2,2048]{1,0:T(2,128)S(1)}, u32[]{:S(2)}, u32[]{:S(2)}) collective-permute-start(f32[2,2048]{1,0:T(2,128)S(1)} %fusion.14), channel_id=1, source_target_pairs={{0,96},{32,0},{64,32},{96,64},{1,97},{33,1},{65,33},{97,65},{2,98}... | collective-permute-start | bytes 49160 | tf_op jit(solution)/shard_map/ppermute | solution.py:27
  258.8 5.2 %collective-permute-start.31 = (f32[2,2048]{1,0:T(2,128)S(1)}, f32[2,2048]{1,0:T(2,128)S(1)}, u32[]{:S(2)}, u32[]{:S(2)}) collective-permute-start(f32[2,2048]{1,0:T(2,128)S(1)} %fusion.14), channel_id=1, source_target_pairs={{0,64},{32,96},{64,0},{96,32},{1,65},{33,97},{65,1},{97,33},{2,66}... | collective-permute-start | bytes 49160 | tf_op jit(solution)/shard_map/ppermute | solution.py:27
  (5 other events, 45.7 us)
Sparse Core Ops, SparseCore 0:
  10.2 50.3 all-gather.1
  217.1 35.8 reduce-scatter.1

commit v2 on v1

--- a/solution.py
+++ b/solution.py
@@ -54,12 +54,43 @@
     )
 
 
+def scatter_features(part_t, sizes):
+    ny, nc = sizes["y"], sizes["c"]
+    width, rows = part_t.shape
+    blk = width // (ny * nc)
+    x = part_t.reshape(ny, nc, blk, rows)
+    if nc == 2:
+        c = lax.axis_index("c")
+        keep = lax.dynamic_index_in_dim(x, c, 1, keepdims=False)
+        send = lax.dynamic_index_in_dim(x, 1 - c, 1, keepdims=False)
+        x = keep + lax.ppermute(send, "c", [(0, 1), (1, 0)])
+    else:
+        x = x[:, 0]
+    if ny == 1:
+        return x[0]
+    got = lax.all_to_all(x, "y", 0, 0, tiled=False)
+    total = got[0]
+    for j in range(1, ny):
+        total = total + got[j]
+    return total
+
+
+def gather_features(points, sizes):
+    n = sizes["x"] * sizes["z"]
+    rows, blk = points.shape
+    if n == 1:
+        return points
+    sent = jnp.broadcast_to(points[None], (n, rows, blk))
+    got = lax.all_to_all(sent, CEN_AXES, 0, 0, tiled=False)
+    return jnp.transpose(got, (1, 0, 2)).reshape(rows, n * blk)
+
+
 def make_local(sizes):
     pts_red = [("c", sizes["c"]), ("y", sizes["y"])]
     cen_red = [("z", sizes["z"]), ("x", sizes["x"])]
 
     def local(points, centroids):
-        gathered = lax.all_gather(points, CEN_AXES, axis=1, tiled=True)
+        gathered = gather_features(points, sizes)
         unit_points = unit_rows(gathered)
         unit_centroids = unit_rows(centroids)
         width = gathered.shape[1]
@@ -80,7 +111,7 @@
         weights = row_scale[:, None] * kernel * col_scale[None, :]
         partial_value = weighted_sum(weights, gathered)
         mass_part = jnp.sum(weights, axis=0) / balance
-        moved = lax.psum_scatter(partial_value, PTS_AXES, scatter_dimension=1, tiled=True)
+        moved = scatter_features(partial_value.T, sizes).T
         squares = jnp.sum(moved * moved, axis=1)
         both = multi_sum(jnp.stack([squares, mass_part]), pts_red)
         squares, masses = both[0], both[1]

time: 274 us -> 263 us (0.960)
  waiting for transfers between devices: 131 us -> 104 us
  starting transfers between devices: 36.8 us -> 61.5 us
  between operations: 14.2 us -> 0.82 us
  local copies, waits for them, and re-layouts: 0.01 us -> 5.93 us
    all_to_all x0 -> x2, waiting for transfers between devices: none -> 70.4 us  [the longest x1 39.8 us: gather_features(): got = lax.all_to_all(sent, CEN_AXES, 0, 0, tiled=False)]
    all_gather x1 -> x0, waiting for transfers between devices: 50.1 us -> none  [local(): gathered = lax.all_gather(points, CEN_AXES, axis=1, tiled=True)]
    reduce_scatter x1 -> x0, waiting for transfers between devices: 27.9 us -> none  [local(): lax.psum_scatter(partial_value, PTS_AXES, scatter_dimension=1, tiled=True)]
    ppermute x34, waiting for transfers between devices: 52.6 us -> 27.9 us  [axis_sum(): lax.ppermute(v, axis, [(i, (i + s) % n) for i in range(n)])]
    ppermute x34, starting transfers between devices: 36.7 us -> 49.8 us  [axis_sum(): lax.ppermute(v, axis, [(i, (i + s) % n) for i in range(n)])]
    all_to_all x0 -> x2, starting transfers between devices: none -> 11.7 us  [the longest x1 7.99 us: gather_features(): got = lax.all_to_all(sent, CEN_AXES, 0, 0, tiled=False)]
    ppermute x0 -> x1, waiting for transfers between devices: none -> 5.78 us  [scatter_features(): x = keep + lax.ppermute(send, 'c', [(0, 1), (1, 0)])]
    add x0 -> x1, other arithmetic: none -> 5.25 us  [scatter_features(): x = keep + lax.ppermute(send, 'c', [(0, 1), (1, 0)])]
  transfers between devices with their start and end apart: 36 -> 37, of which waited for: 26 -> 31; matrix products, arithmetic and copies ran while one was open for 4% -> 4% of each run, Pallas kernels for 0% -> 0%
where the time goes in v2:
time: 263 us; the launch traced here: 262 us
  waiting for transfers between devices  104 us (40%)
  starting transfers between devices  61.5 us (23%)
  other arithmetic  52.7 us (20%)
  matrix products  36.9 us (14%)
  local copies, waits for them, and re-layouts  5.93 us (2%)
    ppermute x34, starting transfers between devices, axis_sum(): lax.ppermute(v, axis, [(i, (i + s) % n) for i in range(n)])  49.8 us
    all_to_all x1, waiting for transfers between devices, gather_features(): got = lax.all_to_all(sent, CEN_AXES, 0, 0, tiled=False)  39.8 us
    all_to_all x1, waiting for transfers between devices, scatter_features(): got = lax.all_to_all(x, 'y', 0, 0, tiled=False)  30.6 us
    ppermute x34, waiting for transfers between devices, axis_sum(): lax.ppermute(v, axis, [(i, (i + s) % n) for i in range(n)])  27.9 us
    dot_general x1, matrix products, weighted_sum(): lax.dot_general(weights, point_rows.astype(jnp.float32), (((0,), (0,)), (...  23.6 us
    reduce_sum x3, other arithmetic, local(): row_part = jnp.sum(kernel * col_scale[None, :], axis=1)  20.9 us
    reduce_sum x2, other arithmetic, local(): col_part = jnp.sum(kernel * row_scale[:, None], axis=0)  13.9 us
    dot_general x1, matrix products, local(): jnp.dot(unit_points, unit_centroids.T, preferred_element_type=jnp.float32)  13.3 us
  transfers between devices with their start and end apart: 37, of which 31 were waited for; matrix products, arithmetic and copies ran while one was open for 4% of the time, Pallas kernels for 0%

profile of v2, /device:TPU:0, one launch (start us, length us, event | category | flops | bytes accessed | tf_op | source)
XLA Modules:
  0.0 262.0 jit_solution(10385049574736483121)
XLA Ops:
  0.6 2.9 %broadcast_in_dim.2 = bf16[16,2048,48]{1,2,0:T(8,128)(2,1)} broadcast(bf16[2048,48]{0,1:T(8,128)(2,1)} %param.2), dimensions={1,2} | broadcast | bytes 3342336 | tf_op jit(solution)/shard_map/broadcast_in_dim | solution.py:83
  3.6 8.0 %all-to-all-start = ((bf16[16,2048,48]{1,2,0:T(8,128)(2,1)}), bf16[16,2048,48]{1,2,0:T(8,128)(2,1)S(1)}, u32[]{:S(2)}, u32[]{:S(2)}) async-start(bf16[16,2048,48]{1,2,0:T(8,128)(2,1)} %broadcast_in_dim.2), calls=%async_computation | async-start | bytes 6291456 | tf_op jit(solution)/shard_map/all_to_all | solution.py:84
  11.6 2.6 fusion.4
  14.2 39.8 %all-to-all-done = bf16[16,2048,48]{1,2,0:T(8,128)(2,1)S(1)} async-done(((bf16[16,2048,48]{1,2,0:T(8,128)(2,1)}), bf16[16,2048,48]{1,2,0:T(8,128)(2,1)S(1)}, u32[]{:S(2)}, u32[]{:S(2)}) %all-to-all-start) | async-done | bytes 3145760 | tf_op jit(solution)/shard_map/all_to_all | solution.py:84
  54.7 13.3 %fusion.15 = (f32[2048]{0:T(1024)S(1)}, f32[2048,2048]{1,0:T(8,128)}) fusion(bf16[2048,768]{1,0:T(8,128)(2,1)} %param.3, f32[2048]{0:T(1024)S(1)} %add_rsqrt_fusion, bf16[2048,768]{0,1:T(8,128)(2,1)S(1)} %bitcast.21, f32[2048]{0:T(1024)S(1)} %add_rsqrt_fusion.1), kind=kOutput, calls=%fused_computation.46 | convolution fusion | flops 6460274688 | bytes 23093248 | tf_op jit(solution)/shard_map/dot_general | solution.py:104
  69.1 3.2 %collective-permute-start.1 = (f32[2048]{0:T(1024)S(1)}, f32[2048]{0:T(1024)S(1)}, u32[]{:S(2)}, u32[]{:S(2)}) collective-permute-start(f32[2048]{0:T(1024)S(1)} %add.154), channel_id=1, source_target_pairs={{0,64},{32,96},{64,0},{96,32},{1,65},{33,97},{65,1},{97,33},{2,66}... | collective-permute-start | bytes 24584 | tf_op jit(solution)/shard_map/ppermute | solution.py:27
  73.0 2.6 collective-permute-start.3
  75.5 1.6 collective-permute-done.2
  77.2 7.0 %multiply_reduce_fusion.4 = f32[2048]{0:T(1024)S(1)} fusion(f32[2048,2048]{1,0:T(8,128)} %get-tuple-element.7, f32[2048]{0:T(1024)S(1)} %add_divide_fusion.5), kind=kLoop, calls=%fused_computation.5 | loop fusion | flops 8386560 | bytes 16793600 | tf_op jit(solution)/shard_map/reduce_sum | solution.py:109
  84.2 2.6 %collective-permute-start.4 = (f32[2048]{0:T(1024)S(1)}, f32[2048]{0:T(1024)S(1)}, u32[]{:S(2)}, u32[]{:S(2)}) collective-permute-start(f32[2048]{0:T(1024)S(1)} %multiply_reduce_fusion.4), channel_id=1, source_target_pairs={{0,2},{1,3},{2,0},{3,1},{4,6},{5,7},{6,4},{7,5},{8,10},{9,11},{10,... | collective-permute-start | bytes 24584 | tf_op jit(solution)/shard_map/ppermute | solution.py:27
  87.1 3.0 %collective-permute-start.6 = (f32[2048]{0:T(1024)S(1)}, f32[2048]{0:T(1024)S(1)}, u32[]{:S(2)}, u32[]{:S(2)}) collective-permute-start(f32[2048]{0:T(1024)S(1)} %multiply_reduce_fusion.4), channel_id=1, source_target_pairs={{0,3},{1,0},{2,1},{3,2},{4,7},{5,4},{6,5},{7,6},{8,11},{9,8},{10,9... | collective-permute-start | bytes 24584 | tf_op jit(solution)/shard_map/ppermute | solution.py:27
  91.7 4.1 %collective-permute-start.7 = (f32[2048]{0:T(1024)S(1)}, f32[2048]{0:T(1024)S(1)}, u32[]{:S(2)}, u32[]{:S(2)}) collective-permute-start(f32[2048]{0:T(1024)S(1)} %add_add_fusion.3), channel_id=1, source_target_pairs={{0,8},{4,12},{8,0},{12,4},{1,9},{5,13},{9,1},{13,5},{2,10},{6,14},... | collective-permute-start | bytes 24584 | tf_op jit(solution)/shard_map/ppermute | solution.py:27
  95.8 3.2 %collective-permute-start.9 = (f32[2048]{0:T(1024)S(1)}, f32[2048]{0:T(1024)S(1)}, u32[]{:S(2)}, u32[]{:S(2)}) collective-permute-start(f32[2048]{0:T(1024)S(1)} %add_add_fusion.3), channel_id=1, source_target_pairs={{0,12},{4,0},{8,4},{12,8},{1,13},{5,1},{9,5},{13,9},{2,14},{6,2},{... | collective-permute-start | bytes 24584 | tf_op jit(solution)/shard_map/ppermute | solution.py:27
  99.1 1.6 collective-permute-done.8
  100.7 6.9 %multiply_reduce_fusion.3 = f32[2048]{0:T(1024)S(1)} fusion(f32[2048,2048]{1,0:T(8,128)} %get-tuple-element.7, f32[2048]{0:T(1024)S(1)} %add_divide_fusion.4), kind=kLoop, calls=%fused_computation.4 | loop fusion | flops 8386560 | bytes 16793600 | tf_op jit(solution)/shard_map/reduce_sum | solution.py:107
  110.5 2.6 %collective-permute-start.12 = (f32[2048]{0:T(1024)S(1)}, f32[2048]{0:T(1024)S(1)}, u32[]{:S(2)}, u32[]{:S(2)}) collective-permute-start(f32[2048]{0:T(1024)S(1)} %add.164), channel_id=1, source_target_pairs={{0,32},{32,64},{64,96},{96,0},{1,33},{33,65},{65,97},{97,1},{2,34}... | collective-permute-start | bytes 24584 | tf_op jit(solution)/shard_map/ppermute | solution.py:27
  116.8 7.0 %multiply_reduce_fusion.2 = f32[2048]{0:T(1024)S(1)} fusion(f32[2048,2048]{1,0:T(8,128)} %get-tuple-element.7, f32[2048]{0:T(1024)S(1)} %add_divide_fusion.3), kind=kLoop, calls=%fused_computation.3 | loop fusion | flops 8386560 | bytes 16793600 | tf_op jit(solution)/shard_map/reduce_sum | solution.py:109
  125.2 2.6 %collective-permute-start.15 = (f32[2048]{0:T(1024)S(1)}, f32[2048]{0:T(1024)S(1)}, u32[]{:S(2)}, u32[]{:S(2)}) collective-permute-start(f32[2048]{0:T(1024)S(1)} %multiply_reduce_fusion.2), channel_id=1, source_target_pairs={{0,1},{1,2},{2,3},{3,0},{4,5},{5,6},{6,7},{7,4},{8,9},{9,10},{10,1... | collective-permute-start | bytes 24584 | tf_op jit(solution)/shard_map/ppermute | solution.py:27
  133.0 2.6 %collective-permute-start.18 = (f32[2048]{0:T(1024)S(1)}, f32[2048]{0:T(1024)S(1)}, u32[]{:S(2)}, u32[]{:S(2)}) collective-permute-start(f32[2048]{0:T(1024)S(1)} %add_add_fusion.2), channel_id=1, source_target_pairs={{0,4},{4,8},{8,12},{12,0},{1,5},{5,9},{9,13},{13,1},{2,6},{6,10},{... | collective-permute-start | bytes 24584 | tf_op jit(solution)/shard_map/ppermute | solution.py:27
  139.2 6.9 %multiply_reduce_fusion.1 = f32[2048]{0:T(1024)S(1)} fusion(f32[2048,2048]{1,0:T(8,128)} %get-tuple-element.7, f32[2048]{0:T(1024)S(1)} %add_divide_fusion.2), kind=kLoop, calls=%fused_computation.2 | loop fusion | flops 8386560 | bytes 16793600 | tf_op jit(solution)/shard_map/reduce_sum | solution.py:107
  148.1 2.1 collective-permute-start.22
  153.8 6.9 %multiply_reduce_fusion = f32[2048]{0:T(1024)S(1)} fusion(f32[2048,2048]{1,0:T(8,128)} %get-tuple-element.7, f32[2048]{0:T(1024)S(1)} %add_divide_fusion.1), kind=kLoop, calls=%fused_computation.1 | loop fusion | flops 8386560 | bytes 16793600 | tf_op jit(solution)/shard_map/reduce_sum | solution.py:109
  161.5 2.0 collective-permute-start.25
  167.8 2.0 collective-permute-start.28
  173.5 23.6 %fusion.1 = f32[2048,768]{0,1:T(8,128)S(1)} fusion(bf16[2048,768]{0,1:T(8,128)(2,1)S(1)} %bitcast.22, f32[2048,2048]{1,0:T(8,128)} %get-tuple-element.7, f32[2048]{0:T(1024)S(1)} %add_divide_fusion, f32[2048]{0:T(1024)S(1)} %add_divide_fusion.1), kind=kOutput, calls=%fused_computation.8 | convolution fusion | flops 38663094272 | bytes 26230784 | tf_op jit(solution)/shard_map/dot_general | solution.py:48
  197.1 2.6 %copy-done = f32[2048,768]{0,1:T(8,128)} copy-done((f32[2048,768]{0,1:T(8,128)}, f32[2048,768]{0,1:T(8,128)S(1)}, u32[]{:S(2)}) %copy-start) | copy-done | bytes 6291480
  200.2 5.8 %collective-permute-done.30 = f32[4,96,2048]{2,1,0:T(8,128)} collective-permute-done((f32[4,96,2048]{2,1,0:T(8,128)S(1)}, f32[4,96,2048]{2,1,0:T(8,128)}, u32[]{:S(2)}, u32[]{:S(2)}) %collective-permute-start.30) | collective-permute-done | bytes 3145760 | tf_op jit(solution)/shard_map/ppermute | solution.py:66
  205.9 5.3 %bitcast_add_fusion = f32[4,96,2048]{2,1,0:T(8,128)} fusion(f32[4,96,2048]{2,1,0:T(8,128)} %collective-permute-done.30, f32[4,2,96,2048]{3,2,1,0:T(8,128)} %bitcast.24, s32[]{:T(128)S(6)} %select_n.7), kind=kLoop, calls=%fused_computation.17 | loop fusion | flops 786432 | bytes 9437188 | tf_op jit(solution)/shard_map/add | solution.py:66
  211.2 3.7 %all-to-all-start.1 = ((f32[4,96,2048]{2,1,0:T(8,128)}), f32[4,96,2048]{2,1,0:T(8,128)S(1)}, u32[]{:S(2)}, u32[]{:S(2)}) async-start(f32[4,96,2048]{2,1,0:T(8,128)} %bitcast_add_fusion), calls=%async_computation.1 | async-start | bytes 6291456 | tf_op jit(solution)/shard_map/all_to_all | solution.py:71
  214.9 7.5 %fusion = f32[2048]{0:T(1024)S(1)} fusion(f32[2048,2048]{1,0:T(8,128)} %get-tuple-element.7, f32[2048]{0:T(1024)S(1)} %add_divide_fusion, f32[2048]{0:T(1024)S(1)} %add_divide_fusion.1), kind=kLoop, calls=%fused_computation.7 | loop fusion | flops 12580864 | bytes 16801792 | tf_op jit(solution)/shard_map/reduce_sum | solution.py:113
  222.4 30.6 %all-to-all-done.1 = f32[4,96,2048]{2,1,0:T(8,128)S(1)} async-done(((f32[4,96,2048]{2,1,0:T(8,128)}), f32[4,96,2048]{2,1,0:T(8,128)S(1)}, u32[]{:S(2)}, u32[]{:S(2)}) %all-to-all-start.1) | async-done | bytes 3145760 | tf_op jit(solution)/shard_map/all_to_all | solution.py:71
  256.7 1.8 collective-permute-start.34
  (78 shorter events, 43.0 us)
Async XLA Ops:
  3.6 50.4 %all-to-all-start = ((bf16[16,2048,48]{1,2,0:T(8,128)(2,1)}), bf16[16,2048,48]{1,2,0:T(8,128)(2,1)S(1)}, u32[]{:S(2)}, u32[]{:S(2)}) async-start(bf16[16,2048,48]{1,2,0:T(8,128)(2,1)} %broadcast_in_dim.2), calls=%async_computation | async-start | bytes 6291456 | tf_op jit(solution)/shard_map/all_to_all | solution.py:84
  69.1 6.4 %collective-permute-start.1 = (f32[2048]{0:T(1024)S(1)}, f32[2048]{0:T(1024)S(1)}, u32[]{:S(2)}, u32[]{:S(2)}) collective-permute-start(f32[2048]{0:T(1024)S(1)} %add.154), channel_id=1, source_target_pairs={{0,64},{32,96},{64,0},{96,32},{1,65},{33,97},{65,1},{97,33},{2,66}... | collective-permute-start | bytes 24584 | tf_op jit(solution)/shard_map/ppermute | solution.py:27
  72.3 4.9 %collective-permute-start.2 = (f32[2048]{0:T(1024)S(1)}, f32[2048]{0:T(1024)S(1)}, u32[]{:S(2)}, u32[]{:S(2)}) collective-permute-start(f32[2048]{0:T(1024)S(1)} %add.154), channel_id=1, source_target_pairs={{0,32},{32,64},{64,96},{96,0},{1,33},{33,65},{65,97},{97,1},{2,34}... | collective-permute-start | bytes 24584 | tf_op jit(solution)/shard_map/ppermute | solution.py:27
  73.0 4.2 %collective-permute-start.3 = (f32[2048]{0:T(1024)S(1)}, f32[2048]{0:T(1024)S(1)}, u32[]{:S(2)}, u32[]{:S(2)}) collective-permute-start(f32[2048]{0:T(1024)S(1)} %add.154), channel_id=1, source_target_pairs={{0,96},{32,0},{64,32},{96,64},{1,97},{33,1},{65,33},{97,65},{2,98}... | collective-permute-start | bytes 24584 | tf_op jit(solution)/shard_map/ppermute | solution.py:27
  84.2 5.9 %collective-permute-start.4 = (f32[2048]{0:T(1024)S(1)}, f32[2048]{0:T(1024)S(1)}, u32[]{:S(2)}, u32[]{:S(2)}) collective-permute-start(f32[2048]{0:T(1024)S(1)} %multiply_reduce_fusion.4), channel_id=1, source_target_pairs={{0,2},{1,3},{2,0},{3,1},{4,6},{5,7},{6,4},{7,5},{8,10},{9,11},{10,... | collective-permute-start | bytes 24584 | tf_op jit(solution)/shard_map/ppermute | solution.py:27
  86.8 4.9 %collective-permute-start.5 = (f32[2048]{0:T(1024)S(1)}, f32[2048]{0:T(1024)S(1)}, u32[]{:S(2)}, u32[]{:S(2)}) collective-permute-start(f32[2048]{0:T(1024)S(1)} %multiply_reduce_fusion.4), channel_id=1, source_target_pairs={{0,1},{1,2},{2,3},{3,0},{4,5},{5,6},{6,7},{7,4},{8,9},{9,10},{10,1... | collective-permute-start | bytes 24584 | tf_op jit(solution)/shard_map/ppermute | solution.py:27
  87.1 4.6 %collective-permute-start.6 = (f32[2048]{0:T(1024)S(1)}, f32[2048]{0:T(1024)S(1)}, u32[]{:S(2)}, u32[]{:S(2)}) collective-permute-start(f32[2048]{0:T(1024)S(1)} %multiply_reduce_fusion.4), channel_id=1, source_target_pairs={{0,3},{1,0},{2,1},{3,2},{4,7},{5,4},{6,5},{7,6},{8,11},{9,8},{10,9... | collective-permute-start | bytes 24584 | tf_op jit(solution)/shard_map/ppermute | solution.py:27
  91.7 7.4 %collective-permute-start.7 = (f32[2048]{0:T(1024)S(1)}, f32[2048]{0:T(1024)S(1)}, u32[]{:S(2)}, u32[]{:S(2)}) collective-permute-start(f32[2048]{0:T(1024)S(1)} %add_add_fusion.3), channel_id=1, source_target_pairs={{0,8},{4,12},{8,0},{12,4},{1,9},{5,13},{9,1},{13,5},{2,10},{6,14},... | collective-permute-start | bytes 24584 | tf_op jit(solution)/shard_map/ppermute | solution.py:27
  95.8 4.9 %collective-permute-start.8 = (f32[2048]{0:T(1024)S(1)}, f32[2048]{0:T(1024)S(1)}, u32[]{:S(2)}, u32[]{:S(2)}) collective-permute-start(f32[2048]{0:T(1024)S(1)} %add_add_fusion.3), channel_id=1, source_target_pairs={{0,4},{4,8},{8,12},{12,0},{1,5},{5,9},{9,13},{13,1},{2,6},{6,10},{... | collective-permute-start | bytes 24584 | tf_op jit(solution)/shard_map/ppermute | solution.py:27
  95.8 4.9 %collective-permute-start.9 = (f32[2048]{0:T(1024)S(1)}, f32[2048]{0:T(1024)S(1)}, u32[]{:S(2)}, u32[]{:S(2)}) collective-permute-start(f32[2048]{0:T(1024)S(1)} %add_add_fusion.3), channel_id=1, source_target_pairs={{0,12},{4,0},{8,4},{12,8},{1,13},{5,1},{9,5},{13,9},{2,14},{6,2},{... | collective-permute-start | bytes 24584 | tf_op jit(solution)/shard_map/ppermute | solution.py:27
  109.1 5.2 %collective-permute-start.11 = (f32[2048]{0:T(1024)S(1)}, f32[2048]{0:T(1024)S(1)}, u32[]{:S(2)}, u32[]{:S(2)}) collective-permute-start(f32[2048]{0:T(1024)S(1)} %add.164), channel_id=1, source_target_pairs={{0,64},{32,96},{64,0},{96,32},{1,65},{33,97},{65,1},{97,33},{2,66}... | collective-permute-start | bytes 24584 | tf_op jit(solution)/shard_map/ppermute | solution.py:27
  110.5 4.9 %collective-permute-start.12 = (f32[2048]{0:T(1024)S(1)}, f32[2048]{0:T(1024)S(1)}, u32[]{:S(2)}, u32[]{:S(2)}) collective-permute-start(f32[2048]{0:T(1024)S(1)} %add.164), channel_id=1, source_target_pairs={{0,32},{32,64},{64,96},{96,0},{1,33},{33,65},{65,97},{97,1},{2,34}... | collective-permute-start | bytes 24584 | tf_op jit(solution)/shard_map/ppermute | solution.py:27
  113.2 3.7 %collective-permute-start.13 = (f32[2048]{0:T(1024)S(1)}, f32[2048]{0:T(1024)S(1)}, u32[]{:S(2)}, u32[]{:S(2)}) collective-permute-start(f32[2048]{0:T(1024)S(1)} %add.164), channel_id=1, source_target_pairs={{0,96},{32,0},{64,32},{96,64},{1,97},{33,1},{65,33},{97,65},{2,98}... | collective-permute-start | bytes 24584 | tf_op jit(solution)/shard_map/ppermute | solution.py:27
  123.8 5.2 %collective-permute-start.14 = (f32[2048]{0:T(1024)S(1)}, f32[2048]{0:T(1024)S(1)}, u32[]{:S(2)}, u32[]{:S(2)}) collective-permute-start(f32[2048]{0:T(1024)S(1)} %multiply_reduce_fusion.2), channel_id=1, source_target_pairs={{0,2},{1,3},{2,0},{3,1},{4,6},{5,7},{6,4},{7,5},{8,10},{9,11},{10,... | collective-permute-start | bytes 24584 | tf_op jit(solution)/shard_map/ppermute | solution.py:27
  125.2 4.9 %collective-permute-start.15 = (f32[2048]{0:T(1024)S(1)}, f32[2048]{0:T(1024)S(1)}, u32[]{:S(2)}, u32[]{:S(2)}) collective-permute-start(f32[2048]{0:T(1024)S(1)} %multiply_reduce_fusion.2), channel_id=1, source_target_pairs={{0,1},{1,2},{2,3},{3,0},{4,5},{5,6},{6,7},{7,4},{8,9},{9,10},{10,1... | collective-permute-start | bytes 24584 | tf_op jit(solution)/shard_map/ppermute | solution.py:27
  127.8 3.7 %collective-permute-start.16 = (f32[2048]{0:T(1024)S(1)}, f32[2048]{0:T(1024)S(1)}, u32[]{:S(2)}, u32[]{:S(2)}) collective-permute-start(f32[2048]{0:T(1024)S(1)} %multiply_reduce_fusion.2), channel_id=1, source_target_pairs={{0,3},{1,0},{2,1},{3,2},{4,7},{5,4},{6,5},{7,6},{8,11},{9,8},{10,9... | collective-permute-start | bytes 24584 | tf_op jit(solution)/shard_map/ppermute | solution.py:27
  131.5 5.2 %collective-permute-start.17 = (f32[2048]{0:T(1024)S(1)}, f32[2048]{0:T(1024)S(1)}, u32[]{:S(2)}, u32[]{:S(2)}) collective-permute-start(f32[2048]{0:T(1024)S(1)} %add_add_fusion.2), channel_id=1, source_target_pairs={{0,8},{4,12},{8,0},{12,4},{1,9},{5,13},{9,1},{13,5},{2,10},{6,14},... | collective-permute-start | bytes 24584 | tf_op jit(solution)/shard_map/ppermute | solution.py:27
  133.0 4.9 %collective-permute-start.18 = (f32[2048]{0:T(1024)S(1)}, f32[2048]{0:T(1024)S(1)}, u32[]{:S(2)}, u32[]{:S(2)}) collective-permute-start(f32[2048]{0:T(1024)S(1)} %add_add_fusion.2), channel_id=1, source_target_pairs={{0,4},{4,8},{8,12},{12,0},{1,5},{5,9},{9,13},{13,1},{2,6},{6,10},{... | collective-permute-start | bytes 24584 | tf_op jit(solution)/shard_map/ppermute | solution.py:27
  135.6 3.7 %collective-permute-start.19 = (f32[2048]{0:T(1024)S(1)}, f32[2048]{0:T(1024)S(1)}, u32[]{:S(2)}, u32[]{:S(2)}) collective-permute-start(f32[2048]{0:T(1024)S(1)} %add_add_fusion.2), channel_id=1, source_target_pairs={{0,12},{4,0},{8,4},{12,8},{1,13},{5,1},{9,5},{13,9},{2,14},{6,2},{... | collective-permute-start | bytes 24584 | tf_op jit(solution)/shard_map/ppermute | solution.py:27
  147.4 5.2 %collective-permute-start.21 = (f32[2048]{0:T(1024)S(1)}, f32[2048]{0:T(1024)S(1)}, u32[]{:S(2)}, u32[]{:S(2)}) collective-permute-start(f32[2048]{0:T(1024)S(1)} %add.174), channel_id=1, source_target_pairs={{0,64},{32,96},{64,0},{96,32},{1,65},{33,97},{65,1},{97,33},{2,66}... | collective-permute-start | bytes 24584 | tf_op jit(solution)/shard_map/ppermute | solution.py:27
  148.1 4.9 %collective-permute-start.22 = (f32[2048]{0:T(1024)S(1)}, f32[2048]{0:T(1024)S(1)}, u32[]{:S(2)}, u32[]{:S(2)}) collective-permute-start(f32[2048]{0:T(1024)S(1)} %add.174), channel_id=1, source_target_pairs={{0,32},{32,64},{64,96},{96,0},{1,33},{33,65},{65,97},{97,1},{2,34}... | collective-permute-start | bytes 24584 | tf_op jit(solution)/shard_map/ppermute | solution.py:27
  150.1 3.7 %collective-permute-start.23 = (f32[2048]{0:T(1024)S(1)}, f32[2048]{0:T(1024)S(1)}, u32[]{:S(2)}, u32[]{:S(2)}) collective-permute-start(f32[2048]{0:T(1024)S(1)} %add.174), channel_id=1, source_target_pairs={{0,96},{32,0},{64,32},{96,64},{1,97},{33,1},{65,33},{97,65},{2,98}... | collective-permute-start | bytes 24584 | tf_op jit(solution)/shard_map/ppermute | solution.py:27
  160.7 5.2 %collective-permute-start.24 = (f32[2048]{0:T(1024)S(1)}, f32[2048]{0:T(1024)S(1)}, u32[]{:S(2)}, u32[]{:S(2)}) collective-permute-start(f32[2048]{0:T(1024)S(1)} %multiply_reduce_fusion), channel_id=1, source_target_pairs={{0,2},{1,3},{2,0},{3,1},{4,6},{5,7},{6,4},{7,5},{8,10},{9,11},{10,... | collective-permute-start | bytes 24584 | tf_op jit(solution)/shard_map/ppermute | solution.py:27
  161.5 4.9 %collective-permute-start.25 = (f32[2048]{0:T(1024)S(1)}, f32[2048]{0:T(1024)S(1)}, u32[]{:S(2)}, u32[]{:S(2)}) collective-permute-start(f32[2048]{0:T(1024)S(1)} %multiply_reduce_fusion), channel_id=1, source_target_pairs={{0,1},{1,2},{2,3},{3,0},{4,5},{5,6},{6,7},{7,4},{8,9},{9,10},{10,1... | collective-permute-start | bytes 24584 | tf_op jit(solution)/shard_map/ppermute | solution.py:27
  167.1 5.2 %collective-permute-start.27 = (f32[2048]{0:T(1024)S(1)}, f32[2048]{0:T(1024)S(1)}, u32[]{:S(2)}, u32[]{:S(2)}) collective-permute-start(f32[2048]{0:T(1024)S(1)} %add_add_fusion.1), channel_id=1, source_target_pairs={{0,8},{4,12},{8,0},{12,4},{1,9},{5,13},{9,1},{13,5},{2,10},{6,14},... | collective-permute-start | bytes 24584 | tf_op jit(solution)/shard_map/ppermute | solution.py:27
  167.8 4.9 %collective-permute-start.28 = (f32[2048]{0:T(1024)S(1)}, f32[2048]{0:T(1024)S(1)}, u32[]{:S(2)}, u32[]{:S(2)}) collective-permute-start(f32[2048]{0:T(1024)S(1)} %add_add_fusion.1), channel_id=1, source_target_pairs={{0,4},{4,8},{8,12},{12,0},{1,5},{5,9},{9,13},{13,1},{2,6},{6,10},{... | collective-permute-start | bytes 24584 | tf_op jit(solution)/shard_map/ppermute | solution.py:27
  169.8 3.7 %collective-permute-start.29 = (f32[2048]{0:T(1024)S(1)}, f32[2048]{0:T(1024)S(1)}, u32[]{:S(2)}, u32[]{:S(2)}) collective-permute-start(f32[2048]{0:T(1024)S(1)} %add_add_fusion.1), channel_id=1, source_target_pairs={{0,12},{4,0},{8,4},{12,8},{1,13},{5,1},{9,5},{13,9},{2,14},{6,2},{... | collective-permute-start | bytes 24584 | tf_op jit(solution)/shard_map/ppermute | solution.py:27
  200.1 5.9 %collective-permute-start.30 = (f32[4,96,2048]{2,1,0:T(8,128)S(1)}, f32[4,96,2048]{2,1,0:T(8,128)}, u32[]{:S(2)}, u32[]{:S(2)}) collective-permute-start(f32[4,96,2048]{2,1,0:T(8,128)S(1)} %dynamic-slice_bitcast_fusion), channel_id=1, source_target_pairs={{0,16},{16,0},{1,17},{17,1},{2,18},{18,2},{3,19},{19,3},{4,20},{20... | collective-permute-start | bytes 9437192 | tf_op jit(solution)/shard_map/ppermute | solution.py:66
  211.2 41.8 %all-to-all-start.1 = ((f32[4,96,2048]{2,1,0:T(8,128)}), f32[4,96,2048]{2,1,0:T(8,128)S(1)}, u32[]{:S(2)}, u32[]{:S(2)}) async-start(f32[4,96,2048]{2,1,0:T(8,128)} %bitcast_add_fusion), calls=%async_computation.1 | async-start | bytes 6291456 | tf_op jit(solution)/shard_map/all_to_all | solution.py:71
  254.6 5.4 %collective-permute-start.32 = (f32[2,2048]{1,0:T(2,128)S(1)}, f32[2,2048]{1,0:T(2,128)S(1)}, u32[]{:S(2)}, u32[]{:S(2)}) collective-permute-start(f32[2,2048]{1,0:T(2,128)S(1)} %fusion.12), channel_id=1, source_target_pairs={{0,64},{32,96},{64,0},{96,32},{1,65},{33,97},{65,1},{97,33},{2,66}... | collective-permute-start | bytes 49160 | tf_op jit(solution)/shard_map/ppermute | solution.py:27
  255.2 4.9 %collective-permute-start.33 = (f32[2,2048]{1,0:T(2,128)S(1)}, f32[2,2048]{1,0:T(2,128)S(1)}, u32[]{:S(2)}, u32[]{:S(2)}) collective-permute-start(f32[2,2048]{1,0:T(2,128)S(1)} %fusion.12), channel_id=1, source_target_pairs={{0,32},{32,64},{64,96},{96,0},{1,33},{33,65},{65,97},{97,1},{2,34}... | collective-permute-start | bytes 49160 | tf_op jit(solution)/shard_map/ppermute | solution.py:27
  256.7 3.7 %collective-permute-start.34 = (f32[2,2048]{1,0:T(2,128)S(1)}, f32[2,2048]{1,0:T(2,128)S(1)}, u32[]{:S(2)}, u32[]{:S(2)}) collective-permute-start(f32[2,2048]{1,0:T(2,128)S(1)} %fusion.12), channel_id=1, source_target_pairs={{0,96},{32,0},{64,32},{96,64},{1,97},{33,1},{65,33},{97,65},{2,98}... | collective-permute-start | bytes 49160 | tf_op jit(solution)/shard_map/ppermute | solution.py:27
  (6 other events, 11.4 us)

commit v3 on v2

--- a/solution.py
+++ b/solution.py
@@ -108,10 +108,17 @@
             col_scale = balance / multi_sum(col_part, pts_red)
             row_part = jnp.sum(kernel * col_scale[None, :], axis=1)
             row_scale = 1.0 / multi_sum(row_part, cen_red)
-        weights = row_scale[:, None] * kernel * col_scale[None, :]
-        partial_value = weighted_sum(weights, gathered)
-        mass_part = jnp.sum(weights, axis=0) / balance
-        moved = scatter_features(partial_value.T, sizes).T
+        scaled = kernel * row_scale[:, None]
+        hi_wide = lax.reduce_precision(scaled, exponent_bits=8, mantissa_bits=7)
+        hi = hi_wide.astype(jnp.bfloat16)
+        lo = (scaled - hi_wide).astype(jnp.bfloat16)
+        dims = (((0,), (0,)), ((), ()))
+        partial_t = lax.dot_general(
+            gathered, hi, dims, preferred_element_type=jnp.float32
+        ) + lax.dot_general(gathered, lo, dims, preferred_element_type=jnp.float32)
+        partial_t = partial_t * col_scale[None, :]
+        mass_part = jnp.sum(scaled, axis=0) * col_scale / balance
+        moved = scatter_features(partial_t, sizes).T
         squares = jnp.sum(moved * moved, axis=1)
         both = multi_sum(jnp.stack([squares, mass_part]), pts_red)
         squares, masses = both[0], both[1]

time: 263 us -> 262 us (level)
    dot_general x1 -> x2, matrix products: 23.6 us -> 23.4 us  [the longest x1 12.1 us: local(): lax.dot_general(gathered, lo, dims, preferred_element_type=jnp.float32)]
where the time goes in v3:
time: 262 us
  waiting for transfers between devices  105 us (40%)
  starting transfers between devices  61.5 us (23%)
  other arithmetic  52.3 us (20%)
  matrix products  36.7 us (14%)
  local copies, waits for them, and re-layouts  5.79 us (2%)
    ppermute x34, starting transfers between devices, axis_sum(): lax.ppermute(v, axis, [(i, (i + s) % n) for i in range(n)])  49.8 us
    all_to_all x1, waiting for transfers between devices, gather_features(): got = lax.all_to_all(sent, CEN_AXES, 0, 0, tiled=False)  39.8 us
    all_to_all x1, waiting for transfers between devices, scatter_features(): got = lax.all_to_all(x, 'y', 0, 0, tiled=False)  31.2 us
    ppermute x34, waiting for transfers between devices, axis_sum(): lax.ppermute(v, axis, [(i, (i + s) % n) for i in range(n)])  27.9 us
    reduce_sum x3, other arithmetic, local(): row_part = jnp.sum(kernel * col_scale[None, :], axis=1)  21 us
    reduce_sum x2, other arithmetic, local(): col_part = jnp.sum(kernel * row_scale[:, None], axis=0)  13.9 us
    dot_general x1, matrix products, local(): jnp.dot(unit_points, unit_centroids.T, preferred_element_type=jnp.float32)  13.3 us
    dot_general x1, matrix products, local(): lax.dot_general(gathered, lo, dims, preferred_element_type=jnp.float32)  12.1 us
  transfers between devices with their start and end apart: 37, of which 31 were waited for; matrix products, arithmetic and copies ran while one was open for 4% of the time, Pallas kernels for 0%

profile of v3, /device:TPU:0, one launch (start us, length us, event | category | flops | bytes accessed | tf_op | source)
XLA Modules:
  0.0 261.8 jit_solution(10188392249454000976)
XLA Ops:
  0.6 2.9 %broadcast_in_dim.2 = bf16[16,2048,48]{1,2,0:T(8,128)(2,1)} broadcast(bf16[2048,48]{0,1:T(8,128)(2,1)} %param.2), dimensions={1,2} | broadcast | bytes 3342336 | tf_op jit(solution)/shard_map/broadcast_in_dim | solution.py:83
  3.6 8.0 %all-to-all-start = ((bf16[16,2048,48]{1,2,0:T(8,128)(2,1)}), bf16[16,2048,48]{1,2,0:T(8,128)(2,1)S(1)}, u32[]{:S(2)}, u32[]{:S(2)}) async-start(bf16[16,2048,48]{1,2,0:T(8,128)(2,1)} %broadcast_in_dim.2), calls=%async_computation | async-start | bytes 6291456 | tf_op jit(solution)/shard_map/all_to_all | solution.py:84
  11.6 2.6 fusion.6
  14.2 39.8 %all-to-all-done = bf16[16,2048,48]{1,2,0:T(8,128)(2,1)S(1)} async-done(((bf16[16,2048,48]{1,2,0:T(8,128)(2,1)}), bf16[16,2048,48]{1,2,0:T(8,128)(2,1)S(1)}, u32[]{:S(2)}, u32[]{:S(2)}) %all-to-all-start) | async-done | bytes 3145760 | tf_op jit(solution)/shard_map/all_to_all | solution.py:84
  54.7 13.3 %fusion.17 = (f32[2048]{0:T(1024)S(1)}, f32[2048,2048]{1,0:T(8,128)}) fusion(bf16[2048,768]{1,0:T(8,128)(2,1)} %param.3, f32[2048]{0:T(1024)S(1)} %add_rsqrt_fusion, bf16[2048,768]{0,1:T(8,128)(2,1)S(1)} %bitcast.22, f32[2048]{0:T(1024)S(1)} %add_rsqrt_fusion.1), kind=kOutput, calls=%fused_computation.50 | convolution fusion | flops 6460274688 | bytes 23093248 | tf_op jit(solution)/shard_map/dot_general | solution.py:104
  69.1 3.2 %collective-permute-start.1 = (f32[2048]{0:T(1024)S(1)}, f32[2048]{0:T(1024)S(1)}, u32[]{:S(2)}, u32[]{:S(2)}) collective-permute-start(f32[2048]{0:T(1024)S(1)} %add.158), channel_id=1, source_target_pairs={{0,64},{32,96},{64,0},{96,32},{1,65},{33,97},{65,1},{97,33},{2,66}... | collective-permute-start | bytes 24584 | tf_op jit(solution)/shard_map/ppermute | solution.py:27
  73.0 2.6 collective-permute-start.3
  75.5 1.6 collective-permute-done.2
  77.2 7.0 %multiply_reduce_fusion.4 = f32[2048]{0:T(1024)S(1)} fusion(f32[2048,2048]{1,0:T(8,128)} %get-tuple-element.7, f32[2048]{0:T(1024)S(1)} %add_divide_fusion.5), kind=kLoop, calls=%fused_computation.7 | loop fusion | flops 8386560 | bytes 16793600 | tf_op jit(solution)/shard_map/reduce_sum | solution.py:109
  84.2 2.6 %collective-permute-start.4 = (f32[2048]{0:T(1024)S(1)}, f32[2048]{0:T(1024)S(1)}, u32[]{:S(2)}, u32[]{:S(2)}) collective-permute-start(f32[2048]{0:T(1024)S(1)} %multiply_reduce_fusion.4), channel_id=1, source_target_pairs={{0,2},{1,3},{2,0},{3,1},{4,6},{5,7},{6,4},{7,5},{8,10},{9,11},{10,... | collective-permute-start | bytes 24584 | tf_op jit(solution)/shard_map/ppermute | solution.py:27
  87.1 3.0 %collective-permute-start.6 = (f32[2048]{0:T(1024)S(1)}, f32[2048]{0:T(1024)S(1)}, u32[]{:S(2)}, u32[]{:S(2)}) collective-permute-start(f32[2048]{0:T(1024)S(1)} %multiply_reduce_fusion.4), channel_id=1, source_target_pairs={{0,3},{1,0},{2,1},{3,2},{4,7},{5,4},{6,5},{7,6},{8,11},{9,8},{10,9... | collective-permute-start | bytes 24584 | tf_op jit(solution)/shard_map/ppermute | solution.py:27
  91.7 4.1 %collective-permute-start.7 = (f32[2048]{0:T(1024)S(1)}, f32[2048]{0:T(1024)S(1)}, u32[]{:S(2)}, u32[]{:S(2)}) collective-permute-start(f32[2048]{0:T(1024)S(1)} %add_add_fusion.3), channel_id=1, source_target_pairs={{0,8},{4,12},{8,0},{12,4},{1,9},{5,13},{9,1},{13,5},{2,10},{6,14},... | collective-permute-start | bytes 24584 | tf_op jit(solution)/shard_map/ppermute | solution.py:27
  95.8 3.2 %collective-permute-start.9 = (f32[2048]{0:T(1024)S(1)}, f32[2048]{0:T(1024)S(1)}, u32[]{:S(2)}, u32[]{:S(2)}) collective-permute-start(f32[2048]{0:T(1024)S(1)} %add_add_fusion.3), channel_id=1, source_target_pairs={{0,12},{4,0},{8,4},{12,8},{1,13},{5,1},{9,5},{13,9},{2,14},{6,2},{... | collective-permute-start | bytes 24584 | tf_op jit(solution)/shard_map/ppermute | solution.py:27
  100.7 6.9 %multiply_reduce_fusion.3 = f32[2048]{0:T(1024)S(1)} fusion(f32[2048,2048]{1,0:T(8,128)} %get-tuple-element.7, f32[2048]{0:T(1024)S(1)} %add_divide_fusion.4), kind=kLoop, calls=%fused_computation.6 | loop fusion | flops 8386560 | bytes 16793600 | tf_op jit(solution)/shard_map/reduce_sum | solution.py:107
  110.5 2.6 %collective-permute-start.12 = (f32[2048]{0:T(1024)S(1)}, f32[2048]{0:T(1024)S(1)}, u32[]{:S(2)}, u32[]{:S(2)}) collective-permute-start(f32[2048]{0:T(1024)S(1)} %add.168), channel_id=1, source_target_pairs={{0,32},{32,64},{64,96},{96,0},{1,33},{33,65},{65,97},{97,1},{2,34}... | collective-permute-start | bytes 24584 | tf_op jit(solution)/shard_map/ppermute | solution.py:27
  116.8 7.0 %multiply_reduce_fusion.2 = f32[2048]{0:T(1024)S(1)} fusion(f32[2048,2048]{1,0:T(8,128)} %get-tuple-element.7, f32[2048]{0:T(1024)S(1)} %add_divide_fusion.3), kind=kLoop, calls=%fused_computation.5 | loop fusion | flops 8386560 | bytes 16793600 | tf_op jit(solution)/shard_map/reduce_sum | solution.py:109
  125.2 2.6 %collective-permute-start.15 = (f32[2048]{0:T(1024)S(1)}, f32[2048]{0:T(1024)S(1)}, u32[]{:S(2)}, u32[]{:S(2)}) collective-permute-start(f32[2048]{0:T(1024)S(1)} %multiply_reduce_fusion.2), channel_id=1, source_target_pairs={{0,1},{1,2},{2,3},{3,0},{4,5},{5,6},{6,7},{7,4},{8,9},{9,10},{10,1... | collective-permute-start | bytes 24584 | tf_op jit(solution)/shard_map/ppermute | solution.py:27
  133.0 2.6 %collective-permute-start.18 = (f32[2048]{0:T(1024)S(1)}, f32[2048]{0:T(1024)S(1)}, u32[]{:S(2)}, u32[]{:S(2)}) collective-permute-start(f32[2048]{0:T(1024)S(1)} %add_add_fusion.2), channel_id=1, source_target_pairs={{0,4},{4,8},{8,12},{12,0},{1,5},{5,9},{9,13},{13,1},{2,6},{6,10},{... | collective-permute-start | bytes 24584 | tf_op jit(solution)/shard_map/ppermute | solution.py:27
  139.2 6.9 %multiply_reduce_fusion.1 = f32[2048]{0:T(1024)S(1)} fusion(f32[2048,2048]{1,0:T(8,128)} %get-tuple-element.7, f32[2048]{0:T(1024)S(1)} %add_divide_fusion.2), kind=kLoop, calls=%fused_computation.4 | loop fusion | flops 8386560 | bytes 16793600 | tf_op jit(solution)/shard_map/reduce_sum | solution.py:107
  148.1 2.1 collective-permute-start.22
  153.8 7.0 %multiply_reduce_fusion = f32[2048]{0:T(1024)S(1)} fusion(f32[2048,2048]{1,0:T(8,128)} %get-tuple-element.7, f32[2048]{0:T(1024)S(1)} %add_divide_fusion.1), kind=kLoop, calls=%fused_computation.3 | loop fusion | flops 8386560 | bytes 16793600 | tf_op jit(solution)/shard_map/reduce_sum | solution.py:109
  161.6 2.0 collective-permute-start.25
  167.9 2.0 collective-permute-start.28
  173.5 12.1 %fusion.1 = f32[2048,768]{0,1:T(8,128)} fusion(bf16[2048,768]{0,1:T(8,128)(2,1)S(1)} %bitcast.23, f32[2048,2048]{1,0:T(8,128)} %get-tuple-element.7, f32[2048]{0:T(1024)S(1)} %add_divide_fusion), kind=kOutput, calls=%fused_computation.10 | convolution fusion | flops 6459228160 | bytes 26222592 | tf_op jit(solution)/shard_map/dot_general | solution.py:118
  185.6 11.3 %add_multiply_fusion = f32[2048,768]{0,1:T(8,128)S(1)} fusion(f32[2048,768]{0,1:T(8,128)} %fusion.1, f32[2048]{0:T(1024)S(1)} %add_divide_fusion.1, bf16[2048,768]{0,1:T(8,128)(2,1)S(1)} %bitcast.24, f32[2048,2048]{1,0:T(8,128)} %get-tuple-element.7, f32[2048]{0:T(1024)S(1)} %add_divide_fusion), kind=kOutput, calls=%fused_computation.18 | convolution fusion | flops 6458179584 | bytes 32522240 | tf_op jit(solution)/shard_map/dot_general | solution.py:116
  197.0 2.6 %copy-done = f32[2048,768]{0,1:T(8,128)} copy-done((f32[2048,768]{0,1:T(8,128)}, f32[2048,768]{0,1:T(8,128)S(1)}, u32[]{:S(2)}) %copy-start) | copy-done | bytes 6291480
  199.9 5.8 %collective-permute-done.30 = f32[4,96,2048]{2,1,0:T(8,128)} collective-permute-done((f32[4,96,2048]{2,1,0:T(8,128)S(1)}, f32[4,96,2048]{2,1,0:T(8,128)}, u32[]{:S(2)}, u32[]{:S(2)}) %collective-permute-start.30) | collective-permute-done | bytes 3145760 | tf_op jit(solution)/shard_map/ppermute | solution.py:66
  205.7 5.3 %bitcast_add_fusion = f32[4,96,2048]{2,1,0:T(8,128)} fusion(f32[4,96,2048]{2,1,0:T(8,128)} %collective-permute-done.30, f32[4,2,96,2048]{3,2,1,0:T(8,128)} %bitcast.26, s32[]{:T(128)S(6)} %select_n.7), kind=kLoop, calls=%fused_computation.21 | loop fusion | flops 786432 | bytes 9437188 | tf_op jit(solution)/shard_map/add | solution.py:66
  210.9 3.7 %all-to-all-start.1 = ((f32[4,96,2048]{2,1,0:T(8,128)}), f32[4,96,2048]{2,1,0:T(8,128)S(1)}, u32[]{:S(2)}, u32[]{:S(2)}) async-start(f32[4,96,2048]{2,1,0:T(8,128)} %bitcast_add_fusion), calls=%async_computation.1 | async-start | bytes 6291456 | tf_op jit(solution)/shard_map/all_to_all | solution.py:71
  214.6 6.9 %multiply_reduce_fusion.5 = f32[2048]{0:T(1024)S(1)} fusion(f32[2048,2048]{1,0:T(8,128)} %get-tuple-element.7, f32[2048]{0:T(1024)S(1)} %add_divide_fusion), kind=kLoop, calls=%fused_computation.9 | loop fusion | flops 8386560 | bytes 16793600 | tf_op jit(solution)/shard_map/reduce_sum | solution.py:120
  221.6 31.2 %all-to-all-done.1 = f32[4,96,2048]{2,1,0:T(8,128)S(1)} async-done(((f32[4,96,2048]{2,1,0:T(8,128)}), f32[4,96,2048]{2,1,0:T(8,128)S(1)}, u32[]{:S(2)}, u32[]{:S(2)}) %all-to-all-start.1) | async-done | bytes 3145760 | tf_op jit(solution)/shard_map/all_to_all | solution.py:71
  256.4 1.8 collective-permute-start.34
  (79 shorter events, 44.5 us)
Async XLA Ops:
  3.6 50.4 %all-to-all-start = ((bf16[16,2048,48]{1,2,0:T(8,128)(2,1)}), bf16[16,2048,48]{1,2,0:T(8,128)(2,1)S(1)}, u32[]{:S(2)}, u32[]{:S(2)}) async-start(bf16[16,2048,48]{1,2,0:T(8,128)(2,1)} %broadcast_in_dim.2), calls=%async_computation | async-start | bytes 6291456 | tf_op jit(solution)/shard_map/all_to_all | solution.py:84
  69.1 6.4 %collective-permute-start.1 = (f32[2048]{0:T(1024)S(1)}, f32[2048]{0:T(1024)S(1)}, u32[]{:S(2)}, u32[]{:S(2)}) collective-permute-start(f32[2048]{0:T(1024)S(1)} %add.158), channel_id=1, source_target_pairs={{0,64},{32,96},{64,0},{96,32},{1,65},{33,97},{65,1},{97,33},{2,66}... | collective-permute-start | bytes 24584 | tf_op jit(solution)/shard_map/ppermute | solution.py:27
  72.3 4.9 %collective-permute-start.2 = (f32[2048]{0:T(1024)S(1)}, f32[2048]{0:T(1024)S(1)}, u32[]{:S(2)}, u32[]{:S(2)}) collective-permute-start(f32[2048]{0:T(1024)S(1)} %add.158), channel_id=1, source_target_pairs={{0,32},{32,64},{64,96},{96,0},{1,33},{33,65},{65,97},{97,1},{2,34}... | collective-permute-start | bytes 24584 | tf_op jit(solution)/shard_map/ppermute | solution.py:27
  73.0 4.2 %collective-permute-start.3 = (f32[2048]{0:T(1024)S(1)}, f32[2048]{0:T(1024)S(1)}, u32[]{:S(2)}, u32[]{:S(2)}) collective-permute-start(f32[2048]{0:T(1024)S(1)} %add.158), channel_id=1, source_target_pairs={{0,96},{32,0},{64,32},{96,64},{1,97},{33,1},{65,33},{97,65},{2,98}... | collective-permute-start | bytes 24584 | tf_op jit(solution)/shard_map/ppermute | solution.py:27
  84.2 5.9 %collective-permute-start.4 = (f32[2048]{0:T(1024)S(1)}, f32[2048]{0:T(1024)S(1)}, u32[]{:S(2)}, u32[]{:S(2)}) collective-permute-start(f32[2048]{0:T(1024)S(1)} %multiply_reduce_fusion.4), channel_id=1, source_target_pairs={{0,2},{1,3},{2,0},{3,1},{4,6},{5,7},{6,4},{7,5},{8,10},{9,11},{10,... | collective-permute-start | bytes 24584 | tf_op jit(solution)/shard_map/ppermute | solution.py:27
  86.8 4.9 %collective-permute-start.5 = (f32[2048]{0:T(1024)S(1)}, f32[2048]{0:T(1024)S(1)}, u32[]{:S(2)}, u32[]{:S(2)}) collective-permute-start(f32[2048]{0:T(1024)S(1)} %multiply_reduce_fusion.4), channel_id=1, source_target_pairs={{0,1},{1,2},{2,3},{3,0},{4,5},{5,6},{6,7},{7,4},{8,9},{9,10},{10,1... | collective-permute-start | bytes 24584 | tf_op jit(solution)/shard_map/ppermute | solution.py:27
  87.1 4.6 %collective-permute-start.6 = (f32[2048]{0:T(1024)S(1)}, f32[2048]{0:T(1024)S(1)}, u32[]{:S(2)}, u32[]{:S(2)}) collective-permute-start(f32[2048]{0:T(1024)S(1)} %multiply_reduce_fusion.4), channel_id=1, source_target_pairs={{0,3},{1,0},{2,1},{3,2},{4,7},{5,4},{6,5},{7,6},{8,11},{9,8},{10,9... | collective-permute-start | bytes 24584 | tf_op jit(solution)/shard_map/ppermute | solution.py:27
  91.7 7.4 %collective-permute-start.7 = (f32[2048]{0:T(1024)S(1)}, f32[2048]{0:T(1024)S(1)}, u32[]{:S(2)}, u32[]{:S(2)}) collective-permute-start(f32[2048]{0:T(1024)S(1)} %add_add_fusion.3), channel_id=1, source_target_pairs={{0,8},{4,12},{8,0},{12,4},{1,9},{5,13},{9,1},{13,5},{2,10},{6,14},... | collective-permute-start | bytes 24584 | tf_op jit(solution)/shard_map/ppermute | solution.py:27
  95.8 4.9 %collective-permute-start.8 = (f32[2048]{0:T(1024)S(1)}, f32[2048]{0:T(1024)S(1)}, u32[]{:S(2)}, u32[]{:S(2)}) collective-permute-start(f32[2048]{0:T(1024)S(1)} %add_add_fusion.3), channel_id=1, source_target_pairs={{0,4},{4,8},{8,12},{12,0},{1,5},{5,9},{9,13},{13,1},{2,6},{6,10},{... | collective-permute-start | bytes 24584 | tf_op jit(solution)/shard_map/ppermute | solution.py:27
  95.8 4.9 %collective-permute-start.9 = (f32[2048]{0:T(1024)S(1)}, f32[2048]{0:T(1024)S(1)}, u32[]{:S(2)}, u32[]{:S(2)}) collective-permute-start(f32[2048]{0:T(1024)S(1)} %add_add_fusion.3), channel_id=1, source_target_pairs={{0,12},{4,0},{8,4},{12,8},{1,13},{5,1},{9,5},{13,9},{2,14},{6,2},{... | collective-permute-start | bytes 24584 | tf_op jit(solution)/shard_map/ppermute | solution.py:27
  109.1 5.2 %collective-permute-start.11 = (f32[2048]{0:T(1024)S(1)}, f32[2048]{0:T(1024)S(1)}, u32[]{:S(2)}, u32[]{:S(2)}) collective-permute-start(f32[2048]{0:T(1024)S(1)} %add.168), channel_id=1, source_target_pairs={{0,64},{32,96},{64,0},{96,32},{1,65},{33,97},{65,1},{97,33},{2,66}... | collective-permute-start | bytes 24584 | tf_op jit(solution)/shard_map/ppermute | solution.py:27
  110.5 4.9 %collective-permute-start.12 = (f32[2048]{0:T(1024)S(1)}, f32[2048]{0:T(1024)S(1)}, u32[]{:S(2)}, u32[]{:S(2)}) collective-permute-start(f32[2048]{0:T(1024)S(1)} %add.168), channel_id=1, source_target_pairs={{0,32},{32,64},{64,96},{96,0},{1,33},{33,65},{65,97},{97,1},{2,34}... | collective-permute-start | bytes 24584 | tf_op jit(solution)/shard_map/ppermute | solution.py:27
  113.2 3.7 %collective-permute-start.13 = (f32[2048]{0:T(1024)S(1)}, f32[2048]{0:T(1024)S(1)}, u32[]{:S(2)}, u32[]{:S(2)}) collective-permute-start(f32[2048]{0:T(1024)S(1)} %add.168), channel_id=1, source_target_pairs={{0,96},{32,0},{64,32},{96,64},{1,97},{33,1},{65,33},{97,65},{2,98}... | collective-permute-start | bytes 24584 | tf_op jit(solution)/shard_map/ppermute | solution.py:27
  123.8 5.2 %collective-permute-start.14 = (f32[2048]{0:T(1024)S(1)}, f32[2048]{0:T(1024)S(1)}, u32[]{:S(2)}, u32[]{:S(2)}) collective-permute-start(f32[2048]{0:T(1024)S(1)} %multiply_reduce_fusion.2), channel_id=1, source_target_pairs={{0,2},{1,3},{2,0},{3,1},{4,6},{5,7},{6,4},{7,5},{8,10},{9,11},{10,... | collective-permute-start | bytes 24584 | tf_op jit(solution)/shard_map/ppermute | solution.py:27
  125.2 4.9 %collective-permute-start.15 = (f32[2048]{0:T(1024)S(1)}, f32[2048]{0:T(1024)S(1)}, u32[]{:S(2)}, u32[]{:S(2)}) collective-permute-start(f32[2048]{0:T(1024)S(1)} %multiply_reduce_fusion.2), channel_id=1, source_target_pairs={{0,1},{1,2},{2,3},{3,0},{4,5},{5,6},{6,7},{7,4},{8,9},{9,10},{10,1... | collective-permute-start | bytes 24584 | tf_op jit(solution)/shard_map/ppermute | solution.py:27
  127.8 3.7 %collective-permute-start.16 = (f32[2048]{0:T(1024)S(1)}, f32[2048]{0:T(1024)S(1)}, u32[]{:S(2)}, u32[]{:S(2)}) collective-permute-start(f32[2048]{0:T(1024)S(1)} %multiply_reduce_fusion.2), channel_id=1, source_target_pairs={{0,3},{1,0},{2,1},{3,2},{4,7},{5,4},{6,5},{7,6},{8,11},{9,8},{10,9... | collective-permute-start | bytes 24584 | tf_op jit(solution)/shard_map/ppermute | solution.py:27
  131.5 5.2 %collective-permute-start.17 = (f32[2048]{0:T(1024)S(1)}, f32[2048]{0:T(1024)S(1)}, u32[]{:S(2)}, u32[]{:S(2)}) collective-permute-start(f32[2048]{0:T(1024)S(1)} %add_add_fusion.2), channel_id=1, source_target_pairs={{0,8},{4,12},{8,0},{12,4},{1,9},{5,13},{9,1},{13,5},{2,10},{6,14},... | collective-permute-start | bytes 24584 | tf_op jit(solution)/shard_map/ppermute | solution.py:27
  133.0 4.9 %collective-permute-start.18 = (f32[2048]{0:T(1024)S(1)}, f32[2048]{0:T(1024)S(1)}, u32[]{:S(2)}, u32[]{:S(2)}) collective-permute-start(f32[2048]{0:T(1024)S(1)} %add_add_fusion.2), channel_id=1, source_target_pairs={{0,4},{4,8},{8,12},{12,0},{1,5},{5,9},{9,13},{13,1},{2,6},{6,10},{... | collective-permute-start | bytes 24584 | tf_op jit(solution)/shard_map/ppermute | solution.py:27
  135.6 3.7 %collective-permute-start.19 = (f32[2048]{0:T(1024)S(1)}, f32[2048]{0:T(1024)S(1)}, u32[]{:S(2)}, u32[]{:S(2)}) collective-permute-start(f32[2048]{0:T(1024)S(1)} %add_add_fusion.2), channel_id=1, source_target_pairs={{0,12},{4,0},{8,4},{12,8},{1,13},{5,1},{9,5},{13,9},{2,14},{6,2},{... | collective-permute-start | bytes 24584 | tf_op jit(solution)/shard_map/ppermute | solution.py:27
  147.4 5.2 %collective-permute-start.21 = (f32[2048]{0:T(1024)S(1)}, f32[2048]{0:T(1024)S(1)}, u32[]{:S(2)}, u32[]{:S(2)}) collective-permute-start(f32[2048]{0:T(1024)S(1)} %add.178), channel_id=1, source_target_pairs={{0,64},{32,96},{64,0},{96,32},{1,65},{33,97},{65,1},{97,33},{2,66}... | collective-permute-start | bytes 24584 | tf_op jit(solution)/shard_map/ppermute | solution.py:27
  148.1 4.9 %collective-permute-start.22 = (f32[2048]{0:T(1024)S(1)}, f32[2048]{0:T(1024)S(1)}, u32[]{:S(2)}, u32[]{:S(2)}) collective-permute-start(f32[2048]{0:T(1024)S(1)} %add.178), channel_id=1, source_target_pairs={{0,32},{32,64},{64,96},{96,0},{1,33},{33,65},{65,97},{97,1},{2,34}... | collective-permute-start | bytes 24584 | tf_op jit(solution)/shard_map/ppermute | solution.py:27
  160.8 5.2 %collective-permute-start.24 = (f32[2048]{0:T(1024)S(1)}, f32[2048]{0:T(1024)S(1)}, u32[]{:S(2)}, u32[]{:S(2)}) collective-permute-start(f32[2048]{0:T(1024)S(1)} %multiply_reduce_fusion), channel_id=1, source_target_pairs={{0,2},{1,3},{2,0},{3,1},{4,6},{5,7},{6,4},{7,5},{8,10},{9,11},{10,... | collective-permute-start | bytes 24584 | tf_op jit(solution)/shard_map/ppermute | solution.py:27
  161.6 4.9 %collective-permute-start.25 = (f32[2048]{0:T(1024)S(1)}, f32[2048]{0:T(1024)S(1)}, u32[]{:S(2)}, u32[]{:S(2)}) collective-permute-start(f32[2048]{0:T(1024)S(1)} %multiply_reduce_fusion), channel_id=1, source_target_pairs={{0,1},{1,2},{2,3},{3,0},{4,5},{5,6},{6,7},{7,4},{8,9},{9,10},{10,1... | collective-permute-start | bytes 24584 | tf_op jit(solution)/shard_map/ppermute | solution.py:27
  163.5 3.7 %collective-permute-start.26 = (f32[2048]{0:T(1024)S(1)}, f32[2048]{0:T(1024)S(1)}, u32[]{:S(2)}, u32[]{:S(2)}) collective-permute-start(f32[2048]{0:T(1024)S(1)} %multiply_reduce_fusion), channel_id=1, source_target_pairs={{0,3},{1,0},{2,1},{3,2},{4,7},{5,4},{6,5},{7,6},{8,11},{9,8},{10,9... | collective-permute-start | bytes 24584 | tf_op jit(solution)/shard_map/ppermute | solution.py:27
  167.2 5.2 %collective-permute-start.27 = (f32[2048]{0:T(1024)S(1)}, f32[2048]{0:T(1024)S(1)}, u32[]{:S(2)}, u32[]{:S(2)}) collective-permute-start(f32[2048]{0:T(1024)S(1)} %add_add_fusion.1), channel_id=1, source_target_pairs={{0,8},{4,12},{8,0},{12,4},{1,9},{5,13},{9,1},{13,5},{2,10},{6,14},... | collective-permute-start | bytes 24584 | tf_op jit(solution)/shard_map/ppermute | solution.py:27
  167.9 4.9 %collective-permute-start.28 = (f32[2048]{0:T(1024)S(1)}, f32[2048]{0:T(1024)S(1)}, u32[]{:S(2)}, u32[]{:S(2)}) collective-permute-start(f32[2048]{0:T(1024)S(1)} %add_add_fusion.1), channel_id=1, source_target_pairs={{0,4},{4,8},{8,12},{12,0},{1,5},{5,9},{9,13},{13,1},{2,6},{6,10},{... | collective-permute-start | bytes 24584 | tf_op jit(solution)/shard_map/ppermute | solution.py:27
  169.9 3.7 %collective-permute-start.29 = (f32[2048]{0:T(1024)S(1)}, f32[2048]{0:T(1024)S(1)}, u32[]{:S(2)}, u32[]{:S(2)}) collective-permute-start(f32[2048]{0:T(1024)S(1)} %add_add_fusion.1), channel_id=1, source_target_pairs={{0,12},{4,0},{8,4},{12,8},{1,13},{5,1},{9,5},{13,9},{2,14},{6,2},{... | collective-permute-start | bytes 24584 | tf_op jit(solution)/shard_map/ppermute | solution.py:27
  199.8 5.9 %collective-permute-start.30 = (f32[4,96,2048]{2,1,0:T(8,128)S(1)}, f32[4,96,2048]{2,1,0:T(8,128)}, u32[]{:S(2)}, u32[]{:S(2)}) collective-permute-start(f32[4,96,2048]{2,1,0:T(8,128)S(1)} %dynamic-slice_bitcast_fusion), channel_id=1, source_target_pairs={{0,16},{16,0},{1,17},{17,1},{2,18},{18,2},{3,19},{19,3},{4,20},{20... | collective-permute-start | bytes 9437192 | tf_op jit(solution)/shard_map/ppermute | solution.py:66
  210.9 41.8 %all-to-all-start.1 = ((f32[4,96,2048]{2,1,0:T(8,128)}), f32[4,96,2048]{2,1,0:T(8,128)S(1)}, u32[]{:S(2)}, u32[]{:S(2)}) async-start(f32[4,96,2048]{2,1,0:T(8,128)} %bitcast_add_fusion), calls=%async_computation.1 | async-start | bytes 6291456 | tf_op jit(solution)/shard_map/all_to_all | solution.py:71
  254.3 5.4 %collective-permute-start.32 = (f32[2,2048]{1,0:T(2,128)S(1)}, f32[2,2048]{1,0:T(2,128)S(1)}, u32[]{:S(2)}, u32[]{:S(2)}) collective-permute-start(f32[2,2048]{1,0:T(2,128)S(1)} %fusion.14), channel_id=1, source_target_pairs={{0,64},{32,96},{64,0},{96,32},{1,65},{33,97},{65,1},{97,33},{2,66}... | collective-permute-start | bytes 49160 | tf_op jit(solution)/shard_map/ppermute | solution.py:27
  254.9 4.9 %collective-permute-start.33 = (f32[2,2048]{1,0:T(2,128)S(1)}, f32[2,2048]{1,0:T(2,128)S(1)}, u32[]{:S(2)}, u32[]{:S(2)}) collective-permute-start(f32[2,2048]{1,0:T(2,128)S(1)} %fusion.14), channel_id=1, source_target_pairs={{0,32},{32,64},{64,96},{96,0},{1,33},{33,65},{65,97},{97,1},{2,34}... | collective-permute-start | bytes 49160 | tf_op jit(solution)/shard_map/ppermute | solution.py:27
  256.4 3.7 %collective-permute-start.34 = (f32[2,2048]{1,0:T(2,128)S(1)}, f32[2,2048]{1,0:T(2,128)S(1)}, u32[]{:S(2)}, u32[]{:S(2)}) collective-permute-start(f32[2,2048]{1,0:T(2,128)S(1)} %fusion.14), channel_id=1, source_target_pairs={{0,96},{32,0},{64,32},{96,64},{1,97},{33,1},{65,33},{97,65},{2,98}... | collective-permute-start | bytes 49160 | tf_op jit(solution)/shard_map/ppermute | solution.py:27
  (6 other events, 11.4 us)

commit v4 on v3

--- a/solution.py
+++ b/solution.py
@@ -35,6 +35,16 @@
     total = canon[0]
     for j in range(1, n):
         total = total + canon[j]
+    return total
+
+
+def group_sum(v, axes, n):
+    if n == 1:
+        return v
+    got = lax.all_to_all(jnp.broadcast_to(v[None], (n,) + v.shape), axes, 0, 0, tiled=False)
+    total = got[0]
+    for j in range(1, n):
+        total = total + got[j]
     return total
 
 
@@ -107,7 +117,7 @@
             col_part = jnp.sum(kernel * row_scale[:, None], axis=0)
             col_scale = balance / multi_sum(col_part, pts_red)
             row_part = jnp.sum(kernel * col_scale[None, :], axis=1)
-            row_scale = 1.0 / multi_sum(row_part, cen_red)
+            row_scale = 1.0 / group_sum(row_part, CEN_AXES, n_cen)
         scaled = kernel * row_scale[:, None]
         hi_wide = lax.reduce_precision(scaled, exponent_bits=8, mantissa_bits=7)
         hi = hi_wide.astype(jnp.bfloat16)

time: 262 us -> 259 us (0.989)
  starting transfers between devices: 61.5 us -> 34.1 us
  blocking collectives: 0 us -> 26.7 us
  waiting for transfers between devices: 105 us -> 101 us
    ppermute x34 -> x16, starting transfers between devices: 49.8 us -> 18.6 us  [axis_sum(): lax.ppermute(v, axis, [(i, (i + s) % n) for i in range(n)])]
    all_to_all x0 -> x2, blocking collectives: none -> 26.7 us  [group_sum(): lax.all_to_all(jnp.broadcast_to(v[None], (n,) + v.shape), axes, 0, 0, til...]
    ppermute x34 -> x16, waiting for transfers between devices: 27.9 us -> 16.4 us  [axis_sum(): lax.ppermute(v, axis, [(i, (i + s) % n) for i in range(n)])]
    all_to_all x0 -> x1, waiting for transfers between devices: none -> 7.84 us  [group_sum(): lax.all_to_all(jnp.broadcast_to(v[None], (n,) + v.shape), axes, 0, 0, til...]
    all_to_all x0 -> x1, starting transfers between devices: none -> 3.6 us  [group_sum(): lax.all_to_all(jnp.broadcast_to(v[None], (n,) + v.shape), axes, 0, 0, til...]
  transfers between devices with their start and end apart: 37 -> 20, of which waited for: 31 -> 17; matrix products, arithmetic and copies ran while one was open for 4% -> 4% of each run, Pallas kernels for 0% -> 0%
where the time goes in v4:
time: 259 us; the launch traced here: 258 us
  waiting for transfers between devices  101 us (39%)
  other arithmetic  52.3 us (20%)
  matrix products  36.7 us (14%)
  starting transfers between devices  34.1 us (13%)
  blocking collectives  26.7 us (10%)
  local copies, waits for them, and re-layouts  6.7 us (3%)
    all_to_all x1, waiting for transfers between devices, gather_features(): got = lax.all_to_all(sent, CEN_AXES, 0, 0, tiled=False)  39.8 us
    all_to_all x1, waiting for transfers between devices, scatter_features(): got = lax.all_to_all(x, 'y', 0, 0, tiled=False)  31.2 us
    all_to_all x2, blocking collectives, group_sum(): lax.all_to_all(jnp.broadcast_to(v[None], (n,) + v.shape), axes, 0, 0, til...  26.7 us
    reduce_sum x3, other arithmetic, local(): row_part = jnp.sum(kernel * col_scale[None, :], axis=1)  20.9 us
    ppermute x16, starting transfers between devices, axis_sum(): lax.ppermute(v, axis, [(i, (i + s) % n) for i in range(n)])  18.6 us
    ppermute x16, waiting for transfers between devices, axis_sum(): lax.ppermute(v, axis, [(i, (i + s) % n) for i in range(n)])  16.4 us
    reduce_sum x2, other arithmetic, local(): col_part = jnp.sum(kernel * row_scale[:, None], axis=0)  13.9 us
    dot_general x1, matrix products, local(): jnp.dot(unit_points, unit_centroids.T, preferred_element_type=jnp.float32)  13.2 us
  transfers between devices with their start and end apart: 20, of which 17 were waited for; matrix products, arithmetic and copies ran while one was open for 4% of the time, Pallas kernels for 0%

profile of v4, /device:TPU:0, one launch (start us, length us, event | category | flops | bytes accessed | tf_op | source)
XLA Modules:
  0.0 258.4 jit_solution(12950367611493071925)
XLA Ops:
  0.6 3.0 %broadcast_in_dim.8 = bf16[16,2048,48]{1,2,0:T(8,128)(2,1)} broadcast(bf16[2048,48]{0,1:T(8,128)(2,1)} %param.2), dimensions={1,2} | broadcast | bytes 3342336 | tf_op jit(solution)/shard_map/broadcast_in_dim | solution.py:93
  3.6 8.0 %all-to-all-start = ((bf16[16,2048,48]{1,2,0:T(8,128)(2,1)}), bf16[16,2048,48]{1,2,0:T(8,128)(2,1)S(1)}, u32[]{:S(2)}, u32[]{:S(2)}) async-start(bf16[16,2048,48]{1,2,0:T(8,128)(2,1)} %broadcast_in_dim.8), calls=%async_computation | async-start | bytes 6291456 | tf_op jit(solution)/shard_map/all_to_all | solution.py:94
  11.6 2.6 fusion.6
  14.2 39.8 %all-to-all-done = bf16[16,2048,48]{1,2,0:T(8,128)(2,1)S(1)} async-done(((bf16[16,2048,48]{1,2,0:T(8,128)(2,1)}), bf16[16,2048,48]{1,2,0:T(8,128)(2,1)S(1)}, u32[]{:S(2)}, u32[]{:S(2)}) %all-to-all-start) | async-done | bytes 3145760 | tf_op jit(solution)/shard_map/all_to_all | solution.py:94
  54.7 13.2 %fusion.20 = (f32[2048]{0:T(1024)S(1)}, f32[2048,2048]{1,0:T(8,128)}) fusion(bf16[2048,768]{1,0:T(8,128)(2,1)} %param.3, f32[2048]{0:T(1024)S(1)} %add_rsqrt_fusion, bf16[2048,768]{0,1:T(8,128)(2,1)S(1)} %bitcast.25, f32[2048]{0:T(1024)S(1)} %add_rsqrt_fusion.1), kind=kOutput, calls=%fused_computation.92 | convolution fusion | flops 6460274688 | bytes 23093248 | tf_op jit(solution)/shard_map/dot_general | solution.py:114
  69.1 3.2 %collective-permute-start.1 = (f32[2048]{0:T(1024)S(1)}, f32[2048]{0:T(1024)S(1)}, u32[]{:S(2)}, u32[]{:S(2)}) collective-permute-start(f32[2048]{0:T(1024)S(1)} %add.437), channel_id=1, source_target_pairs={{0,64},{32,96},{64,0},{96,32},{1,65},{33,97},{65,1},{97,33},{2,66}... | collective-permute-start | bytes 24584 | tf_op jit(solution)/shard_map/ppermute | solution.py:27
  73.0 2.6 collective-permute-start.3
  75.5 1.6 collective-permute-done.2
  77.2 7.0 %multiply_reduce_fusion.4 = f32[2048]{0:T(1024)S(1)} fusion(f32[2048,2048]{1,0:T(8,128)} %get-tuple-element.7, f32[2048]{0:T(1024)S(1)} %add_divide_fusion.2), kind=kLoop, calls=%fused_computation.7 | loop fusion | flops 8386560 | bytes 16793600 | tf_op jit(solution)/shard_map/reduce_sum | solution.py:119
  84.3 15.5 %all_to_all.28 = f32[16,1,2048]{2,1,0:T(1,128)S(1)} all-to-all(f32[16,1,2048]{2,1,0:T(1,128)S(1)} %broadcast_in_dim.9), channel_id=1, replica_groups=mesh['y'=4,'c'=2,'x'=4,'z'=4] {'x','z'}, dimensions={0} | all-to-all | bytes 262144 | tf_op jit(solution)/shard_map/all_to_all | solution.py:44
  99.8 6.9 %multiply_reduce_fusion.3 = f32[2048]{0:T(1024)S(1)} fusion(f32[2048,2048]{1,0:T(8,128)} %get-tuple-element.7, f32[2048]{0:T(1024)S(1)} %bitcast.39), kind=kLoop, calls=%fused_computation.6 | loop fusion | flops 8386560 | bytes 16793600 | tf_op jit(solution)/shard_map/reduce_sum | solution.py:117
  109.5 2.6 %collective-permute-start.6 = (f32[2048]{0:T(1024)S(1)}, f32[2048]{0:T(1024)S(1)}, u32[]{:S(2)}, u32[]{:S(2)}) collective-permute-start(f32[2048]{0:T(1024)S(1)} %add.457), channel_id=1, source_target_pairs={{0,32},{32,64},{64,96},{96,0},{1,33},{33,65},{65,97},{97,1},{2,34}... | collective-permute-start | bytes 24584 | tf_op jit(solution)/shard_map/ppermute | solution.py:27
  115.8 7.0 %multiply_reduce_fusion.2 = f32[2048]{0:T(1024)S(1)} fusion(f32[2048,2048]{1,0:T(8,128)} %get-tuple-element.7, f32[2048]{0:T(1024)S(1)} %add_divide_fusion.1), kind=kLoop, calls=%fused_computation.5 | loop fusion | flops 8386560 | bytes 16793600 | tf_op jit(solution)/shard_map/reduce_sum | solution.py:119
  122.9 11.2 %all_to_all.29 = f32[16,1,2048]{2,1,0:T(1,128)S(1)} all-to-all(f32[16,1,2048]{2,1,0:T(1,128)S(1)} %broadcast_in_dim.10), channel_id=1, replica_groups=mesh['y'=4,'c'=2,'x'=4,'z'=4] {'x','z'}, dimensions={0} | all-to-all | bytes 262144 | tf_op jit(solution)/shard_map/all_to_all | solution.py:44
  134.2 6.9 %multiply_reduce_fusion.1 = f32[2048]{0:T(1024)S(1)} fusion(f32[2048,2048]{1,0:T(8,128)} %get-tuple-element.7, f32[2048]{0:T(1024)S(1)} %bitcast.40), kind=kLoop, calls=%fused_computation.4 | loop fusion | flops 8386560 | bytes 16793600 | tf_op jit(solution)/shard_map/reduce_sum | solution.py:117
  142.4 3.2 %collective-permute-start.11 = (f32[2048]{0:T(1024)S(1)}, f32[2048]{0:T(1024)S(1)}, u32[]{:S(2)}, u32[]{:S(2)}) collective-permute-start(f32[2048]{0:T(1024)S(1)} %add.477), channel_id=1, source_target_pairs={{0,96},{32,0},{64,32},{96,64},{1,97},{33,1},{65,33},{97,65},{2,98}... | collective-permute-start | bytes 24584 | tf_op jit(solution)/shard_map/ppermute | solution.py:27
  145.6 1.6 collective-permute-done.10
  147.2 3.5 %collective-permute-done.9 = f32[2048]{0:T(1024)S(1)} collective-permute-done((f32[2048]{0:T(1024)S(1)}, f32[2048]{0:T(1024)S(1)}, u32[]{:S(2)}, u32[]{:S(2)}) %collective-permute-start.9) | collective-permute-done | bytes 8224 | tf_op jit(solution)/shard_map/ppermute | solution.py:27
  150.8 6.9 %multiply_reduce_fusion = f32[2048]{0:T(1024)S(1)} fusion(f32[2048,2048]{1,0:T(8,128)} %get-tuple-element.7, f32[2048]{0:T(1024)S(1)} %add_divide_fusion), kind=kLoop, calls=%fused_computation.3 | loop fusion | flops 8386560 | bytes 16793600 | tf_op jit(solution)/shard_map/reduce_sum | solution.py:119
  158.4 3.6 %all-to-all-start.3 = ((f32[16,1,2048]{2,1,0:T(1,128)}), f32[16,1,2048]{2,1,0:T(1,128)S(1)}, u32[]{:S(2)}, u32[]{:S(2)}) async-start(f32[16,1,2048]{2,1,0:T(1,128)} %broadcast_in_dim.11), calls=%async_computation.3 | async-start | bytes 262144 | tf_op jit(solution)/shard_map/all_to_all | solution.py:44
  162.0 7.8 %all-to-all-done.3 = f32[16,1,2048]{2,1,0:T(1,128)S(1)} async-done(((f32[16,1,2048]{2,1,0:T(1,128)}), f32[16,1,2048]{2,1,0:T(1,128)S(1)}, u32[]{:S(2)}, u32[]{:S(2)}) %all-to-all-start.3) | async-done | bytes 131104 | tf_op jit(solution)/shard_map/all_to_all | solution.py:44
  169.9 12.1 %fusion.1 = f32[2048,768]{0,1:T(8,128)} fusion(bf16[2048,768]{0,1:T(8,128)(2,1)S(1)} %bitcast.26, f32[2048,2048]{1,0:T(8,128)} %get-tuple-element.7, f32[2048]{0:T(1024)S(1)} %bitcast.36), kind=kOutput, calls=%fused_computation.10 | convolution fusion | flops 6459228160 | bytes 26222592 | tf_op jit(solution)/shard_map/dot_general | solution.py:128
  182.0 11.3 %add_multiply_fusion = f32[2048,768]{0,1:T(8,128)S(1)} fusion(f32[2048,768]{0,1:T(8,128)} %fusion.1, f32[2048]{0:T(1024)S(1)} %add_divide_fusion, bf16[2048,768]{0,1:T(8,128)(2,1)S(1)} %bitcast.27, f32[2048,2048]{1,0:T(8,128)} %get-tuple-element.7, f32[2048]{0:T(1024)S(1)} %bitcast.37), kind=kOutput, calls=%fused_computation.18 | convolution fusion | flops 6458179584 | bytes 32522240 | tf_op jit(solution)/shard_map/dot_general | solution.py:126
  193.4 2.6 %copy-done = f32[2048,768]{0,1:T(8,128)} copy-done((f32[2048,768]{0,1:T(8,128)}, f32[2048,768]{0,1:T(8,128)S(1)}, u32[]{:S(2)}) %copy-start) | copy-done | bytes 6291480
  196.3 5.8 %collective-permute-done.12 = f32[4,96,2048]{2,1,0:T(8,128)} collective-permute-done((f32[4,96,2048]{2,1,0:T(8,128)S(1)}, f32[4,96,2048]{2,1,0:T(8,128)}, u32[]{:S(2)}, u32[]{:S(2)}) %collective-permute-start.12) | collective-permute-done | bytes 3145760 | tf_op jit(solution)/shard_map/ppermute | solution.py:76
  202.1 5.2 %bitcast_add_fusion = f32[4,96,2048]{2,1,0:T(8,128)} fusion(f32[4,96,2048]{2,1,0:T(8,128)} %collective-permute-done.12, f32[4,2,96,2048]{3,2,1,0:T(8,128)} %bitcast.29, s32[]{:T(128)S(6)} %select_n.7), kind=kLoop, calls=%fused_computation.21 | loop fusion | flops 786432 | bytes 9437188 | tf_op jit(solution)/shard_map/add | solution.py:76
  207.3 3.9 %all-to-all-start.4 = ((f32[4,96,2048]{2,1,0:T(8,128)}), f32[4,96,2048]{2,1,0:T(8,128)S(1)}, u32[]{:S(2)}, u32[]{:S(2)}) async-start(f32[4,96,2048]{2,1,0:T(8,128)} %bitcast_add_fusion), calls=%async_computation.4 | async-start | bytes 6291456 | tf_op jit(solution)/shard_map/all_to_all | solution.py:81
  211.3 6.9 %multiply_reduce_fusion.5 = f32[2048]{0:T(1024)S(1)} fusion(f32[2048,2048]{1,0:T(8,128)} %get-tuple-element.7, f32[2048]{0:T(1024)S(1)} %bitcast.38), kind=kLoop, calls=%fused_computation.9 | loop fusion | flops 8386560 | bytes 16793600 | tf_op jit(solution)/shard_map/reduce_sum | solution.py:130
  218.2 31.2 %all-to-all-done.4 = f32[4,96,2048]{2,1,0:T(8,128)S(1)} async-done(((f32[4,96,2048]{2,1,0:T(8,128)}), f32[4,96,2048]{2,1,0:T(8,128)S(1)}, u32[]{:S(2)}, u32[]{:S(2)}) %all-to-all-start.4) | async-done | bytes 3145760 | tf_op jit(solution)/shard_map/all_to_all | solution.py:81
  251.6 1.5 collective-permute-start.15
  253.0 1.8 collective-permute-start.16
  254.8 1.5 collective-permute-done.14
  (47 shorter events, 15.8 us)
Async XLA Ops:
  3.6 50.4 %all-to-all-start = ((bf16[16,2048,48]{1,2,0:T(8,128)(2,1)}), bf16[16,2048,48]{1,2,0:T(8,128)(2,1)S(1)}, u32[]{:S(2)}, u32[]{:S(2)}) async-start(bf16[16,2048,48]{1,2,0:T(8,128)(2,1)} %broadcast_in_dim.8), calls=%async_computation | async-start | bytes 6291456 | tf_op jit(solution)/shard_map/all_to_all | solution.py:94
  67.9 1.2 collective-permute-start
  69.1 6.4 %collective-permute-start.1 = (f32[2048]{0:T(1024)S(1)}, f32[2048]{0:T(1024)S(1)}, u32[]{:S(2)}, u32[]{:S(2)}) collective-permute-start(f32[2048]{0:T(1024)S(1)} %add.437), channel_id=1, source_target_pairs={{0,64},{32,96},{64,0},{96,32},{1,65},{33,97},{65,1},{97,33},{2,66}... | collective-permute-start | bytes 24584 | tf_op jit(solution)/shard_map/ppermute | solution.py:27
  72.3 4.9 %collective-permute-start.2 = (f32[2048]{0:T(1024)S(1)}, f32[2048]{0:T(1024)S(1)}, u32[]{:S(2)}, u32[]{:S(2)}) collective-permute-start(f32[2048]{0:T(1024)S(1)} %add.437), channel_id=1, source_target_pairs={{0,32},{32,64},{64,96},{96,0},{1,33},{33,65},{65,97},{97,1},{2,34}... | collective-permute-start | bytes 24584 | tf_op jit(solution)/shard_map/ppermute | solution.py:27
  73.0 4.2 %collective-permute-start.3 = (f32[2048]{0:T(1024)S(1)}, f32[2048]{0:T(1024)S(1)}, u32[]{:S(2)}, u32[]{:S(2)}) collective-permute-start(f32[2048]{0:T(1024)S(1)} %add.437), channel_id=1, source_target_pairs={{0,96},{32,0},{64,32},{96,64},{1,97},{33,1},{65,33},{97,65},{2,98}... | collective-permute-start | bytes 24584 | tf_op jit(solution)/shard_map/ppermute | solution.py:27
  106.8 1.3 collective-permute-start.4
  108.0 5.2 %collective-permute-start.5 = (f32[2048]{0:T(1024)S(1)}, f32[2048]{0:T(1024)S(1)}, u32[]{:S(2)}, u32[]{:S(2)}) collective-permute-start(f32[2048]{0:T(1024)S(1)} %add.457), channel_id=1, source_target_pairs={{0,64},{32,96},{64,0},{96,32},{1,65},{33,97},{65,1},{97,33},{2,66}... | collective-permute-start | bytes 24584 | tf_op jit(solution)/shard_map/ppermute | solution.py:27
  109.5 4.9 %collective-permute-start.6 = (f32[2048]{0:T(1024)S(1)}, f32[2048]{0:T(1024)S(1)}, u32[]{:S(2)}, u32[]{:S(2)}) collective-permute-start(f32[2048]{0:T(1024)S(1)} %add.457), channel_id=1, source_target_pairs={{0,32},{32,64},{64,96},{96,0},{1,33},{33,65},{65,97},{97,1},{2,34}... | collective-permute-start | bytes 24584 | tf_op jit(solution)/shard_map/ppermute | solution.py:27
  112.1 3.7 %collective-permute-start.7 = (f32[2048]{0:T(1024)S(1)}, f32[2048]{0:T(1024)S(1)}, u32[]{:S(2)}, u32[]{:S(2)}) collective-permute-start(f32[2048]{0:T(1024)S(1)} %add.457), channel_id=1, source_target_pairs={{0,96},{32,0},{64,32},{96,64},{1,97},{33,1},{65,33},{97,65},{2,98}... | collective-permute-start | bytes 24584 | tf_op jit(solution)/shard_map/ppermute | solution.py:27
  141.1 1.3 collective-permute-start.8
  142.4 4.9 %collective-permute-start.10 = (f32[2048]{0:T(1024)S(1)}, f32[2048]{0:T(1024)S(1)}, u32[]{:S(2)}, u32[]{:S(2)}) collective-permute-start(f32[2048]{0:T(1024)S(1)} %add.477), channel_id=1, source_target_pairs={{0,32},{32,64},{64,96},{96,0},{1,33},{33,65},{65,97},{97,1},{2,34}... | collective-permute-start | bytes 24584 | tf_op jit(solution)/shard_map/ppermute | solution.py:27
  142.4 4.9 %collective-permute-start.11 = (f32[2048]{0:T(1024)S(1)}, f32[2048]{0:T(1024)S(1)}, u32[]{:S(2)}, u32[]{:S(2)}) collective-permute-start(f32[2048]{0:T(1024)S(1)} %add.477), channel_id=1, source_target_pairs={{0,96},{32,0},{64,32},{96,64},{1,97},{33,1},{65,33},{97,65},{2,98}... | collective-permute-start | bytes 24584 | tf_op jit(solution)/shard_map/ppermute | solution.py:27
  145.6 5.2 %collective-permute-start.9 = (f32[2048]{0:T(1024)S(1)}, f32[2048]{0:T(1024)S(1)}, u32[]{:S(2)}, u32[]{:S(2)}) collective-permute-start(f32[2048]{0:T(1024)S(1)} %add.477), channel_id=1, source_target_pairs={{0,64},{32,96},{64,0},{96,32},{1,65},{33,97},{65,1},{97,33},{2,66}... | collective-permute-start | bytes 24584 | tf_op jit(solution)/shard_map/ppermute | solution.py:27
  158.4 11.4 %all-to-all-start.3 = ((f32[16,1,2048]{2,1,0:T(1,128)}), f32[16,1,2048]{2,1,0:T(1,128)S(1)}, u32[]{:S(2)}, u32[]{:S(2)}) async-start(f32[16,1,2048]{2,1,0:T(1,128)} %broadcast_in_dim.11), calls=%async_computation.3 | async-start | bytes 262144 | tf_op jit(solution)/shard_map/all_to_all | solution.py:44
  193.4 2.7 %copy-start = (f32[2048,768]{0,1:T(8,128)}, f32[2048,768]{0,1:T(8,128)S(1)}, u32[]{:S(2)}) copy-start(f32[2048,768]{0,1:T(8,128)S(1)} %add_multiply_fusion) | copy-start | bytes 18874372
  196.2 5.9 %collective-permute-start.12 = (f32[4,96,2048]{2,1,0:T(8,128)S(1)}, f32[4,96,2048]{2,1,0:T(8,128)}, u32[]{:S(2)}, u32[]{:S(2)}) collective-permute-start(f32[4,96,2048]{2,1,0:T(8,128)S(1)} %dynamic-slice_bitcast_fusion), channel_id=1, source_target_pairs={{0,16},{16,0},{1,17},{17,1},{2,18},{18,2},{3,19},{19,3},{4,20},{20... | collective-permute-start | bytes 9437192 | tf_op jit(solution)/shard_map/ppermute | solution.py:76
  207.3 42.0 %all-to-all-start.4 = ((f32[4,96,2048]{2,1,0:T(8,128)}), f32[4,96,2048]{2,1,0:T(8,128)S(1)}, u32[]{:S(2)}, u32[]{:S(2)}) async-start(f32[4,96,2048]{2,1,0:T(8,128)} %bitcast_add_fusion), calls=%async_computation.4 | async-start | bytes 6291456 | tf_op jit(solution)/shard_map/all_to_all | solution.py:81
  249.6 1.3 collective-permute-start.13
  250.9 5.4 %collective-permute-start.14 = (f32[2,2048]{1,0:T(2,128)S(1)}, f32[2,2048]{1,0:T(2,128)S(1)}, u32[]{:S(2)}, u32[]{:S(2)}) collective-permute-start(f32[2,2048]{1,0:T(2,128)S(1)} %fusion.17), channel_id=1, source_target_pairs={{0,64},{32,96},{64,0},{96,32},{1,65},{33,97},{65,1},{97,33},{2,66}... | collective-permute-start | bytes 49160 | tf_op jit(solution)/shard_map/ppermute | solution.py:27
  251.6 4.9 %collective-permute-start.15 = (f32[2,2048]{1,0:T(2,128)S(1)}, f32[2,2048]{1,0:T(2,128)S(1)}, u32[]{:S(2)}, u32[]{:S(2)}) collective-permute-start(f32[2,2048]{1,0:T(2,128)S(1)} %fusion.17), channel_id=1, source_target_pairs={{0,32},{32,64},{64,96},{96,0},{1,33},{33,65},{65,97},{97,1},{2,34}... | collective-permute-start | bytes 49160 | tf_op jit(solution)/shard_map/ppermute | solution.py:27
  253.0 3.7 %collective-permute-start.16 = (f32[2,2048]{1,0:T(2,128)S(1)}, f32[2,2048]{1,0:T(2,128)S(1)}, u32[]{:S(2)}, u32[]{:S(2)}) collective-permute-start(f32[2,2048]{1,0:T(2,128)S(1)} %fusion.17), channel_id=1, source_target_pairs={{0,96},{32,0},{64,32},{96,64},{1,97},{33,1},{65,33},{97,65},{2,98}... | collective-permute-start | bytes 49160 | tf_op jit(solution)/shard_map/ppermute | solution.py:27

commit v5 on v4

--- a/solution.py
+++ b/solution.py
@@ -85,14 +85,43 @@
     return total
 
 
+def ring_gather(v, axis, n):
+    if n == 1:
+        return v[None]
+    if n != 4:
+        return lax.all_to_all(jnp.broadcast_to(v[None], (n,) + v.shape), axis, 0, 0, tiled=False)
+    fwd = lax.ppermute(v, axis, [(i, (i + 1) % n) for i in range(n)])
+    bwd = lax.ppermute(v, axis, [(i, (i - 1) % n) for i in range(n)])
+    half = v.shape[-2] // 2
+    far = jnp.concatenate(
+        [
+            lax.ppermute(fwd[..., :half, :], axis, [(i, (i + 1) % n) for i in range(n)]),
+            lax.ppermute(bwd[..., half:, :], axis, [(i, (i - 1) % n) for i in range(n)]),
+        ],
+        axis=-2,
+    )
+    by_offset = jnp.stack([v, fwd, far, bwd])
+    idx = lax.axis_index(axis)
+    return by_offset[(idx - jnp.arange(n)) % n]
+
+
 def gather_features(points, sizes):
-    n = sizes["x"] * sizes["z"]
+    nx, nz = sizes["x"], sizes["z"]
     rows, blk = points.shape
-    if n == 1:
+    if nx * nz == 1:
         return points
-    sent = jnp.broadcast_to(points[None], (n, rows, blk))
-    got = lax.all_to_all(sent, CEN_AXES, 0, 0, tiled=False)
-    return jnp.transpose(got, (1, 0, 2)).reshape(rows, n * blk)
+    if blk % 2 or rows % 2:
+        got = lax.all_to_all(
+            jnp.broadcast_to(points[None], (nx * nz, rows, blk)), CEN_AXES, 0, 0, tiled=False
+        )
+        return jnp.transpose(got, (1, 0, 2)).reshape(rows, nx * nz * blk)
+    part_a, part_b = points[:, : blk // 2], points[:, blk // 2 :]
+    a_z = ring_gather(part_a, "z", nz)
+    b_x = ring_gather(part_b, "x", nx)
+    a_xz = ring_gather(a_z, "x", nx)
+    b_zx = ring_gather(b_x, "z", nz)
+    full = jnp.concatenate([a_xz, jnp.transpose(b_zx, (1, 0, 2, 3))], axis=-1)
+    return jnp.transpose(full, (2, 0, 1, 3)).reshape(rows, nx * nz * blk)
 
 
 def make_local(sizes):

time: 259 us -> 245 us (0.946)
  waiting for transfers between devices: 101 us -> 64.8 us
  starting transfers between devices: 34.1 us -> 53.8 us
  local copies, waits for them, and re-layouts: 6.7 us -> 10.8 us
  other arithmetic: 52.3 us -> 55.5 us
  blocking collectives: 26.7 us -> 24 us
    all_to_all x1 -> x0, waiting for transfers between devices: 39.8 us -> none  [gather_features(): got = lax.all_to_all(sent, CEN_AXES, 0, 0, tiled=False)]
    ppermute x0 -> x16, starting transfers between devices: none -> 27 us  [the longest x4 13.1 us: ring_gather(): lax.ppermute(bwd[..., half:, :], axis, [(i, (i - 1) % n) for i in range(n)])]
    all_to_all x1 -> x0, starting transfers between devices: 7.99 us -> none  [gather_features(): got = lax.all_to_all(sent, CEN_AXES, 0, 0, tiled=False)]
    ppermute x0 -> x16, waiting for transfers between devices: none -> 6.28 us  [the longest x4 4.07 us: ring_gather(): lax.ppermute(fwd[..., :half, :], axis, [(i, (i + 1) % n) for i in range(n)])]
    gather x0 -> x5, local copies, waits for them, and re-layouts: none -> 5.33 us  [ring_gather(): return by_offset[(idx - jnp.arange(n)) % n]]
    broadcast_in_dim x1 -> x0, local copies, waits for them, and re-layouts: 2.98 us -> none  [gather_features(): sent = jnp.broadcast_to(points[None], (n, rows, blk))]
    all_to_all x2, blocking collectives: 26.7 us -> 24 us  [group_sum(): lax.all_to_all(jnp.broadcast_to(v[None], (n,) + v.shape), axes, 0, 0, til...]
    another operation x0 -> x8, other arithmetic: none -> 2.71 us  [ring_gather(): by_offset = jnp.stack([v, fwd, far, bwd])]
  transfers between devices with their start and end apart: 20 -> 35, of which waited for: 17 -> 21; matrix products, arithmetic and copies ran while one was open for 4% -> 5% of each run, Pallas kernels for 0% -> 0%
where the time goes in v5:
time: 245 us; the launch traced here: 244 us
  waiting for transfers between devices  64.8 us (26%)
  other arithmetic  55.5 us (23%)
  starting transfers between devices  53.8 us (22%)
  matrix products  34.2 us (14%)
  blocking collectives  24 us (10%)
  local copies, waits for them, and re-layouts  10.8 us (4%)
    all_to_all x1, waiting for transfers between devices, scatter_features(): got = lax.all_to_all(x, 'y', 0, 0, tiled=False)  31.2 us
    all_to_all x2, blocking collectives, group_sum(): lax.all_to_all(jnp.broadcast_to(v[None], (n,) + v.shape), axes, 0, 0, til...  24 us
    reduce_sum x3, other arithmetic, local(): row_part = jnp.sum(kernel * col_scale[None, :], axis=1)  21.1 us
    ppermute x16, starting transfers between devices, axis_sum(): lax.ppermute(v, axis, [(i, (i + s) % n) for i in range(n)])  19.1 us
    reduce_sum x2, other arithmetic, local(): col_part = jnp.sum(kernel * row_scale[:, None], axis=0)  13.9 us
    ppermute x16, waiting for transfers between devices, axis_sum(): lax.ppermute(v, axis, [(i, (i + s) % n) for i in range(n)])  13.8 us
    ppermute x4, starting transfers between devices, ring_gather(): lax.ppermute(bwd[..., half:, :], axis, [(i, (i - 1) % n) for i in range(n)])  13.1 us
    dot_general x1, matrix products, local(): lax.dot_general(gathered, hi, dims, preferred_element_type=jnp.float32)  12.1 us
  transfers between devices with their start and end apart: 35, of which 21 were waited for; matrix products, arithmetic and copies ran while one was open for 5% of the time, Pallas kernels for 0%

profile of v5, /device:TPU:0, one launch (start us, length us, event | category | flops | bytes accessed | tf_op | source)
XLA Modules:
  0.0 244.1 jit_solution(2495306151718121684)
XLA Ops:
  1.6 2.1 collective-permute-start
  3.7 2.2 collective-permute-start.2
  5.9 2.8 %collective-permute-start.10 = (bf16[2048,24]{0,1:T(8,128)(2,1)S(1)}, bf16[2048,24]{0,1:T(8,128)(2,1)S(1)}, u32[]{:S(2)}, u32[]{:S(2)}) collective-permute-start(bf16[2048,24]{0,1:T(8,128)(2,1)S(1)} %get-tuple-element.6), channel_id=1, source_target_pairs={{0,12},{4,0},{8,4},{12,8},{1,13},{5,1},{9,5},{13,9},{2,14},{6,2},{... | collective-permute-start | bytes 294920 | tf_op jit(solution)/shard_map/ppermute | solution.py:94
  8.8 3.3 %collective-permute-start.3 = (bf16[1024,24]{0,1:T(8,128)(2,1)S(1)}, bf16[1024,24]{0,1:T(8,128)(2,1)S(1)}, u32[]{:S(2)}, u32[]{:S(2)}) collective-permute-start(bf16[1024,24]{0,1:T(8,128)(2,1)S(1)} %slice.313), channel_id=1, source_target_pairs={{0,3},{1,0},{2,1},{3,2},{4,7},{5,4},{6,5},{7,6},{8,11},{9,8},{10,9... | collective-permute-start | bytes 147464 | tf_op jit(solution)/shard_map/ppermute | solution.py:99
  12.1 3.3 %collective-permute-start.11 = (bf16[1024,24]{0,1:T(8,128)(2,1)S(1)}, bf16[1024,24]{0,1:T(8,128)(2,1)S(1)}, u32[]{:S(2)}, u32[]{:S(2)}) collective-permute-start(bf16[1024,24]{0,1:T(8,128)(2,1)S(1)} %slice.317), channel_id=1, source_target_pairs={{0,12},{4,0},{8,4},{12,8},{1,13},{5,1},{9,5},{13,9},{2,14},{6,2},{... | collective-permute-start | bytes 147464 | tf_op jit(solution)/shard_map/ppermute | solution.py:99
  16.3 3.2 %collective-permute-start.6 = (bf16[4,2048,24]{1,2,0:T(8,128)(2,1)S(1)}, bf16[4,2048,24]{1,2,0:T(8,128)(2,1)S(1)}, u32[]{:S(2)}, u32[]{:S(2)}) collective-permute-start(bf16[4,2048,24]{1,2,0:T(8,128)(2,1)S(1)} %gather_fusion), channel_id=1, source_target_pairs={{0,12},{4,0},{8,4},{12,8},{1,13},{5,1},{9,5},{13,9},{2,14},{6,2},{... | collective-permute-start | bytes 1179656 | tf_op jit(solution)/shard_map/ppermute | solution.py:94
  22.1 3.2 %collective-permute-start.14 = (bf16[4,2048,24]{1,2,0:T(8,128)(2,1)S(1)}, bf16[4,2048,24]{1,2,0:T(8,128)(2,1)S(1)}, u32[]{:S(2)}, u32[]{:S(2)}) collective-permute-start(bf16[4,2048,24]{1,2,0:T(8,128)(2,1)S(1)} %gather_fusion.2), channel_id=1, source_target_pairs={{0,3},{1,0},{2,1},{3,2},{4,7},{5,4},{6,5},{7,6},{8,11},{9,8},{10,9... | collective-permute-start | bytes 1179656 | tf_op jit(solution)/shard_map/ppermute | solution.py:94
  27.3 3.3 %collective-permute-start.7 = (bf16[4,1024,24]{1,2,0:T(8,128)(2,1)S(1)}, bf16[4,1024,24]{1,2,0:T(8,128)(2,1)S(1)}, u32[]{:S(2)}, u32[]{:S(2)}) collective-permute-start(bf16[4,1024,24]{1,2,0:T(8,128)(2,1)S(1)} %slice.315), channel_id=1, source_target_pairs={{0,12},{4,0},{8,4},{12,8},{1,13},{5,1},{9,5},{13,9},{2,14},{6,2},{... | collective-permute-start | bytes 589832 | tf_op jit(solution)/shard_map/ppermute | solution.py:99
  30.6 2.6 %fusion.6 = f32[2048]{0:T(1024)S(1)} fusion(bf16[2048,768]{1,0:T(8,128)(2,1)} %param.3), kind=kLoop, calls=%fused_computation.20 | loop fusion | flops 4716544 | bytes 3153920 | tf_op jit(solution)/shard_map/reduce_sum | solution.py:18
  34.7 3.2 %collective-permute-start.15 = (bf16[4,1024,24]{1,2,0:T(8,128)(2,1)}, bf16[4,1024,24]{1,2,0:T(8,128)(2,1)}, u32[]{:S(2)}, u32[]{:S(2)}) collective-permute-start(bf16[4,1024,24]{1,2,0:T(8,128)(2,1)} %slice.319), channel_id=1, source_target_pairs={{0,3},{1,0},{2,1},{3,2},{4,7},{5,4},{6,5},{7,6},{8,11},{9,8},{10,9... | collective-permute-start | bytes 589832 | tf_op jit(solution)/shard_map/ppermute | solution.py:99
  38.8 2.3 collective-permute-done.13
  48.3 11.6 %fusion.24 = (f32[2048]{0:T(1024)S(1)}, f32[2048,2048]{1,0:T(8,128)}) fusion(bf16[2048,768]{1,0:T(8,128)(2,1)S(1)} %copy-done, f32[2048]{0:T(1024)S(1)} %get-tuple-element.12, bf16[2048,768]{0,1:T(8,128)(2,1)S(1)} %bitcast.56, f32[2048]{0:T(1024)S(1)} %get-tuple-element.13), kind=kOutput, calls=%fused_computation.122 | convolution fusion | flops 6460274688 | bytes 23093248 | tf_op jit(solution)/shard_map/dot_general | solution.py:143
  61.1 3.2 %collective-permute-start.17 = (f32[2048]{0:T(1024)S(1)}, f32[2048]{0:T(1024)S(1)}, u32[]{:S(2)}, u32[]{:S(2)}) collective-permute-start(f32[2048]{0:T(1024)S(1)} %add.490), channel_id=1, source_target_pairs={{0,64},{32,96},{64,0},{96,32},{1,65},{33,97},{65,1},{97,33},{2,66}... | collective-permute-start | bytes 24584 | tf_op jit(solution)/shard_map/ppermute | solution.py:27
  65.0 2.6 %collective-permute-start.19 = (f32[2048]{0:T(1024)S(1)}, f32[2048]{0:T(1024)S(1)}, u32[]{:S(2)}, u32[]{:S(2)}) collective-permute-start(f32[2048]{0:T(1024)S(1)} %add.490), channel_id=1, source_target_pairs={{0,96},{32,0},{64,32},{96,64},{1,97},{33,1},{65,33},{97,65},{2,98}... | collective-permute-start | bytes 24584 | tf_op jit(solution)/shard_map/ppermute | solution.py:27
  69.2 7.0 %multiply_reduce_fusion.4 = f32[2048]{0:T(1024)S(1)} fusion(f32[2048,2048]{1,0:T(8,128)} %get-tuple-element.11, f32[2048]{0:T(1024)S(1)} %add_divide_fusion.2), kind=kLoop, calls=%fused_computation.11 | loop fusion | flops 8386560 | bytes 16793600 | tf_op jit(solution)/shard_map/reduce_sum | solution.py:148
  76.3 12.7 %all_to_all.23 = f32[16,1,2048]{2,1,0:T(1,128)S(1)} all-to-all(f32[16,1,2048]{2,1,0:T(1,128)S(1)} %broadcast_in_dim.6), channel_id=1, replica_groups=mesh['y'=4,'c'=2,'x'=4,'z'=4] {'x','z'}, dimensions={0} | all-to-all | bytes 262144 | tf_op jit(solution)/shard_map/all_to_all | solution.py:44
  89.1 6.9 %multiply_reduce_fusion.3 = f32[2048]{0:T(1024)S(1)} fusion(f32[2048,2048]{1,0:T(8,128)} %get-tuple-element.11, f32[2048]{0:T(1024)S(1)} %bitcast.76), kind=kLoop, calls=%fused_computation.10 | loop fusion | flops 8386560 | bytes 16793600 | tf_op jit(solution)/shard_map/reduce_sum | solution.py:146
  98.7 2.6 %collective-permute-start.22 = (f32[2048]{0:T(1024)S(1)}, f32[2048]{0:T(1024)S(1)}, u32[]{:S(2)}, u32[]{:S(2)}) collective-permute-start(f32[2048]{0:T(1024)S(1)} %add.510), channel_id=1, source_target_pairs={{0,32},{32,64},{64,96},{96,0},{1,33},{33,65},{65,97},{97,1},{2,34}... | collective-permute-start | bytes 24584 | tf_op jit(solution)/shard_map/ppermute | solution.py:27
  105.0 7.0 %multiply_reduce_fusion.2 = f32[2048]{0:T(1024)S(1)} fusion(f32[2048,2048]{1,0:T(8,128)} %get-tuple-element.11, f32[2048]{0:T(1024)S(1)} %add_divide_fusion.1), kind=kLoop, calls=%fused_computation.9 | loop fusion | flops 8386560 | bytes 16793600 | tf_op jit(solution)/shard_map/reduce_sum | solution.py:148
  112.1 11.2 %all_to_all.24 = f32[16,1,2048]{2,1,0:T(1,128)S(1)} all-to-all(f32[16,1,2048]{2,1,0:T(1,128)S(1)} %broadcast_in_dim.7), channel_id=1, replica_groups=mesh['y'=4,'c'=2,'x'=4,'z'=4] {'x','z'}, dimensions={0} | all-to-all | bytes 262144 | tf_op jit(solution)/shard_map/all_to_all | solution.py:44
  123.4 6.9 %multiply_reduce_fusion.1 = f32[2048]{0:T(1024)S(1)} fusion(f32[2048,2048]{1,0:T(8,128)} %get-tuple-element.11, f32[2048]{0:T(1024)S(1)} %bitcast.77), kind=kLoop, calls=%fused_computation.8 | loop fusion | flops 8386560 | bytes 16793600 | tf_op jit(solution)/shard_map/reduce_sum | solution.py:146
  138.0 7.1 %multiply_reduce_fusion = f32[2048]{0:T(1024)S(1)} fusion(f32[2048,2048]{1,0:T(8,128)} %get-tuple-element.11, f32[2048]{0:T(1024)S(1)} %add_divide_fusion), kind=kLoop, calls=%fused_computation.7 | loop fusion | flops 8386560 | bytes 16793600 | tf_op jit(solution)/shard_map/reduce_sum | solution.py:148
  145.8 3.6 %all-to-all-start.2 = ((f32[16,1,2048]{2,1,0:T(1,128)}), f32[16,1,2048]{2,1,0:T(1,128)S(1)}, u32[]{:S(2)}, u32[]{:S(2)}) async-start(f32[16,1,2048]{2,1,0:T(1,128)} %broadcast_in_dim.8), calls=%async_computation.2 | async-start | bytes 262144 | tf_op jit(solution)/shard_map/all_to_all | solution.py:44
  149.4 7.8 %all-to-all-done.2 = f32[16,1,2048]{2,1,0:T(1,128)S(1)} async-done(((f32[16,1,2048]{2,1,0:T(1,128)}), f32[16,1,2048]{2,1,0:T(1,128)S(1)}, u32[]{:S(2)}, u32[]{:S(2)}) %all-to-all-start.2) | async-done | bytes 131104 | tf_op jit(solution)/shard_map/all_to_all | solution.py:44
  157.3 10.5 %fusion.1 = f32[768,2048]{1,0:T(8,128)S(1)} fusion(bf16[2048,768]{0,1:T(8,128)(2,1)S(1)} %bitcast.57, f32[2048,2048]{1,0:T(8,128)} %get-tuple-element.11, f32[2048]{0:T(1024)S(1)} %bitcast.73), kind=kOutput, calls=%fused_computation.14 | convolution fusion | flops 6459228160 | bytes 26222592 | tf_op jit(solution)/shard_map/dot_general | solution.py:157
  167.8 12.1 %add_multiply_fusion = f32[768,2048]{1,0:T(8,128)} fusion(f32[768,2048]{1,0:T(8,128)S(1)} %fusion.1, f32[2048]{0:T(1024)S(1)} %add_divide_fusion, bf16[2048,768]{0,1:T(8,128)(2,1)S(1)} %bitcast.58, f32[2048,2048]{1,0:T(8,128)} %get-tuple-element.11, f32[2048]{0:T(1024)S(1)} %bitcast.74), kind=kOutput, calls=%fused_computation.22 | convolution fusion | flops 6458179584 | bytes 32522240 | tf_op jit(solution)/shard_map/dot_general | solution.py:155
  179.8 2.1 dynamic-slice_bitcast_fusion
  182.0 5.8 %collective-permute-done.28 = f32[4,96,2048]{2,1,0:T(8,128)} collective-permute-done((f32[4,96,2048]{2,1,0:T(8,128)S(1)}, f32[4,96,2048]{2,1,0:T(8,128)}, u32[]{:S(2)}, u32[]{:S(2)}) %collective-permute-start.28) | collective-permute-done | bytes 3145760 | tf_op jit(solution)/shard_map/ppermute | solution.py:76
  187.8 5.2 %bitcast_add_fusion = f32[4,96,2048]{2,1,0:T(8,128)} fusion(f32[4,96,2048]{2,1,0:T(8,128)} %collective-permute-done.28, f32[4,2,96,2048]{3,2,1,0:T(8,128)} %bitcast.25, s32[]{:T(128)S(6)} %select_n.62), kind=kLoop, calls=%fused_computation.26 | loop fusion | flops 786432 | bytes 9437188 | tf_op jit(solution)/shard_map/add | solution.py:76
  193.0 4.0 %all-to-all-start.3 = ((f32[4,96,2048]{2,1,0:T(8,128)}), f32[4,96,2048]{2,1,0:T(8,128)S(1)}, u32[]{:S(2)}, u32[]{:S(2)}) async-start(f32[4,96,2048]{2,1,0:T(8,128)} %bitcast_add_fusion), calls=%async_computation.3 | async-start | bytes 6291456 | tf_op jit(solution)/shard_map/all_to_all | solution.py:81
  197.0 6.9 %multiply_reduce_fusion.5 = f32[2048]{0:T(1024)S(1)} fusion(f32[2048,2048]{1,0:T(8,128)} %get-tuple-element.11, f32[2048]{0:T(1024)S(1)} %bitcast.75), kind=kLoop, calls=%fused_computation.13 | loop fusion | flops 8386560 | bytes 16793600 | tf_op jit(solution)/shard_map/reduce_sum | solution.py:159
  204.0 31.2 %all-to-all-done.3 = f32[4,96,2048]{2,1,0:T(8,128)S(1)} async-done(((f32[4,96,2048]{2,1,0:T(8,128)}), f32[4,96,2048]{2,1,0:T(8,128)S(1)}, u32[]{:S(2)}, u32[]{:S(2)}) %all-to-all-start.3) | async-done | bytes 3145760 | tf_op jit(solution)/shard_map/all_to_all | solution.py:81
  (110 shorter events, 43.5 us)
Async XLA Ops:
  1.6 7.1 %collective-permute-start = (bf16[2048,24]{0,1:T(8,128)(2,1)S(1)}, bf16[2048,24]{0,1:T(8,128)(2,1)S(1)}, u32[]{:S(2)}, u32[]{:S(2)}) collective-permute-start(bf16[2048,24]{0,1:T(8,128)(2,1)S(1)} %get-tuple-element.7), channel_id=1, source_target_pairs={{0,1},{1,2},{2,3},{3,0},{4,5},{5,6},{6,7},{7,4},{8,9},{9,10},{10,1... | collective-permute-start | bytes 294920 | tf_op jit(solution)/shard_map/ppermute | solution.py:93
  3.7 5.1 %collective-permute-start.2 = (bf16[2048,24]{0,1:T(8,128)(2,1)S(1)}, bf16[2048,24]{0,1:T(8,128)(2,1)S(1)}, u32[]{:S(2)}, u32[]{:S(2)}) collective-permute-start(bf16[2048,24]{0,1:T(8,128)(2,1)S(1)} %get-tuple-element.7), channel_id=1, source_target_pairs={{0,3},{1,0},{2,1},{3,2},{4,7},{5,4},{6,5},{7,6},{8,11},{9,8},{10,9... | collective-permute-start | bytes 294920 | tf_op jit(solution)/shard_map/ppermute | solution.py:94
  5.9 6.2 %collective-permute-start.10 = (bf16[2048,24]{0,1:T(8,128)(2,1)S(1)}, bf16[2048,24]{0,1:T(8,128)(2,1)S(1)}, u32[]{:S(2)}, u32[]{:S(2)}) collective-permute-start(bf16[2048,24]{0,1:T(8,128)(2,1)S(1)} %get-tuple-element.6), channel_id=1, source_target_pairs={{0,12},{4,0},{8,4},{12,8},{1,13},{5,1},{9,5},{13,9},{2,14},{6,2},{... | collective-permute-start | bytes 294920 | tf_op jit(solution)/shard_map/ppermute | solution.py:94
  8.7 6.8 %collective-permute-start.8 = (bf16[2048,24]{0,1:T(8,128)(2,1)S(1)}, bf16[2048,24]{0,1:T(8,128)(2,1)S(1)}, u32[]{:S(2)}, u32[]{:S(2)}) collective-permute-start(bf16[2048,24]{0,1:T(8,128)(2,1)S(1)} %get-tuple-element.6), channel_id=1, source_target_pairs={{0,4},{4,8},{8,12},{12,0},{1,5},{5,9},{9,13},{13,1},{2,6},{6,10},{... | collective-permute-start | bytes 294920 | tf_op jit(solution)/shard_map/ppermute | solution.py:93
  8.7 6.8 %collective-permute-start.1 = (bf16[1024,24]{0,1:T(8,128)(2,1)S(1)}, bf16[1024,24]{0,1:T(8,128)(2,1)S(1)}, u32[]{:S(2)}, u32[]{:S(2)}) collective-permute-start(bf16[1024,24]{0,1:T(8,128)(2,1)S(1)} %slice.312), channel_id=1, source_target_pairs={{0,1},{1,2},{2,3},{3,0},{4,5},{5,6},{6,7},{7,4},{8,9},{9,10},{10,1... | collective-permute-start | bytes 147464 | tf_op jit(solution)/shard_map/ppermute | solution.py:98
  8.8 6.7 %collective-permute-start.3 = (bf16[1024,24]{0,1:T(8,128)(2,1)S(1)}, bf16[1024,24]{0,1:T(8,128)(2,1)S(1)}, u32[]{:S(2)}, u32[]{:S(2)}) collective-permute-start(bf16[1024,24]{0,1:T(8,128)(2,1)S(1)} %slice.313), channel_id=1, source_target_pairs={{0,3},{1,0},{2,1},{3,2},{4,7},{5,4},{6,5},{7,6},{8,11},{9,8},{10,9... | collective-permute-start | bytes 147464 | tf_op jit(solution)/shard_map/ppermute | solution.py:99
  12.1 7.4 %collective-permute-start.11 = (bf16[1024,24]{0,1:T(8,128)(2,1)S(1)}, bf16[1024,24]{0,1:T(8,128)(2,1)S(1)}, u32[]{:S(2)}, u32[]{:S(2)}) collective-permute-start(bf16[1024,24]{0,1:T(8,128)(2,1)S(1)} %slice.317), channel_id=1, source_target_pairs={{0,12},{4,0},{8,4},{12,8},{1,13},{5,1},{9,5},{13,9},{2,14},{6,2},{... | collective-permute-start | bytes 147464 | tf_op jit(solution)/shard_map/ppermute | solution.py:99
  15.5 5.9 %collective-permute-start.9 = (bf16[1024,24]{0,1:T(8,128)(2,1)S(1)}, bf16[1024,24]{0,1:T(8,128)(2,1)S(1)}, u32[]{:S(2)}, u32[]{:S(2)}) collective-permute-start(bf16[1024,24]{0,1:T(8,128)(2,1)S(1)} %slice.316), channel_id=1, source_target_pairs={{0,4},{4,8},{8,12},{12,0},{1,5},{5,9},{9,13},{13,1},{2,6},{6,10},{... | collective-permute-start | bytes 147464 | tf_op jit(solution)/shard_map/ppermute | solution.py:98
  16.2 11.0 %collective-permute-start.4 = (bf16[4,2048,24]{1,2,0:T(8,128)(2,1)S(1)}, bf16[4,2048,24]{1,2,0:T(8,128)(2,1)S(1)}, u32[]{:S(2)}, u32[]{:S(2)}) collective-permute-start(bf16[4,2048,24]{1,2,0:T(8,128)(2,1)S(1)} %gather_fusion), channel_id=1, source_target_pairs={{0,4},{4,8},{8,12},{12,0},{1,5},{5,9},{9,13},{13,1},{2,6},{6,10},{... | collective-permute-start | bytes 1179656 | tf_op jit(solution)/shard_map/ppermute | solution.py:93
  16.3 10.9 %collective-permute-start.6 = (bf16[4,2048,24]{1,2,0:T(8,128)(2,1)S(1)}, bf16[4,2048,24]{1,2,0:T(8,128)(2,1)S(1)}, u32[]{:S(2)}, u32[]{:S(2)}) collective-permute-start(bf16[4,2048,24]{1,2,0:T(8,128)(2,1)S(1)} %gather_fusion), channel_id=1, source_target_pairs={{0,12},{4,0},{8,4},{12,8},{1,13},{5,1},{9,5},{13,9},{2,14},{6,2},{... | collective-permute-start | bytes 1179656 | tf_op jit(solution)/shard_map/ppermute | solution.py:94
  22.0 11.2 %collective-permute-start.12 = (bf16[4,2048,24]{1,2,0:T(8,128)(2,1)S(1)}, bf16[4,2048,24]{1,2,0:T(8,128)(2,1)S(1)}, u32[]{:S(2)}, u32[]{:S(2)}) collective-permute-start(bf16[4,2048,24]{1,2,0:T(8,128)(2,1)S(1)} %gather_fusion.2), channel_id=1, source_target_pairs={{0,1},{1,2},{2,3},{3,0},{4,5},{5,6},{6,7},{7,4},{8,9},{9,10},{10,1... | collective-permute-start | bytes 1179656 | tf_op jit(solution)/shard_map/ppermute | solution.py:93
  22.1 11.9 %collective-permute-start.14 = (bf16[4,2048,24]{1,2,0:T(8,128)(2,1)S(1)}, bf16[4,2048,24]{1,2,0:T(8,128)(2,1)S(1)}, u32[]{:S(2)}, u32[]{:S(2)}) collective-permute-start(bf16[4,2048,24]{1,2,0:T(8,128)(2,1)S(1)} %gather_fusion.2), channel_id=1, source_target_pairs={{0,3},{1,0},{2,1},{3,2},{4,7},{5,4},{6,5},{7,6},{8,11},{9,8},{10,9... | collective-permute-start | bytes 1179656 | tf_op jit(solution)/shard_map/ppermute | solution.py:94
  27.2 10.7 %collective-permute-start.5 = (bf16[4,1024,24]{1,2,0:T(8,128)(2,1)S(1)}, bf16[4,1024,24]{1,2,0:T(8,128)(2,1)S(1)}, u32[]{:S(2)}, u32[]{:S(2)}) collective-permute-start(bf16[4,1024,24]{1,2,0:T(8,128)(2,1)S(1)} %slice.314), channel_id=1, source_target_pairs={{0,4},{4,8},{8,12},{12,0},{1,5},{5,9},{9,13},{13,1},{2,6},{6,10},{... | collective-permute-start | bytes 589832 | tf_op jit(solution)/shard_map/ppermute | solution.py:98
  27.3 10.6 %collective-permute-start.7 = (bf16[4,1024,24]{1,2,0:T(8,128)(2,1)S(1)}, bf16[4,1024,24]{1,2,0:T(8,128)(2,1)S(1)}, u32[]{:S(2)}, u32[]{:S(2)}) collective-permute-start(bf16[4,1024,24]{1,2,0:T(8,128)(2,1)S(1)} %slice.315), channel_id=1, source_target_pairs={{0,12},{4,0},{8,4},{12,8},{1,13},{5,1},{9,5},{13,9},{2,14},{6,2},{... | collective-permute-start | bytes 589832 | tf_op jit(solution)/shard_map/ppermute | solution.py:99
  33.9 7.2 %collective-permute-start.13 = (bf16[4,1024,24]{1,2,0:T(8,128)(2,1)}, bf16[4,1024,24]{1,2,0:T(8,128)(2,1)}, u32[]{:S(2)}, u32[]{:S(2)}) collective-permute-start(bf16[4,1024,24]{1,2,0:T(8,128)(2,1)} %slice.318), channel_id=1, source_target_pairs={{0,1},{1,2},{2,3},{3,0},{4,5},{5,6},{6,7},{7,4},{8,9},{9,10},{10,1... | collective-permute-start | bytes 589832 | tf_op jit(solution)/shard_map/ppermute | solution.py:98
  34.7 6.7 %collective-permute-start.15 = (bf16[4,1024,24]{1,2,0:T(8,128)(2,1)}, bf16[4,1024,24]{1,2,0:T(8,128)(2,1)}, u32[]{:S(2)}, u32[]{:S(2)}) collective-permute-start(bf16[4,1024,24]{1,2,0:T(8,128)(2,1)} %slice.319), channel_id=1, source_target_pairs={{0,3},{1,0},{2,1},{3,2},{4,7},{5,4},{6,5},{7,6},{8,11},{9,8},{10,9... | collective-permute-start | bytes 589832 | tf_op jit(solution)/shard_map/ppermute | solution.py:99
  61.1 6.4 %collective-permute-start.17 = (f32[2048]{0:T(1024)S(1)}, f32[2048]{0:T(1024)S(1)}, u32[]{:S(2)}, u32[]{:S(2)}) collective-permute-start(f32[2048]{0:T(1024)S(1)} %add.490), channel_id=1, source_target_pairs={{0,64},{32,96},{64,0},{96,32},{1,65},{33,97},{65,1},{97,33},{2,66}... | collective-permute-start | bytes 24584 | tf_op jit(solution)/shard_map/ppermute | solution.py:27
  64.3 4.9 %collective-permute-start.18 = (f32[2048]{0:T(1024)S(1)}, f32[2048]{0:T(1024)S(1)}, u32[]{:S(2)}, u32[]{:S(2)}) collective-permute-start(f32[2048]{0:T(1024)S(1)} %add.490), channel_id=1, source_target_pairs={{0,32},{32,64},{64,96},{96,0},{1,33},{33,65},{65,97},{97,1},{2,34}... | collective-permute-start | bytes 24584 | tf_op jit(solution)/shard_map/ppermute | solution.py:27
  65.0 4.2 %collective-permute-start.19 = (f32[2048]{0:T(1024)S(1)}, f32[2048]{0:T(1024)S(1)}, u32[]{:S(2)}, u32[]{:S(2)}) collective-permute-start(f32[2048]{0:T(1024)S(1)} %add.490), channel_id=1, source_target_pairs={{0,96},{32,0},{64,32},{96,64},{1,97},{33,1},{65,33},{97,65},{2,98}... | collective-permute-start | bytes 24584 | tf_op jit(solution)/shard_map/ppermute | solution.py:27
  97.3 5.2 %collective-permute-start.21 = (f32[2048]{0:T(1024)S(1)}, f32[2048]{0:T(1024)S(1)}, u32[]{:S(2)}, u32[]{:S(2)}) collective-permute-start(f32[2048]{0:T(1024)S(1)} %add.510), channel_id=1, source_target_pairs={{0,64},{32,96},{64,0},{96,32},{1,65},{33,97},{65,1},{97,33},{2,66}... | collective-permute-start | bytes 24584 | tf_op jit(solution)/shard_map/ppermute | solution.py:27
  98.7 4.9 %collective-permute-start.22 = (f32[2048]{0:T(1024)S(1)}, f32[2048]{0:T(1024)S(1)}, u32[]{:S(2)}, u32[]{:S(2)}) collective-permute-start(f32[2048]{0:T(1024)S(1)} %add.510), channel_id=1, source_target_pairs={{0,32},{32,64},{64,96},{96,0},{1,33},{33,65},{65,97},{97,1},{2,34}... | collective-permute-start | bytes 24584 | tf_op jit(solution)/shard_map/ppermute | solution.py:27
  101.4 3.7 %collective-permute-start.23 = (f32[2048]{0:T(1024)S(1)}, f32[2048]{0:T(1024)S(1)}, u32[]{:S(2)}, u32[]{:S(2)}) collective-permute-start(f32[2048]{0:T(1024)S(1)} %add.510), channel_id=1, source_target_pairs={{0,96},{32,0},{64,32},{96,64},{1,97},{33,1},{65,33},{97,65},{2,98}... | collective-permute-start | bytes 24584 | tf_op jit(solution)/shard_map/ppermute | solution.py:27
  131.6 5.2 %collective-permute-start.25 = (f32[2048]{0:T(1024)S(1)}, f32[2048]{0:T(1024)S(1)}, u32[]{:S(2)}, u32[]{:S(2)}) collective-permute-start(f32[2048]{0:T(1024)S(1)} %add.530), channel_id=1, source_target_pairs={{0,64},{32,96},{64,0},{96,32},{1,65},{33,97},{65,1},{97,33},{2,66}... | collective-permute-start | bytes 24584 | tf_op jit(solution)/shard_map/ppermute | solution.py:27
  132.2 4.9 %collective-permute-start.26 = (f32[2048]{0:T(1024)S(1)}, f32[2048]{0:T(1024)S(1)}, u32[]{:S(2)}, u32[]{:S(2)}) collective-permute-start(f32[2048]{0:T(1024)S(1)} %add.530), channel_id=1, source_target_pairs={{0,32},{32,64},{64,96},{96,0},{1,33},{33,65},{65,97},{97,1},{2,34}... | collective-permute-start | bytes 24584 | tf_op jit(solution)/shard_map/ppermute | solution.py:27
  134.3 3.7 %collective-permute-start.27 = (f32[2048]{0:T(1024)S(1)}, f32[2048]{0:T(1024)S(1)}, u32[]{:S(2)}, u32[]{:S(2)}) collective-permute-start(f32[2048]{0:T(1024)S(1)} %add.530), channel_id=1, source_target_pairs={{0,96},{32,0},{64,32},{96,64},{1,97},{33,1},{65,33},{97,65},{2,98}... | collective-permute-start | bytes 24584 | tf_op jit(solution)/shard_map/ppermute | solution.py:27
  145.8 11.4 %all-to-all-start.2 = ((f32[16,1,2048]{2,1,0:T(1,128)}), f32[16,1,2048]{2,1,0:T(1,128)S(1)}, u32[]{:S(2)}, u32[]{:S(2)}) async-start(f32[16,1,2048]{2,1,0:T(1,128)} %broadcast_in_dim.8), calls=%async_computation.2 | async-start | bytes 262144 | tf_op jit(solution)/shard_map/all_to_all | solution.py:44
  181.9 5.9 %collective-permute-start.28 = (f32[4,96,2048]{2,1,0:T(8,128)S(1)}, f32[4,96,2048]{2,1,0:T(8,128)}, u32[]{:S(2)}, u32[]{:S(2)}) collective-permute-start(f32[4,96,2048]{2,1,0:T(8,128)S(1)} %dynamic-slice_bitcast_fusion), channel_id=1, source_target_pairs={{0,16},{16,0},{1,17},{17,1},{2,18},{18,2},{3,19},{19,3},{4,20},{20... | collective-permute-start | bytes 9437192 | tf_op jit(solution)/shard_map/ppermute | solution.py:76
  193.0 42.1 %all-to-all-start.3 = ((f32[4,96,2048]{2,1,0:T(8,128)}), f32[4,96,2048]{2,1,0:T(8,128)S(1)}, u32[]{:S(2)}, u32[]{:S(2)}) async-start(f32[4,96,2048]{2,1,0:T(8,128)} %bitcast_add_fusion), calls=%async_computation.3 | async-start | bytes 6291456 | tf_op jit(solution)/shard_map/all_to_all | solution.py:81
  235.4 1.3 collective-permute-start.29
  236.7 5.4 %collective-permute-start.30 = (f32[2,2048]{1,0:T(2,128)S(1)}, f32[2,2048]{1,0:T(2,128)S(1)}, u32[]{:S(2)}, u32[]{:S(2)}) collective-permute-start(f32[2,2048]{1,0:T(2,128)S(1)} %fusion.21), channel_id=1, source_target_pairs={{0,64},{32,96},{64,0},{96,32},{1,65},{33,97},{65,1},{97,33},{2,66}... | collective-permute-start | bytes 49160 | tf_op jit(solution)/shard_map/ppermute | solution.py:27
  237.3 4.9 %collective-permute-start.31 = (f32[2,2048]{1,0:T(2,128)S(1)}, f32[2,2048]{1,0:T(2,128)S(1)}, u32[]{:S(2)}, u32[]{:S(2)}) collective-permute-start(f32[2,2048]{1,0:T(2,128)S(1)} %fusion.21), channel_id=1, source_target_pairs={{0,32},{32,64},{64,96},{96,0},{1,33},{33,65},{65,97},{97,1},{2,34}... | collective-permute-start | bytes 49160 | tf_op jit(solution)/shard_map/ppermute | solution.py:27
  238.8 3.7 %collective-permute-start.32 = (f32[2,2048]{1,0:T(2,128)S(1)}, f32[2,2048]{1,0:T(2,128)S(1)}, u32[]{:S(2)}, u32[]{:S(2)}) collective-permute-start(f32[2,2048]{1,0:T(2,128)S(1)} %fusion.21), channel_id=1, source_target_pairs={{0,96},{32,0},{64,32},{96,64},{1,97},{33,1},{65,33},{97,65},{2,98}... | collective-permute-start | bytes 49160 | tf_op jit(solution)/shard_map/ppermute | solution.py:27
  (8 other events, 46.2 us)

commit v6 on v5

--- a/solution.py
+++ b/solution.py
@@ -64,18 +64,28 @@
     )
 
 
-def scatter_features(part_t, sizes):
+def scatter_product(point_rows, hi, lo, col_scale, sizes):
     ny, nc = sizes["y"], sizes["c"]
-    width, rows = part_t.shape
+    rows, width = point_rows.shape
     blk = width // (ny * nc)
-    x = part_t.reshape(ny, nc, blk, rows)
+    dims = (((0,), (0,)), ((), ()))
+
+    def product(cols):
+        part = lax.dot_general(cols, hi, dims, preferred_element_type=jnp.float32)
+        part = part + lax.dot_general(cols, lo, dims, preferred_element_type=jnp.float32)
+        return part * col_scale[None, :]
+
+    split = point_rows.reshape(rows, ny, nc, blk)
     if nc == 2:
         c = lax.axis_index("c")
-        keep = lax.dynamic_index_in_dim(x, c, 1, keepdims=False)
-        send = lax.dynamic_index_in_dim(x, 1 - c, 1, keepdims=False)
-        x = keep + lax.ppermute(send, "c", [(0, 1), (1, 0)])
+        send = lax.dynamic_index_in_dim(split, 1 - c, 2, keepdims=False)
+        keep = lax.dynamic_index_in_dim(split, c, 2, keepdims=False)
+        sent = product(send.reshape(rows, ny * blk))
+        got = lax.ppermute(sent, "c", [(0, 1), (1, 0)])
+        x = product(keep.reshape(rows, ny * blk)) + got
     else:
-        x = x[:, 0]
+        x = product(split[:, :, 0].reshape(rows, ny * blk))
+    x = x.reshape(ny, blk, -1)
     if ny == 1:
         return x[0]
     got = lax.all_to_all(x, "y", 0, 0, tiled=False)
@@ -151,13 +161,8 @@
         hi_wide = lax.reduce_precision(scaled, exponent_bits=8, mantissa_bits=7)
         hi = hi_wide.astype(jnp.bfloat16)
         lo = (scaled - hi_wide).astype(jnp.bfloat16)
-        dims = (((0,), (0,)), ((), ()))
-        partial_t = lax.dot_general(
-            gathered, hi, dims, preferred_element_type=jnp.float32
-        ) + lax.dot_general(gathered, lo, dims, preferred_element_type=jnp.float32)
-        partial_t = partial_t * col_scale[None, :]
         mass_part = jnp.sum(scaled, axis=0) * col_scale / balance
-        moved = scatter_features(partial_t, sizes).T
+        moved = scatter_product(gathered, hi, lo, col_scale, sizes).T
         squares = jnp.sum(moved * moved, axis=1)
         both = multi_sum(jnp.stack([squares, mass_part]), pts_red)
         squares, masses = both[0], both[1]

time: 245 us -> 258 us (1.053)
  starting transfers between devices: 53.8 us -> 67.3 us
  matrix products: 34.2 us -> 27.4 us
  waiting for transfers between devices: 64.8 us -> 71.3 us
    ppermute x16, starting transfers between devices: 19.1 us -> 31.6 us  [axis_sum(): lax.ppermute(v, axis, [(i, (i + s) % n) for i in range(n)])]
    dot_general x2 -> x4, matrix products: 22.5 us -> 15.6 us  [the longest x2 8.68 us: product(): lax.dot_general(cols, lo, dims, preferred_element_type=jnp.float32)]
    all_to_all x1, waiting for transfers between devices: 31.2 us -> 37.9 us  [scatter_product(): got = lax.all_to_all(x, 'y', 0, 0, tiled=False)]
    ppermute x16, waiting for transfers between devices: 13.8 us -> 20.1 us  [axis_sum(): lax.ppermute(v, axis, [(i, (i + s) % n) for i in range(n)])]
    add x1 -> x0, other arithmetic: 5.23 us -> none  [scatter_features(): x = keep + lax.ppermute(send, 'c', [(0, 1), (1, 0)])]
    ppermute x1, waiting for transfers between devices: 5.78 us -> 2.14 us  [scatter_product(): got = lax.ppermute(sent, 'c', [(0, 1), (1, 0)])]
    convert_element_type x0 -> x2, other arithmetic: none -> 3.6 us  [the longest x1 2.74 us: unit_rows(): wide = values.astype(jnp.float32)]
  transfers between devices with their start and end apart: 35 -> 35, of which waited for: 21 -> 18; matrix products, arithmetic and copies ran while one was open for 5% -> 5% of each run, Pallas kernels for 0% -> 0%
where the time goes in v6:
time: 258 us; the launch traced here: 259 us
  waiting for transfers between devices  71.3 us (28%)
  starting transfers between devices  67.3 us (26%)
  other arithmetic  55 us (21%)
  matrix products  27.4 us (11%)
  blocking collectives  25.2 us (10%)
  local copies, waits for them, and re-layouts  11.4 us (4%)
    all_to_all x1, waiting for transfers between devices, scatter_product(): got = lax.all_to_all(x, 'y', 0, 0, tiled=False)  37.9 us
    ppermute x16, starting transfers between devices, axis_sum(): lax.ppermute(v, axis, [(i, (i + s) % n) for i in range(n)])  31.6 us
    all_to_all x2, blocking collectives, group_sum(): lax.all_to_all(jnp.broadcast_to(v[None], (n,) + v.shape), axes, 0, 0, til...  25.2 us
    reduce_sum x3, other arithmetic, local(): row_part = jnp.sum(kernel * col_scale[None, :], axis=1)  21.1 us
    ppermute x16, waiting for transfers between devices, axis_sum(): lax.ppermute(v, axis, [(i, (i + s) % n) for i in range(n)])  20.1 us
    reduce_sum x2, other arithmetic, local(): col_part = jnp.sum(kernel * row_scale[:, None], axis=0)  13.9 us
    ppermute x4, starting transfers between devices, ring_gather(): lax.ppermute(bwd[..., half:, :], axis, [(i, (i - 1) % n) for i in range(n)])  13 us
    dot_general x1, matrix products, local(): jnp.dot(unit_points, unit_centroids.T, preferred_element_type=jnp.float32)  11.8 us
  transfers between devices with their start and end apart: 35, of which 18 were waited for; matrix products, arithmetic and copies ran while one was open for 5% of the time, Pallas kernels for 0%

profile of v6, /device:TPU:0, one launch (start us, length us, event | category | flops | bytes accessed | tf_op | source)
XLA Modules:
  0.0 258.8 jit_solution(11658505233447520581)
XLA Ops:
  11.7 3.3 %collective-permute-start.3 = (bf16[1024,24]{0,1:T(8,128)(2,1)S(1)}, bf16[1024,24]{0,1:T(8,128)(2,1)S(1)}, u32[]{:S(2)}, u32[]{:S(2)}) collective-permute-start(bf16[1024,24]{0,1:T(8,128)(2,1)S(1)} %slice.313), channel_id=1, source_target_pairs={{0,3},{1,0},{2,1},{3,2},{4,7},{5,4},{6,5},{7,6},{8,11},{9,8},{10,9... | collective-permute-start | bytes 147464 | tf_op jit(solution)/shard_map/ppermute | solution.py:109
  15.4 3.0 %collective-permute-start.11 = (bf16[1024,24]{0,1:T(8,128)(2,1)S(1)}, bf16[1024,24]{0,1:T(8,128)(2,1)S(1)}, u32[]{:S(2)}, u32[]{:S(2)}) collective-permute-start(bf16[1024,24]{0,1:T(8,128)(2,1)S(1)} %slice.317), channel_id=1, source_target_pairs={{0,12},{4,0},{8,4},{12,8},{1,13},{5,1},{9,5},{13,9},{2,14},{6,2},{... | collective-permute-start | bytes 147464 | tf_op jit(solution)/shard_map/ppermute | solution.py:109
  19.1 3.2 %collective-permute-start.6 = (bf16[4,2048,24]{1,2,0:T(8,128)(2,1)S(1)}, bf16[4,2048,24]{1,2,0:T(8,128)(2,1)S(1)}, u32[]{:S(2)}, u32[]{:S(2)}) collective-permute-start(bf16[4,2048,24]{1,2,0:T(8,128)(2,1)S(1)} %gather_fusion), channel_id=1, source_target_pairs={{0,12},{4,0},{8,4},{12,8},{1,13},{5,1},{9,5},{13,9},{2,14},{6,2},{... | collective-permute-start | bytes 1179656 | tf_op jit(solution)/shard_map/ppermute | solution.py:104
  23.1 3.2 %collective-permute-start.14 = (bf16[4,2048,24]{1,2,0:T(8,128)(2,1)S(1)}, bf16[4,2048,24]{1,2,0:T(8,128)(2,1)S(1)}, u32[]{:S(2)}, u32[]{:S(2)}) collective-permute-start(bf16[4,2048,24]{1,2,0:T(8,128)(2,1)S(1)} %gather_fusion.2), channel_id=1, source_target_pairs={{0,3},{1,0},{2,1},{3,2},{4,7},{5,4},{6,5},{7,6},{8,11},{9,8},{10,9... | collective-permute-start | bytes 1179656 | tf_op jit(solution)/shard_map/ppermute | solution.py:104
  29.0 3.3 %collective-permute-start.7 = (bf16[4,1024,24]{1,2,0:T(8,128)(2,1)S(1)}, bf16[4,1024,24]{1,2,0:T(8,128)(2,1)S(1)}, u32[]{:S(2)}, u32[]{:S(2)}) collective-permute-start(bf16[4,1024,24]{1,2,0:T(8,128)(2,1)S(1)} %slice.315), channel_id=1, source_target_pairs={{0,12},{4,0},{8,4},{12,8},{1,13},{5,1},{9,5},{13,9},{2,14},{6,2},{... | collective-permute-start | bytes 589832 | tf_op jit(solution)/shard_map/ppermute | solution.py:109
  33.8 3.5 %collective-permute-start.15 = (bf16[4,1024,24]{1,2,0:T(8,128)(2,1)}, bf16[4,1024,24]{1,2,0:T(8,128)(2,1)}, u32[]{:S(2)}, u32[]{:S(2)}) collective-permute-start(bf16[4,1024,24]{1,2,0:T(8,128)(2,1)} %slice.319), channel_id=1, source_target_pairs={{0,3},{1,0},{2,1},{3,2},{4,7},{5,4},{6,5},{7,6},{8,11},{9,8},{10,9... | collective-permute-start | bytes 589832 | tf_op jit(solution)/shard_map/ppermute | solution.py:109
  47.1 2.7 %bitcast_convert_fusion = (f32[2048,4,4,48]{0,3,2,1:T(8,128)S(1)}, bf16[4,4,2048,48]{2,3,1,0:T(8,128)(2,1)}) fusion(bf16[4,4,2048,24]{2,3,1,0:T(8,128)(2,1)S(1)} %bitcast.66, bf16[4,4,2048,24]{2,3,1,0:T(8,128)(2,1)S(1)} %gather_fusion.1), kind=kLoop, calls=%fused_computation.22 | loop fusion | flops 7864320 | bytes 12582912 | tf_op jit(solution)/shard_map/convert_element_type | solution.py:17
  51.8 11.8 %fusion.19 = (f32[2048]{0:T(1024)S(1)}, f32[2048,2048]{1,0:T(8,128)}) fusion(bf16[2048,768]{0,1:T(8,128)(2,1)S(1)} %fusion.3, bf16[2048,768]{1,0:T(8,128)(2,1)S(1)} %copy-done.1, f32[2048]{0:T(1024)S(1)} %add_rsqrt_fusion), kind=kOutput, calls=%fused_computation.120 | convolution fusion | flops 6455556096 | bytes 23085056 | tf_op jit(solution)/shard_map/dot_general | solution.py:153
  64.8 3.0 %collective-permute-start.19 = (f32[2048]{0:T(1024)S(1)}, f32[2048]{0:T(1024)S(1)}, u32[]{:S(2)}, u32[]{:S(2)}) collective-permute-start(f32[2048]{0:T(1024)S(1)} %add.494), channel_id=1, source_target_pairs={{0,96},{32,0},{64,32},{96,64},{1,97},{33,1},{65,33},{97,65},{2,98}... | collective-permute-start | bytes 24584 | tf_op jit(solution)/shard_map/ppermute | solution.py:27
  70.0 2.7 %collective-permute-done.18 = f32[2048]{0:T(1024)S(1)} collective-permute-done((f32[2048]{0:T(1024)S(1)}, f32[2048]{0:T(1024)S(1)}, u32[]{:S(2)}, u32[]{:S(2)}) %collective-permute-start.18) | collective-permute-done | bytes 8224 | tf_op jit(solution)/shard_map/ppermute | solution.py:27
  72.9 7.0 %multiply_reduce_fusion.4 = f32[2048]{0:T(1024)S(1)} fusion(f32[2048,2048]{1,0:T(8,128)} %get-tuple-element.18, f32[2048]{0:T(1024)S(1)} %add_divide_fusion.2), kind=kLoop, calls=%fused_computation.11 | loop fusion | flops 8386560 | bytes 16793600 | tf_op jit(solution)/shard_map/reduce_sum | solution.py:158
  80.0 13.9 %all_to_all.23 = f32[16,1,2048]{2,1,0:T(1,128)S(1)} all-to-all(f32[16,1,2048]{2,1,0:T(1,128)S(1)} %broadcast_in_dim.6), channel_id=1, replica_groups=mesh['y'=4,'c'=2,'x'=4,'z'=4] {'x','z'}, dimensions={0} | all-to-all | bytes 262144 | tf_op jit(solution)/shard_map/all_to_all | solution.py:44
  94.0 6.9 %multiply_reduce_fusion.3 = f32[2048]{0:T(1024)S(1)} fusion(f32[2048,2048]{1,0:T(8,128)} %get-tuple-element.18, f32[2048]{0:T(1024)S(1)} %bitcast.87), kind=kLoop, calls=%fused_computation.10 | loop fusion | flops 8386560 | bytes 16793600 | tf_op jit(solution)/shard_map/reduce_sum | solution.py:156
  102.2 16.6 %collective-permute-start.23 = (f32[2048]{0:T(1024)S(1)}, f32[2048]{0:T(1024)S(1)}, u32[]{:S(2)}, u32[]{:S(2)}) collective-permute-start(f32[2048]{0:T(1024)S(1)} %add.514), channel_id=1, source_target_pairs={{0,96},{32,0},{64,32},{96,64},{1,97},{33,1},{65,33},{97,65},{2,98}... | collective-permute-start | bytes 24584 | tf_op jit(solution)/shard_map/ppermute | solution.py:27
  120.3 3.3 %collective-permute-done.22 = f32[2048]{0:T(1024)S(1)} collective-permute-done((f32[2048]{0:T(1024)S(1)}, f32[2048]{0:T(1024)S(1)}, u32[]{:S(2)}, u32[]{:S(2)}) %collective-permute-start.22) | collective-permute-done | bytes 8224 | tf_op jit(solution)/shard_map/ppermute | solution.py:27
  123.9 7.0 %multiply_reduce_fusion.2 = f32[2048]{0:T(1024)S(1)} fusion(f32[2048,2048]{1,0:T(8,128)} %get-tuple-element.18, f32[2048]{0:T(1024)S(1)} %add_divide_fusion.1), kind=kLoop, calls=%fused_computation.9 | loop fusion | flops 8386560 | bytes 16793600 | tf_op jit(solution)/shard_map/reduce_sum | solution.py:158
  131.0 11.2 %all_to_all.24 = f32[16,1,2048]{2,1,0:T(1,128)S(1)} all-to-all(f32[16,1,2048]{2,1,0:T(1,128)S(1)} %broadcast_in_dim.7), channel_id=1, replica_groups=mesh['y'=4,'c'=2,'x'=4,'z'=4] {'x','z'}, dimensions={0} | all-to-all | bytes 262144 | tf_op jit(solution)/shard_map/all_to_all | solution.py:44
  142.3 6.9 %multiply_reduce_fusion.1 = f32[2048]{0:T(1024)S(1)} fusion(f32[2048,2048]{1,0:T(8,128)} %get-tuple-element.18, f32[2048]{0:T(1024)S(1)} %bitcast.88), kind=kLoop, calls=%fused_computation.8 | loop fusion | flops 8386560 | bytes 16793600 | tf_op jit(solution)/shard_map/reduce_sum | solution.py:156
  150.5 3.2 %collective-permute-start.27 = (f32[2048]{0:T(1024)S(1)}, f32[2048]{0:T(1024)S(1)}, u32[]{:S(2)}, u32[]{:S(2)}) collective-permute-start(f32[2048]{0:T(1024)S(1)} %add.534), channel_id=1, source_target_pairs={{0,96},{32,0},{64,32},{96,64},{1,97},{33,1},{65,33},{97,65},{2,98}... | collective-permute-start | bytes 24584 | tf_op jit(solution)/shard_map/ppermute | solution.py:27
  155.2 3.4 %collective-permute-done.26 = f32[2048]{0:T(1024)S(1)} collective-permute-done((f32[2048]{0:T(1024)S(1)}, f32[2048]{0:T(1024)S(1)}, u32[]{:S(2)}, u32[]{:S(2)}) %collective-permute-start.26) | collective-permute-done | bytes 8224 | tf_op jit(solution)/shard_map/ppermute | solution.py:27
  158.9 7.1 %multiply_reduce_fusion = f32[2048]{0:T(1024)S(1)} fusion(f32[2048,2048]{1,0:T(8,128)} %get-tuple-element.18, f32[2048]{0:T(1024)S(1)} %add_divide_fusion), kind=kLoop, calls=%fused_computation.7 | loop fusion | flops 8386560 | bytes 16793600 | tf_op jit(solution)/shard_map/reduce_sum | solution.py:158
  166.8 3.6 %all-to-all-start.2 = ((f32[16,1,2048]{2,1,0:T(1,128)}), f32[16,1,2048]{2,1,0:T(1,128)S(1)}, u32[]{:S(2)}, u32[]{:S(2)}) async-start(f32[16,1,2048]{2,1,0:T(1,128)} %broadcast_in_dim.8), calls=%async_computation.2 | async-start | bytes 262144 | tf_op jit(solution)/shard_map/all_to_all | solution.py:44
  172.3 5.9 %all-to-all-done.2 = f32[16,1,2048]{2,1,0:T(1,128)S(1)} async-done(((f32[16,1,2048]{2,1,0:T(1,128)}), f32[16,1,2048]{2,1,0:T(1,128)S(1)}, u32[]{:S(2)}, u32[]{:S(2)}) %all-to-all-start.2) | async-done | bytes 131104 | tf_op jit(solution)/shard_map/all_to_all | solution.py:44
  178.3 8.3 %multiply_reduce_fusion.5 = (f32[2048]{0:T(1024)S(1)}, bf16[2048,2048]{1,0:T(8,128)(2,1)S(1)}, bf16[2048,2048]{1,0:T(8,128)(2,1)S(1)}) fusion(f32[2048,2048]{1,0:T(8,128)} %get-tuple-element.18, f32[2048]{0:T(1024)S(1)} %bitcast.90), kind=kLoop, calls=%fused_computation.13 | loop fusion | flops 25163776 | bytes 33570816 | tf_op jit(solution)/shard_map/reduce_sum | solution.py:164
  186.6 3.5 %fusion.21 = f32[384,2048]{1,0:T(8,128)S(1)} fusion(bf16[2048,384]{0,1:T(8,128)(2,1)S(1)} %bitcast.71, bf16[2048,2048]{1,0:T(8,128)(2,1)S(1)} %get-tuple-element.6), kind=kOutput, calls=%fused_computation.122 | convolution fusion | flops 3221225472 | bytes 13107200 | tf_op jit(solution)/shard_map/dot_general | solution.py:74
  190.1 3.5 %add_multiply_fusion = f32[384,2048]{1,0:T(8,128)S(1)} fusion(f32[384,2048]{1,0:T(8,128)S(1)} %fusion.21, bf16[2048,384]{0,1:T(8,128)(2,1)S(1)} %bitcast.72, bf16[2048,2048]{1,0:T(8,128)(2,1)S(1)} %get-tuple-element.5, f32[2048]{0:T(1024)S(1)} %add_divide_fusion), kind=kOutput, calls=%fused_computation.23 | convolution fusion | flops 3222798336 | bytes 16261120 | tf_op jit(solution)/shard_map/dot_general | solution.py:75
  193.7 3.5 %fusion.20 = f32[384,2048]{1,0:T(8,128)S(1)} fusion(bf16[2048,384]{0,1:T(8,128)(2,1)S(1)} %bitcast.69, bf16[2048,2048]{1,0:T(8,128)(2,1)S(1)} %get-tuple-element.6), kind=kOutput, calls=%fused_computation.121 | convolution fusion | flops 3221225472 | bytes 13107200 | tf_op jit(solution)/shard_map/dot_general | solution.py:74
  199.4 5.2 %multiply_add_fusion = f32[384,2048]{1,0:T(8,128)} fusion(f32[384,2048]{1,0:T(8,128)S(1)} %collective-permute-done.28, f32[384,2048]{1,0:T(8,128)S(1)} %fusion.20, bf16[2048,384]{0,1:T(8,128)(2,1)S(1)} %bitcast.70, bf16[2048,2048]{1,0:T(8,128)(2,1)S(1)} %get-tuple-element.5, f32[2048]{0:T(1024)S(1)} %add_divide_fusion), kind=kOutput, calls=%fused_computation.24 | convolution fusion | flops 3223584768 | bytes 19406848 | tf_op jit(solution)/shard_map/dot_general | solution.py:75
  204.6 4.5 %all-to-all-start.3 = ((f32[4,96,2048]{2,1,0:T(8,128)}), f32[4,96,2048]{2,1,0:T(8,128)S(1)}, u32[]{:S(2)}, u32[]{:S(2)}) async-start(f32[4,96,2048]{2,1,0:T(8,128)} %bitcast.68), calls=%async_computation.3 | async-start | bytes 6291456 | tf_op jit(solution)/shard_map/all_to_all | solution.py:91
  209.1 37.9 %all-to-all-done.3 = f32[4,96,2048]{2,1,0:T(8,128)S(1)} async-done(((f32[4,96,2048]{2,1,0:T(8,128)}), f32[4,96,2048]{2,1,0:T(8,128)S(1)}, u32[]{:S(2)}, u32[]{:S(2)}) %all-to-all-start.3) | async-done | bytes 3145760 | tf_op jit(solution)/shard_map/all_to_all | solution.py:91
  249.1 2.7 %collective-permute-start.32 = (f32[2,2048]{1,0:T(2,128)S(1)}, f32[2,2048]{1,0:T(2,128)S(1)}, u32[]{:S(2)}, u32[]{:S(2)}) collective-permute-start(f32[2,2048]{1,0:T(2,128)S(1)} %fusion.16), channel_id=1, source_target_pairs={{0,96},{32,0},{64,32},{96,64},{1,97},{33,1},{65,33},{97,65},{2,98}... | collective-permute-start | bytes 49160 | tf_op jit(solution)/shard_map/ppermute | solution.py:27
  253.5 3.5 %collective-permute-done.30 = f32[2,2048]{1,0:T(2,128)S(1)} collective-permute-done((f32[2,2048]{1,0:T(2,128)S(1)}, f32[2,2048]{1,0:T(2,128)S(1)}, u32[]{:S(2)}, u32[]{:S(2)}) %collective-permute-start.30) | collective-permute-done | bytes 16416 | tf_op jit(solution)/shard_map/ppermute | solution.py:27
  (115 shorter events, 49.2 us)
Async XLA Ops:
  1.6 13.4 %collective-permute-start.8 = (bf16[2048,24]{0,1:T(8,128)(2,1)S(1)}, bf16[2048,24]{0,1:T(8,128)(2,1)S(1)}, u32[]{:S(2)}, u32[]{:S(2)}) collective-permute-start(bf16[2048,24]{0,1:T(8,128)(2,1)S(1)} %get-tuple-element.13), channel_id=1, source_target_pairs={{0,4},{4,8},{8,12},{12,0},{1,5},{5,9},{9,13},{13,1},{2,6},{6,10},{... | collective-permute-start | bytes 294920 | tf_op jit(solution)/shard_map/ppermute | solution.py:103
  3.3 12.1 %collective-permute-start.10 = (bf16[2048,24]{0,1:T(8,128)(2,1)S(1)}, bf16[2048,24]{0,1:T(8,128)(2,1)S(1)}, u32[]{:S(2)}, u32[]{:S(2)}) collective-permute-start(bf16[2048,24]{0,1:T(8,128)(2,1)S(1)} %get-tuple-element.13), channel_id=1, source_target_pairs={{0,12},{4,0},{8,4},{12,8},{1,13},{5,1},{9,5},{13,9},{2,14},{6,2},{... | collective-permute-start | bytes 294920 | tf_op jit(solution)/shard_map/ppermute | solution.py:104
  4.9 6.7 %collective-permute-start = (bf16[2048,24]{0,1:T(8,128)(2,1)S(1)}, bf16[2048,24]{0,1:T(8,128)(2,1)S(1)}, u32[]{:S(2)}, u32[]{:S(2)}) collective-permute-start(bf16[2048,24]{0,1:T(8,128)(2,1)S(1)} %get-tuple-element.14), channel_id=1, source_target_pairs={{0,1},{1,2},{2,3},{3,0},{4,5},{5,6},{6,7},{7,4},{8,9},{9,10},{10,1... | collective-permute-start | bytes 294920 | tf_op jit(solution)/shard_map/ppermute | solution.py:103
  6.9 4.7 %collective-permute-start.2 = (bf16[2048,24]{0,1:T(8,128)(2,1)S(1)}, bf16[2048,24]{0,1:T(8,128)(2,1)S(1)}, u32[]{:S(2)}, u32[]{:S(2)}) collective-permute-start(bf16[2048,24]{0,1:T(8,128)(2,1)S(1)} %get-tuple-element.14), channel_id=1, source_target_pairs={{0,3},{1,0},{2,1},{3,2},{4,7},{5,4},{6,5},{7,6},{8,11},{9,8},{10,9... | collective-permute-start | bytes 294920 | tf_op jit(solution)/shard_map/ppermute | solution.py:104
  11.7 6.7 %collective-permute-start.1 = (bf16[1024,24]{0,1:T(8,128)(2,1)S(1)}, bf16[1024,24]{0,1:T(8,128)(2,1)S(1)}, u32[]{:S(2)}, u32[]{:S(2)}) collective-permute-start(bf16[1024,24]{0,1:T(8,128)(2,1)S(1)} %slice.312), channel_id=1, source_target_pairs={{0,1},{1,2},{2,3},{3,0},{4,5},{5,6},{6,7},{7,4},{8,9},{9,10},{10,1... | collective-permute-start | bytes 147464 | tf_op jit(solution)/shard_map/ppermute | solution.py:108
  11.7 6.7 %collective-permute-start.3 = (bf16[1024,24]{0,1:T(8,128)(2,1)S(1)}, bf16[1024,24]{0,1:T(8,128)(2,1)S(1)}, u32[]{:S(2)}, u32[]{:S(2)}) collective-permute-start(bf16[1024,24]{0,1:T(8,128)(2,1)S(1)} %slice.313), channel_id=1, source_target_pairs={{0,3},{1,0},{2,1},{3,2},{4,7},{5,4},{6,5},{7,6},{8,11},{9,8},{10,9... | collective-permute-start | bytes 147464 | tf_op jit(solution)/shard_map/ppermute | solution.py:109
  15.0 7.3 %collective-permute-start.9 = (bf16[1024,24]{0,1:T(8,128)(2,1)S(1)}, bf16[1024,24]{0,1:T(8,128)(2,1)S(1)}, u32[]{:S(2)}, u32[]{:S(2)}) collective-permute-start(bf16[1024,24]{0,1:T(8,128)(2,1)S(1)} %slice.316), channel_id=1, source_target_pairs={{0,4},{4,8},{8,12},{12,0},{1,5},{5,9},{9,13},{13,1},{2,6},{6,10},{... | collective-permute-start | bytes 147464 | tf_op jit(solution)/shard_map/ppermute | solution.py:108
  15.4 7.0 %collective-permute-start.11 = (bf16[1024,24]{0,1:T(8,128)(2,1)S(1)}, bf16[1024,24]{0,1:T(8,128)(2,1)S(1)}, u32[]{:S(2)}, u32[]{:S(2)}) collective-permute-start(bf16[1024,24]{0,1:T(8,128)(2,1)S(1)} %slice.317), channel_id=1, source_target_pairs={{0,12},{4,0},{8,4},{12,8},{1,13},{5,1},{9,5},{13,9},{2,14},{6,2},{... | collective-permute-start | bytes 147464 | tf_op jit(solution)/shard_map/ppermute | solution.py:109
  19.0 9.9 %collective-permute-start.4 = (bf16[4,2048,24]{1,2,0:T(8,128)(2,1)S(1)}, bf16[4,2048,24]{1,2,0:T(8,128)(2,1)S(1)}, u32[]{:S(2)}, u32[]{:S(2)}) collective-permute-start(bf16[4,2048,24]{1,2,0:T(8,128)(2,1)S(1)} %gather_fusion), channel_id=1, source_target_pairs={{0,4},{4,8},{8,12},{12,0},{1,5},{5,9},{9,13},{13,1},{2,6},{6,10},{... | collective-permute-start | bytes 1179656 | tf_op jit(solution)/shard_map/ppermute | solution.py:103
  19.1 9.9 %collective-permute-start.6 = (bf16[4,2048,24]{1,2,0:T(8,128)(2,1)S(1)}, bf16[4,2048,24]{1,2,0:T(8,128)(2,1)S(1)}, u32[]{:S(2)}, u32[]{:S(2)}) collective-permute-start(bf16[4,2048,24]{1,2,0:T(8,128)(2,1)S(1)} %gather_fusion), channel_id=1, source_target_pairs={{0,12},{4,0},{8,4},{12,8},{1,13},{5,1},{9,5},{13,9},{2,14},{6,2},{... | collective-permute-start | bytes 1179656 | tf_op jit(solution)/shard_map/ppermute | solution.py:104
  23.0 9.3 %collective-permute-start.12 = (bf16[4,2048,24]{1,2,0:T(8,128)(2,1)S(1)}, bf16[4,2048,24]{1,2,0:T(8,128)(2,1)S(1)}, u32[]{:S(2)}, u32[]{:S(2)}) collective-permute-start(bf16[4,2048,24]{1,2,0:T(8,128)(2,1)S(1)} %gather_fusion.2), channel_id=1, source_target_pairs={{0,1},{1,2},{2,3},{3,0},{4,5},{5,6},{6,7},{7,4},{8,9},{9,10},{10,1... | collective-permute-start | bytes 1179656 | tf_op jit(solution)/shard_map/ppermute | solution.py:103
  23.1 10.0 %collective-permute-start.14 = (bf16[4,2048,24]{1,2,0:T(8,128)(2,1)S(1)}, bf16[4,2048,24]{1,2,0:T(8,128)(2,1)S(1)}, u32[]{:S(2)}, u32[]{:S(2)}) collective-permute-start(bf16[4,2048,24]{1,2,0:T(8,128)(2,1)S(1)} %gather_fusion.2), channel_id=1, source_target_pairs={{0,3},{1,0},{2,1},{3,2},{4,7},{5,4},{6,5},{7,6},{8,11},{9,8},{10,9... | collective-permute-start | bytes 1179656 | tf_op jit(solution)/shard_map/ppermute | solution.py:104
  28.9 8.4 %collective-permute-start.5 = (bf16[4,1024,24]{1,2,0:T(8,128)(2,1)S(1)}, bf16[4,1024,24]{1,2,0:T(8,128)(2,1)S(1)}, u32[]{:S(2)}, u32[]{:S(2)}) collective-permute-start(bf16[4,1024,24]{1,2,0:T(8,128)(2,1)S(1)} %slice.314), channel_id=1, source_target_pairs={{0,4},{4,8},{8,12},{12,0},{1,5},{5,9},{9,13},{13,1},{2,6},{6,10},{... | collective-permute-start | bytes 589832 | tf_op jit(solution)/shard_map/ppermute | solution.py:108
  29.0 8.2 %collective-permute-start.7 = (bf16[4,1024,24]{1,2,0:T(8,128)(2,1)S(1)}, bf16[4,1024,24]{1,2,0:T(8,128)(2,1)S(1)}, u32[]{:S(2)}, u32[]{:S(2)}) collective-permute-start(bf16[4,1024,24]{1,2,0:T(8,128)(2,1)S(1)} %slice.315), channel_id=1, source_target_pairs={{0,12},{4,0},{8,4},{12,8},{1,13},{5,1},{9,5},{13,9},{2,14},{6,2},{... | collective-permute-start | bytes 589832 | tf_op jit(solution)/shard_map/ppermute | solution.py:109
  33.1 7.2 %collective-permute-start.13 = (bf16[4,1024,24]{1,2,0:T(8,128)(2,1)}, bf16[4,1024,24]{1,2,0:T(8,128)(2,1)}, u32[]{:S(2)}, u32[]{:S(2)}) collective-permute-start(bf16[4,1024,24]{1,2,0:T(8,128)(2,1)} %slice.318), channel_id=1, source_target_pairs={{0,1},{1,2},{2,3},{3,0},{4,5},{5,6},{6,7},{7,4},{8,9},{9,10},{10,1... | collective-permute-start | bytes 589832 | tf_op jit(solution)/shard_map/ppermute | solution.py:108
  33.8 7.0 %collective-permute-start.15 = (bf16[4,1024,24]{1,2,0:T(8,128)(2,1)}, bf16[4,1024,24]{1,2,0:T(8,128)(2,1)}, u32[]{:S(2)}, u32[]{:S(2)}) collective-permute-start(bf16[4,1024,24]{1,2,0:T(8,128)(2,1)} %slice.319), channel_id=1, source_target_pairs={{0,3},{1,0},{2,1},{3,2},{4,7},{5,4},{6,5},{7,6},{8,11},{9,8},{10,9... | collective-permute-start | bytes 589832 | tf_op jit(solution)/shard_map/ppermute | solution.py:109
  64.8 5.2 %collective-permute-start.19 = (f32[2048]{0:T(1024)S(1)}, f32[2048]{0:T(1024)S(1)}, u32[]{:S(2)}, u32[]{:S(2)}) collective-permute-start(f32[2048]{0:T(1024)S(1)} %add.494), channel_id=1, source_target_pairs={{0,96},{32,0},{64,32},{96,64},{1,97},{33,1},{65,33},{97,65},{2,98}... | collective-permute-start | bytes 24584 | tf_op jit(solution)/shard_map/ppermute | solution.py:27
  67.8 4.9 %collective-permute-start.18 = (f32[2048]{0:T(1024)S(1)}, f32[2048]{0:T(1024)S(1)}, u32[]{:S(2)}, u32[]{:S(2)}) collective-permute-start(f32[2048]{0:T(1024)S(1)} %add.494), channel_id=1, source_target_pairs={{0,32},{32,64},{64,96},{96,0},{1,33},{33,65},{65,97},{97,1},{2,34}... | collective-permute-start | bytes 24584 | tf_op jit(solution)/shard_map/ppermute | solution.py:27
  67.8 5.2 %collective-permute-start.17 = (f32[2048]{0:T(1024)S(1)}, f32[2048]{0:T(1024)S(1)}, u32[]{:S(2)}, u32[]{:S(2)}) collective-permute-start(f32[2048]{0:T(1024)S(1)} %add.494), channel_id=1, source_target_pairs={{0,64},{32,96},{64,0},{96,32},{1,65},{33,97},{65,1},{97,33},{2,66}... | collective-permute-start | bytes 24584 | tf_op jit(solution)/shard_map/ppermute | solution.py:27
  102.2 18.1 %collective-permute-start.23 = (f32[2048]{0:T(1024)S(1)}, f32[2048]{0:T(1024)S(1)}, u32[]{:S(2)}, u32[]{:S(2)}) collective-permute-start(f32[2048]{0:T(1024)S(1)} %add.514), channel_id=1, source_target_pairs={{0,96},{32,0},{64,32},{96,64},{1,97},{33,1},{65,33},{97,65},{2,98}... | collective-permute-start | bytes 24584 | tf_op jit(solution)/shard_map/ppermute | solution.py:27
  118.8 4.9 %collective-permute-start.22 = (f32[2048]{0:T(1024)S(1)}, f32[2048]{0:T(1024)S(1)}, u32[]{:S(2)}, u32[]{:S(2)}) collective-permute-start(f32[2048]{0:T(1024)S(1)} %add.514), channel_id=1, source_target_pairs={{0,32},{32,64},{64,96},{96,0},{1,33},{33,65},{65,97},{97,1},{2,34}... | collective-permute-start | bytes 24584 | tf_op jit(solution)/shard_map/ppermute | solution.py:27
  118.8 5.2 %collective-permute-start.21 = (f32[2048]{0:T(1024)S(1)}, f32[2048]{0:T(1024)S(1)}, u32[]{:S(2)}, u32[]{:S(2)}) collective-permute-start(f32[2048]{0:T(1024)S(1)} %add.514), channel_id=1, source_target_pairs={{0,64},{32,96},{64,0},{96,32},{1,65},{33,97},{65,1},{97,33},{2,66}... | collective-permute-start | bytes 24584 | tf_op jit(solution)/shard_map/ppermute | solution.py:27
  150.5 4.7 %collective-permute-start.27 = (f32[2048]{0:T(1024)S(1)}, f32[2048]{0:T(1024)S(1)}, u32[]{:S(2)}, u32[]{:S(2)}) collective-permute-start(f32[2048]{0:T(1024)S(1)} %add.534), channel_id=1, source_target_pairs={{0,96},{32,0},{64,32},{96,64},{1,97},{33,1},{65,33},{97,65},{2,98}... | collective-permute-start | bytes 24584 | tf_op jit(solution)/shard_map/ppermute | solution.py:27
  153.8 4.9 %collective-permute-start.26 = (f32[2048]{0:T(1024)S(1)}, f32[2048]{0:T(1024)S(1)}, u32[]{:S(2)}, u32[]{:S(2)}) collective-permute-start(f32[2048]{0:T(1024)S(1)} %add.534), channel_id=1, source_target_pairs={{0,32},{32,64},{64,96},{96,0},{1,33},{33,65},{65,97},{97,1},{2,34}... | collective-permute-start | bytes 24584 | tf_op jit(solution)/shard_map/ppermute | solution.py:27
  153.8 5.2 %collective-permute-start.25 = (f32[2048]{0:T(1024)S(1)}, f32[2048]{0:T(1024)S(1)}, u32[]{:S(2)}, u32[]{:S(2)}) collective-permute-start(f32[2048]{0:T(1024)S(1)} %add.534), channel_id=1, source_target_pairs={{0,64},{32,96},{64,0},{96,32},{1,65},{33,97},{65,1},{97,33},{2,66}... | collective-permute-start | bytes 24584 | tf_op jit(solution)/shard_map/ppermute | solution.py:27
  166.8 11.4 %all-to-all-start.2 = ((f32[16,1,2048]{2,1,0:T(1,128)}), f32[16,1,2048]{2,1,0:T(1,128)S(1)}, u32[]{:S(2)}, u32[]{:S(2)}) async-start(f32[16,1,2048]{2,1,0:T(1,128)} %broadcast_in_dim.8), calls=%async_computation.2 | async-start | bytes 262144 | tf_op jit(solution)/shard_map/all_to_all | solution.py:44
  193.6 5.7 %collective-permute-start.28 = (f32[384,2048]{1,0:T(8,128)S(1)}, f32[384,2048]{1,0:T(8,128)S(1)}, u32[]{:S(2)}, u32[]{:S(2)}) collective-permute-start(f32[384,2048]{1,0:T(8,128)S(1)} %add_multiply_fusion), channel_id=1, source_target_pairs={{0,16},{16,0},{1,17},{17,1},{2,18},{18,2},{3,19},{19,3},{4,20},{20... | collective-permute-start | bytes 9437192 | tf_op jit(solution)/shard_map/ppermute | solution.py:84
  204.6 42.4 %all-to-all-start.3 = ((f32[4,96,2048]{2,1,0:T(8,128)}), f32[4,96,2048]{2,1,0:T(8,128)S(1)}, u32[]{:S(2)}, u32[]{:S(2)}) async-start(f32[4,96,2048]{2,1,0:T(8,128)} %bitcast.68), calls=%async_computation.3 | async-start | bytes 6291456 | tf_op jit(solution)/shard_map/all_to_all | solution.py:91
  247.2 1.3 collective-permute-start.29
  248.5 5.0 %collective-permute-start.31 = (f32[2,2048]{1,0:T(2,128)S(1)}, f32[2,2048]{1,0:T(2,128)S(1)}, u32[]{:S(2)}, u32[]{:S(2)}) collective-permute-start(f32[2,2048]{1,0:T(2,128)S(1)} %fusion.16), channel_id=1, source_target_pairs={{0,32},{32,64},{64,96},{96,0},{1,33},{33,65},{65,97},{97,1},{2,34}... | collective-permute-start | bytes 49160 | tf_op jit(solution)/shard_map/ppermute | solution.py:27
  249.1 4.4 %collective-permute-start.32 = (f32[2,2048]{1,0:T(2,128)S(1)}, f32[2,2048]{1,0:T(2,128)S(1)}, u32[]{:S(2)}, u32[]{:S(2)}) collective-permute-start(f32[2,2048]{1,0:T(2,128)S(1)} %fusion.16), channel_id=1, source_target_pairs={{0,96},{32,0},{64,32},{96,64},{1,97},{33,1},{65,33},{97,65},{2,98}... | collective-permute-start | bytes 49160 | tf_op jit(solution)/shard_map/ppermute | solution.py:27
  251.8 5.2 %collective-permute-start.30 = (f32[2,2048]{1,0:T(2,128)S(1)}, f32[2,2048]{1,0:T(2,128)S(1)}, u32[]{:S(2)}, u32[]{:S(2)}) collective-permute-start(f32[2,2048]{1,0:T(2,128)S(1)} %fusion.16), channel_id=1, source_target_pairs={{0,64},{32,96},{64,0},{96,32},{1,65},{33,97},{65,1},{97,33},{2,66}... | collective-permute-start | bytes 49160 | tf_op jit(solution)/shard_map/ppermute | solution.py:27
  (9 other events, 38.2 us)

commit v7 on v5

--- a/solution.py
+++ b/solution.py
@@ -1,6 +1,7 @@
 import jax
 import jax.numpy as jnp
 from jax import lax
+from jax.experimental import pallas as pl
 from jax.sharding import Mesh
 from jax.sharding import PartitionSpec as P
 
@@ -124,6 +125,55 @@
     return jnp.transpose(full, (2, 0, 1, 3)).reshape(rows, nx * nz * blk)
 
 
+BLOCK_ROWS = 256
+
+
+def weighted_col_sums(kernel, row_scale):
+    n, m = kernel.shape
+    bn = BLOCK_ROWS if n % BLOCK_ROWS == 0 else n
+
+    def body(k_ref, r_ref, o_ref):
+        @pl.when(pl.program_id(0) == 0)
+        def _():
+            o_ref[...] = jnp.zeros_like(o_ref)
+
+        o_ref[...] += jnp.sum(k_ref[...] * r_ref[...], axis=0, keepdims=True)
+
+    out = pl.pallas_call(
+        body,
+        grid=(n // bn,),
+        in_specs=[
+            pl.BlockSpec((bn, m), lambda i: (i, 0)),
+            pl.BlockSpec((bn, 1), lambda i: (i, 0)),
+        ],
+        out_specs=pl.BlockSpec((1, m), lambda i: (0, 0)),
+        out_shape=jax.ShapeDtypeStruct((1, m), jnp.float32),
+        cost_estimate=pl.CostEstimate(flops=2 * n * m, bytes_accessed=4 * n * m, transcendentals=0),
+    )(kernel, row_scale[:, None])
+    return out[0]
+
+
+def weighted_row_sums(kernel, col_scale):
+    n, m = kernel.shape
+    bn = BLOCK_ROWS if n % BLOCK_ROWS == 0 else n
+
+    def body(k_ref, c_ref, o_ref):
+        o_ref[...] = jnp.sum(k_ref[...] * c_ref[...], axis=1, keepdims=True)
+
+    out = pl.pallas_call(
+        body,
+        grid=(n // bn,),
+        in_specs=[
+            pl.BlockSpec((bn, m), lambda i: (i, 0)),
+            pl.BlockSpec((1, m), lambda i: (0, 0)),
+        ],
+        out_specs=pl.BlockSpec((bn, 1), lambda i: (i, 0)),
+        out_shape=jax.ShapeDtypeStruct((n, 1), jnp.float32),
+        cost_estimate=pl.CostEstimate(flops=2 * n * m, bytes_accessed=4 * n * m, transcendentals=0),
+    )(kernel, col_scale[None, :])
+    return out[:, 0]
+
+
 def make_local(sizes):
     pts_red = [("c", sizes["c"]), ("y", sizes["y"])]
     cen_red = [("z", sizes["z"]), ("x", sizes["x"])]
@@ -143,9 +193,12 @@
         scores = jnp.dot(unit_points, unit_centroids.T, preferred_element_type=jnp.float32)
         kernel = jnp.exp(scores / (width * temper))
         for sweep in range(ITERS):
-            col_part = jnp.sum(kernel * row_scale[:, None], axis=0)
+            if sweep == 0:
+                col_part = jnp.sum(kernel, axis=0)
+            else:
+                col_part = weighted_col_sums(kernel, row_scale)
             col_scale = balance / multi_sum(col_part, pts_red)
-            row_part = jnp.sum(kernel * col_scale[None, :], axis=1)
+            row_part = weighted_row_sums(kernel, col_scale)
             row_scale = 1.0 / group_sum(row_part, CEN_AXES, n_cen)
         scaled = kernel * row_scale[:, None]
         hi_wide = lax.reduce_precision(scaled, exponent_bits=8, mantissa_bits=7)

time: 245 us -> 271 us (1.11)
  Pallas kernels: 0 us -> 46.2 us
  other arithmetic: 55.5 us -> 28.4 us
  local copies, waits for them, and re-layouts: 10.8 us -> 17 us
    pallas_call x0 -> x5, Pallas kernels: none -> 46.2 us  [the longest x3 27.6 us: weighted_row_sums(): pl.pallas_call(body, grid=(n // bn,), in_specs=[pl.BlockSpec((bn, m), lam...]
    reduce_sum x5 -> x0, other arithmetic: 34.9 us -> none  [the longest x3 21.1 us: local(): row_part = jnp.sum(kernel * col_scale[None, :], axis=1)]
    unnamed x10 -> x14, local copies, waits for them, and re-layouts: 0.02 us -> 5.41 us
    pallas_call x0 -> x3, other arithmetic: none -> 4.68 us  [weighted_row_sums(): pl.pallas_call(body, grid=(n // bn,), in_specs=[pl.BlockSpec((bn, m), lam...]
where the time goes in v7:
time: 271 us; the launch traced here: 270 us
  waiting for transfers between devices  65.3 us (24%)
  starting transfers between devices  53.3 us (20%)
  Pallas kernels  46.2 us (17%)
  matrix products  35 us (13%)
  other arithmetic  28.4 us (10%)
  blocking collectives  24 us (9%)
  local copies, waits for them, and re-layouts  17 us (6%)
    all_to_all x1, waiting for transfers between devices, scatter_features(): got = lax.all_to_all(x, 'y', 0, 0, tiled=False)  31.2 us
    pallas_call x3, Pallas kernels, weighted_row_sums(): pl.pallas_call(body, grid=(n // bn,), in_specs=[pl.BlockSpec((bn, m), lam...  27.6 us
    all_to_all x2, blocking collectives, group_sum(): lax.all_to_all(jnp.broadcast_to(v[None], (n,) + v.shape), axes, 0, 0, til...  24 us
    ppermute x16, starting transfers between devices, axis_sum(): lax.ppermute(v, axis, [(i, (i + s) % n) for i in range(n)])  18.9 us
    pallas_call x2, Pallas kernels, weighted_col_sums(): pl.pallas_call(body, grid=(n // bn,), in_specs=[pl.BlockSpec((bn, m), lam...  18.6 us
    ppermute x16, waiting for transfers between devices, axis_sum(): lax.ppermute(v, axis, [(i, (i + s) % n) for i in range(n)])  14.2 us
    ppermute x4, starting transfers between devices, ring_gather(): lax.ppermute(bwd[..., half:, :], axis, [(i, (i - 1) % n) for i in range(n)])  13.1 us
    dot_general x1, matrix products, local(): lax.dot_general(gathered, lo, dims, preferred_element_type=jnp.float32)  12.1 us
  transfers between devices with their start and end apart: 35, of which 21 were waited for; matrix products, arithmetic and copies ran while one was open for 5% of the time, Pallas kernels for 0%

profile of v7, /device:TPU:0, one launch (start us, length us, event | category | flops | bytes accessed | tf_op | source)
XLA Modules:
  0.0 270.3 jit_solution(2811341723311122120)
XLA Ops:
  3.7 2.2 collective-permute-start.2
  5.9 2.8 %collective-permute-start.10 = (bf16[2048,24]{0,1:T(8,128)(2,1)S(1)}, bf16[2048,24]{0,1:T(8,128)(2,1)S(1)}, u32[]{:S(2)}, u32[]{:S(2)}) collective-permute-start(bf16[2048,24]{0,1:T(8,128)(2,1)S(1)} %get-tuple-element.6), channel_id=1, source_target_pairs={{0,12},{4,0},{8,4},{12,8},{1,13},{5,1},{9,5},{13,9},{2,14},{6,2},{... | collective-permute-start | bytes 294920 | tf_op jit(solution)/shard_map/ppermute | solution.py:95
  8.8 3.3 %collective-permute-start.3 = (bf16[1024,24]{0,1:T(8,128)(2,1)S(1)}, bf16[1024,24]{0,1:T(8,128)(2,1)S(1)}, u32[]{:S(2)}, u32[]{:S(2)}) collective-permute-start(bf16[1024,24]{0,1:T(8,128)(2,1)S(1)} %slice.313), channel_id=1, source_target_pairs={{0,3},{1,0},{2,1},{3,2},{4,7},{5,4},{6,5},{7,6},{8,11},{9,8},{10,9... | collective-permute-start | bytes 147464 | tf_op jit(solution)/shard_map/ppermute | solution.py:100
  12.1 3.3 %collective-permute-start.11 = (bf16[1024,24]{0,1:T(8,128)(2,1)S(1)}, bf16[1024,24]{0,1:T(8,128)(2,1)S(1)}, u32[]{:S(2)}, u32[]{:S(2)}) collective-permute-start(bf16[1024,24]{0,1:T(8,128)(2,1)S(1)} %slice.317), channel_id=1, source_target_pairs={{0,12},{4,0},{8,4},{12,8},{1,13},{5,1},{9,5},{13,9},{2,14},{6,2},{... | collective-permute-start | bytes 147464 | tf_op jit(solution)/shard_map/ppermute | solution.py:100
  16.3 3.2 %collective-permute-start.6 = (bf16[4,2048,24]{1,2,0:T(8,128)(2,1)S(1)}, bf16[4,2048,24]{1,2,0:T(8,128)(2,1)S(1)}, u32[]{:S(2)}, u32[]{:S(2)}) collective-permute-start(bf16[4,2048,24]{1,2,0:T(8,128)(2,1)S(1)} %gather_fusion), channel_id=1, source_target_pairs={{0,12},{4,0},{8,4},{12,8},{1,13},{5,1},{9,5},{13,9},{2,14},{6,2},{... | collective-permute-start | bytes 1179656 | tf_op jit(solution)/shard_map/ppermute | solution.py:95
  22.1 3.2 %collective-permute-start.14 = (bf16[4,2048,24]{1,2,0:T(8,128)(2,1)S(1)}, bf16[4,2048,24]{1,2,0:T(8,128)(2,1)S(1)}, u32[]{:S(2)}, u32[]{:S(2)}) collective-permute-start(bf16[4,2048,24]{1,2,0:T(8,128)(2,1)S(1)} %gather_fusion.2), channel_id=1, source_target_pairs={{0,3},{1,0},{2,1},{3,2},{4,7},{5,4},{6,5},{7,6},{8,11},{9,8},{10,9... | collective-permute-start | bytes 1179656 | tf_op jit(solution)/shard_map/ppermute | solution.py:95
  27.3 3.3 %collective-permute-start.7 = (bf16[4,1024,24]{1,2,0:T(8,128)(2,1)S(1)}, bf16[4,1024,24]{1,2,0:T(8,128)(2,1)S(1)}, u32[]{:S(2)}, u32[]{:S(2)}) collective-permute-start(bf16[4,1024,24]{1,2,0:T(8,128)(2,1)S(1)} %slice.315), channel_id=1, source_target_pairs={{0,12},{4,0},{8,4},{12,8},{1,13},{5,1},{9,5},{13,9},{2,14},{6,2},{... | collective-permute-start | bytes 589832 | tf_op jit(solution)/shard_map/ppermute | solution.py:100
  30.6 2.6 fusion.6
  34.7 3.2 %collective-permute-start.15 = (bf16[4,1024,24]{1,2,0:T(8,128)(2,1)}, bf16[4,1024,24]{1,2,0:T(8,128)(2,1)}, u32[]{:S(2)}, u32[]{:S(2)}) collective-permute-start(bf16[4,1024,24]{1,2,0:T(8,128)(2,1)} %slice.319), channel_id=1, source_target_pairs={{0,3},{1,0},{2,1},{3,2},{4,7},{5,4},{6,5},{7,6},{8,11},{9,8},{10,9... | collective-permute-start | bytes 589832 | tf_op jit(solution)/shard_map/ppermute | solution.py:100
  38.9 2.3 collective-permute-done.13
  48.2 2.7 %copy-done.1 = bf16[2048,768]{1,0:T(8,128)(2,1)S(1)} copy-done((bf16[2048,768]{1,0:T(8,128)(2,1)S(1)}, bf16[2048,768]{1,0:T(8,128)(2,1)}, u32[]{:S(2)}) %copy-start.1) | copy-done | bytes 3145752
  50.9 11.6 %fusion.26 = (f32[2048]{0:T(1024)S(1)}, f32[2048,2048]{1,0:T(8,128)}) fusion(bf16[2048,768]{1,0:T(8,128)(2,1)S(1)} %copy-done.1, f32[2048]{0:T(1024)S(1)} %get-tuple-element.12, bf16[2048,768]{0,1:T(8,128)(2,1)S(1)} %bitcast.65, f32[2048]{0:T(1024)S(1)} %get-tuple-element.13), kind=kOutput, calls=%fused_computation.119 | convolution fusion | flops 6460274688 | bytes 23093248 | tf_op jit(solution)/shard_map/dot_general | solution.py:193
  63.7 3.2 %collective-permute-start.17 = (f32[2048]{0:T(1024)S(1)}, f32[2048]{0:T(1024)S(1)}, u32[]{:S(2)}, u32[]{:S(2)}) collective-permute-start(f32[2048]{0:T(1024)S(1)} %add.580), channel_id=1, source_target_pairs={{0,64},{32,96},{64,0},{96,32},{1,65},{33,97},{65,1},{97,33},{2,66}... | collective-permute-start | bytes 24584 | tf_op jit(solution)/shard_map/ppermute | solution.py:28
  67.6 2.6 collective-permute-start.19
  72.4 9.1 %shard_map.41 = f32[2048,1]{1,0:T(8,128)} custom-call(f32[2048,2048]{1,0:T(8,128)} %get-tuple-element.11.k_ref, f32[1,2048]{1,0:T(1,128)} %bitcast.90), custom_call_target="tpu_custom_call" | custom-call | flops 8388608 | bytes 16777216 | tf_op jit(solution)/shard_map/pallas_call | solution.py:163
  83.2 12.7 %all_to_all.23 = f32[16,1,2048]{2,1,0:T(1,128)S(1)} all-to-all(f32[16,1,2048]{2,1,0:T(1,128)S(1)} %broadcast_in_dim.20), channel_id=1, replica_groups=mesh['y'=4,'c'=2,'x'=4,'z'=4] {'x','z'}, dimensions={0} | all-to-all | bytes 262144 | tf_op jit(solution)/shard_map/all_to_all | solution.py:45
  97.3 9.3 %shard_map.42 = f32[1,2048]{1,0:T(1,128)} custom-call(f32[2048,2048]{1,0:T(8,128)} %get-tuple-element.11.k_ref, f32[2048,1]{1,0:T(8,128)} %copy.7.r_ref), custom_call_target="tpu_custom_call" | custom-call | flops 8388608 | bytes 16777216 | tf_op jit(solution)/shard_map/pallas_call | solution.py:142
  110.1 2.6 collective-permute-start.22
  117.0 9.1 %shard_map.43 = f32[2048,1]{1,0:T(8,128)} custom-call(f32[2048,2048]{1,0:T(8,128)} %get-tuple-element.11.k_ref, f32[1,2048]{1,0:T(1,128)} %bitcast.91), custom_call_target="tpu_custom_call" | custom-call | flops 8388608 | bytes 16777216 | tf_op jit(solution)/shard_map/pallas_call | solution.py:163
  127.8 11.2 %all_to_all.24 = f32[16,1,2048]{2,1,0:T(1,128)S(1)} all-to-all(f32[16,1,2048]{2,1,0:T(1,128)S(1)} %broadcast_in_dim.46), channel_id=1, replica_groups=mesh['y'=4,'c'=2,'x'=4,'z'=4] {'x','z'}, dimensions={0} | all-to-all | bytes 262144 | tf_op jit(solution)/shard_map/all_to_all | solution.py:45
  140.4 9.3 %shard_map.44 = f32[1,2048]{1,0:T(1,128)} custom-call(f32[2048,2048]{1,0:T(8,128)} %get-tuple-element.11.k_ref, f32[2048,1]{1,0:T(8,128)} %copy.8.r_ref), custom_call_target="tpu_custom_call" | custom-call | flops 8388608 | bytes 16777216 | tf_op jit(solution)/shard_map/pallas_call | solution.py:142
  158.7 9.4 %shard_map.45 = f32[2048,1]{1,0:T(8,128)} custom-call(f32[2048,2048]{1,0:T(8,128)} %get-tuple-element.11.k_ref, f32[1,2048]{1,0:T(1,128)} %bitcast.82), custom_call_target="tpu_custom_call" | custom-call | flops 8388608 | bytes 16777216 | tf_op jit(solution)/shard_map/pallas_call | solution.py:163
  170.4 3.6 %all-to-all-start.2 = ((f32[16,1,2048]{2,1,0:T(1,128)}), f32[16,1,2048]{2,1,0:T(1,128)S(1)}, u32[]{:S(2)}, u32[]{:S(2)}) async-start(f32[16,1,2048]{2,1,0:T(1,128)} %broadcast_in_dim.49), calls=%async_computation.2 | async-start | bytes 262144 | tf_op jit(solution)/shard_map/all_to_all | solution.py:45
  174.0 7.8 %all-to-all-done.2 = f32[16,1,2048]{2,1,0:T(1,128)S(1)} async-done(((f32[16,1,2048]{2,1,0:T(1,128)}), f32[16,1,2048]{2,1,0:T(1,128)S(1)}, u32[]{:S(2)}, u32[]{:S(2)}) %all-to-all-start.2) | async-done | bytes 131104 | tf_op jit(solution)/shard_map/all_to_all | solution.py:45
  181.9 12.1 %fusion.1 = f32[768,2048]{1,0:T(8,128)} fusion(bf16[2048,768]{0,1:T(8,128)(2,1)S(1)} %bitcast.66, f32[2048,2048]{1,0:T(8,128)} %get-tuple-element.11.k_ref, f32[2048]{0:T(1024)S(1)} %bitcast.83), kind=kOutput, calls=%fused_computation.9 | convolution fusion | flops 6459228160 | bytes 26222592 | tf_op jit(solution)/shard_map/dot_general | solution.py:210
  194.0 11.4 %add_multiply_fusion = f32[768,2048]{1,0:T(8,128)S(1)} fusion(f32[768,2048]{1,0:T(8,128)} %fusion.1, f32[2048]{0:T(1024)S(1)} %copy-done.6, bf16[2048,768]{0,1:T(8,128)(2,1)S(1)} %bitcast.67, f32[2048,2048]{1,0:T(8,128)} %get-tuple-element.11.k_ref, f32[2048]{0:T(1024)S(1)} %bitcast.84), kind=kOutput, calls=%fused_computation.17 | convolution fusion | flops 6458179584 | bytes 32522240 | tf_op jit(solution)/shard_map/dot_general | solution.py:208
  205.3 2.6 copy-done
  208.4 5.8 %collective-permute-done.28 = f32[4,96,2048]{2,1,0:T(8,128)} collective-permute-done((f32[4,96,2048]{2,1,0:T(8,128)S(1)}, f32[4,96,2048]{2,1,0:T(8,128)}, u32[]{:S(2)}, u32[]{:S(2)}) %collective-permute-start.28) | collective-permute-done | bytes 3145760 | tf_op jit(solution)/shard_map/ppermute | solution.py:77
  214.2 5.3 %bitcast_add_fusion = f32[4,96,2048]{2,1,0:T(8,128)} fusion(f32[4,96,2048]{2,1,0:T(8,128)} %collective-permute-done.28, f32[4,2,96,2048]{3,2,1,0:T(8,128)} %bitcast.64, s32[]{:T(128)S(6)} %select_n.62), kind=kLoop, calls=%fused_computation.21 | loop fusion | flops 786432 | bytes 9437188 | tf_op jit(solution)/shard_map/add | solution.py:77
  219.5 3.7 %all-to-all-start.3 = ((f32[4,96,2048]{2,1,0:T(8,128)}), f32[4,96,2048]{2,1,0:T(8,128)S(1)}, u32[]{:S(2)}, u32[]{:S(2)}) async-start(f32[4,96,2048]{2,1,0:T(8,128)} %bitcast_add_fusion), calls=%async_computation.3 | async-start | bytes 6291456 | tf_op jit(solution)/shard_map/all_to_all | solution.py:82
  223.2 6.9 %multiply_reduce_fusion = f32[2048]{0:T(1024)S(1)} fusion(f32[2048,2048]{1,0:T(8,128)} %get-tuple-element.11.k_ref, f32[2048]{0:T(1024)S(1)} %bitcast.85), kind=kLoop, calls=%fused_computation.8 | loop fusion | flops 8386560 | bytes 16793600 | tf_op jit(solution)/shard_map/reduce_sum | solution.py:212
  230.1 31.2 %all-to-all-done.3 = f32[4,96,2048]{2,1,0:T(8,128)S(1)} async-done(((f32[4,96,2048]{2,1,0:T(8,128)}), f32[4,96,2048]{2,1,0:T(8,128)S(1)}, u32[]{:S(2)}, u32[]{:S(2)}) %all-to-all-start.3) | async-done | bytes 3145760 | tf_op jit(solution)/shard_map/all_to_all | solution.py:82
  (119 shorter events, 56.7 us)
Async XLA Ops:
  1.6 7.1 %collective-permute-start = (bf16[2048,24]{0,1:T(8,128)(2,1)S(1)}, bf16[2048,24]{0,1:T(8,128)(2,1)S(1)}, u32[]{:S(2)}, u32[]{:S(2)}) collective-permute-start(bf16[2048,24]{0,1:T(8,128)(2,1)S(1)} %get-tuple-element.7), channel_id=1, source_target_pairs={{0,1},{1,2},{2,3},{3,0},{4,5},{5,6},{6,7},{7,4},{8,9},{9,10},{10,1... | collective-permute-start | bytes 294920 | tf_op jit(solution)/shard_map/ppermute | solution.py:94
  3.7 5.1 %collective-permute-start.2 = (bf16[2048,24]{0,1:T(8,128)(2,1)S(1)}, bf16[2048,24]{0,1:T(8,128)(2,1)S(1)}, u32[]{:S(2)}, u32[]{:S(2)}) collective-permute-start(bf16[2048,24]{0,1:T(8,128)(2,1)S(1)} %get-tuple-element.7), channel_id=1, source_target_pairs={{0,3},{1,0},{2,1},{3,2},{4,7},{5,4},{6,5},{7,6},{8,11},{9,8},{10,9... | collective-permute-start | bytes 294920 | tf_op jit(solution)/shard_map/ppermute | solution.py:95
  5.9 6.2 %collective-permute-start.10 = (bf16[2048,24]{0,1:T(8,128)(2,1)S(1)}, bf16[2048,24]{0,1:T(8,128)(2,1)S(1)}, u32[]{:S(2)}, u32[]{:S(2)}) collective-permute-start(bf16[2048,24]{0,1:T(8,128)(2,1)S(1)} %get-tuple-element.6), channel_id=1, source_target_pairs={{0,12},{4,0},{8,4},{12,8},{1,13},{5,1},{9,5},{13,9},{2,14},{6,2},{... | collective-permute-start | bytes 294920 | tf_op jit(solution)/shard_map/ppermute | solution.py:95
  8.7 6.8 %collective-permute-start.8 = (bf16[2048,24]{0,1:T(8,128)(2,1)S(1)}, bf16[2048,24]{0,1:T(8,128)(2,1)S(1)}, u32[]{:S(2)}, u32[]{:S(2)}) collective-permute-start(bf16[2048,24]{0,1:T(8,128)(2,1)S(1)} %get-tuple-element.6), channel_id=1, source_target_pairs={{0,4},{4,8},{8,12},{12,0},{1,5},{5,9},{9,13},{13,1},{2,6},{6,10},{... | collective-permute-start | bytes 294920 | tf_op jit(solution)/shard_map/ppermute | solution.py:94
  8.7 6.8 %collective-permute-start.1 = (bf16[1024,24]{0,1:T(8,128)(2,1)S(1)}, bf16[1024,24]{0,1:T(8,128)(2,1)S(1)}, u32[]{:S(2)}, u32[]{:S(2)}) collective-permute-start(bf16[1024,24]{0,1:T(8,128)(2,1)S(1)} %slice.312), channel_id=1, source_target_pairs={{0,1},{1,2},{2,3},{3,0},{4,5},{5,6},{6,7},{7,4},{8,9},{9,10},{10,1... | collective-permute-start | bytes 147464 | tf_op jit(solution)/shard_map/ppermute | solution.py:99
  8.8 6.7 %collective-permute-start.3 = (bf16[1024,24]{0,1:T(8,128)(2,1)S(1)}, bf16[1024,24]{0,1:T(8,128)(2,1)S(1)}, u32[]{:S(2)}, u32[]{:S(2)}) collective-permute-start(bf16[1024,24]{0,1:T(8,128)(2,1)S(1)} %slice.313), channel_id=1, source_target_pairs={{0,3},{1,0},{2,1},{3,2},{4,7},{5,4},{6,5},{7,6},{8,11},{9,8},{10,9... | collective-permute-start | bytes 147464 | tf_op jit(solution)/shard_map/ppermute | solution.py:100
  12.1 7.4 %collective-permute-start.11 = (bf16[1024,24]{0,1:T(8,128)(2,1)S(1)}, bf16[1024,24]{0,1:T(8,128)(2,1)S(1)}, u32[]{:S(2)}, u32[]{:S(2)}) collective-permute-start(bf16[1024,24]{0,1:T(8,128)(2,1)S(1)} %slice.317), channel_id=1, source_target_pairs={{0,12},{4,0},{8,4},{12,8},{1,13},{5,1},{9,5},{13,9},{2,14},{6,2},{... | collective-permute-start | bytes 147464 | tf_op jit(solution)/shard_map/ppermute | solution.py:100
  15.5 5.9 %collective-permute-start.9 = (bf16[1024,24]{0,1:T(8,128)(2,1)S(1)}, bf16[1024,24]{0,1:T(8,128)(2,1)S(1)}, u32[]{:S(2)}, u32[]{:S(2)}) collective-permute-start(bf16[1024,24]{0,1:T(8,128)(2,1)S(1)} %slice.316), channel_id=1, source_target_pairs={{0,4},{4,8},{8,12},{12,0},{1,5},{5,9},{9,13},{13,1},{2,6},{6,10},{... | collective-permute-start | bytes 147464 | tf_op jit(solution)/shard_map/ppermute | solution.py:99
  16.2 11.0 %collective-permute-start.4 = (bf16[4,2048,24]{1,2,0:T(8,128)(2,1)S(1)}, bf16[4,2048,24]{1,2,0:T(8,128)(2,1)S(1)}, u32[]{:S(2)}, u32[]{:S(2)}) collective-permute-start(bf16[4,2048,24]{1,2,0:T(8,128)(2,1)S(1)} %gather_fusion), channel_id=1, source_target_pairs={{0,4},{4,8},{8,12},{12,0},{1,5},{5,9},{9,13},{13,1},{2,6},{6,10},{... | collective-permute-start | bytes 1179656 | tf_op jit(solution)/shard_map/ppermute | solution.py:94
  16.3 10.9 %collective-permute-start.6 = (bf16[4,2048,24]{1,2,0:T(8,128)(2,1)S(1)}, bf16[4,2048,24]{1,2,0:T(8,128)(2,1)S(1)}, u32[]{:S(2)}, u32[]{:S(2)}) collective-permute-start(bf16[4,2048,24]{1,2,0:T(8,128)(2,1)S(1)} %gather_fusion), channel_id=1, source_target_pairs={{0,12},{4,0},{8,4},{12,8},{1,13},{5,1},{9,5},{13,9},{2,14},{6,2},{... | collective-permute-start | bytes 1179656 | tf_op jit(solution)/shard_map/ppermute | solution.py:95
  22.0 11.2 %collective-permute-start.12 = (bf16[4,2048,24]{1,2,0:T(8,128)(2,1)S(1)}, bf16[4,2048,24]{1,2,0:T(8,128)(2,1)S(1)}, u32[]{:S(2)}, u32[]{:S(2)}) collective-permute-start(bf16[4,2048,24]{1,2,0:T(8,128)(2,1)S(1)} %gather_fusion.2), channel_id=1, source_target_pairs={{0,1},{1,2},{2,3},{3,0},{4,5},{5,6},{6,7},{7,4},{8,9},{9,10},{10,1... | collective-permute-start | bytes 1179656 | tf_op jit(solution)/shard_map/ppermute | solution.py:94
  22.1 11.9 %collective-permute-start.14 = (bf16[4,2048,24]{1,2,0:T(8,128)(2,1)S(1)}, bf16[4,2048,24]{1,2,0:T(8,128)(2,1)S(1)}, u32[]{:S(2)}, u32[]{:S(2)}) collective-permute-start(bf16[4,2048,24]{1,2,0:T(8,128)(2,1)S(1)} %gather_fusion.2), channel_id=1, source_target_pairs={{0,3},{1,0},{2,1},{3,2},{4,7},{5,4},{6,5},{7,6},{8,11},{9,8},{10,9... | collective-permute-start | bytes 1179656 | tf_op jit(solution)/shard_map/ppermute | solution.py:95
  27.2 10.7 %collective-permute-start.5 = (bf16[4,1024,24]{1,2,0:T(8,128)(2,1)S(1)}, bf16[4,1024,24]{1,2,0:T(8,128)(2,1)S(1)}, u32[]{:S(2)}, u32[]{:S(2)}) collective-permute-start(bf16[4,1024,24]{1,2,0:T(8,128)(2,1)S(1)} %slice.314), channel_id=1, source_target_pairs={{0,4},{4,8},{8,12},{12,0},{1,5},{5,9},{9,13},{13,1},{2,6},{6,10},{... | collective-permute-start | bytes 589832 | tf_op jit(solution)/shard_map/ppermute | solution.py:99
  27.3 10.6 %collective-permute-start.7 = (bf16[4,1024,24]{1,2,0:T(8,128)(2,1)S(1)}, bf16[4,1024,24]{1,2,0:T(8,128)(2,1)S(1)}, u32[]{:S(2)}, u32[]{:S(2)}) collective-permute-start(bf16[4,1024,24]{1,2,0:T(8,128)(2,1)S(1)} %slice.315), channel_id=1, source_target_pairs={{0,12},{4,0},{8,4},{12,8},{1,13},{5,1},{9,5},{13,9},{2,14},{6,2},{... | collective-permute-start | bytes 589832 | tf_op jit(solution)/shard_map/ppermute | solution.py:100
  34.0 7.2 %collective-permute-start.13 = (bf16[4,1024,24]{1,2,0:T(8,128)(2,1)}, bf16[4,1024,24]{1,2,0:T(8,128)(2,1)}, u32[]{:S(2)}, u32[]{:S(2)}) collective-permute-start(bf16[4,1024,24]{1,2,0:T(8,128)(2,1)} %slice.318), channel_id=1, source_target_pairs={{0,1},{1,2},{2,3},{3,0},{4,5},{5,6},{6,7},{7,4},{8,9},{9,10},{10,1... | collective-permute-start | bytes 589832 | tf_op jit(solution)/shard_map/ppermute | solution.py:99
  34.7 6.7 %collective-permute-start.15 = (bf16[4,1024,24]{1,2,0:T(8,128)(2,1)}, bf16[4,1024,24]{1,2,0:T(8,128)(2,1)}, u32[]{:S(2)}, u32[]{:S(2)}) collective-permute-start(bf16[4,1024,24]{1,2,0:T(8,128)(2,1)} %slice.319), channel_id=1, source_target_pairs={{0,3},{1,0},{2,1},{3,2},{4,7},{5,4},{6,5},{7,6},{8,11},{9,8},{10,9... | collective-permute-start | bytes 589832 | tf_op jit(solution)/shard_map/ppermute | solution.py:100
  63.7 6.4 %collective-permute-start.17 = (f32[2048]{0:T(1024)S(1)}, f32[2048]{0:T(1024)S(1)}, u32[]{:S(2)}, u32[]{:S(2)}) collective-permute-start(f32[2048]{0:T(1024)S(1)} %add.580), channel_id=1, source_target_pairs={{0,64},{32,96},{64,0},{96,32},{1,65},{33,97},{65,1},{97,33},{2,66}... | collective-permute-start | bytes 24584 | tf_op jit(solution)/shard_map/ppermute | solution.py:28
  66.9 4.9 %collective-permute-start.18 = (f32[2048]{0:T(1024)S(1)}, f32[2048]{0:T(1024)S(1)}, u32[]{:S(2)}, u32[]{:S(2)}) collective-permute-start(f32[2048]{0:T(1024)S(1)} %add.580), channel_id=1, source_target_pairs={{0,32},{32,64},{64,96},{96,0},{1,33},{33,65},{65,97},{97,1},{2,34}... | collective-permute-start | bytes 24584 | tf_op jit(solution)/shard_map/ppermute | solution.py:28
  67.6 4.2 %collective-permute-start.19 = (f32[2048]{0:T(1024)S(1)}, f32[2048]{0:T(1024)S(1)}, u32[]{:S(2)}, u32[]{:S(2)}) collective-permute-start(f32[2048]{0:T(1024)S(1)} %add.580), channel_id=1, source_target_pairs={{0,96},{32,0},{64,32},{96,64},{1,97},{33,1},{65,33},{97,65},{2,98}... | collective-permute-start | bytes 24584 | tf_op jit(solution)/shard_map/ppermute | solution.py:28
  106.6 1.4 collective-permute-start.20
  108.6 5.2 %collective-permute-start.21 = (f32[2048]{0:T(1024)S(1)}, f32[2048]{0:T(1024)S(1)}, u32[]{:S(2)}, u32[]{:S(2)}) collective-permute-start(f32[2048]{0:T(1024)S(1)} %add.600), channel_id=1, source_target_pairs={{0,64},{32,96},{64,0},{96,32},{1,65},{33,97},{65,1},{97,33},{2,66}... | collective-permute-start | bytes 24584 | tf_op jit(solution)/shard_map/ppermute | solution.py:28
  110.1 4.9 %collective-permute-start.22 = (f32[2048]{0:T(1024)S(1)}, f32[2048]{0:T(1024)S(1)}, u32[]{:S(2)}, u32[]{:S(2)}) collective-permute-start(f32[2048]{0:T(1024)S(1)} %add.600), channel_id=1, source_target_pairs={{0,32},{32,64},{64,96},{96,0},{1,33},{33,65},{65,97},{97,1},{2,34}... | collective-permute-start | bytes 24584 | tf_op jit(solution)/shard_map/ppermute | solution.py:28
  112.7 3.7 %collective-permute-start.23 = (f32[2048]{0:T(1024)S(1)}, f32[2048]{0:T(1024)S(1)}, u32[]{:S(2)}, u32[]{:S(2)}) collective-permute-start(f32[2048]{0:T(1024)S(1)} %add.600), channel_id=1, source_target_pairs={{0,96},{32,0},{64,32},{96,64},{1,97},{33,1},{65,33},{97,65},{2,98}... | collective-permute-start | bytes 24584 | tf_op jit(solution)/shard_map/ppermute | solution.py:28
  151.8 5.2 %collective-permute-start.25 = (f32[2048]{0:T(1024)S(1)}, f32[2048]{0:T(1024)S(1)}, u32[]{:S(2)}, u32[]{:S(2)}) collective-permute-start(f32[2048]{0:T(1024)S(1)} %add.620), channel_id=1, source_target_pairs={{0,64},{32,96},{64,0},{96,32},{1,65},{33,97},{65,1},{97,33},{2,66}... | collective-permute-start | bytes 24584 | tf_op jit(solution)/shard_map/ppermute | solution.py:28
  152.4 4.9 %collective-permute-start.26 = (f32[2048]{0:T(1024)S(1)}, f32[2048]{0:T(1024)S(1)}, u32[]{:S(2)}, u32[]{:S(2)}) collective-permute-start(f32[2048]{0:T(1024)S(1)} %add.620), channel_id=1, source_target_pairs={{0,32},{32,64},{64,96},{96,0},{1,33},{33,65},{65,97},{97,1},{2,34}... | collective-permute-start | bytes 24584 | tf_op jit(solution)/shard_map/ppermute | solution.py:28
  154.4 3.7 %collective-permute-start.27 = (f32[2048]{0:T(1024)S(1)}, f32[2048]{0:T(1024)S(1)}, u32[]{:S(2)}, u32[]{:S(2)}) collective-permute-start(f32[2048]{0:T(1024)S(1)} %add.620), channel_id=1, source_target_pairs={{0,96},{32,0},{64,32},{96,64},{1,97},{33,1},{65,33},{97,65},{2,98}... | collective-permute-start | bytes 24584 | tf_op jit(solution)/shard_map/ppermute | solution.py:28
  170.4 11.4 %all-to-all-start.2 = ((f32[16,1,2048]{2,1,0:T(1,128)}), f32[16,1,2048]{2,1,0:T(1,128)S(1)}, u32[]{:S(2)}, u32[]{:S(2)}) async-start(f32[16,1,2048]{2,1,0:T(1,128)} %broadcast_in_dim.49), calls=%async_computation.2 | async-start | bytes 262144 | tf_op jit(solution)/shard_map/all_to_all | solution.py:45
  208.3 5.9 %collective-permute-start.28 = (f32[4,96,2048]{2,1,0:T(8,128)S(1)}, f32[4,96,2048]{2,1,0:T(8,128)}, u32[]{:S(2)}, u32[]{:S(2)}) collective-permute-start(f32[4,96,2048]{2,1,0:T(8,128)S(1)} %dynamic-slice_bitcast_fusion), channel_id=1, source_target_pairs={{0,16},{16,0},{1,17},{17,1},{2,18},{18,2},{3,19},{19,3},{4,20},{20... | collective-permute-start | bytes 9437192 | tf_op jit(solution)/shard_map/ppermute | solution.py:77
  219.5 41.8 %all-to-all-start.3 = ((f32[4,96,2048]{2,1,0:T(8,128)}), f32[4,96,2048]{2,1,0:T(8,128)S(1)}, u32[]{:S(2)}, u32[]{:S(2)}) async-start(f32[4,96,2048]{2,1,0:T(8,128)} %bitcast_add_fusion), calls=%async_computation.3 | async-start | bytes 6291456 | tf_op jit(solution)/shard_map/all_to_all | solution.py:82
  262.8 5.4 %collective-permute-start.30 = (f32[2,2048]{1,0:T(2,128)S(1)}, f32[2,2048]{1,0:T(2,128)S(1)}, u32[]{:S(2)}, u32[]{:S(2)}) collective-permute-start(f32[2,2048]{1,0:T(2,128)S(1)} %fusion.23), channel_id=1, source_target_pairs={{0,64},{32,96},{64,0},{96,32},{1,65},{33,97},{65,1},{97,33},{2,66}... | collective-permute-start | bytes 49160 | tf_op jit(solution)/shard_map/ppermute | solution.py:28
  263.5 4.9 %collective-permute-start.31 = (f32[2,2048]{1,0:T(2,128)S(1)}, f32[2,2048]{1,0:T(2,128)S(1)}, u32[]{:S(2)}, u32[]{:S(2)}) collective-permute-start(f32[2,2048]{1,0:T(2,128)S(1)} %fusion.23), channel_id=1, source_target_pairs={{0,32},{32,64},{64,96},{96,0},{1,33},{33,65},{65,97},{97,1},{2,34}... | collective-permute-start | bytes 49160 | tf_op jit(solution)/shard_map/ppermute | solution.py:28
  264.9 3.7 %collective-permute-start.32 = (f32[2,2048]{1,0:T(2,128)S(1)}, f32[2,2048]{1,0:T(2,128)S(1)}, u32[]{:S(2)}, u32[]{:S(2)}) collective-permute-start(f32[2,2048]{1,0:T(2,128)S(1)} %fusion.23), channel_id=1, source_target_pairs={{0,96},{32,0},{64,32},{96,64},{1,97},{33,1},{65,33},{97,65},{2,98}... | collective-permute-start | bytes 49160 | tf_op jit(solution)/shard_map/ppermute | solution.py:28
  (10 other events, 67.9 us)

commit v8 on v5

--- a/solution.py
+++ b/solution.py
@@ -116,8 +116,8 @@
         )
         return jnp.transpose(got, (1, 0, 2)).reshape(rows, nx * nz * blk)
     part_a, part_b = points[:, : blk // 2], points[:, blk // 2 :]
-    a_z = ring_gather(part_a, "z", nz)
-    b_x = ring_gather(part_b, "x", nx)
+    a_z = lax.all_to_all(jnp.broadcast_to(part_a[None], (nz,) + part_a.shape), "z", 0, 0, tiled=False)
+    b_x = lax.all_to_all(jnp.broadcast_to(part_b[None], (nx,) + part_b.shape), "x", 0, 0, tiled=False)
     a_xz = ring_gather(a_z, "x", nx)
     b_zx = ring_gather(b_x, "z", nz)
     full = jnp.concatenate([a_xz, jnp.transpose(b_zx, (1, 0, 2, 3))], axis=-1)

time: 245 us -> 253 us (1.033)
  waiting for transfers between devices: 64.8 us -> 73.4 us
  starting transfers between devices: 53.8 us -> 49.6 us
    all_to_all x0 -> x2, waiting for transfers between devices: none -> 11.7 us  [the longest x1 8.07 us: gather_features(): lax.all_to_all(jnp.broadcast_to(part_b[None], (nx,) + part_b.shape), 'x',...]
    all_to_all x0 -> x2, starting transfers between devices: none -> 9.71 us  [the longest x1 5.31 us: gather_features(): lax.all_to_all(jnp.broadcast_to(part_a[None], (nz,) + part_a.shape), 'z',...]
    ppermute x4 -> x2, starting transfers between devices: 11.4 us -> 3.91 us  [ring_gather(): bwd = lax.ppermute(v, axis, [(i, (i - 1) % n) for i in range(n)])]
    ppermute x4 -> x2, starting transfers between devices: 13.1 us -> 6.18 us  [ring_gather(): lax.ppermute(bwd[..., half:, :], axis, [(i, (i - 1) % n) for i in range(n)])]
    ppermute x4 -> x2, waiting for transfers between devices: 4.07 us -> 0.02 us  [ring_gather(): lax.ppermute(fwd[..., :half, :], axis, [(i, (i + 1) % n) for i in range(n)])]
    unnamed x10 -> x16, local copies, waits for them, and re-layouts: 0.02 us -> 2.87 us
    gather x5 -> x3, local copies, waits for them, and re-layouts: 5.33 us -> 2.58 us  [ring_gather(): return by_offset[(idx - jnp.arange(n)) % n]]
  transfers between devices with their start and end apart: 35 -> 29, of which waited for: 21 -> 20; matrix products, arithmetic and copies ran while one was open for 5% -> 6% of each run, Pallas kernels for 0% -> 0%
where the time goes in v8:
time: 253 us
  waiting for transfers between devices  73.4 us (29%)
  other arithmetic  58 us (23%)
  starting transfers between devices  49.6 us (20%)
  matrix products  35.3 us (14%)
  blocking collectives  24.6 us (10%)
  local copies, waits for them, and re-layouts  10.7 us (4%)
    all_to_all x1, waiting for transfers between devices, scatter_features(): got = lax.all_to_all(x, 'y', 0, 0, tiled=False)  31.2 us
    all_to_all x2, blocking collectives, group_sum(): lax.all_to_all(jnp.broadcast_to(v[None], (n,) + v.shape), axes, 0, 0, til...  24.6 us
    reduce_sum x3, other arithmetic, local(): row_part = jnp.sum(kernel * col_scale[None, :], axis=1)  21.1 us
    ppermute x16, starting transfers between devices, axis_sum(): lax.ppermute(v, axis, [(i, (i + s) % n) for i in range(n)])  19.3 us
    ppermute x16, waiting for transfers between devices, axis_sum(): lax.ppermute(v, axis, [(i, (i + s) % n) for i in range(n)])  14.5 us
    reduce_sum x2, other arithmetic, local(): col_part = jnp.sum(kernel * row_scale[:, None], axis=0)  13.9 us
    dot_general x1, matrix products, local(): lax.dot_general(gathered, lo, dims, preferred_element_type=jnp.float32)  12.2 us
    dot_general x1, matrix products, local(): jnp.dot(unit_points, unit_centroids.T, preferred_element_type=jnp.float32)  11.8 us
  transfers between devices with their start and end apart: 29, of which 20 were waited for; matrix products, arithmetic and copies ran while one was open for 6% of the time, Pallas kernels for 0%

profile of v8, /device:TPU:0, one launch (start us, length us, event | category | flops | bytes accessed | tf_op | source)
XLA Modules:
  0.0 252.5 jit_solution(11422147990434247798)
XLA Ops:
  2.4 4.4 %all-to-all-start.1 = ((bf16[4,2048,24]{1,2,0:T(8,128)(2,1)}), bf16[4,2048,24]{1,2,0:T(8,128)(2,1)S(1)}, u32[]{:S(2)}, u32[]{:S(2)}) async-start(bf16[4,2048,24]{1,2,0:T(8,128)(2,1)} %broadcast_in_dim.11), calls=%async_computation.1 | async-start | bytes 786432 | tf_op jit(solution)/shard_map/all_to_all | solution.py:120
  6.8 8.1 %all-to-all-done.1 = bf16[4,2048,24]{1,2,0:T(8,128)(2,1)S(1)} async-done(((bf16[4,2048,24]{1,2,0:T(8,128)(2,1)}), bf16[4,2048,24]{1,2,0:T(8,128)(2,1)S(1)}, u32[]{:S(2)}, u32[]{:S(2)}) %all-to-all-start.1) | async-done | bytes 393248 | tf_op jit(solution)/shard_map/all_to_all | solution.py:120
  15.6 5.3 %all-to-all-start = ((bf16[4,2048,24]{1,2,0:T(8,128)(2,1)}), bf16[4,2048,24]{1,2,0:T(8,128)(2,1)S(1)}, u32[]{:S(2)}, u32[]{:S(2)}) async-start(bf16[4,2048,24]{1,2,0:T(8,128)(2,1)} %broadcast_in_dim.10), calls=%async_computation | async-start | bytes 786432 | tf_op jit(solution)/shard_map/all_to_all | solution.py:119
  20.9 2.0 collective-permute-start.4
  24.2 2.6 %fusion.6 = f32[2048]{0:T(1024)S(1)} fusion(bf16[2048,768]{1,0:T(8,128)(2,1)} %param.3), kind=kLoop, calls=%fused_computation.18 | loop fusion | flops 4716544 | bytes 3153920 | tf_op jit(solution)/shard_map/reduce_sum | solution.py:18
  26.8 3.7 %all-to-all-done = bf16[4,2048,24]{1,2,0:T(8,128)(2,1)S(1)} async-done(((bf16[4,2048,24]{1,2,0:T(8,128)(2,1)}), bf16[4,2048,24]{1,2,0:T(8,128)(2,1)S(1)}, u32[]{:S(2)}, u32[]{:S(2)}) %all-to-all-start) | async-done | bytes 393248 | tf_op jit(solution)/shard_map/all_to_all | solution.py:119
  31.0 2.7 %collective-permute-start.2 = (bf16[4,2048,24]{1,2,0:T(8,128)(2,1)S(1)}, bf16[4,2048,24]{1,2,0:T(8,128)(2,1)S(1)}, u32[]{:S(2)}, u32[]{:S(2)}) collective-permute-start(bf16[4,2048,24]{1,2,0:T(8,128)(2,1)S(1)} %all-to-all-done), channel_id=1, source_target_pairs={{0,12},{4,0},{8,4},{12,8},{1,13},{5,1},{9,5},{13,9},{2,14},{6,2},{... | collective-permute-start | bytes 1179656 | tf_op jit(solution)/shard_map/ppermute | solution.py:94
  33.7 2.0 collective-permute-done.4
  35.9 3.3 %collective-permute-start.7 = (bf16[4,1024,24]{1,2,0:T(8,128)(2,1)S(1)}, bf16[4,1024,24]{1,2,0:T(8,128)(2,1)S(1)}, u32[]{:S(2)}, u32[]{:S(2)}) collective-permute-start(bf16[4,1024,24]{1,2,0:T(8,128)(2,1)S(1)} %slice.295), channel_id=1, source_target_pairs={{0,3},{1,0},{2,1},{3,2},{4,7},{5,4},{6,5},{7,6},{8,11},{9,8},{10,9... | collective-permute-start | bytes 589832 | tf_op jit(solution)/shard_map/ppermute | solution.py:99
  41.2 2.9 %collective-permute-start.3 = (bf16[4,1024,24]{1,2,0:T(8,128)(2,1)}, bf16[4,1024,24]{1,2,0:T(8,128)(2,1)}, u32[]{:S(2)}, u32[]{:S(2)}) collective-permute-start(bf16[4,1024,24]{1,2,0:T(8,128)(2,1)} %slice.293), channel_id=1, source_target_pairs={{0,12},{4,0},{8,4},{12,8},{1,13},{5,1},{9,5},{13,9},{2,14},{6,2},{... | collective-permute-start | bytes 589832 | tf_op jit(solution)/shard_map/ppermute | solution.py:99
  53.5 11.8 %fusion.25 = (f32[2048]{0:T(1024)S(1)}, f32[2048,2048]{1,0:T(8,128)}) fusion(bf16[2048,768]{1,0:T(8,128)(2,1)S(1)} %copy-done.2, f32[2048]{0:T(1024)S(1)} %get-tuple-element.10, bf16[2048,768]{0,1:T(8,128)(2,1)S(1)} %bitcast.44, f32[2048]{0:T(1024)S(1)} %get-tuple-element.11), kind=kOutput, calls=%fused_computation.115 | convolution fusion | flops 6460274688 | bytes 23093248 | tf_op jit(solution)/shard_map/dot_general | solution.py:143
  69.7 2.0 collective-permute-start.9
  71.7 3.2 %collective-permute-done.9 = f32[2048]{0:T(1024)S(1)} collective-permute-done((f32[2048]{0:T(1024)S(1)}, f32[2048]{0:T(1024)S(1)}, u32[]{:S(2)}, u32[]{:S(2)}) %collective-permute-start.9) | collective-permute-done | bytes 8224 | tf_op jit(solution)/shard_map/ppermute | solution.py:27
  74.8 7.0 %multiply_reduce_fusion.4 = f32[2048]{0:T(1024)S(1)} fusion(f32[2048,2048]{1,0:T(8,128)} %get-tuple-element.9, f32[2048]{0:T(1024)S(1)} %add_divide_fusion.2), kind=kLoop, calls=%fused_computation.9 | loop fusion | flops 8386560 | bytes 16793600 | tf_op jit(solution)/shard_map/reduce_sum | solution.py:148
  81.9 13.3 %all_to_all.33 = f32[16,1,2048]{2,1,0:T(1,128)S(1)} all-to-all(f32[16,1,2048]{2,1,0:T(1,128)S(1)} %broadcast_in_dim.12), channel_id=1, replica_groups=mesh['y'=4,'c'=2,'x'=4,'z'=4] {'x','z'}, dimensions={0} | all-to-all | bytes 262144 | tf_op jit(solution)/shard_map/all_to_all | solution.py:44
  95.3 6.9 %multiply_reduce_fusion.3 = f32[2048]{0:T(1024)S(1)} fusion(f32[2048,2048]{1,0:T(8,128)} %get-tuple-element.9, f32[2048]{0:T(1024)S(1)} %bitcast.62), kind=kLoop, calls=%fused_computation.8 | loop fusion | flops 8386560 | bytes 16793600 | tf_op jit(solution)/shard_map/reduce_sum | solution.py:146
  106.2 2.6 %collective-permute-start.15 = (f32[2048]{0:T(1024)S(1)}, f32[2048]{0:T(1024)S(1)}, u32[]{:S(2)}, u32[]{:S(2)}) collective-permute-start(f32[2048]{0:T(1024)S(1)} %add.504), channel_id=1, source_target_pairs={{0,96},{32,0},{64,32},{96,64},{1,97},{33,1},{65,33},{97,65},{2,98}... | collective-permute-start | bytes 24584 | tf_op jit(solution)/shard_map/ppermute | solution.py:27
  110.4 7.0 %multiply_reduce_fusion.2 = f32[2048]{0:T(1024)S(1)} fusion(f32[2048,2048]{1,0:T(8,128)} %get-tuple-element.9, f32[2048]{0:T(1024)S(1)} %add_divide_fusion.1), kind=kLoop, calls=%fused_computation.7 | loop fusion | flops 8386560 | bytes 16793600 | tf_op jit(solution)/shard_map/reduce_sum | solution.py:148
  117.4 11.2 %all_to_all.34 = f32[16,1,2048]{2,1,0:T(1,128)S(1)} all-to-all(f32[16,1,2048]{2,1,0:T(1,128)S(1)} %broadcast_in_dim.13), channel_id=1, replica_groups=mesh['y'=4,'c'=2,'x'=4,'z'=4] {'x','z'}, dimensions={0} | all-to-all | bytes 262144 | tf_op jit(solution)/shard_map/all_to_all | solution.py:44
  128.7 6.9 %multiply_reduce_fusion.1 = f32[2048]{0:T(1024)S(1)} fusion(f32[2048,2048]{1,0:T(8,128)} %get-tuple-element.9, f32[2048]{0:T(1024)S(1)} %bitcast.63), kind=kLoop, calls=%fused_computation.6 | loop fusion | flops 8386560 | bytes 16793600 | tf_op jit(solution)/shard_map/reduce_sum | solution.py:146
  138.4 2.6 %collective-permute-start.18 = (f32[2048]{0:T(1024)S(1)}, f32[2048]{0:T(1024)S(1)}, u32[]{:S(2)}, u32[]{:S(2)}) collective-permute-start(f32[2048]{0:T(1024)S(1)} %add.524), channel_id=1, source_target_pairs={{0,32},{32,64},{64,96},{96,0},{1,33},{33,65},{65,97},{97,1},{2,34}... | collective-permute-start | bytes 24584 | tf_op jit(solution)/shard_map/ppermute | solution.py:27
  144.7 7.1 %multiply_reduce_fusion = f32[2048]{0:T(1024)S(1)} fusion(f32[2048,2048]{1,0:T(8,128)} %get-tuple-element.9, f32[2048]{0:T(1024)S(1)} %add_divide_fusion), kind=kLoop, calls=%fused_computation.5 | loop fusion | flops 8386560 | bytes 16793600 | tf_op jit(solution)/shard_map/reduce_sum | solution.py:148
  152.5 3.8 %all-to-all-start.4 = ((f32[16,1,2048]{2,1,0:T(1,128)}), f32[16,1,2048]{2,1,0:T(1,128)S(1)}, u32[]{:S(2)}, u32[]{:S(2)}) async-start(f32[16,1,2048]{2,1,0:T(1,128)} %broadcast_in_dim.14), calls=%async_computation.4 | async-start | bytes 262144 | tf_op jit(solution)/shard_map/all_to_all | solution.py:44
  156.3 7.7 %all-to-all-done.4 = f32[16,1,2048]{2,1,0:T(1,128)S(1)} async-done(((f32[16,1,2048]{2,1,0:T(1,128)}), f32[16,1,2048]{2,1,0:T(1,128)S(1)}, u32[]{:S(2)}, u32[]{:S(2)}) %all-to-all-start.4) | async-done | bytes 131104 | tf_op jit(solution)/shard_map/all_to_all | solution.py:44
  164.0 12.2 %fusion.1 = f32[768,2048]{1,0:T(8,128)} fusion(bf16[2048,768]{0,1:T(8,128)(2,1)S(1)} %bitcast.45, f32[2048,2048]{1,0:T(8,128)} %get-tuple-element.9, f32[2048]{0:T(1024)S(1)} %bitcast.59), kind=kOutput, calls=%fused_computation.12 | convolution fusion | flops 6459228160 | bytes 26222592 | tf_op jit(solution)/shard_map/dot_general | solution.py:157
  176.2 11.3 %add_multiply_fusion = f32[768,2048]{1,0:T(8,128)S(1)} fusion(f32[768,2048]{1,0:T(8,128)} %fusion.1, f32[2048]{0:T(1024)S(1)} %add_divide_fusion, bf16[2048,768]{0,1:T(8,128)(2,1)S(1)} %bitcast.46, f32[2048,2048]{1,0:T(8,128)} %get-tuple-element.9, f32[2048]{0:T(1024)S(1)} %bitcast.60), kind=kOutput, calls=%fused_computation.20 | convolution fusion | flops 6458179584 | bytes 32522240 | tf_op jit(solution)/shard_map/dot_general | solution.py:155
  187.6 2.7 %copy-done.1 = f32[768,2048]{1,0:T(8,128)} copy-done((f32[768,2048]{1,0:T(8,128)}, f32[768,2048]{1,0:T(8,128)S(1)}, u32[]{:S(2)}) %copy-start.1) | copy-done | bytes 6291480
  190.7 5.8 %collective-permute-done.20 = f32[4,96,2048]{2,1,0:T(8,128)} collective-permute-done((f32[4,96,2048]{2,1,0:T(8,128)S(1)}, f32[4,96,2048]{2,1,0:T(8,128)}, u32[]{:S(2)}, u32[]{:S(2)}) %collective-permute-start.20) | collective-permute-done | bytes 3145760 | tf_op jit(solution)/shard_map/ppermute | solution.py:76
  196.5 5.2 %bitcast_add_fusion = f32[4,96,2048]{2,1,0:T(8,128)} fusion(f32[4,96,2048]{2,1,0:T(8,128)} %collective-permute-done.20, f32[4,2,96,2048]{3,2,1,0:T(8,128)} %bitcast.43, s32[]{:T(128)S(6)} %select_n.56), kind=kLoop, calls=%fused_computation.24 | loop fusion | flops 786432 | bytes 9437188 | tf_op jit(solution)/shard_map/add | solution.py:76
  201.7 3.7 %all-to-all-start.5 = ((f32[4,96,2048]{2,1,0:T(8,128)}), f32[4,96,2048]{2,1,0:T(8,128)S(1)}, u32[]{:S(2)}, u32[]{:S(2)}) async-start(f32[4,96,2048]{2,1,0:T(8,128)} %bitcast_add_fusion), calls=%async_computation.5 | async-start | bytes 6291456 | tf_op jit(solution)/shard_map/all_to_all | solution.py:81
  205.4 6.9 %multiply_reduce_fusion.5 = f32[2048]{0:T(1024)S(1)} fusion(f32[2048,2048]{1,0:T(8,128)} %get-tuple-element.9, f32[2048]{0:T(1024)S(1)} %bitcast.61), kind=kLoop, calls=%fused_computation.11 | loop fusion | flops 8386560 | bytes 16793600 | tf_op jit(solution)/shard_map/reduce_sum | solution.py:159
  212.4 31.2 %all-to-all-done.5 = f32[4,96,2048]{2,1,0:T(8,128)S(1)} async-done(((f32[4,96,2048]{2,1,0:T(8,128)}), f32[4,96,2048]{2,1,0:T(8,128)S(1)}, u32[]{:S(2)}, u32[]{:S(2)}) %all-to-all-start.5) | async-done | bytes 3145760 | tf_op jit(solution)/shard_map/all_to_all | solution.py:81
  (96 shorter events, 42.6 us)
Async XLA Ops:
  2.4 12.5 %all-to-all-start.1 = ((bf16[4,2048,24]{1,2,0:T(8,128)(2,1)}), bf16[4,2048,24]{1,2,0:T(8,128)(2,1)S(1)}, u32[]{:S(2)}, u32[]{:S(2)}) async-start(bf16[4,2048,24]{1,2,0:T(8,128)(2,1)} %broadcast_in_dim.11), calls=%async_computation.1 | async-start | bytes 786432 | tf_op jit(solution)/shard_map/all_to_all | solution.py:120
  15.6 14.8 %all-to-all-start = ((bf16[4,2048,24]{1,2,0:T(8,128)(2,1)}), bf16[4,2048,24]{1,2,0:T(8,128)(2,1)S(1)}, u32[]{:S(2)}, u32[]{:S(2)}) async-start(bf16[4,2048,24]{1,2,0:T(8,128)(2,1)} %broadcast_in_dim.10), calls=%async_computation | async-start | bytes 786432 | tf_op jit(solution)/shard_map/all_to_all | solution.py:119
  20.9 14.8 %collective-permute-start.4 = (bf16[4,2048,24]{1,2,0:T(8,128)(2,1)S(1)}, bf16[4,2048,24]{1,2,0:T(8,128)(2,1)S(1)}, u32[]{:S(2)}, u32[]{:S(2)}) collective-permute-start(bf16[4,2048,24]{1,2,0:T(8,128)(2,1)S(1)} %all-to-all-done.1), channel_id=1, source_target_pairs={{0,1},{1,2},{2,3},{3,0},{4,5},{5,6},{6,7},{7,4},{8,9},{9,10},{10,1... | collective-permute-start | bytes 1179656 | tf_op jit(solution)/shard_map/ppermute | solution.py:93
  23.0 12.9 %collective-permute-start.6 = (bf16[4,2048,24]{1,2,0:T(8,128)(2,1)S(1)}, bf16[4,2048,24]{1,2,0:T(8,128)(2,1)S(1)}, u32[]{:S(2)}, u32[]{:S(2)}) collective-permute-start(bf16[4,2048,24]{1,2,0:T(8,128)(2,1)S(1)} %all-to-all-done.1), channel_id=1, source_target_pairs={{0,3},{1,0},{2,1},{3,2},{4,7},{5,4},{6,5},{7,6},{8,11},{9,8},{10,9... | collective-permute-start | bytes 1179656 | tf_op jit(solution)/shard_map/ppermute | solution.py:94
  30.4 9.0 %collective-permute-start = (bf16[4,2048,24]{1,2,0:T(8,128)(2,1)S(1)}, bf16[4,2048,24]{1,2,0:T(8,128)(2,1)S(1)}, u32[]{:S(2)}, u32[]{:S(2)}) collective-permute-start(bf16[4,2048,24]{1,2,0:T(8,128)(2,1)S(1)} %all-to-all-done), channel_id=1, source_target_pairs={{0,4},{4,8},{8,12},{12,0},{1,5},{5,9},{9,13},{13,1},{2,6},{6,10},{... | collective-permute-start | bytes 1179656 | tf_op jit(solution)/shard_map/ppermute | solution.py:93
  31.0 9.5 %collective-permute-start.2 = (bf16[4,2048,24]{1,2,0:T(8,128)(2,1)S(1)}, bf16[4,2048,24]{1,2,0:T(8,128)(2,1)S(1)}, u32[]{:S(2)}, u32[]{:S(2)}) collective-permute-start(bf16[4,2048,24]{1,2,0:T(8,128)(2,1)S(1)} %all-to-all-done), channel_id=1, source_target_pairs={{0,12},{4,0},{8,4},{12,8},{1,13},{5,1},{9,5},{13,9},{2,14},{6,2},{... | collective-permute-start | bytes 1179656 | tf_op jit(solution)/shard_map/ppermute | solution.py:94
  35.7 8.4 %collective-permute-start.5 = (bf16[4,1024,24]{1,2,0:T(8,128)(2,1)S(1)}, bf16[4,1024,24]{1,2,0:T(8,128)(2,1)S(1)}, u32[]{:S(2)}, u32[]{:S(2)}) collective-permute-start(bf16[4,1024,24]{1,2,0:T(8,128)(2,1)S(1)} %slice.294), channel_id=1, source_target_pairs={{0,1},{1,2},{2,3},{3,0},{4,5},{5,6},{6,7},{7,4},{8,9},{9,10},{10,1... | collective-permute-start | bytes 589832 | tf_op jit(solution)/shard_map/ppermute | solution.py:98
  35.8 8.4 %copy-start.7 = (bf16[4,2048,24]{1,2,0:T(8,128)(2,1)}, bf16[4,2048,24]{1,2,0:T(8,128)(2,1)S(1)}, u32[]{:S(2)}) copy-start(bf16[4,2048,24]{1,2,0:T(8,128)(2,1)S(1)} %collective-permute-done.6) | copy-start | bytes 1179652
  35.9 8.3 %collective-permute-start.7 = (bf16[4,1024,24]{1,2,0:T(8,128)(2,1)S(1)}, bf16[4,1024,24]{1,2,0:T(8,128)(2,1)S(1)}, u32[]{:S(2)}, u32[]{:S(2)}) collective-permute-start(bf16[4,1024,24]{1,2,0:T(8,128)(2,1)S(1)} %slice.295), channel_id=1, source_target_pairs={{0,3},{1,0},{2,1},{3,2},{4,7},{5,4},{6,5},{7,6},{8,11},{9,8},{10,9... | collective-permute-start | bytes 589832 | tf_op jit(solution)/shard_map/ppermute | solution.py:99
  40.1 7.2 %collective-permute-start.1 = (bf16[4,1024,24]{1,2,0:T(8,128)(2,1)}, bf16[4,1024,24]{1,2,0:T(8,128)(2,1)}, u32[]{:S(2)}, u32[]{:S(2)}) collective-permute-start(bf16[4,1024,24]{1,2,0:T(8,128)(2,1)} %slice.292), channel_id=1, source_target_pairs={{0,4},{4,8},{8,12},{12,0},{1,5},{5,9},{9,13},{13,1},{2,6},{6,10},{... | collective-permute-start | bytes 589832 | tf_op jit(solution)/shard_map/ppermute | solution.py:98
  41.2 6.4 %collective-permute-start.3 = (bf16[4,1024,24]{1,2,0:T(8,128)(2,1)}, bf16[4,1024,24]{1,2,0:T(8,128)(2,1)}, u32[]{:S(2)}, u32[]{:S(2)}) collective-permute-start(bf16[4,1024,24]{1,2,0:T(8,128)(2,1)} %slice.293), channel_id=1, source_target_pairs={{0,12},{4,0},{8,4},{12,8},{1,13},{5,1},{9,5},{13,9},{2,14},{6,2},{... | collective-permute-start | bytes 589832 | tf_op jit(solution)/shard_map/ppermute | solution.py:99
  52.6 12.6 %copy-start.3 = (bf16[4,4,2048,48]{2,3,1,0:T(8,128)(2,1)}, bf16[4,4,2048,48]{2,3,1,0:T(8,128)(2,1)S(1)}, u32[]{:S(2)}) copy-start(bf16[4,4,2048,48]{2,3,1,0:T(8,128)(2,1)S(1)} %pad_maximum_fusion) | copy-start | bytes 9437188
  65.3 1.2 collective-permute-start.8
  66.4 5.2 %collective-permute-start.10 = (f32[2048]{0:T(1024)S(1)}, f32[2048]{0:T(1024)S(1)}, u32[]{:S(2)}, u32[]{:S(2)}) collective-permute-start(f32[2048]{0:T(1024)S(1)} %add.484), channel_id=1, source_target_pairs={{0,32},{32,64},{64,96},{96,0},{1,33},{33,65},{65,97},{97,1},{2,34}... | collective-permute-start | bytes 24584 | tf_op jit(solution)/shard_map/ppermute | solution.py:27
  68.0 3.7 %collective-permute-start.11 = (f32[2048]{0:T(1024)S(1)}, f32[2048]{0:T(1024)S(1)}, u32[]{:S(2)}, u32[]{:S(2)}) collective-permute-start(f32[2048]{0:T(1024)S(1)} %add.484), channel_id=1, source_target_pairs={{0,96},{32,0},{64,32},{96,64},{1,97},{33,1},{65,33},{97,65},{2,98}... | collective-permute-start | bytes 24584 | tf_op jit(solution)/shard_map/ppermute | solution.py:27
  69.7 5.2 %collective-permute-start.9 = (f32[2048]{0:T(1024)S(1)}, f32[2048]{0:T(1024)S(1)}, u32[]{:S(2)}, u32[]{:S(2)}) collective-permute-start(f32[2048]{0:T(1024)S(1)} %add.484), channel_id=1, source_target_pairs={{0,64},{32,96},{64,0},{96,32},{1,65},{33,97},{65,1},{97,33},{2,66}... | collective-permute-start | bytes 24584 | tf_op jit(solution)/shard_map/ppermute | solution.py:27
  102.2 1.3 collective-permute-start.12
  103.5 5.2 %collective-permute-start.13 = (f32[2048]{0:T(1024)S(1)}, f32[2048]{0:T(1024)S(1)}, u32[]{:S(2)}, u32[]{:S(2)}) collective-permute-start(f32[2048]{0:T(1024)S(1)} %add.504), channel_id=1, source_target_pairs={{0,64},{32,96},{64,0},{96,32},{1,65},{33,97},{65,1},{97,33},{2,66}... | collective-permute-start | bytes 24584 | tf_op jit(solution)/shard_map/ppermute | solution.py:27
  105.5 4.9 %collective-permute-start.14 = (f32[2048]{0:T(1024)S(1)}, f32[2048]{0:T(1024)S(1)}, u32[]{:S(2)}, u32[]{:S(2)}) collective-permute-start(f32[2048]{0:T(1024)S(1)} %add.504), channel_id=1, source_target_pairs={{0,32},{32,64},{64,96},{96,0},{1,33},{33,65},{65,97},{97,1},{2,34}... | collective-permute-start | bytes 24584 | tf_op jit(solution)/shard_map/ppermute | solution.py:27
  106.2 4.2 %collective-permute-start.15 = (f32[2048]{0:T(1024)S(1)}, f32[2048]{0:T(1024)S(1)}, u32[]{:S(2)}, u32[]{:S(2)}) collective-permute-start(f32[2048]{0:T(1024)S(1)} %add.504), channel_id=1, source_target_pairs={{0,96},{32,0},{64,32},{96,64},{1,97},{33,1},{65,33},{97,65},{2,98}... | collective-permute-start | bytes 24584 | tf_op jit(solution)/shard_map/ppermute | solution.py:27
  135.7 1.3 collective-permute-start.16
  136.9 5.2 %collective-permute-start.17 = (f32[2048]{0:T(1024)S(1)}, f32[2048]{0:T(1024)S(1)}, u32[]{:S(2)}, u32[]{:S(2)}) collective-permute-start(f32[2048]{0:T(1024)S(1)} %add.524), channel_id=1, source_target_pairs={{0,64},{32,96},{64,0},{96,32},{1,65},{33,97},{65,1},{97,33},{2,66}... | collective-permute-start | bytes 24584 | tf_op jit(solution)/shard_map/ppermute | solution.py:27
  138.4 4.9 %collective-permute-start.18 = (f32[2048]{0:T(1024)S(1)}, f32[2048]{0:T(1024)S(1)}, u32[]{:S(2)}, u32[]{:S(2)}) collective-permute-start(f32[2048]{0:T(1024)S(1)} %add.524), channel_id=1, source_target_pairs={{0,32},{32,64},{64,96},{96,0},{1,33},{33,65},{65,97},{97,1},{2,34}... | collective-permute-start | bytes 24584 | tf_op jit(solution)/shard_map/ppermute | solution.py:27
  141.0 3.7 %collective-permute-start.19 = (f32[2048]{0:T(1024)S(1)}, f32[2048]{0:T(1024)S(1)}, u32[]{:S(2)}, u32[]{:S(2)}) collective-permute-start(f32[2048]{0:T(1024)S(1)} %add.524), channel_id=1, source_target_pairs={{0,96},{32,0},{64,32},{96,64},{1,97},{33,1},{65,33},{97,65},{2,98}... | collective-permute-start | bytes 24584 | tf_op jit(solution)/shard_map/ppermute | solution.py:27
  144.7 19.3 %copy-start.4 = (bf16[4,4,2048,48]{2,3,1,0:T(8,128)(2,1)S(1)}, bf16[4,4,2048,48]{2,3,1,0:T(8,128)(2,1)}, u32[]{:S(2)}) copy-start(bf16[4,4,2048,48]{2,3,1,0:T(8,128)(2,1)} %copy-done.3) | copy-start | bytes 9437188
  152.5 11.4 %all-to-all-start.4 = ((f32[16,1,2048]{2,1,0:T(1,128)}), f32[16,1,2048]{2,1,0:T(1,128)S(1)}, u32[]{:S(2)}, u32[]{:S(2)}) async-start(f32[16,1,2048]{2,1,0:T(1,128)} %broadcast_in_dim.14), calls=%async_computation.4 | async-start | bytes 262144 | tf_op jit(solution)/shard_map/all_to_all | solution.py:44
  190.6 5.9 %collective-permute-start.20 = (f32[4,96,2048]{2,1,0:T(8,128)S(1)}, f32[4,96,2048]{2,1,0:T(8,128)}, u32[]{:S(2)}, u32[]{:S(2)}) collective-permute-start(f32[4,96,2048]{2,1,0:T(8,128)S(1)} %dynamic-slice_bitcast_fusion), channel_id=1, source_target_pairs={{0,16},{16,0},{1,17},{17,1},{2,18},{18,2},{3,19},{19,3},{4,20},{20... | collective-permute-start | bytes 9437192 | tf_op jit(solution)/shard_map/ppermute | solution.py:76
  201.7 41.8 %all-to-all-start.5 = ((f32[4,96,2048]{2,1,0:T(8,128)}), f32[4,96,2048]{2,1,0:T(8,128)S(1)}, u32[]{:S(2)}, u32[]{:S(2)}) async-start(f32[4,96,2048]{2,1,0:T(8,128)} %bitcast_add_fusion), calls=%async_computation.5 | async-start | bytes 6291456 | tf_op jit(solution)/shard_map/all_to_all | solution.py:81
  243.8 1.3 collective-permute-start.21
  245.1 5.4 %collective-permute-start.22 = (f32[2,2048]{1,0:T(2,128)S(1)}, f32[2,2048]{1,0:T(2,128)S(1)}, u32[]{:S(2)}, u32[]{:S(2)}) collective-permute-start(f32[2,2048]{1,0:T(2,128)S(1)} %fusion.21), channel_id=1, source_target_pairs={{0,64},{32,96},{64,0},{96,32},{1,65},{33,97},{65,1},{97,33},{2,66}... | collective-permute-start | bytes 49160 | tf_op jit(solution)/shard_map/ppermute | solution.py:27
  245.7 4.9 %collective-permute-start.23 = (f32[2,2048]{1,0:T(2,128)S(1)}, f32[2,2048]{1,0:T(2,128)S(1)}, u32[]{:S(2)}, u32[]{:S(2)}) collective-permute-start(f32[2,2048]{1,0:T(2,128)S(1)} %fusion.21), channel_id=1, source_target_pairs={{0,32},{32,64},{64,96},{96,0},{1,33},{33,65},{65,97},{97,1},{2,34}... | collective-permute-start | bytes 49160 | tf_op jit(solution)/shard_map/ppermute | solution.py:27
  247.2 3.7 %collective-permute-start.24 = (f32[2,2048]{1,0:T(2,128)S(1)}, f32[2,2048]{1,0:T(2,128)S(1)}, u32[]{:S(2)}, u32[]{:S(2)}) collective-permute-start(f32[2,2048]{1,0:T(2,128)S(1)} %fusion.21), channel_id=1, source_target_pairs={{0,96},{32,0},{64,32},{96,64},{1,97},{33,1},{65,33},{97,65},{2,98}... | collective-permute-start | bytes 49160 | tf_op jit(solution)/shard_map/ppermute | solution.py:27
  (5 other events, 15.9 us)

commit v9 on v8

--- a/solution.py
+++ b/solution.py
@@ -85,7 +85,7 @@
     return total
 
 
-def ring_gather(v, axis, n):
+def ring_gather(v, axis, n, split_far=True):
     if n == 1:
         return v[None]
     if n != 4:
@@ -93,13 +93,16 @@
     fwd = lax.ppermute(v, axis, [(i, (i + 1) % n) for i in range(n)])
     bwd = lax.ppermute(v, axis, [(i, (i - 1) % n) for i in range(n)])
     half = v.shape[-2] // 2
-    far = jnp.concatenate(
-        [
-            lax.ppermute(fwd[..., :half, :], axis, [(i, (i + 1) % n) for i in range(n)]),
-            lax.ppermute(bwd[..., half:, :], axis, [(i, (i - 1) % n) for i in range(n)]),
-        ],
-        axis=-2,
-    )
+    if split_far:
+        far = jnp.concatenate(
+            [
+                lax.ppermute(fwd[..., :half, :], axis, [(i, (i + 1) % n) for i in range(n)]),
+                lax.ppermute(bwd[..., half:, :], axis, [(i, (i - 1) % n) for i in range(n)]),
+            ],
+            axis=-2,
+        )
+    else:
+        far = lax.ppermute(fwd, axis, [(i, (i + 1) % n) for i in range(n)])
     by_offset = jnp.stack([v, fwd, far, bwd])
     idx = lax.axis_index(axis)
     return by_offset[(idx - jnp.arange(n)) % n]
@@ -116,8 +119,8 @@
         )
         return jnp.transpose(got, (1, 0, 2)).reshape(rows, nx * nz * blk)
     part_a, part_b = points[:, : blk // 2], points[:, blk // 2 :]
-    a_z = lax.all_to_all(jnp.broadcast_to(part_a[None], (nz,) + part_a.shape), "z", 0, 0, tiled=False)
-    b_x = lax.all_to_all(jnp.broadcast_to(part_b[None], (nx,) + part_b.shape), "x", 0, 0, tiled=False)
+    a_z = ring_gather(part_a, "z", nz, split_far=False)
+    b_x = ring_gather(part_b, "x", nx, split_far=False)
     a_xz = ring_gather(a_z, "x", nx)
     b_zx = ring_gather(b_x, "z", nz)
     full = jnp.concatenate([a_xz, jnp.transpose(b_zx, (1, 0, 2, 3))], axis=-1)

time: 253 us -> 244 us (0.964)
  waiting for transfers between devices: 73.4 us -> 69.7 us
  other arithmetic: 58 us -> 55.4 us
    all_to_all x2 -> x0, waiting for transfers between devices: 11.7 us -> none  [the longest x1 8.07 us: gather_features(): lax.all_to_all(jnp.broadcast_to(part_b[None], (nx,) + part_b.shape), 'x',...]
    all_to_all x2 -> x0, starting transfers between devices: 9.71 us -> none  [the longest x1 5.31 us: gather_features(): lax.all_to_all(jnp.broadcast_to(part_a[None], (nz,) + part_a.shape), 'z',...]
    ppermute x2 -> x4, starting transfers between devices: 3.91 us -> 9.55 us  [ring_gather(): bwd = lax.ppermute(v, axis, [(i, (i - 1) % n) for i in range(n)])]
    ppermute x2 -> x4, waiting for transfers between devices: 2.28 us -> 5.45 us  [ring_gather(): fwd = lax.ppermute(v, axis, [(i, (i + 1) % n) for i in range(n)])]
    ppermute x0 -> x2, waiting for transfers between devices: none -> 3.07 us  [ring_gather(): far = lax.ppermute(fwd, axis, [(i, (i + 1) % n) for i in range(n)])]
    unnamed x16 -> x10, local copies, waits for them, and re-layouts: 2.87 us -> 0.02 us
    gather x3 -> x5, local copies, waits for them, and re-layouts: 2.58 us -> 5.33 us  [ring_gather(): return by_offset[(idx - jnp.arange(n)) % n]]
  transfers between devices with their start and end apart: 29 -> 33, of which waited for: 20 -> 22; matrix products, arithmetic and copies ran while one was open for 6% -> 5% of each run, Pallas kernels for 0% -> 0%
where the time goes in v9:
time: 244 us; the launch traced here: 243 us
  waiting for transfers between devices  69.7 us (29%)
  other arithmetic  55.4 us (23%)
  starting transfers between devices  47.8 us (20%)
  matrix products  34.2 us (14%)
  blocking collectives  24 us (10%)
  local copies, waits for them, and re-layouts  10.8 us (4%)
    all_to_all x1, waiting for transfers between devices, scatter_features(): got = lax.all_to_all(x, 'y', 0, 0, tiled=False)  31.2 us
    all_to_all x2, blocking collectives, group_sum(): lax.all_to_all(jnp.broadcast_to(v[None], (n,) + v.shape), axes, 0, 0, til...  24 us
    reduce_sum x3, other arithmetic, local(): row_part = jnp.sum(kernel * col_scale[None, :], axis=1)  21.1 us
    ppermute x16, starting transfers between devices, axis_sum(): lax.ppermute(v, axis, [(i, (i + s) % n) for i in range(n)])  19.1 us
    reduce_sum x2, other arithmetic, local(): col_part = jnp.sum(kernel * row_scale[:, None], axis=0)  13.9 us
    ppermute x16, waiting for transfers between devices, axis_sum(): lax.ppermute(v, axis, [(i, (i + s) % n) for i in range(n)])  13.8 us
    dot_general x1, matrix products, local(): lax.dot_general(gathered, hi, dims, preferred_element_type=jnp.float32)  12.1 us
    dot_general x1, matrix products, local(): jnp.dot(unit_points, unit_centroids.T, preferred_element_type=jnp.float32)  11.7 us
  transfers between devices with their start and end apart: 33, of which 22 were waited for; matrix products, arithmetic and copies ran while one was open for 5% of the time, Pallas kernels for 0%

profile of v9, /device:TPU:0, one launch (start us, length us, event | category | flops | bytes accessed | tf_op | source)
XLA Modules:
  0.0 243.0 jit_solution(1440405016961091128)
XLA Ops:
  1.6 2.1 collective-permute-start
  3.7 2.2 collective-permute-start.2
  9.3 2.4 %collective-permute-done.7 = bf16[2048,24]{0,1:T(8,128)(2,1)S(1)} collective-permute-done((bf16[2048,24]{0,1:T(8,128)(2,1)S(1)}, bf16[2048,24]{0,1:T(8,128)(2,1)S(1)}, u32[]{:S(2)}, u32[]{:S(2)}) %collective-permute-start.7) | collective-permute-done | bytes 98336 | tf_op jit(solution)/shard_map/ppermute | solution.py:93
  12.0 3.1 %collective-permute-done.1 = bf16[2048,24]{0,1:T(8,128)(2,1)S(1)} collective-permute-done((bf16[2048,24]{0,1:T(8,128)(2,1)S(1)}, bf16[2048,24]{0,1:T(8,128)(2,1)S(1)}, u32[]{:S(2)}, u32[]{:S(2)}) %collective-permute-start.1) | collective-permute-done | bytes 98336 | tf_op jit(solution)/shard_map/ppermute | solution.py:105
  16.6 2.4 collective-permute-start.5
  19.8 3.2 %collective-permute-start.12 = (bf16[4,2048,24]{1,2,0:T(8,128)(2,1)S(1)}, bf16[4,2048,24]{1,2,0:T(8,128)(2,1)S(1)}, u32[]{:S(2)}, u32[]{:S(2)}) collective-permute-start(bf16[4,2048,24]{1,2,0:T(8,128)(2,1)S(1)} %gather_fusion.2), channel_id=1, source_target_pairs={{0,3},{1,0},{2,1},{3,2},{4,7},{5,4},{6,5},{7,6},{8,11},{9,8},{10,9... | collective-permute-start | bytes 1179656 | tf_op jit(solution)/shard_map/ppermute | solution.py:94
  23.0 3.0 %collective-permute-done.3 = bf16[4,2048,24]{1,2,0:T(8,128)(2,1)S(1)} collective-permute-done((bf16[4,2048,24]{1,2,0:T(8,128)(2,1)S(1)}, bf16[4,2048,24]{1,2,0:T(8,128)(2,1)S(1)}, u32[]{:S(2)}, u32[]{:S(2)}) %collective-permute-start.3) | collective-permute-done | bytes 393248 | tf_op jit(solution)/shard_map/ppermute | solution.py:93
  26.1 3.3 %collective-permute-start.6 = (bf16[4,1024,24]{1,2,0:T(8,128)(2,1)S(1)}, bf16[4,1024,24]{1,2,0:T(8,128)(2,1)S(1)}, u32[]{:S(2)}, u32[]{:S(2)}) collective-permute-start(bf16[4,1024,24]{1,2,0:T(8,128)(2,1)S(1)} %slice.297), channel_id=1, source_target_pairs={{0,12},{4,0},{8,4},{12,8},{1,13},{5,1},{9,5},{13,9},{2,14},{6,2},{... | collective-permute-start | bytes 589832 | tf_op jit(solution)/shard_map/ppermute | solution.py:100
  29.4 2.6 %fusion.6 = f32[2048]{0:T(1024)S(1)} fusion(bf16[2048,768]{1,0:T(8,128)(2,1)} %param.3), kind=kLoop, calls=%fused_computation.20 | loop fusion | flops 4716544 | bytes 3153920 | tf_op jit(solution)/shard_map/reduce_sum | solution.py:18
  33.5 3.2 %collective-permute-start.13 = (bf16[4,1024,24]{1,2,0:T(8,128)(2,1)}, bf16[4,1024,24]{1,2,0:T(8,128)(2,1)}, u32[]{:S(2)}, u32[]{:S(2)}) collective-permute-start(bf16[4,1024,24]{1,2,0:T(8,128)(2,1)} %slice.299), channel_id=1, source_target_pairs={{0,3},{1,0},{2,1},{3,2},{4,7},{5,4},{6,5},{7,6},{8,11},{9,8},{10,9... | collective-permute-start | bytes 589832 | tf_op jit(solution)/shard_map/ppermute | solution.py:100
  37.6 2.3 collective-permute-done.11
  47.1 11.7 %fusion.24 = (f32[2048]{0:T(1024)S(1)}, f32[2048,2048]{1,0:T(8,128)}) fusion(bf16[2048,768]{1,0:T(8,128)(2,1)S(1)} %copy-done, f32[2048]{0:T(1024)S(1)} %get-tuple-element.12, bf16[2048,768]{0,1:T(8,128)(2,1)S(1)} %bitcast.54, f32[2048]{0:T(1024)S(1)} %get-tuple-element.13), kind=kOutput, calls=%fused_computation.120 | convolution fusion | flops 6460274688 | bytes 23093248 | tf_op jit(solution)/shard_map/dot_general | solution.py:146
  60.0 3.2 %collective-permute-start.15 = (f32[2048]{0:T(1024)S(1)}, f32[2048]{0:T(1024)S(1)}, u32[]{:S(2)}, u32[]{:S(2)}) collective-permute-start(f32[2048]{0:T(1024)S(1)} %add.490), channel_id=1, source_target_pairs={{0,64},{32,96},{64,0},{96,32},{1,65},{33,97},{65,1},{97,33},{2,66}... | collective-permute-start | bytes 24584 | tf_op jit(solution)/shard_map/ppermute | solution.py:27
  63.9 2.6 %collective-permute-start.17 = (f32[2048]{0:T(1024)S(1)}, f32[2048]{0:T(1024)S(1)}, u32[]{:S(2)}, u32[]{:S(2)}) collective-permute-start(f32[2048]{0:T(1024)S(1)} %add.490), channel_id=1, source_target_pairs={{0,96},{32,0},{64,32},{96,64},{1,97},{33,1},{65,33},{97,65},{2,98}... | collective-permute-start | bytes 24584 | tf_op jit(solution)/shard_map/ppermute | solution.py:27
  68.1 7.0 %multiply_reduce_fusion.4 = f32[2048]{0:T(1024)S(1)} fusion(f32[2048,2048]{1,0:T(8,128)} %get-tuple-element.11, f32[2048]{0:T(1024)S(1)} %add_divide_fusion.2), kind=kLoop, calls=%fused_computation.11 | loop fusion | flops 8386560 | bytes 16793600 | tf_op jit(solution)/shard_map/reduce_sum | solution.py:151
  75.1 12.7 %all_to_all.23 = f32[16,1,2048]{2,1,0:T(1,128)S(1)} all-to-all(f32[16,1,2048]{2,1,0:T(1,128)S(1)} %broadcast_in_dim.6), channel_id=1, replica_groups=mesh['y'=4,'c'=2,'x'=4,'z'=4] {'x','z'}, dimensions={0} | all-to-all | bytes 262144 | tf_op jit(solution)/shard_map/all_to_all | solution.py:44
  87.9 6.9 %multiply_reduce_fusion.3 = f32[2048]{0:T(1024)S(1)} fusion(f32[2048,2048]{1,0:T(8,128)} %get-tuple-element.11, f32[2048]{0:T(1024)S(1)} %bitcast.76), kind=kLoop, calls=%fused_computation.10 | loop fusion | flops 8386560 | bytes 16793600 | tf_op jit(solution)/shard_map/reduce_sum | solution.py:149
  97.6 2.6 %collective-permute-start.20 = (f32[2048]{0:T(1024)S(1)}, f32[2048]{0:T(1024)S(1)}, u32[]{:S(2)}, u32[]{:S(2)}) collective-permute-start(f32[2048]{0:T(1024)S(1)} %add.510), channel_id=1, source_target_pairs={{0,32},{32,64},{64,96},{96,0},{1,33},{33,65},{65,97},{97,1},{2,34}... | collective-permute-start | bytes 24584 | tf_op jit(solution)/shard_map/ppermute | solution.py:27
  103.9 7.0 %multiply_reduce_fusion.2 = f32[2048]{0:T(1024)S(1)} fusion(f32[2048,2048]{1,0:T(8,128)} %get-tuple-element.11, f32[2048]{0:T(1024)S(1)} %add_divide_fusion.1), kind=kLoop, calls=%fused_computation.9 | loop fusion | flops 8386560 | bytes 16793600 | tf_op jit(solution)/shard_map/reduce_sum | solution.py:151
  110.9 11.2 %all_to_all.24 = f32[16,1,2048]{2,1,0:T(1,128)S(1)} all-to-all(f32[16,1,2048]{2,1,0:T(1,128)S(1)} %broadcast_in_dim.7), channel_id=1, replica_groups=mesh['y'=4,'c'=2,'x'=4,'z'=4] {'x','z'}, dimensions={0} | all-to-all | bytes 262144 | tf_op jit(solution)/shard_map/all_to_all | solution.py:44
  122.2 6.9 %multiply_reduce_fusion.1 = f32[2048]{0:T(1024)S(1)} fusion(f32[2048,2048]{1,0:T(8,128)} %get-tuple-element.11, f32[2048]{0:T(1024)S(1)} %bitcast.77), kind=kLoop, calls=%fused_computation.8 | loop fusion | flops 8386560 | bytes 16793600 | tf_op jit(solution)/shard_map/reduce_sum | solution.py:149
  136.8 7.1 %multiply_reduce_fusion = f32[2048]{0:T(1024)S(1)} fusion(f32[2048,2048]{1,0:T(8,128)} %get-tuple-element.11, f32[2048]{0:T(1024)S(1)} %add_divide_fusion), kind=kLoop, calls=%fused_computation.7 | loop fusion | flops 8386560 | bytes 16793600 | tf_op jit(solution)/shard_map/reduce_sum | solution.py:151
  144.6 3.6 %all-to-all-start.2 = ((f32[16,1,2048]{2,1,0:T(1,128)}), f32[16,1,2048]{2,1,0:T(1,128)S(1)}, u32[]{:S(2)}, u32[]{:S(2)}) async-start(f32[16,1,2048]{2,1,0:T(1,128)} %broadcast_in_dim.8), calls=%async_computation.2 | async-start | bytes 262144 | tf_op jit(solution)/shard_map/all_to_all | solution.py:44
  148.2 7.8 %all-to-all-done.2 = f32[16,1,2048]{2,1,0:T(1,128)S(1)} async-done(((f32[16,1,2048]{2,1,0:T(1,128)}), f32[16,1,2048]{2,1,0:T(1,128)S(1)}, u32[]{:S(2)}, u32[]{:S(2)}) %all-to-all-start.2) | async-done | bytes 131104 | tf_op jit(solution)/shard_map/all_to_all | solution.py:44
  156.1 10.5 %fusion.1 = f32[768,2048]{1,0:T(8,128)S(1)} fusion(bf16[2048,768]{0,1:T(8,128)(2,1)S(1)} %bitcast.55, f32[2048,2048]{1,0:T(8,128)} %get-tuple-element.11, f32[2048]{0:T(1024)S(1)} %bitcast.73), kind=kOutput, calls=%fused_computation.14 | convolution fusion | flops 6459228160 | bytes 26222592 | tf_op jit(solution)/shard_map/dot_general | solution.py:160
  166.6 12.1 %add_multiply_fusion = f32[768,2048]{1,0:T(8,128)} fusion(f32[768,2048]{1,0:T(8,128)S(1)} %fusion.1, f32[2048]{0:T(1024)S(1)} %add_divide_fusion, bf16[2048,768]{0,1:T(8,128)(2,1)S(1)} %bitcast.56, f32[2048,2048]{1,0:T(8,128)} %get-tuple-element.11, f32[2048]{0:T(1024)S(1)} %bitcast.74), kind=kOutput, calls=%fused_computation.22 | convolution fusion | flops 6458179584 | bytes 32522240 | tf_op jit(solution)/shard_map/dot_general | solution.py:158
  178.7 2.1 dynamic-slice_bitcast_fusion
  180.9 5.8 %collective-permute-done.26 = f32[4,96,2048]{2,1,0:T(8,128)} collective-permute-done((f32[4,96,2048]{2,1,0:T(8,128)S(1)}, f32[4,96,2048]{2,1,0:T(8,128)}, u32[]{:S(2)}, u32[]{:S(2)}) %collective-permute-start.26) | collective-permute-done | bytes 3145760 | tf_op jit(solution)/shard_map/ppermute | solution.py:76
  186.6 5.2 %bitcast_add_fusion = f32[4,96,2048]{2,1,0:T(8,128)} fusion(f32[4,96,2048]{2,1,0:T(8,128)} %collective-permute-done.26, f32[4,2,96,2048]{3,2,1,0:T(8,128)} %bitcast.25, s32[]{:T(128)S(6)} %select_n.62), kind=kLoop, calls=%fused_computation.26 | loop fusion | flops 786432 | bytes 9437188 | tf_op jit(solution)/shard_map/add | solution.py:76
  191.9 4.0 %all-to-all-start.3 = ((f32[4,96,2048]{2,1,0:T(8,128)}), f32[4,96,2048]{2,1,0:T(8,128)S(1)}, u32[]{:S(2)}, u32[]{:S(2)}) async-start(f32[4,96,2048]{2,1,0:T(8,128)} %bitcast_add_fusion), calls=%async_computation.3 | async-start | bytes 6291456 | tf_op jit(solution)/shard_map/all_to_all | solution.py:81
  195.9 6.9 %multiply_reduce_fusion.5 = f32[2048]{0:T(1024)S(1)} fusion(f32[2048,2048]{1,0:T(8,128)} %get-tuple-element.11, f32[2048]{0:T(1024)S(1)} %bitcast.75), kind=kLoop, calls=%fused_computation.13 | loop fusion | flops 8386560 | bytes 16793600 | tf_op jit(solution)/shard_map/reduce_sum | solution.py:162
  202.8 31.2 %all-to-all-done.3 = f32[4,96,2048]{2,1,0:T(8,128)S(1)} async-done(((f32[4,96,2048]{2,1,0:T(8,128)}), f32[4,96,2048]{2,1,0:T(8,128)S(1)}, u32[]{:S(2)}, u32[]{:S(2)}) %all-to-all-start.3) | async-done | bytes 3145760 | tf_op jit(solution)/shard_map/all_to_all | solution.py:81
  (100 shorter events, 44.0 us)
Async XLA Ops:
  1.6 7.6 %collective-permute-start = (bf16[2048,24]{0,1:T(8,128)(2,1)S(1)}, bf16[2048,24]{0,1:T(8,128)(2,1)S(1)}, u32[]{:S(2)}, u32[]{:S(2)}) collective-permute-start(bf16[2048,24]{0,1:T(8,128)(2,1)S(1)} %get-tuple-element.7), channel_id=1, source_target_pairs={{0,1},{1,2},{2,3},{3,0},{4,5},{5,6},{6,7},{7,4},{8,9},{9,10},{10,1... | collective-permute-start | bytes 294920 | tf_op jit(solution)/shard_map/ppermute | solution.py:93
  3.7 8.3 %collective-permute-start.2 = (bf16[2048,24]{0,1:T(8,128)(2,1)S(1)}, bf16[2048,24]{0,1:T(8,128)(2,1)S(1)}, u32[]{:S(2)}, u32[]{:S(2)}) collective-permute-start(bf16[2048,24]{0,1:T(8,128)(2,1)S(1)} %get-tuple-element.7), channel_id=1, source_target_pairs={{0,3},{1,0},{2,1},{3,2},{4,7},{5,4},{6,5},{7,6},{8,11},{9,8},{10,9... | collective-permute-start | bytes 294920 | tf_op jit(solution)/shard_map/ppermute | solution.py:94
  5.9 5.8 %collective-permute-start.7 = (bf16[2048,24]{0,1:T(8,128)(2,1)S(1)}, bf16[2048,24]{0,1:T(8,128)(2,1)S(1)}, u32[]{:S(2)}, u32[]{:S(2)}) collective-permute-start(bf16[2048,24]{0,1:T(8,128)(2,1)S(1)} %get-tuple-element.6), channel_id=1, source_target_pairs={{0,4},{4,8},{8,12},{12,0},{1,5},{5,9},{9,13},{13,1},{2,6},{6,10},{... | collective-permute-start | bytes 294920 | tf_op jit(solution)/shard_map/ppermute | solution.py:93
  7.4 11.6 %collective-permute-start.9 = (bf16[2048,24]{0,1:T(8,128)(2,1)S(1)}, bf16[2048,24]{0,1:T(8,128)(2,1)S(1)}, u32[]{:S(2)}, u32[]{:S(2)}) collective-permute-start(bf16[2048,24]{0,1:T(8,128)(2,1)S(1)} %get-tuple-element.6), channel_id=1, source_target_pairs={{0,12},{4,0},{8,4},{12,8},{1,13},{5,1},{9,5},{13,9},{2,14},{6,2},{... | collective-permute-start | bytes 294920 | tf_op jit(solution)/shard_map/ppermute | solution.py:94
  9.2 5.9 %collective-permute-start.1 = (bf16[2048,24]{0,1:T(8,128)(2,1)S(1)}, bf16[2048,24]{0,1:T(8,128)(2,1)S(1)}, u32[]{:S(2)}, u32[]{:S(2)}) collective-permute-start(bf16[2048,24]{0,1:T(8,128)(2,1)S(1)} %collective-permute-done), channel_id=1, source_target_pairs={{0,1},{1,2},{2,3},{3,0},{4,5},{5,6},{6,7},{7,4},{8,9},{9,10},{10,1... | collective-permute-start | bytes 294920 | tf_op jit(solution)/shard_map/ppermute | solution.py:105
  11.7 7.3 %collective-permute-start.8 = (bf16[2048,24]{0,1:T(8,128)(2,1)S(1)}, bf16[2048,24]{0,1:T(8,128)(2,1)S(1)}, u32[]{:S(2)}, u32[]{:S(2)}) collective-permute-start(bf16[2048,24]{0,1:T(8,128)(2,1)S(1)} %collective-permute-done.7), channel_id=1, source_target_pairs={{0,4},{4,8},{8,12},{12,0},{1,5},{5,9},{9,13},{13,1},{2,6},{6,10},{... | collective-permute-start | bytes 294920 | tf_op jit(solution)/shard_map/ppermute | solution.py:105
  15.7 10.3 %collective-permute-start.3 = (bf16[4,2048,24]{1,2,0:T(8,128)(2,1)S(1)}, bf16[4,2048,24]{1,2,0:T(8,128)(2,1)S(1)}, u32[]{:S(2)}, u32[]{:S(2)}) collective-permute-start(bf16[4,2048,24]{1,2,0:T(8,128)(2,1)S(1)} %gather_fusion), channel_id=1, source_target_pairs={{0,4},{4,8},{8,12},{12,0},{1,5},{5,9},{9,13},{13,1},{2,6},{6,10},{... | collective-permute-start | bytes 1179656 | tf_op jit(solution)/shard_map/ppermute | solution.py:93
  16.6 9.4 %collective-permute-start.5 = (bf16[4,2048,24]{1,2,0:T(8,128)(2,1)S(1)}, bf16[4,2048,24]{1,2,0:T(8,128)(2,1)S(1)}, u32[]{:S(2)}, u32[]{:S(2)}) collective-permute-start(bf16[4,2048,24]{1,2,0:T(8,128)(2,1)S(1)} %gather_fusion), channel_id=1, source_target_pairs={{0,12},{4,0},{8,4},{12,8},{1,13},{5,1},{9,5},{13,9},{2,14},{6,2},{... | collective-permute-start | bytes 1179656 | tf_op jit(solution)/shard_map/ppermute | solution.py:94
  19.7 12.3 %collective-permute-start.10 = (bf16[4,2048,24]{1,2,0:T(8,128)(2,1)S(1)}, bf16[4,2048,24]{1,2,0:T(8,128)(2,1)S(1)}, u32[]{:S(2)}, u32[]{:S(2)}) collective-permute-start(bf16[4,2048,24]{1,2,0:T(8,128)(2,1)S(1)} %gather_fusion.2), channel_id=1, source_target_pairs={{0,1},{1,2},{2,3},{3,0},{4,5},{5,6},{6,7},{7,4},{8,9},{9,10},{10,1... | collective-permute-start | bytes 1179656 | tf_op jit(solution)/shard_map/ppermute | solution.py:93
  19.8 13.0 %collective-permute-start.12 = (bf16[4,2048,24]{1,2,0:T(8,128)(2,1)S(1)}, bf16[4,2048,24]{1,2,0:T(8,128)(2,1)S(1)}, u32[]{:S(2)}, u32[]{:S(2)}) collective-permute-start(bf16[4,2048,24]{1,2,0:T(8,128)(2,1)S(1)} %gather_fusion.2), channel_id=1, source_target_pairs={{0,3},{1,0},{2,1},{3,2},{4,7},{5,4},{6,5},{7,6},{8,11},{9,8},{10,9... | collective-permute-start | bytes 1179656 | tf_op jit(solution)/shard_map/ppermute | solution.py:94
  26.0 10.7 %collective-permute-start.4 = (bf16[4,1024,24]{1,2,0:T(8,128)(2,1)S(1)}, bf16[4,1024,24]{1,2,0:T(8,128)(2,1)S(1)}, u32[]{:S(2)}, u32[]{:S(2)}) collective-permute-start(bf16[4,1024,24]{1,2,0:T(8,128)(2,1)S(1)} %slice.296), channel_id=1, source_target_pairs={{0,4},{4,8},{8,12},{12,0},{1,5},{5,9},{9,13},{13,1},{2,6},{6,10},{... | collective-permute-start | bytes 589832 | tf_op jit(solution)/shard_map/ppermute | solution.py:99
  26.1 10.6 %collective-permute-start.6 = (bf16[4,1024,24]{1,2,0:T(8,128)(2,1)S(1)}, bf16[4,1024,24]{1,2,0:T(8,128)(2,1)S(1)}, u32[]{:S(2)}, u32[]{:S(2)}) collective-permute-start(bf16[4,1024,24]{1,2,0:T(8,128)(2,1)S(1)} %slice.297), channel_id=1, source_target_pairs={{0,12},{4,0},{8,4},{12,8},{1,13},{5,1},{9,5},{13,9},{2,14},{6,2},{... | collective-permute-start | bytes 589832 | tf_op jit(solution)/shard_map/ppermute | solution.py:100
  32.7 7.2 %collective-permute-start.11 = (bf16[4,1024,24]{1,2,0:T(8,128)(2,1)}, bf16[4,1024,24]{1,2,0:T(8,128)(2,1)}, u32[]{:S(2)}, u32[]{:S(2)}) collective-permute-start(bf16[4,1024,24]{1,2,0:T(8,128)(2,1)} %slice.298), channel_id=1, source_target_pairs={{0,1},{1,2},{2,3},{3,0},{4,5},{5,6},{6,7},{7,4},{8,9},{9,10},{10,1... | collective-permute-start | bytes 589832 | tf_op jit(solution)/shard_map/ppermute | solution.py:99
  33.5 6.7 %collective-permute-start.13 = (bf16[4,1024,24]{1,2,0:T(8,128)(2,1)}, bf16[4,1024,24]{1,2,0:T(8,128)(2,1)}, u32[]{:S(2)}, u32[]{:S(2)}) collective-permute-start(bf16[4,1024,24]{1,2,0:T(8,128)(2,1)} %slice.299), channel_id=1, source_target_pairs={{0,3},{1,0},{2,1},{3,2},{4,7},{5,4},{6,5},{7,6},{8,11},{9,8},{10,9... | collective-permute-start | bytes 589832 | tf_op jit(solution)/shard_map/ppermute | solution.py:100
  60.0 6.4 %collective-permute-start.15 = (f32[2048]{0:T(1024)S(1)}, f32[2048]{0:T(1024)S(1)}, u32[]{:S(2)}, u32[]{:S(2)}) collective-permute-start(f32[2048]{0:T(1024)S(1)} %add.490), channel_id=1, source_target_pairs={{0,64},{32,96},{64,0},{96,32},{1,65},{33,97},{65,1},{97,33},{2,66}... | collective-permute-start | bytes 24584 | tf_op jit(solution)/shard_map/ppermute | solution.py:27
  63.2 4.9 %collective-permute-start.16 = (f32[2048]{0:T(1024)S(1)}, f32[2048]{0:T(1024)S(1)}, u32[]{:S(2)}, u32[]{:S(2)}) collective-permute-start(f32[2048]{0:T(1024)S(1)} %add.490), channel_id=1, source_target_pairs={{0,32},{32,64},{64,96},{96,0},{1,33},{33,65},{65,97},{97,1},{2,34}... | collective-permute-start | bytes 24584 | tf_op jit(solution)/shard_map/ppermute | solution.py:27
  63.9 4.2 %collective-permute-start.17 = (f32[2048]{0:T(1024)S(1)}, f32[2048]{0:T(1024)S(1)}, u32[]{:S(2)}, u32[]{:S(2)}) collective-permute-start(f32[2048]{0:T(1024)S(1)} %add.490), channel_id=1, source_target_pairs={{0,96},{32,0},{64,32},{96,64},{1,97},{33,1},{65,33},{97,65},{2,98}... | collective-permute-start | bytes 24584 | tf_op jit(solution)/shard_map/ppermute | solution.py:27
  94.8 1.3 collective-permute-start.18
  96.1 5.2 %collective-permute-start.19 = (f32[2048]{0:T(1024)S(1)}, f32[2048]{0:T(1024)S(1)}, u32[]{:S(2)}, u32[]{:S(2)}) collective-permute-start(f32[2048]{0:T(1024)S(1)} %add.510), channel_id=1, source_target_pairs={{0,64},{32,96},{64,0},{96,32},{1,65},{33,97},{65,1},{97,33},{2,66}... | collective-permute-start | bytes 24584 | tf_op jit(solution)/shard_map/ppermute | solution.py:27
  97.6 4.9 %collective-permute-start.20 = (f32[2048]{0:T(1024)S(1)}, f32[2048]{0:T(1024)S(1)}, u32[]{:S(2)}, u32[]{:S(2)}) collective-permute-start(f32[2048]{0:T(1024)S(1)} %add.510), channel_id=1, source_target_pairs={{0,32},{32,64},{64,96},{96,0},{1,33},{33,65},{65,97},{97,1},{2,34}... | collective-permute-start | bytes 24584 | tf_op jit(solution)/shard_map/ppermute | solution.py:27
  100.2 3.7 %collective-permute-start.21 = (f32[2048]{0:T(1024)S(1)}, f32[2048]{0:T(1024)S(1)}, u32[]{:S(2)}, u32[]{:S(2)}) collective-permute-start(f32[2048]{0:T(1024)S(1)} %add.510), channel_id=1, source_target_pairs={{0,96},{32,0},{64,32},{96,64},{1,97},{33,1},{65,33},{97,65},{2,98}... | collective-permute-start | bytes 24584 | tf_op jit(solution)/shard_map/ppermute | solution.py:27
  129.2 1.3 collective-permute-start.22
  130.4 5.2 %collective-permute-start.23 = (f32[2048]{0:T(1024)S(1)}, f32[2048]{0:T(1024)S(1)}, u32[]{:S(2)}, u32[]{:S(2)}) collective-permute-start(f32[2048]{0:T(1024)S(1)} %add.530), channel_id=1, source_target_pairs={{0,64},{32,96},{64,0},{96,32},{1,65},{33,97},{65,1},{97,33},{2,66}... | collective-permute-start | bytes 24584 | tf_op jit(solution)/shard_map/ppermute | solution.py:27
  131.0 4.9 %collective-permute-start.24 = (f32[2048]{0:T(1024)S(1)}, f32[2048]{0:T(1024)S(1)}, u32[]{:S(2)}, u32[]{:S(2)}) collective-permute-start(f32[2048]{0:T(1024)S(1)} %add.530), channel_id=1, source_target_pairs={{0,32},{32,64},{64,96},{96,0},{1,33},{33,65},{65,97},{97,1},{2,34}... | collective-permute-start | bytes 24584 | tf_op jit(solution)/shard_map/ppermute | solution.py:27
  133.1 3.7 %collective-permute-start.25 = (f32[2048]{0:T(1024)S(1)}, f32[2048]{0:T(1024)S(1)}, u32[]{:S(2)}, u32[]{:S(2)}) collective-permute-start(f32[2048]{0:T(1024)S(1)} %add.530), channel_id=1, source_target_pairs={{0,96},{32,0},{64,32},{96,64},{1,97},{33,1},{65,33},{97,65},{2,98}... | collective-permute-start | bytes 24584 | tf_op jit(solution)/shard_map/ppermute | solution.py:27
  144.6 11.4 %all-to-all-start.2 = ((f32[16,1,2048]{2,1,0:T(1,128)}), f32[16,1,2048]{2,1,0:T(1,128)S(1)}, u32[]{:S(2)}, u32[]{:S(2)}) async-start(f32[16,1,2048]{2,1,0:T(1,128)} %broadcast_in_dim.8), calls=%async_computation.2 | async-start | bytes 262144 | tf_op jit(solution)/shard_map/all_to_all | solution.py:44
  180.8 5.9 %collective-permute-start.26 = (f32[4,96,2048]{2,1,0:T(8,128)S(1)}, f32[4,96,2048]{2,1,0:T(8,128)}, u32[]{:S(2)}, u32[]{:S(2)}) collective-permute-start(f32[4,96,2048]{2,1,0:T(8,128)S(1)} %dynamic-slice_bitcast_fusion), channel_id=1, source_target_pairs={{0,16},{16,0},{1,17},{17,1},{2,18},{18,2},{3,19},{19,3},{4,20},{20... | collective-permute-start | bytes 9437192 | tf_op jit(solution)/shard_map/ppermute | solution.py:76
  191.9 42.1 %all-to-all-start.3 = ((f32[4,96,2048]{2,1,0:T(8,128)}), f32[4,96,2048]{2,1,0:T(8,128)S(1)}, u32[]{:S(2)}, u32[]{:S(2)}) async-start(f32[4,96,2048]{2,1,0:T(8,128)} %bitcast_add_fusion), calls=%async_computation.3 | async-start | bytes 6291456 | tf_op jit(solution)/shard_map/all_to_all | solution.py:81
  234.2 1.3 collective-permute-start.27
  235.5 5.4 %collective-permute-start.28 = (f32[2,2048]{1,0:T(2,128)S(1)}, f32[2,2048]{1,0:T(2,128)S(1)}, u32[]{:S(2)}, u32[]{:S(2)}) collective-permute-start(f32[2,2048]{1,0:T(2,128)S(1)} %fusion.21), channel_id=1, source_target_pairs={{0,64},{32,96},{64,0},{96,32},{1,65},{33,97},{65,1},{97,33},{2,66}... | collective-permute-start | bytes 49160 | tf_op jit(solution)/shard_map/ppermute | solution.py:27
  236.2 4.9 %collective-permute-start.29 = (f32[2,2048]{1,0:T(2,128)S(1)}, f32[2,2048]{1,0:T(2,128)S(1)}, u32[]{:S(2)}, u32[]{:S(2)}) collective-permute-start(f32[2,2048]{1,0:T(2,128)S(1)} %fusion.21), channel_id=1, source_target_pairs={{0,32},{32,64},{64,96},{96,0},{1,33},{33,65},{65,97},{97,1},{2,34}... | collective-permute-start | bytes 49160 | tf_op jit(solution)/shard_map/ppermute | solution.py:27
  237.6 3.7 %collective-permute-start.30 = (f32[2,2048]{1,0:T(2,128)S(1)}, f32[2,2048]{1,0:T(2,128)S(1)}, u32[]{:S(2)}, u32[]{:S(2)}) collective-permute-start(f32[2,2048]{1,0:T(2,128)S(1)} %fusion.21), channel_id=1, source_target_pairs={{0,96},{32,0},{64,32},{96,64},{1,97},{33,1},{65,33},{97,65},{2,98}... | collective-permute-start | bytes 49160 | tf_op jit(solution)/shard_map/ppermute | solution.py:27
  (6 other events, 43.7 us)

commit v10 on v9

--- a/solution.py
+++ b/solution.py
@@ -64,18 +64,29 @@
     )
 
 
+def own_first(point_rows, sizes):
+    ny, nc = sizes["y"], sizes["c"]
+    rows, width = point_rows.shape
+    if nc != 2:
+        return point_rows
+    blk = width // (ny * nc)
+    split = point_rows.reshape(rows, ny, nc, blk)
+    c = lax.axis_index("c")
+    keep = lax.dynamic_index_in_dim(split, c, 2, keepdims=False)
+    send = lax.dynamic_index_in_dim(split, 1 - c, 2, keepdims=False)
+    return jnp.stack([keep, send], axis=1).reshape(rows, width)
+
+
 def scatter_features(part_t, sizes):
     ny, nc = sizes["y"], sizes["c"]
     width, rows = part_t.shape
     blk = width // (ny * nc)
-    x = part_t.reshape(ny, nc, blk, rows)
     if nc == 2:
-        c = lax.axis_index("c")
-        keep = lax.dynamic_index_in_dim(x, c, 1, keepdims=False)
-        send = lax.dynamic_index_in_dim(x, 1 - c, 1, keepdims=False)
+        keep, send = part_t[: width // 2], part_t[width // 2 :]
         x = keep + lax.ppermute(send, "c", [(0, 1), (1, 0)])
     else:
-        x = x[:, 0]
+        x = part_t
+    x = x.reshape(ny, blk, rows)
     if ny == 1:
         return x[0]
     got = lax.all_to_all(x, "y", 0, 0, tiled=False)
@@ -155,9 +166,10 @@
         hi = hi_wide.astype(jnp.bfloat16)
         lo = (scaled - hi_wide).astype(jnp.bfloat16)
         dims = (((0,), (0,)), ((), ()))
+        ordered = own_first(gathered, sizes)
         partial_t = lax.dot_general(
-            gathered, hi, dims, preferred_element_type=jnp.float32
-        ) + lax.dot_general(gathered, lo, dims, preferred_element_type=jnp.float32)
+            ordered, hi, dims, preferred_element_type=jnp.float32
+        ) + lax.dot_general(ordered, lo, dims, preferred_element_type=jnp.float32)
         partial_t = partial_t * col_scale[None, :]
         mass_part = jnp.sum(scaled, axis=0) * col_scale / balance
         moved = scatter_features(partial_t, sizes).T

time: 244 us -> 250 us (1.025)
    ppermute x16, waiting for transfers between devices: 13.8 us -> 18.4 us  [axis_sum(): lax.ppermute(v, axis, [(i, (i + s) % n) for i in range(n)])]
    convert_element_type x0 -> x2, other arithmetic: none -> 3.59 us  [the longest x1 2.73 us: unit_rows(): wide = values.astype(jnp.float32)]
    add x1, other arithmetic: 5.24 us -> 2.13 us  [scatter_features(): x = keep + lax.ppermute(send, 'c', [(0, 1), (1, 0)])]
    ppermute x4, waiting for transfers between devices: 5.45 us -> 2.55 us  [ring_gather(): fwd = lax.ppermute(v, axis, [(i, (i + 1) % n) for i in range(n)])]
  transfers between devices with their start and end apart: 33 -> 33, of which waited for: 22 -> 19; matrix products, arithmetic and copies ran while one was open for 5% -> 7% of each run, Pallas kernels for 0% -> 0%
where the time goes in v10:
time: 250 us
  waiting for transfers between devices  71.2 us (28%)
  other arithmetic  57.8 us (23%)
  starting transfers between devices  47.6 us (19%)
  matrix products  36.4 us (15%)
  blocking collectives  24 us (10%)
  local copies, waits for them, and re-layouts  11.6 us (5%)
    all_to_all x1, waiting for transfers between devices, scatter_features(): got = lax.all_to_all(x, 'y', 0, 0, tiled=False)  30.9 us
    all_to_all x2, blocking collectives, group_sum(): lax.all_to_all(jnp.broadcast_to(v[None], (n,) + v.shape), axes, 0, 0, til...  24 us
    reduce_sum x3, other arithmetic, local(): row_part = jnp.sum(kernel * col_scale[None, :], axis=1)  21.1 us
    ppermute x16, waiting for transfers between devices, axis_sum(): lax.ppermute(v, axis, [(i, (i + s) % n) for i in range(n)])  18.4 us
    ppermute x16, starting transfers between devices, axis_sum(): lax.ppermute(v, axis, [(i, (i + s) % n) for i in range(n)])  18.2 us
    reduce_sum x2, other arithmetic, local(): col_part = jnp.sum(kernel * row_scale[:, None], axis=0)  14 us
    dot_general x1, matrix products, local(): lax.dot_general(ordered, lo, dims, preferred_element_type=jnp.float32)  13.2 us
    dot_general x1, matrix products, local(): jnp.dot(unit_points, unit_centroids.T, preferred_element_type=jnp.float32)  11.8 us
  transfers between devices with their start and end apart: 33, of which 19 were waited for; matrix products, arithmetic and copies ran while one was open for 7% of the time, Pallas kernels for 0%

profile of v10, /device:TPU:0, one launch (start us, length us, event | category | flops | bytes accessed | tf_op | source)
XLA Modules:
  0.0 249.5 jit_solution(18278922534366778628)
XLA Ops:
  9.1 2.5 %collective-permute-done = bf16[2048,24]{0,1:T(8,128)(2,1)S(1)} collective-permute-done((bf16[2048,24]{0,1:T(8,128)(2,1)S(1)}, bf16[2048,24]{0,1:T(8,128)(2,1)S(1)}, u32[]{:S(2)}, u32[]{:S(2)}) %collective-permute-start) | collective-permute-done | bytes 98336 | tf_op jit(solution)/shard_map/ppermute | solution.py:104
  12.0 5.5 %collective-permute-done.1 = bf16[2048,24]{0,1:T(8,128)(2,1)S(1)} collective-permute-done((bf16[2048,24]{0,1:T(8,128)(2,1)S(1)}, bf16[2048,24]{0,1:T(8,128)(2,1)S(1)}, u32[]{:S(2)}, u32[]{:S(2)}) %collective-permute-start.1) | collective-permute-done | bytes 98336 | tf_op jit(solution)/shard_map/ppermute | solution.py:116
  18.5 3.0 %collective-permute-start.5 = (bf16[4,2048,24]{1,2,0:T(8,128)(2,1)S(1)}, bf16[4,2048,24]{1,2,0:T(8,128)(2,1)S(1)}, u32[]{:S(2)}, u32[]{:S(2)}) collective-permute-start(bf16[4,2048,24]{1,2,0:T(8,128)(2,1)S(1)} %gather_fusion), channel_id=1, source_target_pairs={{0,12},{4,0},{8,4},{12,8},{1,13},{5,1},{9,5},{13,9},{2,14},{6,2},{... | collective-permute-start | bytes 1179656 | tf_op jit(solution)/shard_map/ppermute | solution.py:105
  22.2 3.2 %collective-permute-start.12 = (bf16[4,2048,24]{1,2,0:T(8,128)(2,1)S(1)}, bf16[4,2048,24]{1,2,0:T(8,128)(2,1)S(1)}, u32[]{:S(2)}, u32[]{:S(2)}) collective-permute-start(bf16[4,2048,24]{1,2,0:T(8,128)(2,1)S(1)} %gather_fusion.2), channel_id=1, source_target_pairs={{0,3},{1,0},{2,1},{3,2},{4,7},{5,4},{6,5},{7,6},{8,11},{9,8},{10,9... | collective-permute-start | bytes 1179656 | tf_op jit(solution)/shard_map/ppermute | solution.py:105
  25.4 2.6 %fusion.6 = f32[2048]{0:T(1024)S(1)} fusion(bf16[2048,768]{1,0:T(8,128)(2,1)} %param.3), kind=kLoop, calls=%fused_computation.20 | loop fusion | flops 4716544 | bytes 3153920 | tf_op jit(solution)/shard_map/reduce_sum | solution.py:18
  28.1 3.3 %collective-permute-start.6 = (bf16[4,1024,24]{1,2,0:T(8,128)(2,1)S(1)}, bf16[4,1024,24]{1,2,0:T(8,128)(2,1)S(1)}, u32[]{:S(2)}, u32[]{:S(2)}) collective-permute-start(bf16[4,1024,24]{1,2,0:T(8,128)(2,1)S(1)} %slice.305), channel_id=1, source_target_pairs={{0,12},{4,0},{8,4},{12,8},{1,13},{5,1},{9,5},{13,9},{2,14},{6,2},{... | collective-permute-start | bytes 589832 | tf_op jit(solution)/shard_map/ppermute | solution.py:111
  32.9 3.2 %collective-permute-start.13 = (bf16[4,1024,24]{1,2,0:T(8,128)(2,1)}, bf16[4,1024,24]{1,2,0:T(8,128)(2,1)}, u32[]{:S(2)}, u32[]{:S(2)}) collective-permute-start(bf16[4,1024,24]{1,2,0:T(8,128)(2,1)} %slice.307), channel_id=1, source_target_pairs={{0,3},{1,0},{2,1},{3,2},{4,7},{5,4},{6,5},{7,6},{8,11},{9,8},{10,9... | collective-permute-start | bytes 589832 | tf_op jit(solution)/shard_map/ppermute | solution.py:111
  37.1 2.3 collective-permute-done.11
  46.0 2.7 %bitcast_convert_fusion = (f32[2048,4,4,48]{0,3,2,1:T(8,128)S(1)}, bf16[4,4,2048,48]{2,3,1,0:T(8,128)(2,1)}) fusion(bf16[4,4,2048,24]{2,3,1,0:T(8,128)(2,1)S(1)} %bitcast.61, bf16[4,4,2048,24]{2,3,1,0:T(8,128)(2,1)S(1)} %gather_fusion.1), kind=kLoop, calls=%fused_computation.29 | loop fusion | flops 7864320 | bytes 12582912 | tf_op jit(solution)/shard_map/convert_element_type | solution.py:17
  50.7 11.8 %fusion.24 = (f32[2048]{0:T(1024)S(1)}, f32[2048,2048]{1,0:T(8,128)}) fusion(bf16[2048,768]{0,1:T(8,128)(2,1)S(1)} %fusion.8, bf16[2048,768]{1,0:T(8,128)(2,1)S(1)} %copy-done.3, f32[2048]{0:T(1024)S(1)} %add_rsqrt_fusion), kind=kOutput, calls=%fused_computation.123 | convolution fusion | flops 6455556096 | bytes 23085056 | tf_op jit(solution)/shard_map/dot_general | solution.py:157
  63.6 3.0 %collective-permute-start.17 = (f32[2048]{0:T(1024)S(1)}, f32[2048]{0:T(1024)S(1)}, u32[]{:S(2)}, u32[]{:S(2)}) collective-permute-start(f32[2048]{0:T(1024)S(1)} %add.492), channel_id=1, source_target_pairs={{0,96},{32,0},{64,32},{96,64},{1,97},{33,1},{65,33},{97,65},{2,98}... | collective-permute-start | bytes 24584 | tf_op jit(solution)/shard_map/ppermute | solution.py:27
  68.8 2.7 %collective-permute-done.16 = f32[2048]{0:T(1024)S(1)} collective-permute-done((f32[2048]{0:T(1024)S(1)}, f32[2048]{0:T(1024)S(1)}, u32[]{:S(2)}, u32[]{:S(2)}) %collective-permute-start.16) | collective-permute-done | bytes 8224 | tf_op jit(solution)/shard_map/ppermute | solution.py:27
  71.8 7.0 %multiply_reduce_fusion.4 = f32[2048]{0:T(1024)S(1)} fusion(f32[2048,2048]{1,0:T(8,128)} %get-tuple-element.15, f32[2048]{0:T(1024)S(1)} %add_divide_fusion.2), kind=kLoop, calls=%fused_computation.11 | loop fusion | flops 8386560 | bytes 16793600 | tf_op jit(solution)/shard_map/reduce_sum | solution.py:162
  78.9 12.7 %all_to_all.23 = f32[16,1,2048]{2,1,0:T(1,128)S(1)} all-to-all(f32[16,1,2048]{2,1,0:T(1,128)S(1)} %broadcast_in_dim.6), channel_id=1, replica_groups=mesh['y'=4,'c'=2,'x'=4,'z'=4] {'x','z'}, dimensions={0} | all-to-all | bytes 262144 | tf_op jit(solution)/shard_map/all_to_all | solution.py:44
  91.7 6.9 %multiply_reduce_fusion.3 = f32[2048]{0:T(1024)S(1)} fusion(f32[2048,2048]{1,0:T(8,128)} %get-tuple-element.15, f32[2048]{0:T(1024)S(1)} %bitcast.85), kind=kLoop, calls=%fused_computation.10 | loop fusion | flops 8386560 | bytes 16793600 | tf_op jit(solution)/shard_map/reduce_sum | solution.py:160
  99.9 3.2 %collective-permute-start.21 = (f32[2048]{0:T(1024)S(1)}, f32[2048]{0:T(1024)S(1)}, u32[]{:S(2)}, u32[]{:S(2)}) collective-permute-start(f32[2048]{0:T(1024)S(1)} %add.512), channel_id=1, source_target_pairs={{0,96},{32,0},{64,32},{96,64},{1,97},{33,1},{65,33},{97,65},{2,98}... | collective-permute-start | bytes 24584 | tf_op jit(solution)/shard_map/ppermute | solution.py:27
  104.6 3.4 %collective-permute-done.20 = f32[2048]{0:T(1024)S(1)} collective-permute-done((f32[2048]{0:T(1024)S(1)}, f32[2048]{0:T(1024)S(1)}, u32[]{:S(2)}, u32[]{:S(2)}) %collective-permute-start.20) | collective-permute-done | bytes 8224 | tf_op jit(solution)/shard_map/ppermute | solution.py:27
  108.3 7.0 %multiply_reduce_fusion.2 = f32[2048]{0:T(1024)S(1)} fusion(f32[2048,2048]{1,0:T(8,128)} %get-tuple-element.15, f32[2048]{0:T(1024)S(1)} %add_divide_fusion.1), kind=kLoop, calls=%fused_computation.9 | loop fusion | flops 8386560 | bytes 16793600 | tf_op jit(solution)/shard_map/reduce_sum | solution.py:162
  115.3 11.2 %all_to_all.24 = f32[16,1,2048]{2,1,0:T(1,128)S(1)} all-to-all(f32[16,1,2048]{2,1,0:T(1,128)S(1)} %broadcast_in_dim.7), channel_id=1, replica_groups=mesh['y'=4,'c'=2,'x'=4,'z'=4] {'x','z'}, dimensions={0} | all-to-all | bytes 262144 | tf_op jit(solution)/shard_map/all_to_all | solution.py:44
  126.6 7.1 %multiply_reduce_fusion.1 = f32[2048]{0:T(1024)S(1)} fusion(f32[2048,2048]{1,0:T(8,128)} %get-tuple-element.15, f32[2048]{0:T(1024)S(1)} %bitcast.86), kind=kLoop, calls=%fused_computation.8 | loop fusion | flops 8386560 | bytes 16793600 | tf_op jit(solution)/shard_map/reduce_sum | solution.py:160
  135.0 3.2 %collective-permute-start.25 = (f32[2048]{0:T(1024)S(1)}, f32[2048]{0:T(1024)S(1)}, u32[]{:S(2)}, u32[]{:S(2)}) collective-permute-start(f32[2048]{0:T(1024)S(1)} %add.532), channel_id=1, source_target_pairs={{0,96},{32,0},{64,32},{96,64},{1,97},{33,1},{65,33},{97,65},{2,98}... | collective-permute-start | bytes 24584 | tf_op jit(solution)/shard_map/ppermute | solution.py:27
  143.4 7.1 %multiply_reduce_fusion = f32[2048]{0:T(1024)S(1)} fusion(f32[2048,2048]{1,0:T(8,128)} %get-tuple-element.15, f32[2048]{0:T(1024)S(1)} %add_divide_fusion), kind=kLoop, calls=%fused_computation.7 | loop fusion | flops 8386560 | bytes 16793600 | tf_op jit(solution)/shard_map/reduce_sum | solution.py:162
  151.2 3.8 %all-to-all-start.2 = ((f32[16,1,2048]{2,1,0:T(1,128)}), f32[16,1,2048]{2,1,0:T(1,128)S(1)}, u32[]{:S(2)}, u32[]{:S(2)}) async-start(f32[16,1,2048]{2,1,0:T(1,128)} %broadcast_in_dim.8), calls=%async_computation.2 | async-start | bytes 262144 | tf_op jit(solution)/shard_map/all_to_all | solution.py:44
  157.0 5.7 %all-to-all-done.2 = f32[16,1,2048]{2,1,0:T(1,128)S(1)} async-done(((f32[16,1,2048]{2,1,0:T(1,128)}), f32[16,1,2048]{2,1,0:T(1,128)S(1)}, u32[]{:S(2)}, u32[]{:S(2)}) %all-to-all-start.2) | async-done | bytes 131104 | tf_op jit(solution)/shard_map/all_to_all | solution.py:44
  162.8 13.2 %fusion.1 = f32[768,2048]{1,0:T(8,128)} fusion(bf16[2048,768]{0,1:T(8,128)(2,1)} %bitcast.64, f32[2048,2048]{1,0:T(8,128)} %get-tuple-element.15, f32[2048]{0:T(1024)S(1)} %bitcast.82), kind=kOutput, calls=%fused_computation.14 | convolution fusion | flops 6459228160 | bytes 26222592 | tf_op jit(solution)/shard_map/dot_general | solution.py:172
  176.0 11.4 %add_multiply_fusion = f32[768,2048]{1,0:T(8,128)S(1)} fusion(f32[768,2048]{1,0:T(8,128)} %fusion.1, f32[2048]{0:T(1024)S(1)} %add_divide_fusion, bf16[2048,768]{0,1:T(8,128)(2,1)S(1)} %bitcast.65, f32[2048,2048]{1,0:T(8,128)} %get-tuple-element.15, f32[2048]{0:T(1024)S(1)} %bitcast.83), kind=kOutput, calls=%fused_computation.24 | convolution fusion | flops 6458179584 | bytes 32522240 | tf_op jit(solution)/shard_map/dot_general | solution.py:170
  187.7 5.6 %collective-permute-done.26 = f32[384,2048]{1,0:T(8,128)S(1)} collective-permute-done((f32[384,2048]{1,0:T(8,128)S(1)}, f32[384,2048]{1,0:T(8,128)S(1)}, u32[]{:S(2)}, u32[]{:S(2)}) %collective-permute-start.26) | collective-permute-done | bytes 3145760 | tf_op jit(solution)/shard_map/ppermute | solution.py:86
  195.4 4.5 %all-to-all-start.3 = ((f32[4,96,2048]{2,1,0:T(8,128)}), f32[4,96,2048]{2,1,0:T(8,128)S(1)}, u32[]{:S(2)}, u32[]{:S(2)}) async-start(f32[4,96,2048]{2,1,0:T(8,128)} %bitcast.62), calls=%async_computation.3 | async-start | bytes 6291456 | tf_op jit(solution)/shard_map/all_to_all | solution.py:92
  199.9 6.9 %multiply_reduce_fusion.5 = f32[2048]{0:T(1024)S(1)} fusion(f32[2048,2048]{1,0:T(8,128)} %get-tuple-element.15, f32[2048]{0:T(1024)S(1)} %bitcast.84), kind=kLoop, calls=%fused_computation.13 | loop fusion | flops 8386560 | bytes 16793600 | tf_op jit(solution)/shard_map/reduce_sum | solution.py:174
  206.9 30.9 %all-to-all-done.3 = f32[4,96,2048]{2,1,0:T(8,128)S(1)} async-done(((f32[4,96,2048]{2,1,0:T(8,128)}), f32[4,96,2048]{2,1,0:T(8,128)S(1)}, u32[]{:S(2)}, u32[]{:S(2)}) %all-to-all-start.3) | async-done | bytes 3145760 | tf_op jit(solution)/shard_map/all_to_all | solution.py:92
  240.0 2.7 %collective-permute-start.30 = (f32[2,2048]{1,0:T(2,128)S(1)}, f32[2,2048]{1,0:T(2,128)S(1)}, u32[]{:S(2)}, u32[]{:S(2)}) collective-permute-start(f32[2,2048]{1,0:T(2,128)S(1)} %fusion.21), channel_id=1, source_target_pairs={{0,96},{32,0},{64,32},{96,64},{1,97},{33,1},{65,33},{97,65},{2,98}... | collective-permute-start | bytes 49160 | tf_op jit(solution)/shard_map/ppermute | solution.py:27
  244.4 3.5 %collective-permute-done.28 = f32[2,2048]{1,0:T(2,128)S(1)} collective-permute-done((f32[2,2048]{1,0:T(2,128)S(1)}, f32[2,2048]{1,0:T(2,128)S(1)}, u32[]{:S(2)}, u32[]{:S(2)}) %collective-permute-start.28) | collective-permute-done | bytes 16416 | tf_op jit(solution)/shard_map/ppermute | solution.py:27
  (108 shorter events, 45.6 us)
Async XLA Ops:
  1.6 10.1 %collective-permute-start.7 = (bf16[2048,24]{0,1:T(8,128)(2,1)S(1)}, bf16[2048,24]{0,1:T(8,128)(2,1)S(1)}, u32[]{:S(2)}, u32[]{:S(2)}) collective-permute-start(bf16[2048,24]{0,1:T(8,128)(2,1)S(1)} %get-tuple-element.10), channel_id=1, source_target_pairs={{0,4},{4,8},{8,12},{12,0},{1,5},{5,9},{9,13},{13,1},{2,6},{6,10},{... | collective-permute-start | bytes 294920 | tf_op jit(solution)/shard_map/ppermute | solution.py:104
  3.3 18.1 %collective-permute-start.9 = (bf16[2048,24]{0,1:T(8,128)(2,1)S(1)}, bf16[2048,24]{0,1:T(8,128)(2,1)S(1)}, u32[]{:S(2)}, u32[]{:S(2)}) collective-permute-start(bf16[2048,24]{0,1:T(8,128)(2,1)S(1)} %get-tuple-element.10), channel_id=1, source_target_pairs={{0,12},{4,0},{8,4},{12,8},{1,13},{5,1},{9,5},{13,9},{2,14},{6,2},{... | collective-permute-start | bytes 294920 | tf_op jit(solution)/shard_map/ppermute | solution.py:105
  4.9 6.7 %collective-permute-start = (bf16[2048,24]{0,1:T(8,128)(2,1)S(1)}, bf16[2048,24]{0,1:T(8,128)(2,1)S(1)}, u32[]{:S(2)}, u32[]{:S(2)}) collective-permute-start(bf16[2048,24]{0,1:T(8,128)(2,1)S(1)} %get-tuple-element.11), channel_id=1, source_target_pairs={{0,1},{1,2},{2,3},{3,0},{4,5},{5,6},{6,7},{7,4},{8,9},{9,10},{10,1... | collective-permute-start | bytes 294920 | tf_op jit(solution)/shard_map/ppermute | solution.py:104
  6.9 5.1 %collective-permute-start.2 = (bf16[2048,24]{0,1:T(8,128)(2,1)S(1)}, bf16[2048,24]{0,1:T(8,128)(2,1)S(1)}, u32[]{:S(2)}, u32[]{:S(2)}) collective-permute-start(bf16[2048,24]{0,1:T(8,128)(2,1)S(1)} %get-tuple-element.11), channel_id=1, source_target_pairs={{0,3},{1,0},{2,1},{3,2},{4,7},{5,4},{6,5},{7,6},{8,11},{9,8},{10,9... | collective-permute-start | bytes 294920 | tf_op jit(solution)/shard_map/ppermute | solution.py:105
  11.7 5.8 %collective-permute-start.1 = (bf16[2048,24]{0,1:T(8,128)(2,1)S(1)}, bf16[2048,24]{0,1:T(8,128)(2,1)S(1)}, u32[]{:S(2)}, u32[]{:S(2)}) collective-permute-start(bf16[2048,24]{0,1:T(8,128)(2,1)S(1)} %collective-permute-done), channel_id=1, source_target_pairs={{0,1},{1,2},{2,3},{3,0},{4,5},{5,6},{6,7},{7,4},{8,9},{9,10},{10,1... | collective-permute-start | bytes 294920 | tf_op jit(solution)/shard_map/ppermute | solution.py:116
  11.7 9.8 %collective-permute-start.8 = (bf16[2048,24]{0,1:T(8,128)(2,1)S(1)}, bf16[2048,24]{0,1:T(8,128)(2,1)S(1)}, u32[]{:S(2)}, u32[]{:S(2)}) collective-permute-start(bf16[2048,24]{0,1:T(8,128)(2,1)S(1)} %collective-permute-done.7), channel_id=1, source_target_pairs={{0,4},{4,8},{8,12},{12,0},{1,5},{5,9},{9,13},{13,1},{2,6},{6,10},{... | collective-permute-start | bytes 294920 | tf_op jit(solution)/shard_map/ppermute | solution.py:116
  18.1 9.8 %collective-permute-start.3 = (bf16[4,2048,24]{1,2,0:T(8,128)(2,1)S(1)}, bf16[4,2048,24]{1,2,0:T(8,128)(2,1)S(1)}, u32[]{:S(2)}, u32[]{:S(2)}) collective-permute-start(bf16[4,2048,24]{1,2,0:T(8,128)(2,1)S(1)} %gather_fusion), channel_id=1, source_target_pairs={{0,4},{4,8},{8,12},{12,0},{1,5},{5,9},{9,13},{13,1},{2,6},{6,10},{... | collective-permute-start | bytes 1179656 | tf_op jit(solution)/shard_map/ppermute | solution.py:104
  18.5 9.6 %collective-permute-start.5 = (bf16[4,2048,24]{1,2,0:T(8,128)(2,1)S(1)}, bf16[4,2048,24]{1,2,0:T(8,128)(2,1)S(1)}, u32[]{:S(2)}, u32[]{:S(2)}) collective-permute-start(bf16[4,2048,24]{1,2,0:T(8,128)(2,1)S(1)} %gather_fusion), channel_id=1, source_target_pairs={{0,12},{4,0},{8,4},{12,8},{1,13},{5,1},{9,5},{13,9},{2,14},{6,2},{... | collective-permute-start | bytes 1179656 | tf_op jit(solution)/shard_map/ppermute | solution.py:105
  22.1 9.3 %collective-permute-start.10 = (bf16[4,2048,24]{1,2,0:T(8,128)(2,1)S(1)}, bf16[4,2048,24]{1,2,0:T(8,128)(2,1)S(1)}, u32[]{:S(2)}, u32[]{:S(2)}) collective-permute-start(bf16[4,2048,24]{1,2,0:T(8,128)(2,1)S(1)} %gather_fusion.2), channel_id=1, source_target_pairs={{0,1},{1,2},{2,3},{3,0},{4,5},{5,6},{6,7},{7,4},{8,9},{9,10},{10,1... | collective-permute-start | bytes 1179656 | tf_op jit(solution)/shard_map/ppermute | solution.py:104
  22.2 10.0 %collective-permute-start.12 = (bf16[4,2048,24]{1,2,0:T(8,128)(2,1)S(1)}, bf16[4,2048,24]{1,2,0:T(8,128)(2,1)S(1)}, u32[]{:S(2)}, u32[]{:S(2)}) collective-permute-start(bf16[4,2048,24]{1,2,0:T(8,128)(2,1)S(1)} %gather_fusion.2), channel_id=1, source_target_pairs={{0,3},{1,0},{2,1},{3,2},{4,7},{5,4},{6,5},{7,6},{8,11},{9,8},{10,9... | collective-permute-start | bytes 1179656 | tf_op jit(solution)/shard_map/ppermute | solution.py:105
  28.0 8.2 %collective-permute-start.4 = (bf16[4,1024,24]{1,2,0:T(8,128)(2,1)S(1)}, bf16[4,1024,24]{1,2,0:T(8,128)(2,1)S(1)}, u32[]{:S(2)}, u32[]{:S(2)}) collective-permute-start(bf16[4,1024,24]{1,2,0:T(8,128)(2,1)S(1)} %slice.304), channel_id=1, source_target_pairs={{0,4},{4,8},{8,12},{12,0},{1,5},{5,9},{9,13},{13,1},{2,6},{6,10},{... | collective-permute-start | bytes 589832 | tf_op jit(solution)/shard_map/ppermute | solution.py:110
  28.1 8.0 %collective-permute-start.6 = (bf16[4,1024,24]{1,2,0:T(8,128)(2,1)S(1)}, bf16[4,1024,24]{1,2,0:T(8,128)(2,1)S(1)}, u32[]{:S(2)}, u32[]{:S(2)}) collective-permute-start(bf16[4,1024,24]{1,2,0:T(8,128)(2,1)S(1)} %slice.305), channel_id=1, source_target_pairs={{0,12},{4,0},{8,4},{12,8},{1,13},{5,1},{9,5},{13,9},{2,14},{6,2},{... | collective-permute-start | bytes 589832 | tf_op jit(solution)/shard_map/ppermute | solution.py:111
  32.1 7.2 %collective-permute-start.11 = (bf16[4,1024,24]{1,2,0:T(8,128)(2,1)}, bf16[4,1024,24]{1,2,0:T(8,128)(2,1)}, u32[]{:S(2)}, u32[]{:S(2)}) collective-permute-start(bf16[4,1024,24]{1,2,0:T(8,128)(2,1)} %slice.306), channel_id=1, source_target_pairs={{0,1},{1,2},{2,3},{3,0},{4,5},{5,6},{6,7},{7,4},{8,9},{9,10},{10,1... | collective-permute-start | bytes 589832 | tf_op jit(solution)/shard_map/ppermute | solution.py:110
  32.9 6.7 %collective-permute-start.13 = (bf16[4,1024,24]{1,2,0:T(8,128)(2,1)}, bf16[4,1024,24]{1,2,0:T(8,128)(2,1)}, u32[]{:S(2)}, u32[]{:S(2)}) collective-permute-start(bf16[4,1024,24]{1,2,0:T(8,128)(2,1)} %slice.307), channel_id=1, source_target_pairs={{0,3},{1,0},{2,1},{3,2},{4,7},{5,4},{6,5},{7,6},{8,11},{9,8},{10,9... | collective-permute-start | bytes 589832 | tf_op jit(solution)/shard_map/ppermute | solution.py:111
  63.6 5.2 %collective-permute-start.17 = (f32[2048]{0:T(1024)S(1)}, f32[2048]{0:T(1024)S(1)}, u32[]{:S(2)}, u32[]{:S(2)}) collective-permute-start(f32[2048]{0:T(1024)S(1)} %add.492), channel_id=1, source_target_pairs={{0,96},{32,0},{64,32},{96,64},{1,97},{33,1},{65,33},{97,65},{2,98}... | collective-permute-start | bytes 24584 | tf_op jit(solution)/shard_map/ppermute | solution.py:27
  66.6 4.9 %collective-permute-start.16 = (f32[2048]{0:T(1024)S(1)}, f32[2048]{0:T(1024)S(1)}, u32[]{:S(2)}, u32[]{:S(2)}) collective-permute-start(f32[2048]{0:T(1024)S(1)} %add.492), channel_id=1, source_target_pairs={{0,32},{32,64},{64,96},{96,0},{1,33},{33,65},{65,97},{97,1},{2,34}... | collective-permute-start | bytes 24584 | tf_op jit(solution)/shard_map/ppermute | solution.py:27
  66.6 5.2 %collective-permute-start.15 = (f32[2048]{0:T(1024)S(1)}, f32[2048]{0:T(1024)S(1)}, u32[]{:S(2)}, u32[]{:S(2)}) collective-permute-start(f32[2048]{0:T(1024)S(1)} %add.492), channel_id=1, source_target_pairs={{0,64},{32,96},{64,0},{96,32},{1,65},{33,97},{65,1},{97,33},{2,66}... | collective-permute-start | bytes 24584 | tf_op jit(solution)/shard_map/ppermute | solution.py:27
  98.6 1.3 collective-permute-start.18
  99.9 4.7 %collective-permute-start.21 = (f32[2048]{0:T(1024)S(1)}, f32[2048]{0:T(1024)S(1)}, u32[]{:S(2)}, u32[]{:S(2)}) collective-permute-start(f32[2048]{0:T(1024)S(1)} %add.512), channel_id=1, source_target_pairs={{0,96},{32,0},{64,32},{96,64},{1,97},{33,1},{65,33},{97,65},{2,98}... | collective-permute-start | bytes 24584 | tf_op jit(solution)/shard_map/ppermute | solution.py:27
  103.1 4.9 %collective-permute-start.20 = (f32[2048]{0:T(1024)S(1)}, f32[2048]{0:T(1024)S(1)}, u32[]{:S(2)}, u32[]{:S(2)}) collective-permute-start(f32[2048]{0:T(1024)S(1)} %add.512), channel_id=1, source_target_pairs={{0,32},{32,64},{64,96},{96,0},{1,33},{33,65},{65,97},{97,1},{2,34}... | collective-permute-start | bytes 24584 | tf_op jit(solution)/shard_map/ppermute | solution.py:27
  103.1 5.2 %collective-permute-start.19 = (f32[2048]{0:T(1024)S(1)}, f32[2048]{0:T(1024)S(1)}, u32[]{:S(2)}, u32[]{:S(2)}) collective-permute-start(f32[2048]{0:T(1024)S(1)} %add.512), channel_id=1, source_target_pairs={{0,64},{32,96},{64,0},{96,32},{1,65},{33,97},{65,1},{97,33},{2,66}... | collective-permute-start | bytes 24584 | tf_op jit(solution)/shard_map/ppermute | solution.py:27
  133.7 1.3 collective-permute-start.22
  135.0 6.6 %collective-permute-start.25 = (f32[2048]{0:T(1024)S(1)}, f32[2048]{0:T(1024)S(1)}, u32[]{:S(2)}, u32[]{:S(2)}) collective-permute-start(f32[2048]{0:T(1024)S(1)} %add.532), channel_id=1, source_target_pairs={{0,96},{32,0},{64,32},{96,64},{1,97},{33,1},{65,33},{97,65},{2,98}... | collective-permute-start | bytes 24584 | tf_op jit(solution)/shard_map/ppermute | solution.py:27
  138.2 4.9 %collective-permute-start.24 = (f32[2048]{0:T(1024)S(1)}, f32[2048]{0:T(1024)S(1)}, u32[]{:S(2)}, u32[]{:S(2)}) collective-permute-start(f32[2048]{0:T(1024)S(1)} %add.532), channel_id=1, source_target_pairs={{0,32},{32,64},{64,96},{96,0},{1,33},{33,65},{65,97},{97,1},{2,34}... | collective-permute-start | bytes 24584 | tf_op jit(solution)/shard_map/ppermute | solution.py:27
  138.2 5.2 %collective-permute-start.23 = (f32[2048]{0:T(1024)S(1)}, f32[2048]{0:T(1024)S(1)}, u32[]{:S(2)}, u32[]{:S(2)}) collective-permute-start(f32[2048]{0:T(1024)S(1)} %add.532), channel_id=1, source_target_pairs={{0,64},{32,96},{64,0},{96,32},{1,65},{33,97},{65,1},{97,33},{2,66}... | collective-permute-start | bytes 24584 | tf_op jit(solution)/shard_map/ppermute | solution.py:27
  151.2 11.4 %all-to-all-start.2 = ((f32[16,1,2048]{2,1,0:T(1,128)}), f32[16,1,2048]{2,1,0:T(1,128)S(1)}, u32[]{:S(2)}, u32[]{:S(2)}) async-start(f32[16,1,2048]{2,1,0:T(1,128)} %broadcast_in_dim.8), calls=%async_computation.2 | async-start | bytes 262144 | tf_op jit(solution)/shard_map/all_to_all | solution.py:44
  187.6 5.7 %collective-permute-start.26 = (f32[384,2048]{1,0:T(8,128)S(1)}, f32[384,2048]{1,0:T(8,128)S(1)}, u32[]{:S(2)}, u32[]{:S(2)}) collective-permute-start(f32[384,2048]{1,0:T(8,128)S(1)} %slice.357), channel_id=1, source_target_pairs={{0,16},{16,0},{1,17},{17,1},{2,18},{18,2},{3,19},{19,3},{4,20},{20... | collective-permute-start | bytes 9437192 | tf_op jit(solution)/shard_map/ppermute | solution.py:86
  195.4 42.4 %all-to-all-start.3 = ((f32[4,96,2048]{2,1,0:T(8,128)}), f32[4,96,2048]{2,1,0:T(8,128)S(1)}, u32[]{:S(2)}, u32[]{:S(2)}) async-start(f32[4,96,2048]{2,1,0:T(8,128)} %bitcast.62), calls=%async_computation.3 | async-start | bytes 6291456 | tf_op jit(solution)/shard_map/all_to_all | solution.py:92
  238.1 1.3 collective-permute-start.27
  239.3 5.0 %collective-permute-start.29 = (f32[2,2048]{1,0:T(2,128)S(1)}, f32[2,2048]{1,0:T(2,128)S(1)}, u32[]{:S(2)}, u32[]{:S(2)}) collective-permute-start(f32[2,2048]{1,0:T(2,128)S(1)} %fusion.21), channel_id=1, source_target_pairs={{0,32},{32,64},{64,96},{96,0},{1,33},{33,65},{65,97},{97,1},{2,34}... | collective-permute-start | bytes 49160 | tf_op jit(solution)/shard_map/ppermute | solution.py:27
  240.0 4.4 %collective-permute-start.30 = (f32[2,2048]{1,0:T(2,128)S(1)}, f32[2,2048]{1,0:T(2,128)S(1)}, u32[]{:S(2)}, u32[]{:S(2)}) collective-permute-start(f32[2,2048]{1,0:T(2,128)S(1)} %fusion.21), channel_id=1, source_target_pairs={{0,96},{32,0},{64,32},{96,64},{1,97},{33,1},{65,33},{97,65},{2,98}... | collective-permute-start | bytes 49160 | tf_op jit(solution)/shard_map/ppermute | solution.py:27
  242.7 5.2 %collective-permute-start.28 = (f32[2,2048]{1,0:T(2,128)S(1)}, f32[2,2048]{1,0:T(2,128)S(1)}, u32[]{:S(2)}, u32[]{:S(2)}) collective-permute-start(f32[2,2048]{1,0:T(2,128)S(1)} %fusion.21), channel_id=1, source_target_pairs={{0,64},{32,96},{64,0},{96,32},{1,65},{33,97},{65,1},{97,33},{2,66}... | collective-permute-start | bytes 49160 | tf_op jit(solution)/shard_map/ppermute | solution.py:27
  (8 other events, 61.4 us)

commit v11 on v9

--- a/solution.py
+++ b/solution.py
@@ -121,8 +121,8 @@
     part_a, part_b = points[:, : blk // 2], points[:, blk // 2 :]
     a_z = ring_gather(part_a, "z", nz, split_far=False)
     b_x = ring_gather(part_b, "x", nx, split_far=False)
-    a_xz = ring_gather(a_z, "x", nx)
-    b_zx = ring_gather(b_x, "z", nz)
+    a_xz = ring_gather(a_z, "x", nx, split_far=False)
+    b_zx = ring_gather(b_x, "z", nz, split_far=False)
     full = jnp.concatenate([a_xz, jnp.transpose(b_zx, (1, 0, 2, 3))], axis=-1)
     return jnp.transpose(full, (2, 0, 1, 3)).reshape(rows, nx * nz * blk)
 

time: 244 us -> 239 us (0.980)
  starting transfers between devices: 47.8 us -> 38.7 us
  waiting for transfers between devices: 69.7 us -> 78 us
    ppermute x2 -> x4, waiting for transfers between devices: 3.07 us -> 10.5 us  [ring_gather(): far = lax.ppermute(fwd, axis, [(i, (i + 1) % n) for i in range(n)])]
    ppermute x4 -> x0, starting transfers between devices: 6.59 us -> none  [the longest x2 6.51 us: ring_gather(): lax.ppermute(bwd[..., half:, :], axis, [(i, (i - 1) % n) for i in range(n)])]
    ppermute x4, waiting for transfers between devices: 5.45 us -> 9.06 us  [ring_gather(): fwd = lax.ppermute(v, axis, [(i, (i + 1) % n) for i in range(n)])]
    ppermute x4, starting transfers between devices: 9.55 us -> 6.53 us  [ring_gather(): bwd = lax.ppermute(v, axis, [(i, (i - 1) % n) for i in range(n)])]
    ppermute x4 -> x0, waiting for transfers between devices: 2.59 us -> none  [the longest x2 2.3 us: ring_gather(): lax.ppermute(fwd[..., :half, :], axis, [(i, (i + 1) % n) for i in range(n)])]
  transfers between devices with their start and end apart: 33 -> 31, of which waited for: 22 -> 24; matrix products, arithmetic and copies ran while one was open for 5% -> 5% of each run, Pallas kernels for 0% -> 0%
where the time goes in v11:
time: 239 us
  waiting for transfers between devices  78 us (33%)
  other arithmetic  54.5 us (23%)
  starting transfers between devices  38.7 us (16%)
  matrix products  34.2 us (14%)
  blocking collectives  23.2 us (10%)
  local copies, waits for them, and re-layouts  9.25 us (4%)
    all_to_all x1, waiting for transfers between devices, scatter_features(): got = lax.all_to_all(x, 'y', 0, 0, tiled=False)  31.2 us
    all_to_all x2, blocking collectives, group_sum(): lax.all_to_all(jnp.broadcast_to(v[None], (n,) + v.shape), axes, 0, 0, til...  23.2 us
    reduce_sum x3, other arithmetic, local(): row_part = jnp.sum(kernel * col_scale[None, :], axis=1)  21.1 us
    ppermute x16, starting transfers between devices, axis_sum(): lax.ppermute(v, axis, [(i, (i + s) % n) for i in range(n)])  19.1 us
    reduce_sum x2, other arithmetic, local(): col_part = jnp.sum(kernel * row_scale[:, None], axis=0)  13.9 us
    ppermute x16, waiting for transfers between devices, axis_sum(): lax.ppermute(v, axis, [(i, (i + s) % n) for i in range(n)])  13.8 us
    dot_general x1, matrix products, local(): lax.dot_general(gathered, hi, dims, preferred_element_type=jnp.float32)  12.1 us
    dot_general x1, matrix products, local(): jnp.dot(unit_points, unit_centroids.T, preferred_element_type=jnp.float32)  11.7 us
  transfers between devices with their start and end apart: 31, of which 24 were waited for; matrix products, arithmetic and copies ran while one was open for 5% of the time, Pallas kernels for 0%

profile of v11, /device:TPU:0, one launch (start us, length us, event | category | flops | bytes accessed | tf_op | source)
XLA Modules:
  0.0 238.8 jit_solution(16191362680948113353)
XLA Ops:
  1.6 2.1 collective-permute-start
  3.7 2.2 collective-permute-start.2
  9.3 2.4 %collective-permute-done.6 = bf16[2048,24]{0,1:T(8,128)(2,1)S(1)} collective-permute-done((bf16[2048,24]{0,1:T(8,128)(2,1)S(1)}, bf16[2048,24]{0,1:T(8,128)(2,1)S(1)}, u32[]{:S(2)}, u32[]{:S(2)}) %collective-permute-start.6) | collective-permute-done | bytes 98336 | tf_op jit(solution)/shard_map/ppermute | solution.py:93
  12.0 3.1 %collective-permute-done.1 = bf16[2048,24]{0,1:T(8,128)(2,1)S(1)} collective-permute-done((bf16[2048,24]{0,1:T(8,128)(2,1)S(1)}, bf16[2048,24]{0,1:T(8,128)(2,1)S(1)}, u32[]{:S(2)}, u32[]{:S(2)}) %collective-permute-start.1) | collective-permute-done | bytes 98336 | tf_op jit(solution)/shard_map/ppermute | solution.py:105
  19.8 6.2 %collective-permute-done.3 = bf16[4,2048,24]{1,2,0:T(8,128)(2,1)S(1)} collective-permute-done((bf16[4,2048,24]{1,2,0:T(8,128)(2,1)S(1)}, bf16[4,2048,24]{1,2,0:T(8,128)(2,1)S(1)}, u32[]{:S(2)}, u32[]{:S(2)}) %collective-permute-start.3) | collective-permute-done | bytes 393248 | tf_op jit(solution)/shard_map/ppermute | solution.py:93
  28.2 2.6 %fusion.6 = f32[2048]{0:T(1024)S(1)} fusion(bf16[2048,768]{1,0:T(8,128)(2,1)} %param.3), kind=kLoop, calls=%fused_computation.20 | loop fusion | flops 4716544 | bytes 3153920 | tf_op jit(solution)/shard_map/reduce_sum | solution.py:18
  30.7 4.6 %collective-permute-done.4 = bf16[4,2048,24]{1,2,0:T(8,128)(2,1)S(1)} collective-permute-done((bf16[4,2048,24]{1,2,0:T(8,128)(2,1)S(1)}, bf16[4,2048,24]{1,2,0:T(8,128)(2,1)S(1)}, u32[]{:S(2)}, u32[]{:S(2)}) %collective-permute-start.4) | collective-permute-done | bytes 393248 | tf_op jit(solution)/shard_map/ppermute | solution.py:105
  36.2 1.8 collective-permute-done.10
  39.4 1.8 gather_fusion.3
  44.0 11.7 %fusion.24 = (f32[2048]{0:T(1024)S(1)}, f32[2048,2048]{1,0:T(8,128)}) fusion(bf16[2048,768]{1,0:T(8,128)(2,1)S(1)} %copy-done, f32[2048]{0:T(1024)S(1)} %get-tuple-element.12, bf16[2048,768]{0,1:T(8,128)(2,1)S(1)} %bitcast.52, f32[2048]{0:T(1024)S(1)} %get-tuple-element.13), kind=kOutput, calls=%fused_computation.118 | convolution fusion | flops 6460274688 | bytes 23093248 | tf_op jit(solution)/shard_map/dot_general | solution.py:146
  56.8 3.2 %collective-permute-start.13 = (f32[2048]{0:T(1024)S(1)}, f32[2048]{0:T(1024)S(1)}, u32[]{:S(2)}, u32[]{:S(2)}) collective-permute-start(f32[2048]{0:T(1024)S(1)} %add.490), channel_id=1, source_target_pairs={{0,64},{32,96},{64,0},{96,32},{1,65},{33,97},{65,1},{97,33},{2,66}... | collective-permute-start | bytes 24584 | tf_op jit(solution)/shard_map/ppermute | solution.py:27
  60.7 2.6 %collective-permute-start.15 = (f32[2048]{0:T(1024)S(1)}, f32[2048]{0:T(1024)S(1)}, u32[]{:S(2)}, u32[]{:S(2)}) collective-permute-start(f32[2048]{0:T(1024)S(1)} %add.490), channel_id=1, source_target_pairs={{0,96},{32,0},{64,32},{96,64},{1,97},{33,1},{65,33},{97,65},{2,98}... | collective-permute-start | bytes 24584 | tf_op jit(solution)/shard_map/ppermute | solution.py:27
  64.9 7.0 %multiply_reduce_fusion.4 = f32[2048]{0:T(1024)S(1)} fusion(f32[2048,2048]{1,0:T(8,128)} %get-tuple-element.11, f32[2048]{0:T(1024)S(1)} %add_divide_fusion.2), kind=kLoop, calls=%fused_computation.11 | loop fusion | flops 8386560 | bytes 16793600 | tf_op jit(solution)/shard_map/reduce_sum | solution.py:151
  72.0 12.0 %all_to_all.23 = f32[16,1,2048]{2,1,0:T(1,128)S(1)} all-to-all(f32[16,1,2048]{2,1,0:T(1,128)S(1)} %broadcast_in_dim.6), channel_id=1, replica_groups=mesh['y'=4,'c'=2,'x'=4,'z'=4] {'x','z'}, dimensions={0} | all-to-all | bytes 262144 | tf_op jit(solution)/shard_map/all_to_all | solution.py:44
  84.0 6.9 %multiply_reduce_fusion.3 = f32[2048]{0:T(1024)S(1)} fusion(f32[2048,2048]{1,0:T(8,128)} %get-tuple-element.11, f32[2048]{0:T(1024)S(1)} %bitcast.73), kind=kLoop, calls=%fused_computation.10 | loop fusion | flops 8386560 | bytes 16793600 | tf_op jit(solution)/shard_map/reduce_sum | solution.py:149
  93.7 2.6 %collective-permute-start.18 = (f32[2048]{0:T(1024)S(1)}, f32[2048]{0:T(1024)S(1)}, u32[]{:S(2)}, u32[]{:S(2)}) collective-permute-start(f32[2048]{0:T(1024)S(1)} %add.510), channel_id=1, source_target_pairs={{0,32},{32,64},{64,96},{96,0},{1,33},{33,65},{65,97},{97,1},{2,34}... | collective-permute-start | bytes 24584 | tf_op jit(solution)/shard_map/ppermute | solution.py:27
  99.9 7.0 %multiply_reduce_fusion.2 = f32[2048]{0:T(1024)S(1)} fusion(f32[2048,2048]{1,0:T(8,128)} %get-tuple-element.11, f32[2048]{0:T(1024)S(1)} %add_divide_fusion.1), kind=kLoop, calls=%fused_computation.9 | loop fusion | flops 8386560 | bytes 16793600 | tf_op jit(solution)/shard_map/reduce_sum | solution.py:151
  107.0 11.2 %all_to_all.24 = f32[16,1,2048]{2,1,0:T(1,128)S(1)} all-to-all(f32[16,1,2048]{2,1,0:T(1,128)S(1)} %broadcast_in_dim.7), channel_id=1, replica_groups=mesh['y'=4,'c'=2,'x'=4,'z'=4] {'x','z'}, dimensions={0} | all-to-all | bytes 262144 | tf_op jit(solution)/shard_map/all_to_all | solution.py:44
  118.3 6.9 %multiply_reduce_fusion.1 = f32[2048]{0:T(1024)S(1)} fusion(f32[2048,2048]{1,0:T(8,128)} %get-tuple-element.11, f32[2048]{0:T(1024)S(1)} %bitcast.74), kind=kLoop, calls=%fused_computation.8 | loop fusion | flops 8386560 | bytes 16793600 | tf_op jit(solution)/shard_map/reduce_sum | solution.py:149
  127.1 2.1 collective-permute-start.22
  132.9 7.1 %multiply_reduce_fusion = f32[2048]{0:T(1024)S(1)} fusion(f32[2048,2048]{1,0:T(8,128)} %get-tuple-element.11, f32[2048]{0:T(1024)S(1)} %add_divide_fusion), kind=kLoop, calls=%fused_computation.7 | loop fusion | flops 8386560 | bytes 16793600 | tf_op jit(solution)/shard_map/reduce_sum | solution.py:151
  140.7 3.8 %all-to-all-start.2 = ((f32[16,1,2048]{2,1,0:T(1,128)}), f32[16,1,2048]{2,1,0:T(1,128)S(1)}, u32[]{:S(2)}, u32[]{:S(2)}) async-start(f32[16,1,2048]{2,1,0:T(1,128)} %broadcast_in_dim.8), calls=%async_computation.2 | async-start | bytes 262144 | tf_op jit(solution)/shard_map/all_to_all | solution.py:44
  144.5 7.7 %all-to-all-done.2 = f32[16,1,2048]{2,1,0:T(1,128)S(1)} async-done(((f32[16,1,2048]{2,1,0:T(1,128)}), f32[16,1,2048]{2,1,0:T(1,128)S(1)}, u32[]{:S(2)}, u32[]{:S(2)}) %all-to-all-start.2) | async-done | bytes 131104 | tf_op jit(solution)/shard_map/all_to_all | solution.py:44
  152.2 10.5 %fusion.1 = f32[768,2048]{1,0:T(8,128)S(1)} fusion(bf16[2048,768]{0,1:T(8,128)(2,1)S(1)} %bitcast.53, f32[2048,2048]{1,0:T(8,128)} %get-tuple-element.11, f32[2048]{0:T(1024)S(1)} %bitcast.70), kind=kOutput, calls=%fused_computation.14 | convolution fusion | flops 6459228160 | bytes 26222592 | tf_op jit(solution)/shard_map/dot_general | solution.py:160
  162.7 12.1 %add_multiply_fusion = f32[768,2048]{1,0:T(8,128)} fusion(f32[768,2048]{1,0:T(8,128)S(1)} %fusion.1, f32[2048]{0:T(1024)S(1)} %add_divide_fusion, bf16[2048,768]{0,1:T(8,128)(2,1)S(1)} %bitcast.54, f32[2048,2048]{1,0:T(8,128)} %get-tuple-element.11, f32[2048]{0:T(1024)S(1)} %bitcast.71), kind=kOutput, calls=%fused_computation.22 | convolution fusion | flops 6458179584 | bytes 32522240 | tf_op jit(solution)/shard_map/dot_general | solution.py:158
  174.8 2.1 dynamic-slice_bitcast_fusion
  177.0 5.8 %collective-permute-done.24 = f32[4,96,2048]{2,1,0:T(8,128)} collective-permute-done((f32[4,96,2048]{2,1,0:T(8,128)S(1)}, f32[4,96,2048]{2,1,0:T(8,128)}, u32[]{:S(2)}, u32[]{:S(2)}) %collective-permute-start.24) | collective-permute-done | bytes 3145760 | tf_op jit(solution)/shard_map/ppermute | solution.py:76
  182.7 5.2 %bitcast_add_fusion = f32[4,96,2048]{2,1,0:T(8,128)} fusion(f32[4,96,2048]{2,1,0:T(8,128)} %collective-permute-done.24, f32[4,2,96,2048]{3,2,1,0:T(8,128)} %bitcast.25, s32[]{:T(128)S(6)} %select_n.62), kind=kLoop, calls=%fused_computation.26 | loop fusion | flops 786432 | bytes 9437188 | tf_op jit(solution)/shard_map/add | solution.py:76
  188.0 3.7 %all-to-all-start.3 = ((f32[4,96,2048]{2,1,0:T(8,128)}), f32[4,96,2048]{2,1,0:T(8,128)S(1)}, u32[]{:S(2)}, u32[]{:S(2)}) async-start(f32[4,96,2048]{2,1,0:T(8,128)} %bitcast_add_fusion), calls=%async_computation.3 | async-start | bytes 6291456 | tf_op jit(solution)/shard_map/all_to_all | solution.py:81
  191.7 6.9 %multiply_reduce_fusion.5 = f32[2048]{0:T(1024)S(1)} fusion(f32[2048,2048]{1,0:T(8,128)} %get-tuple-element.11, f32[2048]{0:T(1024)S(1)} %bitcast.72), kind=kLoop, calls=%fused_computation.13 | loop fusion | flops 8386560 | bytes 16793600 | tf_op jit(solution)/shard_map/reduce_sum | solution.py:162
  198.6 31.2 %all-to-all-done.3 = f32[4,96,2048]{2,1,0:T(8,128)S(1)} async-done(((f32[4,96,2048]{2,1,0:T(8,128)}), f32[4,96,2048]{2,1,0:T(8,128)S(1)}, u32[]{:S(2)}, u32[]{:S(2)}) %all-to-all-start.3) | async-done | bytes 3145760 | tf_op jit(solution)/shard_map/all_to_all | solution.py:81
  233.5 1.8 collective-permute-start.28
  (86 shorter events, 40.1 us)
Async XLA Ops:
  1.6 7.6 %collective-permute-start = (bf16[2048,24]{0,1:T(8,128)(2,1)S(1)}, bf16[2048,24]{0,1:T(8,128)(2,1)S(1)}, u32[]{:S(2)}, u32[]{:S(2)}) collective-permute-start(bf16[2048,24]{0,1:T(8,128)(2,1)S(1)} %get-tuple-element.7), channel_id=1, source_target_pairs={{0,1},{1,2},{2,3},{3,0},{4,5},{5,6},{6,7},{7,4},{8,9},{9,10},{10,1... | collective-permute-start | bytes 294920 | tf_op jit(solution)/shard_map/ppermute | solution.py:93
  3.7 8.3 %collective-permute-start.2 = (bf16[2048,24]{0,1:T(8,128)(2,1)S(1)}, bf16[2048,24]{0,1:T(8,128)(2,1)S(1)}, u32[]{:S(2)}, u32[]{:S(2)}) collective-permute-start(bf16[2048,24]{0,1:T(8,128)(2,1)S(1)} %get-tuple-element.7), channel_id=1, source_target_pairs={{0,3},{1,0},{2,1},{3,2},{4,7},{5,4},{6,5},{7,6},{8,11},{9,8},{10,9... | collective-permute-start | bytes 294920 | tf_op jit(solution)/shard_map/ppermute | solution.py:94
  5.9 5.8 %collective-permute-start.6 = (bf16[2048,24]{0,1:T(8,128)(2,1)S(1)}, bf16[2048,24]{0,1:T(8,128)(2,1)S(1)}, u32[]{:S(2)}, u32[]{:S(2)}) collective-permute-start(bf16[2048,24]{0,1:T(8,128)(2,1)S(1)} %get-tuple-element.6), channel_id=1, source_target_pairs={{0,4},{4,8},{8,12},{12,0},{1,5},{5,9},{9,13},{13,1},{2,6},{6,10},{... | collective-permute-start | bytes 294920 | tf_op jit(solution)/shard_map/ppermute | solution.py:93
  7.4 9.2 %collective-permute-start.8 = (bf16[2048,24]{0,1:T(8,128)(2,1)S(1)}, bf16[2048,24]{0,1:T(8,128)(2,1)S(1)}, u32[]{:S(2)}, u32[]{:S(2)}) collective-permute-start(bf16[2048,24]{0,1:T(8,128)(2,1)S(1)} %get-tuple-element.6), channel_id=1, source_target_pairs={{0,12},{4,0},{8,4},{12,8},{1,13},{5,1},{9,5},{13,9},{2,14},{6,2},{... | collective-permute-start | bytes 294920 | tf_op jit(solution)/shard_map/ppermute | solution.py:94
  9.2 5.9 %collective-permute-start.1 = (bf16[2048,24]{0,1:T(8,128)(2,1)S(1)}, bf16[2048,24]{0,1:T(8,128)(2,1)S(1)}, u32[]{:S(2)}, u32[]{:S(2)}) collective-permute-start(bf16[2048,24]{0,1:T(8,128)(2,1)S(1)} %collective-permute-done), channel_id=1, source_target_pairs={{0,1},{1,2},{2,3},{3,0},{4,5},{5,6},{6,7},{7,4},{8,9},{9,10},{10,1... | collective-permute-start | bytes 294920 | tf_op jit(solution)/shard_map/ppermute | solution.py:105
  11.7 5.9 %collective-permute-start.7 = (bf16[2048,24]{0,1:T(8,128)(2,1)S(1)}, bf16[2048,24]{0,1:T(8,128)(2,1)S(1)}, u32[]{:S(2)}, u32[]{:S(2)}) collective-permute-start(bf16[2048,24]{0,1:T(8,128)(2,1)S(1)} %collective-permute-done.6), channel_id=1, source_target_pairs={{0,4},{4,8},{8,12},{12,0},{1,5},{5,9},{9,13},{13,1},{2,6},{6,10},{... | collective-permute-start | bytes 294920 | tf_op jit(solution)/shard_map/ppermute | solution.py:105
  15.7 10.3 %collective-permute-start.3 = (bf16[4,2048,24]{1,2,0:T(8,128)(2,1)S(1)}, bf16[4,2048,24]{1,2,0:T(8,128)(2,1)S(1)}, u32[]{:S(2)}, u32[]{:S(2)}) collective-permute-start(bf16[4,2048,24]{1,2,0:T(8,128)(2,1)S(1)} %gather_fusion), channel_id=1, source_target_pairs={{0,4},{4,8},{8,12},{12,0},{1,5},{5,9},{9,13},{13,1},{2,6},{6,10},{... | collective-permute-start | bytes 1179656 | tf_op jit(solution)/shard_map/ppermute | solution.py:93
  18.3 9.9 %collective-permute-start.9 = (bf16[4,2048,24]{1,2,0:T(8,128)(2,1)S(1)}, bf16[4,2048,24]{1,2,0:T(8,128)(2,1)}, u32[]{:S(2)}, u32[]{:S(2)}) collective-permute-start(bf16[4,2048,24]{1,2,0:T(8,128)(2,1)S(1)} %gather_fusion.2), channel_id=1, source_target_pairs={{0,1},{1,2},{2,3},{3,0},{4,5},{5,6},{6,7},{7,4},{8,9},{9,10},{10,1... | collective-permute-start | bytes 1179656 | tf_op jit(solution)/shard_map/ppermute | solution.py:93
  18.9 11.8 %collective-permute-start.5 = (bf16[4,2048,24]{1,2,0:T(8,128)(2,1)S(1)}, bf16[4,2048,24]{1,2,0:T(8,128)(2,1)S(1)}, u32[]{:S(2)}, u32[]{:S(2)}) collective-permute-start(bf16[4,2048,24]{1,2,0:T(8,128)(2,1)S(1)} %gather_fusion), channel_id=1, source_target_pairs={{0,12},{4,0},{8,4},{12,8},{1,13},{5,1},{9,5},{13,9},{2,14},{6,2},{... | collective-permute-start | bytes 1179656 | tf_op jit(solution)/shard_map/ppermute | solution.py:94
  26.0 9.3 %collective-permute-start.4 = (bf16[4,2048,24]{1,2,0:T(8,128)(2,1)S(1)}, bf16[4,2048,24]{1,2,0:T(8,128)(2,1)S(1)}, u32[]{:S(2)}, u32[]{:S(2)}) collective-permute-start(bf16[4,2048,24]{1,2,0:T(8,128)(2,1)S(1)} %collective-permute-done.3), channel_id=1, source_target_pairs={{0,4},{4,8},{8,12},{12,0},{1,5},{5,9},{9,13},{13,1},{2,6},{6,10},{... | collective-permute-start | bytes 1179656 | tf_op jit(solution)/shard_map/ppermute | solution.py:105
  26.0 10.2 %collective-permute-start.11 = (bf16[4,2048,24]{1,2,0:T(8,128)(2,1)S(1)}, bf16[4,2048,24]{1,2,0:T(8,128)(2,1)}, u32[]{:S(2)}, u32[]{:S(2)}) collective-permute-start(bf16[4,2048,24]{1,2,0:T(8,128)(2,1)S(1)} %gather_fusion.2), channel_id=1, source_target_pairs={{0,3},{1,0},{2,1},{3,2},{4,7},{5,4},{6,5},{7,6},{8,11},{9,8},{10,9... | collective-permute-start | bytes 1179656 | tf_op jit(solution)/shard_map/ppermute | solution.py:94
  28.2 9.9 %collective-permute-start.10 = (bf16[4,2048,24]{1,2,0:T(8,128)(2,1)}, bf16[4,2048,24]{1,2,0:T(8,128)(2,1)}, u32[]{:S(2)}, u32[]{:S(2)}) collective-permute-start(bf16[4,2048,24]{1,2,0:T(8,128)(2,1)} %collective-permute-done.9), channel_id=1, source_target_pairs={{0,1},{1,2},{2,3},{3,0},{4,5},{5,6},{6,7},{7,4},{8,9},{9,10},{10,1... | collective-permute-start | bytes 1179656 | tf_op jit(solution)/shard_map/ppermute | solution.py:105
  55.6 1.2 collective-permute-start.12
  56.8 6.4 %collective-permute-start.13 = (f32[2048]{0:T(1024)S(1)}, f32[2048]{0:T(1024)S(1)}, u32[]{:S(2)}, u32[]{:S(2)}) collective-permute-start(f32[2048]{0:T(1024)S(1)} %add.490), channel_id=1, source_target_pairs={{0,64},{32,96},{64,0},{96,32},{1,65},{33,97},{65,1},{97,33},{2,66}... | collective-permute-start | bytes 24584 | tf_op jit(solution)/shard_map/ppermute | solution.py:27
  60.0 4.9 %collective-permute-start.14 = (f32[2048]{0:T(1024)S(1)}, f32[2048]{0:T(1024)S(1)}, u32[]{:S(2)}, u32[]{:S(2)}) collective-permute-start(f32[2048]{0:T(1024)S(1)} %add.490), channel_id=1, source_target_pairs={{0,32},{32,64},{64,96},{96,0},{1,33},{33,65},{65,97},{97,1},{2,34}... | collective-permute-start | bytes 24584 | tf_op jit(solution)/shard_map/ppermute | solution.py:27
  60.7 4.2 %collective-permute-start.15 = (f32[2048]{0:T(1024)S(1)}, f32[2048]{0:T(1024)S(1)}, u32[]{:S(2)}, u32[]{:S(2)}) collective-permute-start(f32[2048]{0:T(1024)S(1)} %add.490), channel_id=1, source_target_pairs={{0,96},{32,0},{64,32},{96,64},{1,97},{33,1},{65,33},{97,65},{2,98}... | collective-permute-start | bytes 24584 | tf_op jit(solution)/shard_map/ppermute | solution.py:27
  90.9 1.3 collective-permute-start.16
  92.2 5.2 %collective-permute-start.17 = (f32[2048]{0:T(1024)S(1)}, f32[2048]{0:T(1024)S(1)}, u32[]{:S(2)}, u32[]{:S(2)}) collective-permute-start(f32[2048]{0:T(1024)S(1)} %add.510), channel_id=1, source_target_pairs={{0,64},{32,96},{64,0},{96,32},{1,65},{33,97},{65,1},{97,33},{2,66}... | collective-permute-start | bytes 24584 | tf_op jit(solution)/shard_map/ppermute | solution.py:27
  93.7 4.9 %collective-permute-start.18 = (f32[2048]{0:T(1024)S(1)}, f32[2048]{0:T(1024)S(1)}, u32[]{:S(2)}, u32[]{:S(2)}) collective-permute-start(f32[2048]{0:T(1024)S(1)} %add.510), channel_id=1, source_target_pairs={{0,32},{32,64},{64,96},{96,0},{1,33},{33,65},{65,97},{97,1},{2,34}... | collective-permute-start | bytes 24584 | tf_op jit(solution)/shard_map/ppermute | solution.py:27
  96.3 3.7 %collective-permute-start.19 = (f32[2048]{0:T(1024)S(1)}, f32[2048]{0:T(1024)S(1)}, u32[]{:S(2)}, u32[]{:S(2)}) collective-permute-start(f32[2048]{0:T(1024)S(1)} %add.510), channel_id=1, source_target_pairs={{0,96},{32,0},{64,32},{96,64},{1,97},{33,1},{65,33},{97,65},{2,98}... | collective-permute-start | bytes 24584 | tf_op jit(solution)/shard_map/ppermute | solution.py:27
  125.3 1.3 collective-permute-start.20
  126.5 5.2 %collective-permute-start.21 = (f32[2048]{0:T(1024)S(1)}, f32[2048]{0:T(1024)S(1)}, u32[]{:S(2)}, u32[]{:S(2)}) collective-permute-start(f32[2048]{0:T(1024)S(1)} %add.530), channel_id=1, source_target_pairs={{0,64},{32,96},{64,0},{96,32},{1,65},{33,97},{65,1},{97,33},{2,66}... | collective-permute-start | bytes 24584 | tf_op jit(solution)/shard_map/ppermute | solution.py:27
  127.1 4.9 %collective-permute-start.22 = (f32[2048]{0:T(1024)S(1)}, f32[2048]{0:T(1024)S(1)}, u32[]{:S(2)}, u32[]{:S(2)}) collective-permute-start(f32[2048]{0:T(1024)S(1)} %add.530), channel_id=1, source_target_pairs={{0,32},{32,64},{64,96},{96,0},{1,33},{33,65},{65,97},{97,1},{2,34}... | collective-permute-start | bytes 24584 | tf_op jit(solution)/shard_map/ppermute | solution.py:27
  129.2 3.7 %collective-permute-start.23 = (f32[2048]{0:T(1024)S(1)}, f32[2048]{0:T(1024)S(1)}, u32[]{:S(2)}, u32[]{:S(2)}) collective-permute-start(f32[2048]{0:T(1024)S(1)} %add.530), channel_id=1, source_target_pairs={{0,96},{32,0},{64,32},{96,64},{1,97},{33,1},{65,33},{97,65},{2,98}... | collective-permute-start | bytes 24584 | tf_op jit(solution)/shard_map/ppermute | solution.py:27
  132.9 19.3 %copy-start.2 = (bf16[4,4,2048,48]{2,3,1,0:T(8,128)(2,1)S(1)}, bf16[4,4,2048,48]{2,3,1,0:T(8,128)(2,1)}, u32[]{:S(2)}) copy-start(bf16[4,4,2048,48]{2,3,1,0:T(8,128)(2,1)} %copy-done.1) | copy-start | bytes 9437188
  140.7 11.4 %all-to-all-start.2 = ((f32[16,1,2048]{2,1,0:T(1,128)}), f32[16,1,2048]{2,1,0:T(1,128)S(1)}, u32[]{:S(2)}, u32[]{:S(2)}) async-start(f32[16,1,2048]{2,1,0:T(1,128)} %broadcast_in_dim.8), calls=%async_computation.2 | async-start | bytes 262144 | tf_op jit(solution)/shard_map/all_to_all | solution.py:44
  176.9 5.9 %collective-permute-start.24 = (f32[4,96,2048]{2,1,0:T(8,128)S(1)}, f32[4,96,2048]{2,1,0:T(8,128)}, u32[]{:S(2)}, u32[]{:S(2)}) collective-permute-start(f32[4,96,2048]{2,1,0:T(8,128)S(1)} %dynamic-slice_bitcast_fusion), channel_id=1, source_target_pairs={{0,16},{16,0},{1,17},{17,1},{2,18},{18,2},{3,19},{19,3},{4,20},{20... | collective-permute-start | bytes 9437192 | tf_op jit(solution)/shard_map/ppermute | solution.py:76
  188.0 41.8 %all-to-all-start.3 = ((f32[4,96,2048]{2,1,0:T(8,128)}), f32[4,96,2048]{2,1,0:T(8,128)S(1)}, u32[]{:S(2)}, u32[]{:S(2)}) async-start(f32[4,96,2048]{2,1,0:T(8,128)} %bitcast_add_fusion), calls=%async_computation.3 | async-start | bytes 6291456 | tf_op jit(solution)/shard_map/all_to_all | solution.py:81
  230.1 1.3 collective-permute-start.25
  231.3 5.4 %collective-permute-start.26 = (f32[2,2048]{1,0:T(2,128)S(1)}, f32[2,2048]{1,0:T(2,128)S(1)}, u32[]{:S(2)}, u32[]{:S(2)}) collective-permute-start(f32[2,2048]{1,0:T(2,128)S(1)} %fusion.21), channel_id=1, source_target_pairs={{0,64},{32,96},{64,0},{96,32},{1,65},{33,97},{65,1},{97,33},{2,66}... | collective-permute-start | bytes 49160 | tf_op jit(solution)/shard_map/ppermute | solution.py:27
  232.0 4.9 %collective-permute-start.27 = (f32[2,2048]{1,0:T(2,128)S(1)}, f32[2,2048]{1,0:T(2,128)S(1)}, u32[]{:S(2)}, u32[]{:S(2)}) collective-permute-start(f32[2,2048]{1,0:T(2,128)S(1)} %fusion.21), channel_id=1, source_target_pairs={{0,32},{32,64},{64,96},{96,0},{1,33},{33,65},{65,97},{97,1},{2,34}... | collective-permute-start | bytes 49160 | tf_op jit(solution)/shard_map/ppermute | solution.py:27
  233.5 3.7 %collective-permute-start.28 = (f32[2,2048]{1,0:T(2,128)S(1)}, f32[2,2048]{1,0:T(2,128)S(1)}, u32[]{:S(2)}, u32[]{:S(2)}) collective-permute-start(f32[2,2048]{1,0:T(2,128)S(1)} %fusion.21), channel_id=1, source_target_pairs={{0,96},{32,0},{64,32},{96,64},{1,97},{33,1},{65,33},{97,65},{2,98}... | collective-permute-start | bytes 49160 | tf_op jit(solution)/shard_map/ppermute | solution.py:27
  (2 other events, 14.4 us)

commit v12 on v11

--- a/solution.py
+++ b/solution.py
@@ -147,7 +147,7 @@
         kernel = jnp.exp(scores / (width * temper))
         for sweep in range(ITERS):
             col_part = jnp.sum(kernel * row_scale[:, None], axis=0)
-            col_scale = balance / multi_sum(col_part, pts_red)
+            col_scale = balance / group_sum(col_part, PTS_AXES, n_pts)
             row_part = jnp.sum(kernel * col_scale[None, :], axis=1)
             row_scale = 1.0 / group_sum(row_part, CEN_AXES, n_cen)
         scaled = kernel * row_scale[:, None]
@@ -162,7 +162,7 @@
         mass_part = jnp.sum(scaled, axis=0) * col_scale / balance
         moved = scatter_features(partial_t, sizes).T
         squares = jnp.sum(moved * moved, axis=1)
-        both = multi_sum(jnp.stack([squares, mass_part]), pts_red)
+        both = group_sum(jnp.stack([squares, mass_part]), PTS_AXES, n_pts)
         squares, masses = both[0], both[1]
         new_centroids = moved * lax.rsqrt(squares / width + 1e-06)[:, None]
         return (new_centroids, masses)

time: 239 us -> 242 us (1.013)
  blocking collectives: 23.2 us -> 57.6 us
  starting transfers between devices: 38.7 us -> 19.6 us
  waiting for transfers between devices: 78 us -> 64.1 us
    all_to_all x2 -> x6, blocking collectives: 23.2 us -> 57.6 us  [group_sum(): lax.all_to_all(jnp.broadcast_to(v[None], (n,) + v.shape), axes, 0, 0, til...]
    ppermute x16 -> x0, starting transfers between devices: 19.1 us -> none  [axis_sum(): lax.ppermute(v, axis, [(i, (i + s) % n) for i in range(n)])]
    ppermute x16 -> x0, waiting for transfers between devices: 13.8 us -> none  [axis_sum(): lax.ppermute(v, axis, [(i, (i + s) % n) for i in range(n)])]
  transfers between devices with their start and end apart: 31 -> 15, of which waited for: 24 -> 10; matrix products, arithmetic and copies ran while one was open for 5% -> 5% of each run, Pallas kernels for 0% -> 0%
where the time goes in v12:
time: 242 us; the launch traced here: 240 us
  waiting for transfers between devices  64.1 us (26%)
  blocking collectives  57.6 us (24%)
  other arithmetic  54.6 us (23%)
  matrix products  34.2 us (14%)
  starting transfers between devices  19.6 us (8%)
  local copies, waits for them, and re-layouts  9.4 us (4%)
    all_to_all x6, blocking collectives, group_sum(): lax.all_to_all(jnp.broadcast_to(v[None], (n,) + v.shape), axes, 0, 0, til...  57.6 us
    all_to_all x1, waiting for transfers between devices, scatter_features(): got = lax.all_to_all(x, 'y', 0, 0, tiled=False)  31.1 us
    reduce_sum x3, other arithmetic, local(): row_part = jnp.sum(kernel * col_scale[None, :], axis=1)  21.1 us
    reduce_sum x2, other arithmetic, local(): col_part = jnp.sum(kernel * row_scale[:, None], axis=0)  13.9 us
    dot_general x1, matrix products, local(): lax.dot_general(gathered, hi, dims, preferred_element_type=jnp.float32)  12.1 us
    dot_general x1, matrix products, local(): jnp.dot(unit_points, unit_centroids.T, preferred_element_type=jnp.float32)  11.6 us
    ppermute x4, waiting for transfers between devices, ring_gather(): far = lax.ppermute(fwd, axis, [(i, (i + 1) % n) for i in range(n)])  10.5 us
    dot_general x1, matrix products, local(): lax.dot_general(gathered, lo, dims, preferred_element_type=jnp.float32)  10.5 us
  transfers between devices with their start and end apart: 15, of which 10 were waited for; matrix products, arithmetic and copies ran while one was open for 5% of the time, Pallas kernels for 0%

profile of v12, /device:TPU:0, one launch (start us, length us, event | category | flops | bytes accessed | tf_op | source)
XLA Modules:
  0.0 240.4 jit_solution(7617123759182253883)
XLA Ops:
  1.6 2.1 collective-permute-start
  3.7 2.2 collective-permute-start.2
  7.4 1.7 collective-permute-start.8
  9.3 2.4 %collective-permute-done.6 = bf16[2048,24]{0,1:T(8,128)(2,1)S(1)} collective-permute-done((bf16[2048,24]{0,1:T(8,128)(2,1)S(1)}, bf16[2048,24]{0,1:T(8,128)(2,1)S(1)}, u32[]{:S(2)}, u32[]{:S(2)}) %collective-permute-start.6) | collective-permute-done | bytes 98336 | tf_op jit(solution)/shard_map/ppermute | solution.py:93
  12.0 3.1 %collective-permute-done.1 = bf16[2048,24]{0,1:T(8,128)(2,1)S(1)} collective-permute-done((bf16[2048,24]{0,1:T(8,128)(2,1)S(1)}, bf16[2048,24]{0,1:T(8,128)(2,1)S(1)}, u32[]{:S(2)}, u32[]{:S(2)}) %collective-permute-start.1) | collective-permute-done | bytes 98336 | tf_op jit(solution)/shard_map/ppermute | solution.py:105
  19.8 6.2 %collective-permute-done.3 = bf16[4,2048,24]{1,2,0:T(8,128)(2,1)S(1)} collective-permute-done((bf16[4,2048,24]{1,2,0:T(8,128)(2,1)S(1)}, bf16[4,2048,24]{1,2,0:T(8,128)(2,1)S(1)}, u32[]{:S(2)}, u32[]{:S(2)}) %collective-permute-start.3) | collective-permute-done | bytes 393248 | tf_op jit(solution)/shard_map/ppermute | solution.py:93
  28.2 2.6 %fusion.6 = f32[2048]{0:T(1024)S(1)} fusion(bf16[2048,768]{1,0:T(8,128)(2,1)} %param.3), kind=kLoop, calls=%fused_computation.20 | loop fusion | flops 4716544 | bytes 3153920 | tf_op jit(solution)/shard_map/reduce_sum | solution.py:18
  30.7 4.6 %collective-permute-done.4 = bf16[4,2048,24]{1,2,0:T(8,128)(2,1)S(1)} collective-permute-done((bf16[4,2048,24]{1,2,0:T(8,128)(2,1)S(1)}, bf16[4,2048,24]{1,2,0:T(8,128)(2,1)S(1)}, u32[]{:S(2)}, u32[]{:S(2)}) %collective-permute-start.4) | collective-permute-done | bytes 393248 | tf_op jit(solution)/shard_map/ppermute | solution.py:105
  36.2 1.8 collective-permute-done.10
  39.4 1.8 gather_fusion.3
  44.0 11.6 %fusion.27 = (f32[2048]{0:T(1024)S(1)}, f32[2048,2048]{1,0:T(8,128)}) fusion(bf16[2048,768]{1,0:T(8,128)(2,1)S(1)} %copy-done, f32[2048]{0:T(1024)S(1)} %get-tuple-element.12, bf16[2048,768]{0,1:T(8,128)(2,1)S(1)} %bitcast.59, f32[2048]{0:T(1024)S(1)} %get-tuple-element.13), kind=kOutput, calls=%fused_computation.145 | convolution fusion | flops 6460274688 | bytes 23093248 | tf_op jit(solution)/shard_map/dot_general | solution.py:146
  55.6 9.9 %all_to_all.46 = f32[8,1,2048]{2,1,0:T(1,128)S(1)} all-to-all(f32[8,1,2048]{2,1,0:T(1,128)S(1)} %broadcast_in_dim.14), channel_id=1, replica_groups=mesh['y'=4,'c'=2,'x'=4,'z'=4] {'y','c'}, dimensions={0} | all-to-all | bytes 131072 | tf_op jit(solution)/shard_map/all_to_all | solution.py:44
  65.6 7.0 %multiply_reduce_fusion.4 = f32[2048]{0:T(1024)S(1)} fusion(f32[2048,2048]{1,0:T(8,128)} %get-tuple-element.11, f32[2048]{0:T(1024)S(1)} %bitcast.77), kind=kLoop, calls=%fused_computation.11 | loop fusion | flops 8386560 | bytes 16793600 | tf_op jit(solution)/shard_map/reduce_sum | solution.py:151
  72.7 12.0 %all_to_all.47 = f32[16,1,2048]{2,1,0:T(1,128)S(1)} all-to-all(f32[16,1,2048]{2,1,0:T(1,128)S(1)} %broadcast_in_dim.15), channel_id=1, replica_groups=mesh['y'=4,'c'=2,'x'=4,'z'=4] {'x','z'}, dimensions={0} | all-to-all | bytes 262144 | tf_op jit(solution)/shard_map/all_to_all | solution.py:44
  84.7 6.9 %multiply_reduce_fusion.3 = f32[2048]{0:T(1024)S(1)} fusion(f32[2048,2048]{1,0:T(8,128)} %get-tuple-element.11, f32[2048]{0:T(1024)S(1)} %bitcast.78), kind=kLoop, calls=%fused_computation.10 | loop fusion | flops 8386560 | bytes 16793600 | tf_op jit(solution)/shard_map/reduce_sum | solution.py:149
  91.7 8.0 %all_to_all.48 = f32[8,1,2048]{2,1,0:T(1,128)S(1)} all-to-all(f32[8,1,2048]{2,1,0:T(1,128)S(1)} %broadcast_in_dim.16), channel_id=1, replica_groups=mesh['y'=4,'c'=2,'x'=4,'z'=4] {'y','c'}, dimensions={0} | all-to-all | bytes 131072 | tf_op jit(solution)/shard_map/all_to_all | solution.py:44
  99.7 7.0 %multiply_reduce_fusion.2 = f32[2048]{0:T(1024)S(1)} fusion(f32[2048,2048]{1,0:T(8,128)} %get-tuple-element.11, f32[2048]{0:T(1024)S(1)} %bitcast.79), kind=kLoop, calls=%fused_computation.9 | loop fusion | flops 8386560 | bytes 16793600 | tf_op jit(solution)/shard_map/reduce_sum | solution.py:151
  106.8 11.2 %all_to_all.49 = f32[16,1,2048]{2,1,0:T(1,128)S(1)} all-to-all(f32[16,1,2048]{2,1,0:T(1,128)S(1)} %broadcast_in_dim.17), channel_id=1, replica_groups=mesh['y'=4,'c'=2,'x'=4,'z'=4] {'x','z'}, dimensions={0} | all-to-all | bytes 262144 | tf_op jit(solution)/shard_map/all_to_all | solution.py:44
  118.1 6.9 %multiply_reduce_fusion.1 = f32[2048]{0:T(1024)S(1)} fusion(f32[2048,2048]{1,0:T(8,128)} %get-tuple-element.11, f32[2048]{0:T(1024)S(1)} %bitcast.80), kind=kLoop, calls=%fused_computation.8 | loop fusion | flops 8386560 | bytes 16793600 | tf_op jit(solution)/shard_map/reduce_sum | solution.py:149
  125.1 8.0 %all_to_all.50 = f32[8,1,2048]{2,1,0:T(1,128)S(1)} all-to-all(f32[8,1,2048]{2,1,0:T(1,128)S(1)} %broadcast_in_dim.18), channel_id=1, replica_groups=mesh['y'=4,'c'=2,'x'=4,'z'=4] {'y','c'}, dimensions={0} | all-to-all | bytes 131072 | tf_op jit(solution)/shard_map/all_to_all | solution.py:44
  133.1 7.1 %multiply_reduce_fusion = f32[2048]{0:T(1024)S(1)} fusion(f32[2048,2048]{1,0:T(8,128)} %get-tuple-element.11, f32[2048]{0:T(1024)S(1)} %bitcast.71), kind=kLoop, calls=%fused_computation.7 | loop fusion | flops 8386560 | bytes 16793600 | tf_op jit(solution)/shard_map/reduce_sum | solution.py:151
  140.9 3.8 %all-to-all-start.5 = ((f32[16,1,2048]{2,1,0:T(1,128)}), f32[16,1,2048]{2,1,0:T(1,128)S(1)}, u32[]{:S(2)}, u32[]{:S(2)}) async-start(f32[16,1,2048]{2,1,0:T(1,128)} %broadcast_in_dim.19), calls=%async_computation.5 | async-start | bytes 262144 | tf_op jit(solution)/shard_map/all_to_all | solution.py:44
  144.7 7.7 %all-to-all-done.5 = f32[16,1,2048]{2,1,0:T(1,128)S(1)} async-done(((f32[16,1,2048]{2,1,0:T(1,128)}), f32[16,1,2048]{2,1,0:T(1,128)S(1)}, u32[]{:S(2)}, u32[]{:S(2)}) %all-to-all-start.5) | async-done | bytes 131104 | tf_op jit(solution)/shard_map/all_to_all | solution.py:44
  152.5 10.5 %fusion.1 = f32[768,2048]{1,0:T(8,128)S(1)} fusion(bf16[2048,768]{0,1:T(8,128)(2,1)S(1)} %bitcast.60, f32[2048,2048]{1,0:T(8,128)} %get-tuple-element.11, f32[2048]{0:T(1024)S(1)} %bitcast.73), kind=kOutput, calls=%fused_computation.14 | convolution fusion | flops 6459228160 | bytes 26222592 | tf_op jit(solution)/shard_map/dot_general | solution.py:160
  162.9 12.1 %add_multiply_fusion = f32[768,2048]{1,0:T(8,128)} fusion(f32[768,2048]{1,0:T(8,128)S(1)} %fusion.1, bf16[2048,768]{0,1:T(8,128)(2,1)S(1)} %bitcast.61, f32[2048,2048]{1,0:T(8,128)} %get-tuple-element.11, f32[2048]{0:T(1024)S(1)} %bitcast.74, f32[2048]{0:T(1024)S(1)} %bitcast.72), kind=kOutput, calls=%fused_computation.22 | convolution fusion | flops 6458179584 | bytes 32522240 | tf_op jit(solution)/shard_map/dot_general | solution.py:158
  175.0 2.1 dynamic-slice_bitcast_fusion
  177.2 5.8 %collective-permute-done.12 = f32[4,96,2048]{2,1,0:T(8,128)} collective-permute-done((f32[4,96,2048]{2,1,0:T(8,128)S(1)}, f32[4,96,2048]{2,1,0:T(8,128)}, u32[]{:S(2)}, u32[]{:S(2)}) %collective-permute-start.12) | collective-permute-done | bytes 3145760 | tf_op jit(solution)/shard_map/ppermute | solution.py:76
  183.0 5.2 %bitcast_add_fusion = f32[4,96,2048]{2,1,0:T(8,128)} fusion(f32[4,96,2048]{2,1,0:T(8,128)} %collective-permute-done.12, f32[4,2,96,2048]{3,2,1,0:T(8,128)} %bitcast.28, s32[]{:T(128)S(6)} %select_n.62), kind=kLoop, calls=%fused_computation.26 | loop fusion | flops 786432 | bytes 9437188 | tf_op jit(solution)/shard_map/add | solution.py:76
  188.2 3.7 %all-to-all-start.6 = ((f32[4,96,2048]{2,1,0:T(8,128)}), f32[4,96,2048]{2,1,0:T(8,128)S(1)}, u32[]{:S(2)}, u32[]{:S(2)}) async-start(f32[4,96,2048]{2,1,0:T(8,128)} %bitcast_add_fusion), calls=%async_computation.6 | async-start | bytes 6291456 | tf_op jit(solution)/shard_map/all_to_all | solution.py:81
  191.9 6.9 %multiply_reduce_fusion.5 = f32[2048]{0:T(1024)S(1)} fusion(f32[2048,2048]{1,0:T(8,128)} %get-tuple-element.11, f32[2048]{0:T(1024)S(1)} %bitcast.75), kind=kLoop, calls=%fused_computation.13 | loop fusion | flops 8386560 | bytes 16793600 | tf_op jit(solution)/shard_map/reduce_sum | solution.py:162
  198.9 31.1 %all-to-all-done.6 = f32[4,96,2048]{2,1,0:T(8,128)S(1)} async-done(((f32[4,96,2048]{2,1,0:T(8,128)}), f32[4,96,2048]{2,1,0:T(8,128)S(1)}, u32[]{:S(2)}, u32[]{:S(2)}) %all-to-all-start.6) | async-done | bytes 3145760 | tf_op jit(solution)/shard_map/all_to_all | solution.py:81
  230.3 8.5 %all_to_all.51 = f32[8,2,2048]{2,1,0:T(2,128)S(1)} all-to-all(f32[8,2,2048]{2,1,0:T(2,128)S(1)} %broadcast_in_dim.20), channel_id=1, replica_groups=mesh['y'=4,'c'=2,'x'=4,'z'=4] {'y','c'}, dimensions={0} | all-to-all | bytes 262144 | tf_op jit(solution)/shard_map/all_to_all | solution.py:44
  (58 shorter events, 18.0 us)
Async XLA Ops:
  1.6 7.6 %collective-permute-start = (bf16[2048,24]{0,1:T(8,128)(2,1)S(1)}, bf16[2048,24]{0,1:T(8,128)(2,1)S(1)}, u32[]{:S(2)}, u32[]{:S(2)}) collective-permute-start(bf16[2048,24]{0,1:T(8,128)(2,1)S(1)} %get-tuple-element.7), channel_id=1, source_target_pairs={{0,1},{1,2},{2,3},{3,0},{4,5},{5,6},{6,7},{7,4},{8,9},{9,10},{10,1... | collective-permute-start | bytes 294920 | tf_op jit(solution)/shard_map/ppermute | solution.py:93
  3.7 8.3 %collective-permute-start.2 = (bf16[2048,24]{0,1:T(8,128)(2,1)S(1)}, bf16[2048,24]{0,1:T(8,128)(2,1)S(1)}, u32[]{:S(2)}, u32[]{:S(2)}) collective-permute-start(bf16[2048,24]{0,1:T(8,128)(2,1)S(1)} %get-tuple-element.7), channel_id=1, source_target_pairs={{0,3},{1,0},{2,1},{3,2},{4,7},{5,4},{6,5},{7,6},{8,11},{9,8},{10,9... | collective-permute-start | bytes 294920 | tf_op jit(solution)/shard_map/ppermute | solution.py:94
  5.9 5.8 %collective-permute-start.6 = (bf16[2048,24]{0,1:T(8,128)(2,1)S(1)}, bf16[2048,24]{0,1:T(8,128)(2,1)S(1)}, u32[]{:S(2)}, u32[]{:S(2)}) collective-permute-start(bf16[2048,24]{0,1:T(8,128)(2,1)S(1)} %get-tuple-element.6), channel_id=1, source_target_pairs={{0,4},{4,8},{8,12},{12,0},{1,5},{5,9},{9,13},{13,1},{2,6},{6,10},{... | collective-permute-start | bytes 294920 | tf_op jit(solution)/shard_map/ppermute | solution.py:93
  7.4 9.2 %collective-permute-start.8 = (bf16[2048,24]{0,1:T(8,128)(2,1)S(1)}, bf16[2048,24]{0,1:T(8,128)(2,1)S(1)}, u32[]{:S(2)}, u32[]{:S(2)}) collective-permute-start(bf16[2048,24]{0,1:T(8,128)(2,1)S(1)} %get-tuple-element.6), channel_id=1, source_target_pairs={{0,12},{4,0},{8,4},{12,8},{1,13},{5,1},{9,5},{13,9},{2,14},{6,2},{... | collective-permute-start | bytes 294920 | tf_op jit(solution)/shard_map/ppermute | solution.py:94
  9.2 5.9 %collective-permute-start.1 = (bf16[2048,24]{0,1:T(8,128)(2,1)S(1)}, bf16[2048,24]{0,1:T(8,128)(2,1)S(1)}, u32[]{:S(2)}, u32[]{:S(2)}) collective-permute-start(bf16[2048,24]{0,1:T(8,128)(2,1)S(1)} %collective-permute-done), channel_id=1, source_target_pairs={{0,1},{1,2},{2,3},{3,0},{4,5},{5,6},{6,7},{7,4},{8,9},{9,10},{10,1... | collective-permute-start | bytes 294920 | tf_op jit(solution)/shard_map/ppermute | solution.py:105
  11.7 5.9 %collective-permute-start.7 = (bf16[2048,24]{0,1:T(8,128)(2,1)S(1)}, bf16[2048,24]{0,1:T(8,128)(2,1)S(1)}, u32[]{:S(2)}, u32[]{:S(2)}) collective-permute-start(bf16[2048,24]{0,1:T(8,128)(2,1)S(1)} %collective-permute-done.6), channel_id=1, source_target_pairs={{0,4},{4,8},{8,12},{12,0},{1,5},{5,9},{9,13},{13,1},{2,6},{6,10},{... | collective-permute-start | bytes 294920 | tf_op jit(solution)/shard_map/ppermute | solution.py:105
  15.7 10.3 %collective-permute-start.3 = (bf16[4,2048,24]{1,2,0:T(8,128)(2,1)S(1)}, bf16[4,2048,24]{1,2,0:T(8,128)(2,1)S(1)}, u32[]{:S(2)}, u32[]{:S(2)}) collective-permute-start(bf16[4,2048,24]{1,2,0:T(8,128)(2,1)S(1)} %gather_fusion), channel_id=1, source_target_pairs={{0,4},{4,8},{8,12},{12,0},{1,5},{5,9},{9,13},{13,1},{2,6},{6,10},{... | collective-permute-start | bytes 1179656 | tf_op jit(solution)/shard_map/ppermute | solution.py:93
  18.3 9.9 %collective-permute-start.9 = (bf16[4,2048,24]{1,2,0:T(8,128)(2,1)S(1)}, bf16[4,2048,24]{1,2,0:T(8,128)(2,1)}, u32[]{:S(2)}, u32[]{:S(2)}) collective-permute-start(bf16[4,2048,24]{1,2,0:T(8,128)(2,1)S(1)} %gather_fusion.2), channel_id=1, source_target_pairs={{0,1},{1,2},{2,3},{3,0},{4,5},{5,6},{6,7},{7,4},{8,9},{9,10},{10,1... | collective-permute-start | bytes 1179656 | tf_op jit(solution)/shard_map/ppermute | solution.py:93
  18.9 11.8 %collective-permute-start.5 = (bf16[4,2048,24]{1,2,0:T(8,128)(2,1)S(1)}, bf16[4,2048,24]{1,2,0:T(8,128)(2,1)S(1)}, u32[]{:S(2)}, u32[]{:S(2)}) collective-permute-start(bf16[4,2048,24]{1,2,0:T(8,128)(2,1)S(1)} %gather_fusion), channel_id=1, source_target_pairs={{0,12},{4,0},{8,4},{12,8},{1,13},{5,1},{9,5},{13,9},{2,14},{6,2},{... | collective-permute-start | bytes 1179656 | tf_op jit(solution)/shard_map/ppermute | solution.py:94
  26.0 9.3 %collective-permute-start.4 = (bf16[4,2048,24]{1,2,0:T(8,128)(2,1)S(1)}, bf16[4,2048,24]{1,2,0:T(8,128)(2,1)S(1)}, u32[]{:S(2)}, u32[]{:S(2)}) collective-permute-start(bf16[4,2048,24]{1,2,0:T(8,128)(2,1)S(1)} %collective-permute-done.3), channel_id=1, source_target_pairs={{0,4},{4,8},{8,12},{12,0},{1,5},{5,9},{9,13},{13,1},{2,6},{6,10},{... | collective-permute-start | bytes 1179656 | tf_op jit(solution)/shard_map/ppermute | solution.py:105
  26.0 10.2 %collective-permute-start.11 = (bf16[4,2048,24]{1,2,0:T(8,128)(2,1)S(1)}, bf16[4,2048,24]{1,2,0:T(8,128)(2,1)}, u32[]{:S(2)}, u32[]{:S(2)}) collective-permute-start(bf16[4,2048,24]{1,2,0:T(8,128)(2,1)S(1)} %gather_fusion.2), channel_id=1, source_target_pairs={{0,3},{1,0},{2,1},{3,2},{4,7},{5,4},{6,5},{7,6},{8,11},{9,8},{10,9... | collective-permute-start | bytes 1179656 | tf_op jit(solution)/shard_map/ppermute | solution.py:94
  28.2 9.9 %collective-permute-start.10 = (bf16[4,2048,24]{1,2,0:T(8,128)(2,1)}, bf16[4,2048,24]{1,2,0:T(8,128)(2,1)}, u32[]{:S(2)}, u32[]{:S(2)}) collective-permute-start(bf16[4,2048,24]{1,2,0:T(8,128)(2,1)} %collective-permute-done.9), channel_id=1, source_target_pairs={{0,1},{1,2},{2,3},{3,0},{4,5},{5,6},{6,7},{7,4},{8,9},{9,10},{10,1... | collective-permute-start | bytes 1179656 | tf_op jit(solution)/shard_map/ppermute | solution.py:105
  41.2 2.7 %copy-start = (bf16[2048,768]{1,0:T(8,128)(2,1)S(1)}, bf16[2048,768]{1,0:T(8,128)(2,1)}, u32[]{:S(2)}) copy-start(bf16[2048,768]{1,0:T(8,128)(2,1)} %param.3) | copy-start | bytes 9437188
  43.9 11.7 %copy-start.1 = (bf16[4,4,2048,48]{2,3,1,0:T(8,128)(2,1)}, bf16[4,4,2048,48]{2,3,1,0:T(8,128)(2,1)S(1)}, u32[]{:S(2)}) copy-start(bf16[4,4,2048,48]{2,3,1,0:T(8,128)(2,1)S(1)} %pad_maximum_fusion) | copy-start | bytes 9437188
  133.1 19.3 %copy-start.2 = (bf16[4,4,2048,48]{2,3,1,0:T(8,128)(2,1)S(1)}, bf16[4,4,2048,48]{2,3,1,0:T(8,128)(2,1)}, u32[]{:S(2)}) copy-start(bf16[4,4,2048,48]{2,3,1,0:T(8,128)(2,1)} %copy-done.1) | copy-start | bytes 9437188
  140.9 11.4 %all-to-all-start.5 = ((f32[16,1,2048]{2,1,0:T(1,128)}), f32[16,1,2048]{2,1,0:T(1,128)S(1)}, u32[]{:S(2)}, u32[]{:S(2)}) async-start(f32[16,1,2048]{2,1,0:T(1,128)} %broadcast_in_dim.19), calls=%async_computation.5 | async-start | bytes 262144 | tf_op jit(solution)/shard_map/all_to_all | solution.py:44
  177.1 5.9 %collective-permute-start.12 = (f32[4,96,2048]{2,1,0:T(8,128)S(1)}, f32[4,96,2048]{2,1,0:T(8,128)}, u32[]{:S(2)}, u32[]{:S(2)}) collective-permute-start(f32[4,96,2048]{2,1,0:T(8,128)S(1)} %dynamic-slice_bitcast_fusion), channel_id=1, source_target_pairs={{0,16},{16,0},{1,17},{17,1},{2,18},{18,2},{3,19},{19,3},{4,20},{20... | collective-permute-start | bytes 9437192 | tf_op jit(solution)/shard_map/ppermute | solution.py:76
  188.2 41.8 %all-to-all-start.6 = ((f32[4,96,2048]{2,1,0:T(8,128)}), f32[4,96,2048]{2,1,0:T(8,128)S(1)}, u32[]{:S(2)}, u32[]{:S(2)}) async-start(f32[4,96,2048]{2,1,0:T(8,128)} %bitcast_add_fusion), calls=%async_computation.6 | async-start | bytes 6291456 | tf_op jit(solution)/shard_map/all_to_all | solution.py:81

commit v13 on v11

--- a/solution.py
+++ b/solution.py
@@ -85,7 +85,7 @@
     return total
 
 
-def ring_gather(v, axis, n, split_far=True):
+def ring_gather(v, axis, n, split_far=True, reorder=True):
     if n == 1:
         return v[None]
     if n != 4:
@@ -104,6 +104,8 @@
     else:
         far = lax.ppermute(fwd, axis, [(i, (i + 1) % n) for i in range(n)])
     by_offset = jnp.stack([v, fwd, far, bwd])
+    if not reorder:
+        return by_offset
     idx = lax.axis_index(axis)
     return by_offset[(idx - jnp.arange(n)) % n]
 
@@ -119,10 +121,25 @@
         )
         return jnp.transpose(got, (1, 0, 2)).reshape(rows, nx * nz * blk)
     part_a, part_b = points[:, : blk // 2], points[:, blk // 2 :]
-    a_z = ring_gather(part_a, "z", nz, split_far=False)
-    b_x = ring_gather(part_b, "x", nx, split_far=False)
-    a_xz = ring_gather(a_z, "x", nx, split_far=False)
-    b_zx = ring_gather(b_x, "z", nz, split_far=False)
+    if nx != 4 or nz != 4:
+        a_xz = ring_gather(ring_gather(part_a, "z", nz, split_far=False), "x", nx, split_far=False)
+        b_zx = ring_gather(ring_gather(part_b, "x", nx, split_far=False), "z", nz, split_far=False)
+    else:
+        ix, iz = lax.axis_index("x"), lax.axis_index("z")
+        a_off = ring_gather(
+            ring_gather(part_a, "z", nz, split_far=False, reorder=False),
+            "x", nx, split_far=False, reorder=False,
+        )
+        b_off = ring_gather(
+            ring_gather(part_b, "x", nx, split_far=False, reorder=False),
+            "z", nz, split_far=False, reorder=False,
+        )
+        ox = (ix - jnp.arange(nx)) % nx
+        oz = (iz - jnp.arange(nz)) % nz
+        a_sel = (ox[:, None] * nz + oz[None, :]).reshape(-1)
+        b_sel = (oz[:, None] * nx + ox[None, :]).reshape(-1)
+        a_xz = a_off.reshape((nx * nz,) + a_off.shape[2:])[a_sel].reshape(a_off.shape)
+        b_zx = b_off.reshape((nx * nz,) + b_off.shape[2:])[b_sel].reshape(b_off.shape)
     full = jnp.concatenate([a_xz, jnp.transpose(b_zx, (1, 0, 2, 3))], axis=-1)
     return jnp.transpose(full, (2, 0, 1, 3)).reshape(rows, nx * nz * blk)
 

time: 239 us -> 242 us (1.013)
  other arithmetic: 54.5 us -> 57.1 us
    gather x5 -> x2, local copies, waits for them, and re-layouts: 5.32 us -> 1.3 us  [the longest x1 0.65 us: gather_features(): b_off.reshape((nx * nz,) + b_off.shape[2:])[b_sel].reshape(b_off.shape)]
    ppermute x4, waiting for transfers between devices: 9.06 us -> 5.61 us  [ring_gather(): fwd = lax.ppermute(v, axis, [(i, (i + 1) % n) for i in range(n)])]
    unnamed x6 -> x10, local copies, waits for them, and re-layouts: 0.01 us -> 2.85 us
    ppermute x4, waiting for transfers between devices: 10.5 us -> 13.1 us  [ring_gather(): far = lax.ppermute(fwd, axis, [(i, (i + 1) % n) for i in range(n)])]
  transfers between devices with their start and end apart: 31 -> 31, of which waited for: 24 -> 22; matrix products, arithmetic and copies ran while one was open for 5% -> 5% of each run, Pallas kernels for 0% -> 0%
where the time goes in v13:
time: 242 us; the launch traced here: 241 us
  waiting for transfers between devices  77.2 us (32%)
  other arithmetic  57.1 us (24%)
  starting transfers between devices  39.9 us (16%)
  matrix products  35.3 us (15%)
  blocking collectives  23.2 us (10%)
  local copies, waits for them, and re-layouts  7.77 us (3%)
    all_to_all x1, waiting for transfers between devices, scatter_features(): got = lax.all_to_all(x, 'y', 0, 0, tiled=False)  31.2 us
    all_to_all x2, blocking collectives, group_sum(): lax.all_to_all(jnp.broadcast_to(v[None], (n,) + v.shape), axes, 0, 0, til...  23.2 us
    reduce_sum x3, other arithmetic, local(): row_part = jnp.sum(kernel * col_scale[None, :], axis=1)  21.1 us
    ppermute x16, starting transfers between devices, axis_sum(): lax.ppermute(v, axis, [(i, (i + s) % n) for i in range(n)])  19.1 us
    reduce_sum x2, other arithmetic, local(): col_part = jnp.sum(kernel * row_scale[:, None], axis=0)  13.9 us
    ppermute x16, waiting for transfers between devices, axis_sum(): lax.ppermute(v, axis, [(i, (i + s) % n) for i in range(n)])  13.8 us
    ppermute x4, waiting for transfers between devices, ring_gather(): far = lax.ppermute(fwd, axis, [(i, (i + 1) % n) for i in range(n)])  13.1 us
    dot_general x1, matrix products, local(): lax.dot_general(gathered, lo, dims, preferred_element_type=jnp.float32)  12.2 us
  transfers between devices with their start and end apart: 31, of which 22 were waited for; matrix products, arithmetic and copies ran while one was open for 5% of the time, Pallas kernels for 0%

profile of v13, /device:TPU:0, one launch (start us, length us, event | category | flops | bytes accessed | tf_op | source)
XLA Modules:
  0.0 241.4 jit_solution(15044894863857380181)
XLA Ops:
  1.6 2.1 collective-permute-start
  3.7 2.2 collective-permute-start.2
  7.4 1.7 collective-permute-start.8
  9.2 2.6 %fusion.6 = f32[2048]{0:T(1024)S(1)} fusion(bf16[2048,768]{1,0:T(8,128)(2,1)} %param.3), kind=kLoop, calls=%fused_computation.18 | loop fusion | flops 4716544 | bytes 3153920 | tf_op jit(solution)/shard_map/reduce_sum | solution.py:18
  12.4 5.3 %collective-permute-done.7 = bf16[2048,24]{0,1:T(8,128)(2,1)S(1)} collective-permute-done((bf16[2048,24]{0,1:T(8,128)(2,1)S(1)}, bf16[2048,24]{0,1:T(8,128)(2,1)S(1)}, u32[]{:S(2)}, u32[]{:S(2)}) %collective-permute-start.7) | collective-permute-done | bytes 98336 | tf_op jit(solution)/shard_map/ppermute | solution.py:105
  19.0 2.5 %collective-permute-start.3 = (bf16[4,2048,24]{1,2,0:T(8,128)(2,1)}, bf16[4,2048,24]{1,2,0:T(8,128)(2,1)}, u32[]{:S(2)}, u32[]{:S(2)}) collective-permute-start(bf16[4,2048,24]{1,2,0:T(8,128)(2,1)} %get-tuple-element.5), channel_id=1, source_target_pairs={{0,4},{4,8},{8,12},{12,0},{1,5},{5,9},{9,13},{13,1},{2,6},{6,10},{... | collective-permute-start | bytes 1179656 | tf_op jit(solution)/shard_map/ppermute | solution.py:93
  22.3 5.6 %collective-permute-done.9 = bf16[4,2048,24]{1,2,0:T(8,128)(2,1)S(1)} collective-permute-done((bf16[4,2048,24]{1,2,0:T(8,128)(2,1)S(1)}, bf16[4,2048,24]{1,2,0:T(8,128)(2,1)S(1)}, u32[]{:S(2)}, u32[]{:S(2)}) %collective-permute-start.9) | collective-permute-done | bytes 393248 | tf_op jit(solution)/shard_map/ppermute | solution.py:93
  30.0 7.2 %collective-permute-done.10 = bf16[4,2048,24]{1,2,0:T(8,128)(2,1)S(1)} collective-permute-done((bf16[4,2048,24]{1,2,0:T(8,128)(2,1)S(1)}, bf16[4,2048,24]{1,2,0:T(8,128)(2,1)S(1)}, u32[]{:S(2)}, u32[]{:S(2)}) %collective-permute-start.10) | collective-permute-done | bytes 393248 | tf_op jit(solution)/shard_map/ppermute | solution.py:105
  41.7 1.9 pad_maximum_fusion
  44.5 11.8 %fusion.26 = (f32[2048]{0:T(1024)S(1)}, f32[2048,2048]{1,0:T(8,128)}) fusion(bf16[2048,768]{1,0:T(8,128)(2,1)S(1)} %copy-done.2, f32[2048]{0:T(1024)S(1)} %add_rsqrt_fusion, bf16[2048,768]{0,1:T(8,128)(2,1)S(1)} %bitcast.63, f32[2048]{0:T(1024)S(1)} %add_rsqrt_fusion.1), kind=kOutput, calls=%fused_computation.122 | convolution fusion | flops 6460274688 | bytes 23093248 | tf_op jit(solution)/shard_map/dot_general | solution.py:163
  57.5 3.2 %collective-permute-start.13 = (f32[2048]{0:T(1024)S(1)}, f32[2048]{0:T(1024)S(1)}, u32[]{:S(2)}, u32[]{:S(2)}) collective-permute-start(f32[2048]{0:T(1024)S(1)} %add.542), channel_id=1, source_target_pairs={{0,64},{32,96},{64,0},{96,32},{1,65},{33,97},{65,1},{97,33},{2,66}... | collective-permute-start | bytes 24584 | tf_op jit(solution)/shard_map/ppermute | solution.py:27
  61.4 2.6 %collective-permute-start.15 = (f32[2048]{0:T(1024)S(1)}, f32[2048]{0:T(1024)S(1)}, u32[]{:S(2)}, u32[]{:S(2)}) collective-permute-start(f32[2048]{0:T(1024)S(1)} %add.542), channel_id=1, source_target_pairs={{0,96},{32,0},{64,32},{96,64},{1,97},{33,1},{65,33},{97,65},{2,98}... | collective-permute-start | bytes 24584 | tf_op jit(solution)/shard_map/ppermute | solution.py:27
  65.6 7.0 %multiply_reduce_fusion.4 = f32[2048]{0:T(1024)S(1)} fusion(f32[2048,2048]{1,0:T(8,128)} %get-tuple-element.15, f32[2048]{0:T(1024)S(1)} %add_divide_fusion.2), kind=kLoop, calls=%fused_computation.9 | loop fusion | flops 8386560 | bytes 16793600 | tf_op jit(solution)/shard_map/reduce_sum | solution.py:168
  72.6 12.0 %all_to_all.23 = f32[16,1,2048]{2,1,0:T(1,128)S(1)} all-to-all(f32[16,1,2048]{2,1,0:T(1,128)S(1)} %broadcast_in_dim.6), channel_id=1, replica_groups=mesh['y'=4,'c'=2,'x'=4,'z'=4] {'x','z'}, dimensions={0} | all-to-all | bytes 262144 | tf_op jit(solution)/shard_map/all_to_all | solution.py:44
  84.7 6.9 %multiply_reduce_fusion.3 = f32[2048]{0:T(1024)S(1)} fusion(f32[2048,2048]{1,0:T(8,128)} %get-tuple-element.15, f32[2048]{0:T(1024)S(1)} %bitcast.84), kind=kLoop, calls=%fused_computation.8 | loop fusion | flops 8386560 | bytes 16793600 | tf_op jit(solution)/shard_map/reduce_sum | solution.py:166
  94.3 2.6 %collective-permute-start.18 = (f32[2048]{0:T(1024)S(1)}, f32[2048]{0:T(1024)S(1)}, u32[]{:S(2)}, u32[]{:S(2)}) collective-permute-start(f32[2048]{0:T(1024)S(1)} %add.562), channel_id=1, source_target_pairs={{0,32},{32,64},{64,96},{96,0},{1,33},{33,65},{65,97},{97,1},{2,34}... | collective-permute-start | bytes 24584 | tf_op jit(solution)/shard_map/ppermute | solution.py:27
  100.6 7.0 %multiply_reduce_fusion.2 = f32[2048]{0:T(1024)S(1)} fusion(f32[2048,2048]{1,0:T(8,128)} %get-tuple-element.15, f32[2048]{0:T(1024)S(1)} %add_divide_fusion.1), kind=kLoop, calls=%fused_computation.7 | loop fusion | flops 8386560 | bytes 16793600 | tf_op jit(solution)/shard_map/reduce_sum | solution.py:168
  107.7 11.2 %all_to_all.24 = f32[16,1,2048]{2,1,0:T(1,128)S(1)} all-to-all(f32[16,1,2048]{2,1,0:T(1,128)S(1)} %broadcast_in_dim.7), channel_id=1, replica_groups=mesh['y'=4,'c'=2,'x'=4,'z'=4] {'x','z'}, dimensions={0} | all-to-all | bytes 262144 | tf_op jit(solution)/shard_map/all_to_all | solution.py:44
  119.0 6.9 %multiply_reduce_fusion.1 = f32[2048]{0:T(1024)S(1)} fusion(f32[2048,2048]{1,0:T(8,128)} %get-tuple-element.15, f32[2048]{0:T(1024)S(1)} %bitcast.85), kind=kLoop, calls=%fused_computation.6 | loop fusion | flops 8386560 | bytes 16793600 | tf_op jit(solution)/shard_map/reduce_sum | solution.py:166
  127.8 2.1 collective-permute-start.22
  133.6 7.1 %multiply_reduce_fusion = f32[2048]{0:T(1024)S(1)} fusion(f32[2048,2048]{1,0:T(8,128)} %get-tuple-element.15, f32[2048]{0:T(1024)S(1)} %add_divide_fusion), kind=kLoop, calls=%fused_computation.5 | loop fusion | flops 8386560 | bytes 16793600 | tf_op jit(solution)/shard_map/reduce_sum | solution.py:168
  141.4 3.8 %all-to-all-start.2 = ((f32[16,1,2048]{2,1,0:T(1,128)}), f32[16,1,2048]{2,1,0:T(1,128)S(1)}, u32[]{:S(2)}, u32[]{:S(2)}) async-start(f32[16,1,2048]{2,1,0:T(1,128)} %broadcast_in_dim.8), calls=%async_computation.2 | async-start | bytes 262144 | tf_op jit(solution)/shard_map/all_to_all | solution.py:44
  145.1 7.7 %all-to-all-done.2 = f32[16,1,2048]{2,1,0:T(1,128)S(1)} async-done(((f32[16,1,2048]{2,1,0:T(1,128)}), f32[16,1,2048]{2,1,0:T(1,128)S(1)}, u32[]{:S(2)}, u32[]{:S(2)}) %all-to-all-start.2) | async-done | bytes 131104 | tf_op jit(solution)/shard_map/all_to_all | solution.py:44
  152.9 12.2 %fusion.1 = f32[768,2048]{1,0:T(8,128)} fusion(bf16[2048,768]{0,1:T(8,128)(2,1)S(1)} %bitcast.64, f32[2048,2048]{1,0:T(8,128)} %get-tuple-element.15, f32[2048]{0:T(1024)S(1)} %bitcast.81), kind=kOutput, calls=%fused_computation.12 | convolution fusion | flops 6459228160 | bytes 26222592 | tf_op jit(solution)/shard_map/dot_general | solution.py:177
  165.1 11.3 %add_multiply_fusion = f32[768,2048]{1,0:T(8,128)S(1)} fusion(f32[768,2048]{1,0:T(8,128)} %fusion.1, f32[2048]{0:T(1024)S(1)} %add_divide_fusion, bf16[2048,768]{0,1:T(8,128)(2,1)S(1)} %bitcast.65, f32[2048,2048]{1,0:T(8,128)} %get-tuple-element.15, f32[2048]{0:T(1024)S(1)} %bitcast.82), kind=kOutput, calls=%fused_computation.20 | convolution fusion | flops 6458179584 | bytes 32522240 | tf_op jit(solution)/shard_map/dot_general | solution.py:175
  176.5 2.7 %copy-done.1 = f32[768,2048]{1,0:T(8,128)} copy-done((f32[768,2048]{1,0:T(8,128)}, f32[768,2048]{1,0:T(8,128)S(1)}, u32[]{:S(2)}) %copy-start.1) | copy-done | bytes 6291480
  179.6 5.8 %collective-permute-done.24 = f32[4,96,2048]{2,1,0:T(8,128)} collective-permute-done((f32[4,96,2048]{2,1,0:T(8,128)S(1)}, f32[4,96,2048]{2,1,0:T(8,128)}, u32[]{:S(2)}, u32[]{:S(2)}) %collective-permute-start.24) | collective-permute-done | bytes 3145760 | tf_op jit(solution)/shard_map/ppermute | solution.py:76
  185.3 5.2 %bitcast_add_fusion = f32[4,96,2048]{2,1,0:T(8,128)} fusion(f32[4,96,2048]{2,1,0:T(8,128)} %collective-permute-done.24, f32[4,2,96,2048]{3,2,1,0:T(8,128)} %bitcast.62, s32[]{:T(128)S(6)} %select_n.58), kind=kLoop, calls=%fused_computation.24 | loop fusion | flops 786432 | bytes 9437188 | tf_op jit(solution)/shard_map/add | solution.py:76
  190.6 3.7 %all-to-all-start.3 = ((f32[4,96,2048]{2,1,0:T(8,128)}), f32[4,96,2048]{2,1,0:T(8,128)S(1)}, u32[]{:S(2)}, u32[]{:S(2)}) async-start(f32[4,96,2048]{2,1,0:T(8,128)} %bitcast_add_fusion), calls=%async_computation.3 | async-start | bytes 6291456 | tf_op jit(solution)/shard_map/all_to_all | solution.py:81
  194.3 6.9 %multiply_reduce_fusion.5 = f32[2048]{0:T(1024)S(1)} fusion(f32[2048,2048]{1,0:T(8,128)} %get-tuple-element.15, f32[2048]{0:T(1024)S(1)} %bitcast.83), kind=kLoop, calls=%fused_computation.11 | loop fusion | flops 8386560 | bytes 16793600 | tf_op jit(solution)/shard_map/reduce_sum | solution.py:179
  201.2 31.2 %all-to-all-done.3 = f32[4,96,2048]{2,1,0:T(8,128)S(1)} async-done(((f32[4,96,2048]{2,1,0:T(8,128)}), f32[4,96,2048]{2,1,0:T(8,128)S(1)}, u32[]{:S(2)}, u32[]{:S(2)}) %all-to-all-start.3) | async-done | bytes 3145760 | tf_op jit(solution)/shard_map/all_to_all | solution.py:81
  236.1 1.8 collective-permute-start.28
  (95 shorter events, 36.7 us)
Async XLA Ops:
  1.6 10.8 %collective-permute-start = (bf16[2048,24]{0,1:T(8,128)(2,1)S(1)}, bf16[2048,24]{0,1:T(8,128)(2,1)S(1)}, u32[]{:S(2)}, u32[]{:S(2)}) collective-permute-start(bf16[2048,24]{0,1:T(8,128)(2,1)S(1)} %get-tuple-element.11), channel_id=1, source_target_pairs={{0,1},{1,2},{2,3},{3,0},{4,5},{5,6},{6,7},{7,4},{8,9},{9,10},{10,1... | collective-permute-start | bytes 294920 | tf_op jit(solution)/shard_map/ppermute | solution.py:93
  3.7 14.1 %collective-permute-start.2 = (bf16[2048,24]{0,1:T(8,128)(2,1)S(1)}, bf16[2048,24]{0,1:T(8,128)(2,1)S(1)}, u32[]{:S(2)}, u32[]{:S(2)}) collective-permute-start(bf16[2048,24]{0,1:T(8,128)(2,1)S(1)} %get-tuple-element.11), channel_id=1, source_target_pairs={{0,3},{1,0},{2,1},{3,2},{4,7},{5,4},{6,5},{7,6},{8,11},{9,8},{10,9... | collective-permute-start | bytes 294920 | tf_op jit(solution)/shard_map/ppermute | solution.py:94
  5.9 5.9 %collective-permute-start.6 = (bf16[2048,24]{0,1:T(8,128)(2,1)S(1)}, bf16[2048,24]{0,1:T(8,128)(2,1)S(1)}, u32[]{:S(2)}, u32[]{:S(2)}) collective-permute-start(bf16[2048,24]{0,1:T(8,128)(2,1)S(1)} %get-tuple-element.10), channel_id=1, source_target_pairs={{0,4},{4,8},{8,12},{12,0},{1,5},{5,9},{9,13},{13,1},{2,6},{6,10},{... | collective-permute-start | bytes 294920 | tf_op jit(solution)/shard_map/ppermute | solution.py:93
  7.4 5.0 %collective-permute-start.8 = (bf16[2048,24]{0,1:T(8,128)(2,1)S(1)}, bf16[2048,24]{0,1:T(8,128)(2,1)S(1)}, u32[]{:S(2)}, u32[]{:S(2)}) collective-permute-start(bf16[2048,24]{0,1:T(8,128)(2,1)S(1)} %get-tuple-element.10), channel_id=1, source_target_pairs={{0,12},{4,0},{8,4},{12,8},{1,13},{5,1},{9,5},{13,9},{2,14},{6,2},{... | collective-permute-start | bytes 294920 | tf_op jit(solution)/shard_map/ppermute | solution.py:94
  11.8 5.8 %collective-permute-start.7 = (bf16[2048,24]{0,1:T(8,128)(2,1)S(1)}, bf16[2048,24]{0,1:T(8,128)(2,1)S(1)}, u32[]{:S(2)}, u32[]{:S(2)}) collective-permute-start(bf16[2048,24]{0,1:T(8,128)(2,1)S(1)} %collective-permute-done.6), channel_id=1, source_target_pairs={{0,4},{4,8},{8,12},{12,0},{1,5},{5,9},{9,13},{13,1},{2,6},{6,10},{... | collective-permute-start | bytes 294920 | tf_op jit(solution)/shard_map/ppermute | solution.py:105
  12.4 5.8 %collective-permute-start.1 = (bf16[2048,24]{0,1:T(8,128)(2,1)S(1)}, bf16[2048,24]{0,1:T(8,128)(2,1)S(1)}, u32[]{:S(2)}, u32[]{:S(2)}) collective-permute-start(bf16[2048,24]{0,1:T(8,128)(2,1)S(1)} %collective-permute-done), channel_id=1, source_target_pairs={{0,1},{1,2},{2,3},{3,0},{4,5},{5,6},{6,7},{7,4},{8,9},{9,10},{10,1... | collective-permute-start | bytes 294920 | tf_op jit(solution)/shard_map/ppermute | solution.py:105
  17.8 10.1 %collective-permute-start.9 = (bf16[4,2048,24]{1,2,0:T(8,128)(2,1)S(1)}, bf16[4,2048,24]{1,2,0:T(8,128)(2,1)S(1)}, u32[]{:S(2)}, u32[]{:S(2)}) collective-permute-start(bf16[4,2048,24]{1,2,0:T(8,128)(2,1)S(1)} %get-tuple-element.7), channel_id=1, source_target_pairs={{0,1},{1,2},{2,3},{3,0},{4,5},{5,6},{6,7},{7,4},{8,9},{9,10},{10,1... | collective-permute-start | bytes 1179656 | tf_op jit(solution)/shard_map/ppermute | solution.py:93
  19.0 10.3 %collective-permute-start.3 = (bf16[4,2048,24]{1,2,0:T(8,128)(2,1)}, bf16[4,2048,24]{1,2,0:T(8,128)(2,1)}, u32[]{:S(2)}, u32[]{:S(2)}) collective-permute-start(bf16[4,2048,24]{1,2,0:T(8,128)(2,1)} %get-tuple-element.5), channel_id=1, source_target_pairs={{0,4},{4,8},{8,12},{12,0},{1,5},{5,9},{9,13},{13,1},{2,6},{6,10},{... | collective-permute-start | bytes 1179656 | tf_op jit(solution)/shard_map/ppermute | solution.py:93
  21.6 8.4 %collective-permute-start.11 = (bf16[4,2048,24]{1,2,0:T(8,128)(2,1)S(1)}, bf16[4,2048,24]{1,2,0:T(8,128)(2,1)S(1)}, u32[]{:S(2)}, u32[]{:S(2)}) collective-permute-start(bf16[4,2048,24]{1,2,0:T(8,128)(2,1)S(1)} %get-tuple-element.7), channel_id=1, source_target_pairs={{0,3},{1,0},{2,1},{3,2},{4,7},{5,4},{6,5},{7,6},{8,11},{9,8},{10,9... | collective-permute-start | bytes 1179656 | tf_op jit(solution)/shard_map/ppermute | solution.py:94
  27.9 9.2 %collective-permute-start.10 = (bf16[4,2048,24]{1,2,0:T(8,128)(2,1)S(1)}, bf16[4,2048,24]{1,2,0:T(8,128)(2,1)S(1)}, u32[]{:S(2)}, u32[]{:S(2)}) collective-permute-start(bf16[4,2048,24]{1,2,0:T(8,128)(2,1)S(1)} %collective-permute-done.9), channel_id=1, source_target_pairs={{0,1},{1,2},{2,3},{3,0},{4,5},{5,6},{6,7},{7,4},{8,9},{9,10},{10,1... | collective-permute-start | bytes 1179656 | tf_op jit(solution)/shard_map/ppermute | solution.py:105
  27.9 11.4 %collective-permute-start.5 = (bf16[4,2048,24]{1,2,0:T(8,128)(2,1)}, bf16[4,2048,24]{1,2,0:T(8,128)(2,1)}, u32[]{:S(2)}, u32[]{:S(2)}) collective-permute-start(bf16[4,2048,24]{1,2,0:T(8,128)(2,1)} %get-tuple-element.5), channel_id=1, source_target_pairs={{0,12},{4,0},{8,4},{12,8},{1,13},{5,1},{9,5},{13,9},{2,14},{6,2},{... | collective-permute-start | bytes 1179656 | tf_op jit(solution)/shard_map/ppermute | solution.py:94
  29.3 10.3 %collective-permute-start.4 = (bf16[4,2048,24]{1,2,0:T(8,128)(2,1)}, bf16[4,2048,24]{1,2,0:T(8,128)(2,1)}, u32[]{:S(2)}, u32[]{:S(2)}) collective-permute-start(bf16[4,2048,24]{1,2,0:T(8,128)(2,1)} %collective-permute-done.3), channel_id=1, source_target_pairs={{0,4},{4,8},{8,12},{12,0},{1,5},{5,9},{9,13},{13,1},{2,6},{6,10},{... | collective-permute-start | bytes 1179656 | tf_op jit(solution)/shard_map/ppermute | solution.py:105
  56.3 1.2 collective-permute-start.12
  57.5 6.4 %collective-permute-start.13 = (f32[2048]{0:T(1024)S(1)}, f32[2048]{0:T(1024)S(1)}, u32[]{:S(2)}, u32[]{:S(2)}) collective-permute-start(f32[2048]{0:T(1024)S(1)} %add.542), channel_id=1, source_target_pairs={{0,64},{32,96},{64,0},{96,32},{1,65},{33,97},{65,1},{97,33},{2,66}... | collective-permute-start | bytes 24584 | tf_op jit(solution)/shard_map/ppermute | solution.py:27
  60.7 4.9 %collective-permute-start.14 = (f32[2048]{0:T(1024)S(1)}, f32[2048]{0:T(1024)S(1)}, u32[]{:S(2)}, u32[]{:S(2)}) collective-permute-start(f32[2048]{0:T(1024)S(1)} %add.542), channel_id=1, source_target_pairs={{0,32},{32,64},{64,96},{96,0},{1,33},{33,65},{65,97},{97,1},{2,34}... | collective-permute-start | bytes 24584 | tf_op jit(solution)/shard_map/ppermute | solution.py:27
  61.4 4.2 %collective-permute-start.15 = (f32[2048]{0:T(1024)S(1)}, f32[2048]{0:T(1024)S(1)}, u32[]{:S(2)}, u32[]{:S(2)}) collective-permute-start(f32[2048]{0:T(1024)S(1)} %add.542), channel_id=1, source_target_pairs={{0,96},{32,0},{64,32},{96,64},{1,97},{33,1},{65,33},{97,65},{2,98}... | collective-permute-start | bytes 24584 | tf_op jit(solution)/shard_map/ppermute | solution.py:27
  91.6 1.3 collective-permute-start.16
  92.9 5.2 %collective-permute-start.17 = (f32[2048]{0:T(1024)S(1)}, f32[2048]{0:T(1024)S(1)}, u32[]{:S(2)}, u32[]{:S(2)}) collective-permute-start(f32[2048]{0:T(1024)S(1)} %add.562), channel_id=1, source_target_pairs={{0,64},{32,96},{64,0},{96,32},{1,65},{33,97},{65,1},{97,33},{2,66}... | collective-permute-start | bytes 24584 | tf_op jit(solution)/shard_map/ppermute | solution.py:27
  94.3 4.9 %collective-permute-start.18 = (f32[2048]{0:T(1024)S(1)}, f32[2048]{0:T(1024)S(1)}, u32[]{:S(2)}, u32[]{:S(2)}) collective-permute-start(f32[2048]{0:T(1024)S(1)} %add.562), channel_id=1, source_target_pairs={{0,32},{32,64},{64,96},{96,0},{1,33},{33,65},{65,97},{97,1},{2,34}... | collective-permute-start | bytes 24584 | tf_op jit(solution)/shard_map/ppermute | solution.py:27
  97.0 3.7 %collective-permute-start.19 = (f32[2048]{0:T(1024)S(1)}, f32[2048]{0:T(1024)S(1)}, u32[]{:S(2)}, u32[]{:S(2)}) collective-permute-start(f32[2048]{0:T(1024)S(1)} %add.562), channel_id=1, source_target_pairs={{0,96},{32,0},{64,32},{96,64},{1,97},{33,1},{65,33},{97,65},{2,98}... | collective-permute-start | bytes 24584 | tf_op jit(solution)/shard_map/ppermute | solution.py:27
  126.0 1.3 collective-permute-start.20
  127.2 5.2 %collective-permute-start.21 = (f32[2048]{0:T(1024)S(1)}, f32[2048]{0:T(1024)S(1)}, u32[]{:S(2)}, u32[]{:S(2)}) collective-permute-start(f32[2048]{0:T(1024)S(1)} %add.582), channel_id=1, source_target_pairs={{0,64},{32,96},{64,0},{96,32},{1,65},{33,97},{65,1},{97,33},{2,66}... | collective-permute-start | bytes 24584 | tf_op jit(solution)/shard_map/ppermute | solution.py:27
  127.8 4.9 %collective-permute-start.22 = (f32[2048]{0:T(1024)S(1)}, f32[2048]{0:T(1024)S(1)}, u32[]{:S(2)}, u32[]{:S(2)}) collective-permute-start(f32[2048]{0:T(1024)S(1)} %add.582), channel_id=1, source_target_pairs={{0,32},{32,64},{64,96},{96,0},{1,33},{33,65},{65,97},{97,1},{2,34}... | collective-permute-start | bytes 24584 | tf_op jit(solution)/shard_map/ppermute | solution.py:27
  129.9 3.7 %collective-permute-start.23 = (f32[2048]{0:T(1024)S(1)}, f32[2048]{0:T(1024)S(1)}, u32[]{:S(2)}, u32[]{:S(2)}) collective-permute-start(f32[2048]{0:T(1024)S(1)} %add.582), channel_id=1, source_target_pairs={{0,96},{32,0},{64,32},{96,64},{1,97},{33,1},{65,33},{97,65},{2,98}... | collective-permute-start | bytes 24584 | tf_op jit(solution)/shard_map/ppermute | solution.py:27
  133.6 19.3 %copy-start.4 = (bf16[4,4,2048,48]{2,3,1,0:T(8,128)(2,1)S(1)}, bf16[4,4,2048,48]{2,3,1,0:T(8,128)(2,1)}, u32[]{:S(2)}) copy-start(bf16[4,4,2048,48]{2,3,1,0:T(8,128)(2,1)} %copy-done.3) | copy-start | bytes 9437188
  141.4 11.4 %all-to-all-start.2 = ((f32[16,1,2048]{2,1,0:T(1,128)}), f32[16,1,2048]{2,1,0:T(1,128)S(1)}, u32[]{:S(2)}, u32[]{:S(2)}) async-start(f32[16,1,2048]{2,1,0:T(1,128)} %broadcast_in_dim.8), calls=%async_computation.2 | async-start | bytes 262144 | tf_op jit(solution)/shard_map/all_to_all | solution.py:44
  179.5 5.9 %collective-permute-start.24 = (f32[4,96,2048]{2,1,0:T(8,128)S(1)}, f32[4,96,2048]{2,1,0:T(8,128)}, u32[]{:S(2)}, u32[]{:S(2)}) collective-permute-start(f32[4,96,2048]{2,1,0:T(8,128)S(1)} %dynamic-slice_bitcast_fusion), channel_id=1, source_target_pairs={{0,16},{16,0},{1,17},{17,1},{2,18},{18,2},{3,19},{19,3},{4,20},{20... | collective-permute-start | bytes 9437192 | tf_op jit(solution)/shard_map/ppermute | solution.py:76
  190.6 41.8 %all-to-all-start.3 = ((f32[4,96,2048]{2,1,0:T(8,128)}), f32[4,96,2048]{2,1,0:T(8,128)S(1)}, u32[]{:S(2)}, u32[]{:S(2)}) async-start(f32[4,96,2048]{2,1,0:T(8,128)} %bitcast_add_fusion), calls=%async_computation.3 | async-start | bytes 6291456 | tf_op jit(solution)/shard_map/all_to_all | solution.py:81
  232.7 1.3 collective-permute-start.25
  233.9 5.4 %collective-permute-start.26 = (f32[2,2048]{1,0:T(2,128)S(1)}, f32[2,2048]{1,0:T(2,128)S(1)}, u32[]{:S(2)}, u32[]{:S(2)}) collective-permute-start(f32[2,2048]{1,0:T(2,128)S(1)} %fusion.21), channel_id=1, source_target_pairs={{0,64},{32,96},{64,0},{96,32},{1,65},{33,97},{65,1},{97,33},{2,66}... | collective-permute-start | bytes 49160 | tf_op jit(solution)/shard_map/ppermute | solution.py:27
  234.6 4.9 %collective-permute-start.27 = (f32[2,2048]{1,0:T(2,128)S(1)}, f32[2,2048]{1,0:T(2,128)S(1)}, u32[]{:S(2)}, u32[]{:S(2)}) collective-permute-start(f32[2,2048]{1,0:T(2,128)S(1)} %fusion.21), channel_id=1, source_target_pairs={{0,32},{32,64},{64,96},{96,0},{1,33},{33,65},{65,97},{97,1},{2,34}... | collective-permute-start | bytes 49160 | tf_op jit(solution)/shard_map/ppermute | solution.py:27
  236.1 3.7 %collective-permute-start.28 = (f32[2,2048]{1,0:T(2,128)S(1)}, f32[2,2048]{1,0:T(2,128)S(1)}, u32[]{:S(2)}, u32[]{:S(2)}) collective-permute-start(f32[2,2048]{1,0:T(2,128)S(1)} %fusion.21), channel_id=1, source_target_pairs={{0,96},{32,0},{64,32},{96,64},{1,97},{33,1},{65,33},{97,65},{2,98}... | collective-permute-start | bytes 49160 | tf_op jit(solution)/shard_map/ppermute | solution.py:27
  (4 other events, 20.1 us)
